TPU v7x, 128 devices: a whole 4x4x4 slice. The times are simulated.
128 devices in a mesh: dp: 8 (over y, core), expert: 16 (over x, z).
Axes of the slice: x: 4, y: 4, z: 4, core: 2. Of those that a mesh axis runs over, the one named last changes fastest.
Arguments:
- tokens: bfloat16 [16384, 7168], P(('dp', 'expert')), may hold values from -6 to 6
- chosen: int32 [16, 288], replicated, may hold values from 0 to 16383, as said below
- combine_fixed: int32 [16, 288], replicated, may hold values from 6554 to 65535
- w_gate: bfloat16 [16, 7168, 2048], P('expert', None, 'dp'), may hold values from -0.0625 to 0.0625
- w_up: bfloat16 [16, 7168, 2048], P('expert', None, 'dp'), may hold values from -0.0625 to 0.0625
- w_down: bfloat16 [16, 2048, 7168], P('expert', 'dp'), may hold values from -0.125 to 0.125
Outputs:
- mixed: bfloat16 [16384, 7168], P(('dp', 'expert'))
Inputs may be any that keep to these rules, and one draw needn't show every extreme that they name: `chosen`: in each row the 288 token numbers differ. Call tokens k * 128 to (k + 1) * 128 - 1 the tokens of device k: a row holds at most 4 tokens of one device, and exactly 4 of some device.
All inputs are finite; a program needn't handle non-finite values.
Results may differ from a plain program's by a relative error of at most 0.015.
Values may be sent and summed in bfloat16 or wider, within the bound.
No kernel may reach another device: no remote copies, remote signals or barrier semaphores. Data moves between devices by JAX's collectives and lax.ppermute only.
A program may use at most 128 MiB of HBM per device.

v0:
```python
import jax
import jax.numpy as jnp
from jax import lax
from jax.sharding import PartitionSpec as P


def slot_tables(chosen, tok_count, worker_ordinal):
    owners = chosen // tok_count
    onehot = (
        owners[:, :, None] == jnp.arange(worker_ordinal, dtype=jnp.int32)[None, None, :]
    ).astype(jnp.int32)
    earlier = jnp.cumsum(onehot, axis=1) - onehot
    ranks = jnp.sum(earlier * onehot, axis=2)
    return (owners, ranks)


def shards(tokens, chosen, combine_fixed, w_gate, w_up, w_down):
    dp_count = lax.axis_size("dp")
    ex_count = lax.axis_size("expert")
    worker_ordinal = dp_count * ex_count
    tok_count, model_width = tokens.shape
    expert_total, capacity = chosen.shape
    slot_count = min(tok_count, max(4, 2 * capacity // worker_ordinal))
    my_index = lax.axis_index("dp") * ex_count + lax.axis_index("expert")
    owners, ranks = slot_tables(chosen, tok_count, worker_ordinal)
    local_idx = chosen - owners * tok_count
    is_mine = owners == my_index
    matches = is_mine[:, :, None] & (
        ranks[:, :, None] == jnp.arange(slot_count, dtype=jnp.int32)[None, None, :]
    )
    match_int = matches.astype(jnp.int32)
    source_idx = jnp.sum(match_int * local_idx[:, :, None], axis=1)
    present = jnp.sum(match_int, axis=1)
    scaled = combine_fixed.astype(jnp.float32) / 65536.0
    weights = jnp.sum(matches.astype(jnp.float32) * scaled[:, :, None], axis=1)
    send_rows = jnp.take(tokens, source_idx.reshape(-1), axis=0)
    send_rows = jnp.where(present.reshape(-1, 1) > 0, send_rows, jnp.zeros_like(send_rows))
    send_rows = send_rows.reshape(expert_total, slot_count, model_width)
    my_expert = lax.axis_index("expert")
    my_owners = lax.dynamic_index_in_dim(owners, my_expert, 0, keepdims=False)
    my_ranks = lax.dynamic_index_in_dim(ranks, my_expert, 0, keepdims=False)
    positions = my_owners * slot_count + my_ranks
    spread = jnp.broadcast_to(send_rows[None], (dp_count, expert_total, slot_count, model_width))
    spread = spread.reshape(worker_ordinal, slot_count, model_width)
    arrived = lax.all_to_all(spread, ("dp", "expert"), split_axis=0, concat_axis=0, tiled=True)
    arrived_rows = arrived.reshape(worker_ordinal * slot_count, model_width)
    picked = jnp.take(arrived_rows, positions, axis=0)
    gate_act = jnp.dot(picked, w_gate[0], preferred_element_type=jnp.float32)
    up_act = jnp.dot(picked, w_up[0], preferred_element_type=jnp.float32)
    hidden = (jax.nn.silu(gate_act) * up_act).astype(jnp.bfloat16)
    result = jnp.dot(hidden, w_down[0], preferred_element_type=jnp.float32).astype(jnp.bfloat16)
    back_rows = (
        jnp.zeros((worker_ordinal * slot_count, model_width), jnp.bfloat16)
        .at[positions]
        .set(result)
    )
    returned = lax.all_to_all(
        back_rows.reshape(worker_ordinal, slot_count, model_width),
        ("dp", "expert"),
        split_axis=0,
        concat_axis=0,
        tiled=True,
    )
    summed = jnp.sum(
        returned.reshape(dp_count, expert_total, slot_count, model_width), axis=0, dtype=jnp.float32
    )
    placed = (jnp.arange(tok_count, dtype=jnp.int32)[:, None] == source_idx.reshape(1, -1)) & (
        present.reshape(1, -1) > 0
    )
    mixing = jnp.where(placed, weights.reshape(1, -1), 0.0)
    mixed = jnp.dot(
        mixing,
        summed.reshape(-1, model_width),
        precision=lax.Precision.HIGHEST,
        preferred_element_type=jnp.float32,
    )
    return mixed.astype(jnp.bfloat16)


def solution(mesh):
    in_specs = (
        P(("dp", "expert"), None),
        P(),
        P(),
        P("expert", None, "dp"),
        P("expert", None, "dp"),
        P("expert", "dp", None),
    )
    out_specs = P(("dp", "expert"), None)
    return jax.shard_map(shards, mesh=mesh, in_specs=in_specs, out_specs=out_specs, check_vma=False)
```

profile of v0, /device:TPU:6, one launch (start us, length us, event | category | flops | bytes accessed | tf_op | source)
XLA Modules:
  0.0 365.9 jit_solution(12126968162565784281)
XLA Ops:
  0.0 0.9 multiply_subtract_fusion
  0.9 0.8 broadcast_compare_fusion
  1.8 0.9 iota_compare_fusion
  2.6 0.2 pad_convert_fusion
  2.9 71.5 %fusion.32 = s32[16,128,3,128]{1,0,3,2:T(8,128)S(1)} fusion(s32[16,128,3,128]{1,0,3,2:T(8,128)S(1)} %bitcast.33), kind=kOutput, calls=%fused_computation.64 | output fusion | flops 99876864 | bytes 6291456 | tf_op jit(solution)/shard_map/reduce-window
  74.4 0.2 broadcast_add_fusion
  74.6 5.8 %fusion.8 = s32[16,288]{0,1:T(8,128)S(1)} fusion(s32[16,384,128]{2,0,1:T(8,128)S(1)} %bitcast.34, s32[16,288]{0,1:T(8,128)S(1)} %copy.87), kind=kLoop, calls=%fused_computation.17 | loop fusion | flops 2944512 | bytes 2396160 | tf_op jit(solution)/shard_map/reduce_sum | solution.py:13
  80.5 0.3 convert_reduce_fusion.1
  80.8 0.1 copy.95
  81.2 1.1 gather_fusion
  82.3 0.3 gather.11
  82.6 0.5 select_select_fusion
  83.2 5.5 %broadcast_in_dim.71 = bf16[8,16,4,7168]{3,2,1,0:T(4,128)(2,1)} broadcast(bf16[16,4,7168]{2,1,0:T(4,128)(2,1)S(1)} %select_select_fusion), dimensions={1,2,3} | broadcast | bytes 8257536 | tf_op jit(solution)/shard_map/broadcast_in_dim | solution.py:43
  88.7 11.3 %all-to-all-start = ((bf16[128,4,7168]{2,1,0:T(4,128)(2,1)}), bf16[128,4,7168]{2,1,0:T(4,128)(2,1)}, u32[]{:S(2)}, u32[]{:S(2)}) async-start(bf16[128,4,7168]{2,1,0:T(4,128)(2,1)} %bitcast.31), calls=%async_computation | async-start | bytes 14680064 | tf_op jit(solution)/shard_map/all_to_all | solution.py:45
  100.1 88.8 %all-to-all-done = bf16[128,4,7168]{2,1,0:T(4,128)(2,1)} async-done(((bf16[128,4,7168]{2,1,0:T(4,128)(2,1)}), bf16[128,4,7168]{2,1,0:T(4,128)(2,1)}, u32[]{:S(2)}, u32[]{:S(2)}) %all-to-all-start) | async-done | bytes 7340064 | tf_op jit(solution)/shard_map/all_to_all | solution.py:45
  188.9 12.1 %reshape.155 = bf16[512,7168]{1,0:T(8,128)(2,1)} reshape(bf16[128,4,7168]{2,1,0:T(4,128)(2,1)} %all-to-all-done) | data formatting | bytes 14680064 | tf_op jit(solution)/shard_map/reshape | solution.py:46
  201.0 17.2 %gather_fusion.1 = bf16[288,7168]{1,0:T(8,128)(2,1)} fusion(bf16[512,7168]{1,0:T(8,128)(2,1)} %reshape.155, s32[1024]{0:T(1024)S(1)} %pad_clamp_fusion), kind=kCustom, calls=%fused_computation.1 | custom fusion | bytes 8258688 | tf_op jit(solution)/shard_map/jit(_take)/gather | solution.py:47
  218.2 4.7 %fusion.3 = f32[288,256]{1,0:T(8,128)S(1)} fusion(bf16[1,7168,256]{2,1,0:T(8,128)(2,1)} %param.9, bf16[288,7168]{1,0:T(8,128)(2,1)} %gather_fusion.1, pred[288]{0:T(512)(128)(4,1)S(1)} %compare_and_fusion.1), kind=kOutput, calls=%fused_computation.10 | convolution fusion | flops 1059028992 | bytes 8093984 | tf_op jit(solution)/shard_map/dot_general | solution.py:48
  222.9 0.8 copy-done.5
  223.8 1.3 fusion.12
  225.1 0.8 copy-done.3
  225.8 3.3 convolution_convert_fusion
  229.1 11.9 %scatter_custom_fusion = bf16[512,7168]{1,0:T(8,128)(2,1)} fusion(s32[288]{0:T(512)S(1)} %fusion.26, bf16[288,7168]{1,0:T(8,128)(2,1)} %convolution_convert_fusion, bf16[]{:T(256)} %constant.82.clone.1), kind=kCustom, calls=%fused_computation.12 | custom fusion | bytes 7340544 | tf_op jit(solution)/shard_map/scatter | solution.py:55
  241.0 12.6 %reshape.156 = bf16[128,4,7168]{2,1,0:T(4,128)(2,1)} reshape(bf16[512,7168]{1,0:T(8,128)(2,1)} %scatter_custom_fusion) | data formatting | bytes 14680064 | tf_op jit(solution)/shard_map/reshape | solution.py:58
  253.7 5.4 %all-to-all-start.1 = ((bf16[128,4,7168]{2,1,0:T(4,128)(2,1)}), bf16[128,4,7168]{2,1,0:T(4,128)(2,1)}, u32[]{:S(2)}, u32[]{:S(2)}) async-start(bf16[128,4,7168]{2,1,0:T(4,128)(2,1)} %reshape.156), calls=%async_computation.1 | async-start | bytes 14680064 | tf_op jit(solution)/shard_map/all_to_all | solution.py:57
  259.3 0.1 select_reduce_fusion
  259.6 88.5 %all-to-all-done.1 = bf16[128,4,7168]{2,1,0:T(4,128)(2,1)} async-done(((bf16[128,4,7168]{2,1,0:T(4,128)(2,1)}), bf16[128,4,7168]{2,1,0:T(4,128)(2,1)}, u32[]{:S(2)}, u32[]{:S(2)}) %all-to-all-start.1) | async-done | bytes 7340064 | tf_op jit(solution)/shard_map/all_to_all | solution.py:57
  348.1 5.3 %copy.97 = bf16[128,4,7168]{2,0,1:T(8,128)(2,1)S(1)} copy(bf16[128,4,7168]{2,1,0:T(4,128)(2,1)} %all-to-all-done.1) | data formatting | bytes 14680064 | tf_op jit(solution)/shard_map/all_to_all | solution.py:57
  353.4 1.2 convert_reduce_fusion
  354.6 2.4 copy.99
  357.0 2.9 reshape.157
  359.9 5.8 %convolution_convert_fusion.1 = bf16[128,7168]{1,0:T(8,128)(2,1)} fusion(f32[64,7168]{1,0:T(8,128)} %reshape.157, f32[64]{0:T(128)S(1)} %broadcast_in_dim.62, s32[64]{0:T(128)S(1)} %eq.66, pred[64]{0:T(512)(128)(4,1)S(1)} %gt.25), kind=kOutput, calls=%fused_computation.5 | convolution fusion | flops 705585152 | bytes 3670592 | tf_op jit(solution)/shard_map/dot_general | solution.py:71
  (29 shorter events, 0.9 us)
Async XLA Ops:
  0.0 81.2 %copy-start = (bf16[128,7168]{1,0:T(8,128)(2,1)S(1)}, bf16[128,7168]{1,0:T(8,128)(2,1)}, u32[]{:S(2)}) copy-start(bf16[128,7168]{1,0:T(8,128)(2,1)} %param.6) | copy-start | bytes 5505028
  88.7 100.2 %all-to-all-start = ((bf16[128,4,7168]{2,1,0:T(4,128)(2,1)}), bf16[128,4,7168]{2,1,0:T(4,128)(2,1)}, u32[]{:S(2)}, u32[]{:S(2)}) async-start(bf16[128,4,7168]{2,1,0:T(4,128)(2,1)} %bitcast.31), calls=%async_computation | async-start | bytes 14680064 | tf_op jit(solution)/shard_map/all_to_all | solution.py:45
  218.2 4.7 %copy-start.2 = (bf16[288,7168]{1,0:T(8,128)(2,1)S(1)}, bf16[288,7168]{1,0:T(8,128)(2,1)}, u32[]{:S(2)}) copy-start(bf16[288,7168]{1,0:T(8,128)(2,1)} %gather_fusion.1) | copy-start | bytes 12386308
  218.2 5.6 %copy-start.5 = (bf16[1,7168,256]{2,1,0:T(8,128)(2,1)S(1)}, bf16[1,7168,256]{2,1,0:T(8,128)(2,1)}, u32[]{:S(2)}) copy-start(bf16[1,7168,256]{2,1,0:T(8,128)(2,1)} %param.10) | copy-start | bytes 11010052
  223.8 2.0 copy-start.3
  253.7 5.6 %copy-start.4 = (s32[16,288]{1,0:T(8,128)S(1)}, s32[16,288]{1,0:T(8,128)}, u32[]{:S(2)}) copy-start(s32[16,288]{1,0:T(8,128)} %param.8) | copy-start | bytes 55300
  253.7 94.4 %all-to-all-start.1 = ((bf16[128,4,7168]{2,1,0:T(4,128)(2,1)}), bf16[128,4,7168]{2,1,0:T(4,128)(2,1)}, u32[]{:S(2)}, u32[]{:S(2)}) async-start(bf16[128,4,7168]{2,1,0:T(4,128)(2,1)} %reshape.156), calls=%async_computation.1 | async-start | bytes 14680064 | tf_op jit(solution)/shard_map/all_to_all | solution.py:57
  354.6 11.1 %copy-start.1 = (bf16[128,7168]{1,0:T(8,128)(2,1)S(1)}, bf16[128,7168]{1,0:T(8,128)(2,1)}, u32[]{:S(2)}) copy-start(bf16[128,7168]{1,0:T(8,128)(2,1)} %param.6) | copy-start | bytes 5505028
where the time goes:
time: 372 us; the launch traced here: 366 us
  waiting for transfers between devices  177 us (48%)
  other arithmetic  82.4 us (22%)
  local copies, waits for them, and re-layouts  73.9 us (20%)
  starting transfers between devices  16.7 us (4%)
  matrix products  15.1 us (4%)
    all_to_all x1, waiting for transfers between devices, shards(): lax.all_to_all(spread, ('dp', 'expert'), split_axis=0, concat_axis=0, til...  88.8 us
    all_to_all x1, waiting for transfers between devices, shards(): lax.all_to_all(back_rows.reshape(worker_ordinal, slot_count, model_width)...  88.5 us
    another operation x4, other arithmetic  71.9 us
    gather x1, local copies, waits for them, and re-layouts, shards(): picked = jnp.take(arrived_rows, positions, axis=0)  17.2 us
    reshape x1, local copies, waits for them, and re-layouts, shards(): back_rows.reshape(worker_ordinal, slot_count, model_width)  12.6 us
    reshape x1, local copies, waits for them, and re-layouts, shards(): arrived_rows = arrived.reshape(worker_ordinal * slot_count, model_width)  12.1 us
    scatter x1, local copies, waits for them, and re-layouts, shards(): back_rows = jnp.zeros((worker_ordinal * slot_count, model_width), jnp.bfl...  11.9 us
    all_to_all x1, starting transfers between devices, shards(): lax.all_to_all(spread, ('dp', 'expert'), split_axis=0, concat_axis=0, til...  11.3 us
  transfers between devices with their start and end apart: 2, of which 2 were waited for; matrix products, arithmetic and copies ran while one was open for 0% of the time, Pallas kernels for 0%

commit v1 on v0

v1 whole, which is shorter than its diff:
```python
import jax
import jax.numpy as jnp
from jax import lax
from jax.sharding import PartitionSpec as P


def slot_tables(chosen, tok_count):
    owners = chosen // tok_count
    capacity = chosen.shape[1]
    same = owners[:, :, None] == owners[:, None, :]
    earlier = (
        jnp.arange(capacity, dtype=jnp.int32)[None, :]
        < jnp.arange(capacity, dtype=jnp.int32)[:, None]
    )
    ranks = jnp.sum((same & earlier[None]).astype(jnp.int32), axis=2)
    return (owners, ranks)


def shards(tokens, chosen, combine_fixed, w_gate, w_up, w_down):
    dp_count = lax.axis_size("dp")
    ex_count = lax.axis_size("expert")
    worker_ordinal = dp_count * ex_count
    tok_count, model_width = tokens.shape
    expert_total, capacity = chosen.shape
    slot_count = min(tok_count, max(4, 2 * capacity // worker_ordinal))
    my_index = lax.axis_index("dp") * ex_count + lax.axis_index("expert")
    owners, ranks = slot_tables(chosen, tok_count)
    local_idx = chosen - owners * tok_count
    is_mine = owners == my_index
    matches = is_mine[:, :, None] & (
        ranks[:, :, None] == jnp.arange(slot_count, dtype=jnp.int32)[None, None, :]
    )
    match_int = matches.astype(jnp.int32)
    source_idx = jnp.sum(match_int * local_idx[:, :, None], axis=1)
    present = jnp.sum(match_int, axis=1)
    scaled = combine_fixed.astype(jnp.float32) / 65536.0
    weights = jnp.sum(matches.astype(jnp.float32) * scaled[:, :, None], axis=1)
    send_rows = jnp.take(tokens, source_idx.reshape(-1), axis=0)
    send_rows = jnp.where(present.reshape(-1, 1) > 0, send_rows, jnp.zeros_like(send_rows))
    send_rows = send_rows.reshape(expert_total, slot_count, model_width)
    row_in = lax.all_to_all(send_rows, "expert", split_axis=0, concat_axis=0, tiled=True)
    picked = lax.all_gather(row_in, "dp", axis=0, tiled=False)
    picked = picked.reshape(dp_count * ex_count * slot_count, model_width)
    gate_act = jnp.dot(picked, w_gate[0], preferred_element_type=jnp.float32)
    up_act = jnp.dot(picked, w_up[0], preferred_element_type=jnp.float32)
    hidden = (jax.nn.silu(gate_act) * up_act).astype(jnp.bfloat16)
    result = jnp.dot(hidden, w_down[0], preferred_element_type=jnp.float32).astype(jnp.bfloat16)
    result = result.reshape(dp_count, ex_count * slot_count, model_width)
    summed = lax.psum_scatter(result, "dp", scatter_dimension=0, tiled=False)
    summed = summed.reshape(ex_count, slot_count, model_width)
    returned = lax.all_to_all(summed, "expert", split_axis=0, concat_axis=0, tiled=True)
    placed = (jnp.arange(tok_count, dtype=jnp.int32)[:, None] == source_idx.reshape(1, -1)) & (
        present.reshape(1, -1) > 0
    )
    mixing = jnp.where(placed, weights.reshape(1, -1), 0.0)
    mixed = jnp.dot(
        mixing,
        returned.reshape(-1, model_width).astype(jnp.float32),
        precision=lax.Precision.HIGHEST,
        preferred_element_type=jnp.float32,
    )
    return mixed.astype(jnp.bfloat16)


def solution(mesh):
    in_specs = (
        P(("dp", "expert"), None),
        P(),
        P(),
        P("expert", None, "dp"),
        P("expert", None, "dp"),
        P("expert", "dp", None),
    )
    out_specs = P(("dp", "expert"), None)
    return jax.shard_map(shards, mesh=mesh, in_specs=in_specs, out_specs=out_specs, check_vma=False)
```

time: 372 us -> 202 us (0.54)
  other arithmetic: 82.4 us -> 6.05 us
  waiting for transfers between devices: 177 us -> 105 us
  local copies, waits for them, and re-layouts: 73.9 us -> 18.9 us
  blocking collectives: 0 us -> 21.7 us
  between operations: 0.44 us -> 13.5 us
  matrix products: 15.1 us -> 26.1 us
  starting transfers between devices: 16.7 us -> 7.63 us
    all_to_all x2 -> x1, waiting for transfers between devices: 177 us -> 12.7 us  [shards(): lax.all_to_all(summed, 'expert', split_axis=0, concat_axis=0, tiled=True)]
    another operation x4 -> x0, other arithmetic: 71.9 us -> none
    reduce_scatter x0 -> x1, waiting for transfers between devices: none -> 47.7 us  [shards(): summed = lax.psum_scatter(result, 'dp', scatter_dimension=0, tiled=False)]
    all_gather x0 -> x1, waiting for transfers between devices: none -> 44.9 us  [shards(): picked = lax.all_gather(row_in, 'dp', axis=0, tiled=False)]
    all_to_all x0 -> x1, blocking collectives: none -> 21.7 us  [shards(): lax.all_to_all(send_rows, 'expert', split_axis=0, concat_axis=0, tiled=True)]
    gather x1 -> x0, local copies, waits for them, and re-layouts: 17.2 us -> none  [shards(): picked = jnp.take(arrived_rows, positions, axis=0)]
    reshape x3 -> x2, local copies, waits for them, and re-layouts: 27.7 us -> 13.2 us  [the longest x1 12.1 us: shards(): picked = picked.reshape(dp_count * ex_count * slot_count, model_width)]
    dot_general x1, matrix products: 3.32 us -> 16 us  [shards(): jnp.dot(hidden, w_down[0], preferred_element_type=jnp.float32)]
  transfers between devices with their start and end apart: 2 -> 3, of which waited for: 2 -> 3; matrix products, arithmetic and copies ran while one was open for 0% -> 0% of each run, Pallas kernels for 0% -> 0%
where the time goes in v1:
time: 202 us; the launch traced here: 199 us
  waiting for transfers between devices  105 us (52%)
  matrix products  26.1 us (13%)
  blocking collectives  21.7 us (11%)
  local copies, waits for them, and re-layouts  18.9 us (9%)
  between operations  13.5 us (7%)
  starting transfers between devices  7.63 us (4%)
  other arithmetic  6.05 us (3%)
    reduce_scatter x1, waiting for transfers between devices, shards(): summed = lax.psum_scatter(result, 'dp', scatter_dimension=0, tiled=False)  47.7 us
    all_gather x1, waiting for transfers between devices, shards(): picked = lax.all_gather(row_in, 'dp', axis=0, tiled=False)  44.9 us
    all_to_all x1, blocking collectives, shards(): lax.all_to_all(send_rows, 'expert', split_axis=0, concat_axis=0, tiled=True)  21.7 us
    dot_general x1, matrix products, shards(): jnp.dot(hidden, w_down[0], preferred_element_type=jnp.float32)  16 us
    all_to_all x1, waiting for transfers between devices, shards(): lax.all_to_all(summed, 'expert', split_axis=0, concat_axis=0, tiled=True)  12.7 us
    reshape x1, local copies, waits for them, and re-layouts, shards(): picked = picked.reshape(dp_count * ex_count * slot_count, model_width)  12.1 us
    all_to_all x1, starting transfers between devices, shards(): lax.all_to_all(summed, 'expert', split_axis=0, concat_axis=0, tiled=True)  7.4 us
    dot_general x1, matrix products, shards(): gate_act = jnp.dot(picked, w_gate[0], preferred_element_type=jnp.float32)  6.18 us
  transfers between devices with their start and end apart: 3, of which 3 were waited for; matrix products, arithmetic and copies ran while one was open for 0% of the time, Pallas kernels for 0%

profile of v1, /device:TPU:6, one launch (start us, length us, event | category | flops | bytes accessed | tf_op | source)
XLA Modules:
  0.0 199.3 jit_solution(7698414001086665519)
XLA Ops:
  6.5 0.0 all-gather.3.cloned.1.call-start
  6.6 0.9 multiply_subtract_fusion
  7.5 0.8 broadcast_compare_fusion
  8.2 2.3 %convert_reduce_fusion = s32[16,288]{1,0:T(8,128)S(1)} fusion(s32[16,288]{1,0:T(8,128)S(1)} %get-tuple-element.8, pred[288,288]{1,0:T(8,128)(4,1)S(1)} %iota_compare_fusion), kind=kLoop, calls=%fused_computation.3 | loop fusion | flops 5303808 | bytes 119808 | tf_op jit(solution)/shard_map/reduce_sum | solution.py:15
  10.5 0.2 convert_reduce_fusion.1
  10.8 0.1 copy.7
  10.9 0.1 copy.11
  11.0 0.1 copy.8
  11.1 0.1 reshape.96
  11.2 1.1 gather_fusion
  12.3 1.3 gather.7
  13.6 1.7 select_select_fusion
  15.3 21.7 %all_to_all.10 = bf16[16,4,7168]{2,1,0:T(4,128)(2,1)} all-to-all(bf16[16,4,7168]{2,1,0:T(4,128)(2,1)S(1)} %select_select_fusion), channel_id=1, replica_groups=mesh['dp'=8,'expert'=16] {'expert'}, dimensions={0} | all-to-all | bytes 1835008 | tf_op jit(solution)/shard_map/all_to_all | solution.py:41
  37.0 0.0 all-gather.3.cloned.1.call-update
  37.1 0.2 reduce-scatter.2.cloned.1.call-start
  37.3 44.9 %all-gather.3.cloned.1.call-done = bf16[128,4,7168]{2,1,0:T(4,128)(2,1)} async-done(((bf16[16,4,7168]{2,1,0:T(4,128)(2,1)}), bf16[128,4,7168]{2,1,0:T(4,128)(2,1)}) %all-gather.3.cloned.1.call-update) | async-done | bytes 7340048 | tf_op jit(solution)/shard_map/all_gather | solution.py:42
  82.2 12.1 %reshape.97 = bf16[512,7168]{1,0:T(8,128)(2,1)} reshape(bf16[128,4,7168]{2,1,0:T(4,128)(2,1)} %all-gather.3.cloned.1.call-done) | data formatting | bytes 14680064 | tf_op jit(solution)/shard_map/reshape | solution.py:43
  94.3 6.2 %fusion.3 = f32[512,256]{1,0:T(8,128)S(1)} fusion(bf16[512,7168]{1,0:T(8,128)(2,1)} %reshape.97, bf16[1,7168,256]{2,1,0:T(8,128)(2,1)} %param.9), kind=kOutput, calls=%fused_computation.7 | convolution fusion | flops 1879048192 | bytes 11534336 | tf_op jit(solution)/shard_map/dot_general | solution.py:44
  100.5 16.0 %convolution_convert_fusion = bf16[512,7168]{1,0:T(8,128)(2,1)} fusion(bf16[1,256,7168]{2,1,0:T(8,128)(2,1)} %param.11, bf16[512,7168]{1,0:T(8,128)(2,1)} %reshape.97, bf16[1,7168,256]{2,1,0:T(8,128)(2,1)} %param.10, f32[512,256]{1,0:T(8,128)S(1)} %fusion.3), kind=kOutput, calls=%fused_computation.1 | convolution fusion | flops 3762552832 | bytes 22544384 | tf_op jit(solution)/shard_map/dot_general | solution.py:47
  116.4 0.0 reduce-scatter.2.cloned.1.call-update
  116.5 0.0 copy-start.1
  116.5 47.7 %reduce-scatter.2.cloned.1.call-done = bf16[1,64,7168]{2,1,0:T(8,128)(2,1)} async-done(((bf16[8,64,7168]{2,1,0:T(8,128)(2,1)}), bf16[1,64,7168]{2,1,0:T(8,128)(2,1)}) %reduce-scatter.2.cloned.1.call-update) | async-done | bytes 917520 | tf_op jit(solution)/shard_map/reduce_scatter | solution.py:49
  164.2 2.5 %reshape_reduce_scatter.3 = bf16[16,4,7168]{2,1,0:T(4,128)(2,1)} reshape(bf16[1,64,7168]{2,1,0:T(8,128)(2,1)} %reduce-scatter.2.cloned.1.call-done) | data formatting | bytes 1835008 | tf_op jit(solution)/shard_map/reshape;reduce_scatter | solution.py:50
  166.7 7.4 %all-to-all-start.1 = ((bf16[16,4,7168]{2,1,0:T(4,128)(2,1)}), bf16[16,4,7168]{2,1,0:T(4,128)(2,1)S(1)}, u32[]{:S(2)}, u32[]{:S(2)}) async-start(bf16[16,4,7168]{2,1,0:T(4,128)(2,1)} %reshape_reduce_scatter.3), calls=%async_computation.2 | async-start | bytes 1835008 | tf_op jit(solution)/shard_map/all_to_all | solution.py:51
  174.1 0.1 gt.25
  174.2 0.1 eq.56
  174.3 0.1 select_reduce_fusion
  174.4 0.1 copy.9
  174.5 0.1 broadcast_in_dim.46
  174.6 12.7 %all-to-all-done.1 = bf16[16,4,7168]{2,1,0:T(4,128)(2,1)S(1)} async-done(((bf16[16,4,7168]{2,1,0:T(4,128)(2,1)}), bf16[16,4,7168]{2,1,0:T(4,128)(2,1)S(1)}, u32[]{:S(2)}, u32[]{:S(2)}) %all-to-all-start.1) | async-done | bytes 917536 | tf_op jit(solution)/shard_map/all_to_all | solution.py:51
  187.3 1.1 reshape.99
  188.5 4.0 %convolution_convert_fusion.1 = bf16[128,7168]{1,0:T(8,128)(2,1)} fusion(bf16[64,7168]{1,0:T(8,128)(2,1)} %reshape.99, f32[64]{0:T(128)S(1)} %broadcast_in_dim.46, s32[64]{0:T(128)S(1)} %eq.56, pred[64]{0:T(512)(128)(4,1)S(1)} %gt.25), kind=kOutput, calls=%fused_computation.2 | convolution fusion | flops 705585152 | bytes 2753088 | tf_op jit(solution)/shard_map/dot_general | solution.py:56
  (8 shorter events, 0.1 us)
Async XLA Ops:
  6.5 4.7 %copy-start = (bf16[128,7168]{1,0:T(8,128)(2,1)S(1)}, bf16[128,7168]{1,0:T(8,128)(2,1)}, u32[]{:S(2)}) copy-start(bf16[128,7168]{1,0:T(8,128)(2,1)} %param.6) | copy-start | bytes 5505028
  6.5 75.7 %all-gather.3.cloned.1.call-start = ((), (), s32[]{:S(2)}) async-start(), calls=%async_computation.4 | async-start | bytes 8257536 | tf_op jit(solution)/shard_map/all_gather | solution.py:42
  37.1 127.2 %reduce-scatter.2.cloned.1.call-start = ((), (), s32[]{:S(2)}) async-start(), calls=%async_computation.3 | async-start | bytes 8257536 | tf_op jit(solution)/shard_map/reduce_scatter | solution.py:49
  116.5 57.9 %copy-start.1 = (s32[16,288]{1,0:T(8,128)S(1)}, s32[16,288]{1,0:T(8,128)}, u32[]{:S(2)}) copy-start(s32[16,288]{1,0:T(8,128)} %param.8) | copy-start | bytes 55300
  166.7 20.6 %all-to-all-start.1 = ((bf16[16,4,7168]{2,1,0:T(4,128)(2,1)}), bf16[16,4,7168]{2,1,0:T(4,128)(2,1)S(1)}, u32[]{:S(2)}, u32[]{:S(2)}) async-start(bf16[16,4,7168]{2,1,0:T(4,128)(2,1)} %reshape_reduce_scatter.3), calls=%async_computation.2 | async-start | bytes 1835008 | tf_op jit(solution)/shard_map/all_to_all | solution.py:51
Sparse Core Ops, SparseCore 0:
  37.2 44.9 all-gather.2
  116.6 47.5 reduce-scatter.1

commit v2 on v1

--- a/solution.py
+++ b/solution.py
@@ -2,6 +2,8 @@
 import jax.numpy as jnp
 from jax import lax
 from jax.sharding import PartitionSpec as P
+
+CHUNKS = 4
 
 
 def slot_tables(chosen, tok_count):
@@ -37,28 +39,37 @@
     weights = jnp.sum(matches.astype(jnp.float32) * scaled[:, :, None], axis=1)
     send_rows = jnp.take(tokens, source_idx.reshape(-1), axis=0)
     send_rows = jnp.where(present.reshape(-1, 1) > 0, send_rows, jnp.zeros_like(send_rows))
-    send_rows = send_rows.reshape(expert_total, slot_count, model_width)
-    row_in = lax.all_to_all(send_rows, "expert", split_axis=0, concat_axis=0, tiled=True)
-    picked = lax.all_gather(row_in, "dp", axis=0, tiled=False)
-    picked = picked.reshape(dp_count * ex_count * slot_count, model_width)
-    gate_act = jnp.dot(picked, w_gate[0], preferred_element_type=jnp.float32)
-    up_act = jnp.dot(picked, w_up[0], preferred_element_type=jnp.float32)
-    hidden = (jax.nn.silu(gate_act) * up_act).astype(jnp.bfloat16)
-    result = jnp.dot(hidden, w_down[0], preferred_element_type=jnp.float32).astype(jnp.bfloat16)
-    result = result.reshape(dp_count, ex_count * slot_count, model_width)
-    summed = lax.psum_scatter(result, "dp", scatter_dimension=0, tiled=False)
-    summed = summed.reshape(ex_count, slot_count, model_width)
-    returned = lax.all_to_all(summed, "expert", split_axis=0, concat_axis=0, tiled=True)
     placed = (jnp.arange(tok_count, dtype=jnp.int32)[:, None] == source_idx.reshape(1, -1)) & (
         present.reshape(1, -1) > 0
     )
     mixing = jnp.where(placed, weights.reshape(1, -1), 0.0)
-    mixed = jnp.dot(
-        mixing,
-        returned.reshape(-1, model_width).astype(jnp.float32),
-        precision=lax.Precision.HIGHEST,
-        preferred_element_type=jnp.float32,
-    )
+    width = model_width // CHUNKS
+    gate_act = None
+    up_act = None
+    for c in range(CHUNKS):
+        cols = slice(c * width, (c + 1) * width)
+        row_in = lax.all_to_all(send_rows[:, cols], "expert", split_axis=0, concat_axis=0, tiled=True)
+        picked = lax.all_gather(row_in, "dp", axis=0, tiled=True)
+        g = jnp.dot(picked, w_gate[0, cols], preferred_element_type=jnp.float32)
+        u = jnp.dot(picked, w_up[0, cols], preferred_element_type=jnp.float32)
+        gate_act = g if gate_act is None else gate_act + g
+        up_act = u if up_act is None else up_act + u
+    hidden = (jax.nn.silu(gate_act) * up_act).astype(jnp.bfloat16)
+    pieces = []
+    for c in range(CHUNKS):
+        cols = slice(c * width, (c + 1) * width)
+        result = jnp.dot(hidden, w_down[0, :, cols], preferred_element_type=jnp.float32).astype(jnp.bfloat16)
+        summed = lax.psum_scatter(result, "dp", scatter_dimension=0, tiled=True)
+        returned = lax.all_to_all(summed, "expert", split_axis=0, concat_axis=0, tiled=True)
+        pieces.append(
+            jnp.dot(
+                mixing,
+                returned.astype(jnp.float32),
+                precision=lax.Precision.HIGHEST,
+                preferred_element_type=jnp.float32,
+            )
+        )
+    mixed = jnp.concatenate(pieces, axis=1)
     return mixed.astype(jnp.bfloat16)
 
 

time: 202 us -> 331 us (1.64)
  waiting for transfers between devices: 105 us -> 183 us
  blocking collectives: 21.7 us -> 49.6 us
  starting transfers between devices: 7.63 us -> 26.6 us
  matrix products: 26.1 us -> 36.3 us
  local copies, waits for them, and re-layouts: 18.9 us -> 13.4 us
    reduce_scatter x1 -> x4, waiting for transfers between devices: 47.7 us -> 116 us  [shards(): summed = lax.psum_scatter(result, 'dp', scatter_dimension=0, tiled=True)]
    all_to_all x1 -> x4, blocking collectives: 21.7 us -> 49.6 us  [shards(): lax.all_to_all(send_rows[:, cols], 'expert', split_axis=0, concat_axis=0,...]
    all_to_all x1 -> x4, starting transfers between devices: 7.4 us -> 26.3 us  [shards(): lax.all_to_all(summed, 'expert', split_axis=0, concat_axis=0, tiled=True)]
    reshape x2 -> x0, local copies, waits for them, and re-layouts: 13.2 us -> none  [the longest x1 12.1 us: shards(): picked = picked.reshape(dp_count * ex_count * slot_count, model_width)]
    all_to_all x0 -> x16, local copies, waits for them, and re-layouts: none -> 11.5 us  [the longest x8 8.34 us: shards(): lax.all_to_all(summed, 'expert', split_axis=0, concat_axis=0, tiled=True)]
    dot_general x3 -> x16, matrix products: 26.1 us -> 36.3 us  [the longest x4 12.3 us: shards(): jnp.dot(hidden, w_down[0, :, cols], preferred_element_type=jnp.float32)]
    all_gather x1 -> x4, waiting for transfers between devices: 44.9 us -> 51.6 us  [shards(): picked = lax.all_gather(row_in, 'dp', axis=0, tiled=True)]
    all_to_all x1 -> x4, waiting for transfers between devices: 12.7 us -> 15.3 us  [shards(): lax.all_to_all(summed, 'expert', split_axis=0, concat_axis=0, tiled=True)]
  transfers between devices with their start and end apart: 3 -> 12, of which waited for: 3 -> 10; matrix products, arithmetic and copies ran while one was open for 0% -> 8% of each run, Pallas kernels for 0% -> 0%
where the time goes in v2:
time: 331 us; the launch traced here: 328 us
  waiting for transfers between devices  183 us (55%)
  blocking collectives  49.6 us (15%)
  matrix products  36.3 us (11%)
  starting transfers between devices  26.6 us (8%)
  between operations  13.8 us (4%)
  local copies, waits for them, and re-layouts  13.4 us (4%)
  other arithmetic  5.93 us (2%)
    reduce_scatter x4, waiting for transfers between devices, shards(): summed = lax.psum_scatter(result, 'dp', scatter_dimension=0, tiled=True)  116 us
    all_gather x4, waiting for transfers between devices, shards(): picked = lax.all_gather(row_in, 'dp', axis=0, tiled=True)  51.6 us
    all_to_all x4, blocking collectives, shards(): lax.all_to_all(send_rows[:, cols], 'expert', split_axis=0, concat_axis=0,...  49.6 us
    all_to_all x4, starting transfers between devices, shards(): lax.all_to_all(summed, 'expert', split_axis=0, concat_axis=0, tiled=True)  26.3 us
    all_to_all x4, waiting for transfers between devices, shards(): lax.all_to_all(summed, 'expert', split_axis=0, concat_axis=0, tiled=True)  15.3 us
    dot_general x4, matrix products, shards(): jnp.dot(hidden, w_down[0, :, cols], preferred_element_type=jnp.float32)  12.3 us
    dot_general x4, matrix products, shards(): g = jnp.dot(picked, w_gate[0, cols], preferred_element_type=jnp.float32)  10.5 us
    dot_general x4, matrix products, shards(): u = jnp.dot(picked, w_up[0, cols], preferred_element_type=jnp.float32)  9.59 us
  transfers between devices with their start and end apart: 12, of which 10 were waited for; matrix products, arithmetic and copies ran while one was open for 8% of the time, Pallas kernels for 0%

profile of v2, /device:TPU:6, one launch (start us, length us, event | category | flops | bytes accessed | tf_op | source)
XLA Modules:
  0.0 328.1 jit_solution(7978583228814977756)
XLA Ops:
  8.2 2.3 convert_reduce_fusion
  12.7 14.3 %all_to_all.96 = bf16[16,4,1792]{2,1,0:T(4,128)(2,1)S(1)} all-to-all(bf16[16,4,1792]{2,1,0:T(4,128)(2,1)S(1)} %all_to_all.64), channel_id=1, replica_groups=mesh['dp'=8,'expert'=16] {'expert'}, dimensions={0} | all-to-all | bytes 458752 | tf_op jit(solution)/shard_map/all_to_all | solution.py:51
  27.9 11.8 %all_to_all.97 = bf16[16,4,1792]{2,1,0:T(4,128)(2,1)S(1)} all-to-all(bf16[16,4,1792]{2,1,0:T(4,128)(2,1)S(1)} %all_to_all.67), channel_id=1, replica_groups=mesh['dp'=8,'expert'=16] {'expert'}, dimensions={0} | all-to-all | bytes 458752 | tf_op jit(solution)/shard_map/all_to_all | solution.py:51
  40.6 11.8 %all_to_all.98 = bf16[16,4,1792]{2,1,0:T(4,128)(2,1)S(1)} all-to-all(bf16[16,4,1792]{2,1,0:T(4,128)(2,1)S(1)} %all_to_all.70), channel_id=1, replica_groups=mesh['dp'=8,'expert'=16] {'expert'}, dimensions={0} | all-to-all | bytes 458752 | tf_op jit(solution)/shard_map/all_to_all | solution.py:51
  53.2 11.8 %all_to_all.99 = bf16[16,4,1792]{2,1,0:T(4,128)(2,1)S(1)} all-to-all(bf16[16,4,1792]{2,1,0:T(4,128)(2,1)S(1)} %all_to_all.73), channel_id=1, replica_groups=mesh['dp'=8,'expert'=16] {'expert'}, dimensions={0} | all-to-all | bytes 458752 | tf_op jit(solution)/shard_map/all_to_all | solution.py:51
  65.8 2.5 fusion.9
  68.4 2.6 fusion.14
  71.0 8.5 %all-gather.7.cloned.1.call-done = bf16[512,1792]{1,0:T(8,128)(2,1)} async-done(((bf16[64,1792]{1,0:T(8,128)(2,1)}), bf16[512,1792]{1,0:T(8,128)(2,1)}) %all-gather.7.cloned.1.call-update) | async-done | bytes 1835024 | tf_op jit(solution)/shard_map/all_gather | solution.py:52
  79.5 2.6 convolution_add_fusion.5
  82.2 2.6 convolution_add_fusion.2
  84.8 21.6 %all-gather.9.cloned.1.call-done = bf16[512,1792]{1,0:T(8,128)(2,1)} async-done(((bf16[64,1792]{1,0:T(8,128)(2,1)}), bf16[512,1792]{1,0:T(8,128)(2,1)}) %all-gather.9.cloned.1.call-update) | async-done | bytes 1835024 | tf_op jit(solution)/shard_map/all_gather | solution.py:52
  106.4 2.6 convolution_add_fusion.1
  109.0 2.6 convolution_add_fusion.4
  111.7 21.4 %all-gather.11.cloned.1.call-done = bf16[512,1792]{1,0:T(8,128)(2,1)} async-done(((bf16[64,1792]{1,0:T(8,128)(2,1)}), bf16[512,1792]{1,0:T(8,128)(2,1)}) %all-gather.11.cloned.1.call-update) | async-done | bytes 1835024 | tf_op jit(solution)/shard_map/all_gather | solution.py:52
  133.1 2.6 convolution_add_fusion.3
  135.8 1.8 fusion.1
  137.6 3.1 convolution_convert_fusion
  140.7 3.1 convolution_convert_fusion.1
  143.9 3.1 convolution_convert_fusion.2
  147.0 3.1 convolution_convert_fusion.3
  150.1 24.4 %reduce-scatter.11.cloned.1.call-done = bf16[64,1792]{1,0:T(8,128)(2,1)} async-done(((bf16[512,1792]{1,0:T(8,128)(2,1)}), bf16[64,1792]{1,0:T(8,128)(2,1)}) %reduce-scatter.11.cloned.1.call-update) | async-done | bytes 229392 | tf_op jit(solution)/shard_map/reduce_scatter | solution.py:62
  176.2 7.4 %all-to-all-start.7 = ((bf16[16,4,1792]{2,1,0:T(4,128)(2,1)}), bf16[16,4,1792]{2,1,0:T(4,128)(2,1)S(1)}, u32[]{:S(2)}, u32[]{:S(2)}) async-start(bf16[16,4,1792]{2,1,0:T(4,128)(2,1)} %all_to_all.85), calls=%async_computation.11 | async-start | bytes 458752 | tf_op jit(solution)/shard_map/all_to_all | solution.py:63
  183.9 25.1 %reduce-scatter.9.cloned.1.call-done = bf16[64,1792]{1,0:T(8,128)(2,1)} async-done(((bf16[512,1792]{1,0:T(8,128)(2,1)}), bf16[64,1792]{1,0:T(8,128)(2,1)}) %reduce-scatter.9.cloned.1.call-update) | async-done | bytes 229392 | tf_op jit(solution)/shard_map/reduce_scatter | solution.py:62
  209.0 1.7 all_to_all.82
  210.7 33.0 %reduce-scatter.7.cloned.1.call-done = bf16[64,1792]{1,0:T(8,128)(2,1)} async-done(((bf16[512,1792]{1,0:T(8,128)(2,1)}), bf16[64,1792]{1,0:T(8,128)(2,1)}) %reduce-scatter.7.cloned.1.call-update) | async-done | bytes 229392 | tf_op jit(solution)/shard_map/reduce_scatter | solution.py:62
  245.4 33.0 %reduce-scatter.5.cloned.1.call-done = bf16[64,1792]{1,0:T(8,128)(2,1)} async-done(((bf16[512,1792]{1,0:T(8,128)(2,1)}), bf16[64,1792]{1,0:T(8,128)(2,1)}) %reduce-scatter.5.cloned.1.call-update) | async-done | bytes 229392 | tf_op jit(solution)/shard_map/reduce_scatter | solution.py:62
  280.1 7.4 %all-to-all-start.6 = ((bf16[16,4,1792]{2,1,0:T(4,128)(2,1)}), bf16[16,4,1792]{2,1,0:T(4,128)(2,1)S(1)}, u32[]{:S(2)}, u32[]{:S(2)}) async-start(bf16[16,4,1792]{2,1,0:T(4,128)(2,1)} %all_to_all.82), calls=%async_computation.9 | async-start | bytes 458752 | tf_op jit(solution)/shard_map/all_to_all | solution.py:63
  288.1 5.7 %all-to-all-done.6 = bf16[16,4,1792]{2,1,0:T(4,128)(2,1)S(1)} async-done(((bf16[16,4,1792]{2,1,0:T(4,128)(2,1)}), bf16[16,4,1792]{2,1,0:T(4,128)(2,1)S(1)}, u32[]{:S(2)}, u32[]{:S(2)}) %all-to-all-start.6) | async-done | bytes 229408 | tf_op jit(solution)/shard_map/all_to_all | solution.py:63
  293.7 5.7 %all-to-all-start.5 = ((bf16[16,4,1792]{2,1,0:T(4,128)(2,1)}), bf16[16,4,1792]{2,1,0:T(4,128)(2,1)S(1)}, u32[]{:S(2)}, u32[]{:S(2)}) async-start(bf16[16,4,1792]{2,1,0:T(4,128)(2,1)} %all_to_all.79), calls=%async_computation.7 | async-start | bytes 458752 | tf_op jit(solution)/shard_map/all_to_all | solution.py:63
  300.1 5.7 %all-to-all-done.5 = bf16[16,4,1792]{2,1,0:T(4,128)(2,1)S(1)} async-done(((bf16[16,4,1792]{2,1,0:T(4,128)(2,1)}), bf16[16,4,1792]{2,1,0:T(4,128)(2,1)S(1)}, u32[]{:S(2)}, u32[]{:S(2)}) %all-to-all-start.5) | async-done | bytes 229408 | tf_op jit(solution)/shard_map/all_to_all | solution.py:63
  305.7 5.7 %all-to-all-start.4 = ((bf16[16,4,1792]{2,1,0:T(4,128)(2,1)}), bf16[16,4,1792]{2,1,0:T(4,128)(2,1)S(1)}, u32[]{:S(2)}, u32[]{:S(2)}) async-start(bf16[16,4,1792]{2,1,0:T(4,128)(2,1)} %all_to_all.76), calls=%async_computation.5 | async-start | bytes 458752 | tf_op jit(solution)/shard_map/all_to_all | solution.py:63
  313.6 4.0 %all-to-all-done.4 = bf16[16,4,1792]{2,1,0:T(4,128)(2,1)S(1)} async-done(((bf16[16,4,1792]{2,1,0:T(4,128)(2,1)}), bf16[16,4,1792]{2,1,0:T(4,128)(2,1)S(1)}, u32[]{:S(2)}, u32[]{:S(2)}) %all-to-all-start.4) | async-done | bytes 229408 | tf_op jit(solution)/shard_map/all_to_all | solution.py:63
  (70 shorter events, 19.7 us)
Async XLA Ops:
  6.5 4.8 %copy-start = (bf16[128,7168]{1,0:T(8,128)(2,1)S(1)}, bf16[128,7168]{1,0:T(8,128)(2,1)}, u32[]{:S(2)}) copy-start(bf16[128,7168]{1,0:T(8,128)(2,1)} %param.6) | copy-start | bytes 5505028
  6.5 59.3 %all-gather.5.cloned.1.call-start = ((), (), s32[]{:S(2)}) async-start(), calls=%async_computation.12 | async-start | bytes 2064384 | tf_op jit(solution)/shard_map/all_gather | solution.py:52
  27.8 51.7 %all-gather.7.cloned.1.call-start = ((), (), s32[]{:S(2)}) async-start(), calls=%async_computation.13 | async-start | bytes 2064384 | tf_op jit(solution)/shard_map/all_gather | solution.py:52
  40.4 65.9 %all-gather.9.cloned.1.call-start = ((), (), s32[]{:S(2)}) async-start(), calls=%async_computation.14 | async-start | bytes 2064384 | tf_op jit(solution)/shard_map/all_gather | solution.py:52
  53.1 80.0 %all-gather.11.cloned.1.call-start = ((), (), s32[]{:S(2)}) async-start(), calls=%async_computation.15 | async-start | bytes 2064384 | tf_op jit(solution)/shard_map/all_gather | solution.py:52
  65.7 108.8 %reduce-scatter.11.cloned.1.call-start = ((), (), s32[]{:S(2)}) async-start(), calls=%async_computation.19 | async-start | bytes 2064384 | tf_op jit(solution)/shard_map/reduce_scatter | solution.py:62
  65.8 2.5 copy-start.2
  79.5 2.7 copy-start.3
  106.4 2.7 copy-start.4
  133.1 2.7 copy-start.5
  140.7 68.4 %reduce-scatter.9.cloned.1.call-start = ((), (), s32[]{:S(2)}) async-start(), calls=%async_computation.18 | async-start | bytes 2064384 | tf_op jit(solution)/shard_map/reduce_scatter | solution.py:62
  143.8 99.9 %reduce-scatter.7.cloned.1.call-start = ((), (), s32[]{:S(2)}) async-start(), calls=%async_computation.17 | async-start | bytes 2064384 | tf_op jit(solution)/shard_map/reduce_scatter | solution.py:62
  147.0 131.4 %reduce-scatter.5.cloned.1.call-start = ((), (), s32[]{:S(2)}) async-start(), calls=%async_computation.16 | async-start | bytes 2064384 | tf_op jit(solution)/shard_map/reduce_scatter | solution.py:62
  150.1 33.5 %copy-start.1 = (s32[16,288]{1,0:T(8,128)S(1)}, s32[16,288]{1,0:T(8,128)}, u32[]{:S(2)}) copy-start(s32[16,288]{1,0:T(8,128)} %param.8) | copy-start | bytes 55300
  176.2 103.9 %all-to-all-start.7 = ((bf16[16,4,1792]{2,1,0:T(4,128)(2,1)}), bf16[16,4,1792]{2,1,0:T(4,128)(2,1)S(1)}, u32[]{:S(2)}, u32[]{:S(2)}) async-start(bf16[16,4,1792]{2,1,0:T(4,128)(2,1)} %all_to_all.85), calls=%async_computation.11 | async-start | bytes 458752 | tf_op jit(solution)/shard_map/all_to_all | solution.py:63
  280.1 13.6 %all-to-all-start.6 = ((bf16[16,4,1792]{2,1,0:T(4,128)(2,1)}), bf16[16,4,1792]{2,1,0:T(4,128)(2,1)S(1)}, u32[]{:S(2)}, u32[]{:S(2)}) async-start(bf16[16,4,1792]{2,1,0:T(4,128)(2,1)} %all_to_all.82), calls=%async_computation.9 | async-start | bytes 458752 | tf_op jit(solution)/shard_map/all_to_all | solution.py:63
  293.7 12.0 %all-to-all-start.5 = ((bf16[16,4,1792]{2,1,0:T(4,128)(2,1)}), bf16[16,4,1792]{2,1,0:T(4,128)(2,1)S(1)}, u32[]{:S(2)}, u32[]{:S(2)}) async-start(bf16[16,4,1792]{2,1,0:T(4,128)(2,1)} %all_to_all.79), calls=%async_computation.7 | async-start | bytes 458752 | tf_op jit(solution)/shard_map/all_to_all | solution.py:63
  305.7 12.0 %all-to-all-start.4 = ((bf16[16,4,1792]{2,1,0:T(4,128)(2,1)}), bf16[16,4,1792]{2,1,0:T(4,128)(2,1)S(1)}, u32[]{:S(2)}, u32[]{:S(2)}) async-start(bf16[16,4,1792]{2,1,0:T(4,128)(2,1)} %all_to_all.76), calls=%async_computation.5 | async-start | bytes 458752 | tf_op jit(solution)/shard_map/all_to_all | solution.py:63
Sparse Core Ops, SparseCore 0:
  27.9 24.6 all-gather.4
  54.3 25.1 all-gather.6
  81.2 25.1 all-gather.8
  107.9 25.1 all-gather.10
  140.8 33.6 reduce-scatter.10
  176.8 32.2 reduce-scatter.8
  211.5 32.2 reduce-scatter.6
  246.2 32.2 reduce-scatter.4

commit v3 on v1

--- a/solution.py
+++ b/solution.py
@@ -37,27 +37,23 @@
     weights = jnp.sum(matches.astype(jnp.float32) * scaled[:, :, None], axis=1)
     send_rows = jnp.take(tokens, source_idx.reshape(-1), axis=0)
     send_rows = jnp.where(present.reshape(-1, 1) > 0, send_rows, jnp.zeros_like(send_rows))
-    send_rows = send_rows.reshape(expert_total, slot_count, model_width)
     row_in = lax.all_to_all(send_rows, "expert", split_axis=0, concat_axis=0, tiled=True)
-    picked = lax.all_gather(row_in, "dp", axis=0, tiled=False)
-    picked = picked.reshape(dp_count * ex_count * slot_count, model_width)
+    picked = lax.all_gather(row_in, "dp", axis=0, tiled=True)
     gate_act = jnp.dot(picked, w_gate[0], preferred_element_type=jnp.float32)
     up_act = jnp.dot(picked, w_up[0], preferred_element_type=jnp.float32)
     hidden = (jax.nn.silu(gate_act) * up_act).astype(jnp.bfloat16)
+    hidden = lax.optimization_barrier(hidden)
     result = jnp.dot(hidden, w_down[0], preferred_element_type=jnp.float32).astype(jnp.bfloat16)
-    result = result.reshape(dp_count, ex_count * slot_count, model_width)
-    summed = lax.psum_scatter(result, "dp", scatter_dimension=0, tiled=False)
-    summed = summed.reshape(ex_count, slot_count, model_width)
+    summed = lax.psum_scatter(result, "dp", scatter_dimension=0, tiled=True)
     returned = lax.all_to_all(summed, "expert", split_axis=0, concat_axis=0, tiled=True)
     placed = (jnp.arange(tok_count, dtype=jnp.int32)[:, None] == source_idx.reshape(1, -1)) & (
         present.reshape(1, -1) > 0
     )
     mixing = jnp.where(placed, weights.reshape(1, -1), 0.0)
-    mixed = jnp.dot(
-        mixing,
-        returned.reshape(-1, model_width).astype(jnp.float32),
-        precision=lax.Precision.HIGHEST,
-        preferred_element_type=jnp.float32,
+    mix_hi = mixing.astype(jnp.bfloat16)
+    mix_lo = (mixing - mix_hi.astype(jnp.float32)).astype(jnp.bfloat16)
+    mixed = jnp.dot(mix_hi, returned, preferred_element_type=jnp.float32) + jnp.dot(
+        mix_lo, returned, preferred_element_type=jnp.float32
     )
     return mixed.astype(jnp.bfloat16)
 

time: 202 us -> 182 us (0.901)
  matrix products: 26.1 us -> 15.9 us
  local copies, waits for them, and re-layouts: 18.9 us -> 9.33 us
    reshape x2 -> x0, local copies, waits for them, and re-layouts: 13.2 us -> none  [the longest x1 12.1 us: shards(): picked = picked.reshape(dp_count * ex_count * slot_count, model_width)]
    dot_general x1, matrix products: 16 us -> 5.04 us  [shards(): jnp.dot(hidden, w_down[0], preferred_element_type=jnp.float32)]
    all_to_all x0 -> x3, local copies, waits for them, and re-layouts: none -> 5.3 us  [the longest x2 4.17 us: shards(): lax.all_to_all(summed, 'expert', split_axis=0, concat_axis=0, tiled=True)]
    another operation x1 -> x0, local copies, waits for them, and re-layouts: 2.52 us -> none  [shards(): summed = summed.reshape(ex_count, slot_count, model_width)]
    dot_general x1 -> x3, matrix products: 3.99 us -> 4.54 us  [the longest x1 2.05 us: shards(): up_act = jnp.dot(picked, w_up[0], preferred_element_type=jnp.float32)]
where the time goes in v3:
time: 182 us; the launch traced here: 180 us
  waiting for transfers between devices  106 us (58%)
  blocking collectives  21.6 us (12%)
  matrix products  15.9 us (9%)
  between operations  13.5 us (7%)
  local copies, waits for them, and re-layouts  9.33 us (5%)
  starting transfers between devices  7.45 us (4%)
  other arithmetic  6.06 us (3%)
    reduce_scatter x1, waiting for transfers between devices, shards(): summed = lax.psum_scatter(result, 'dp', scatter_dimension=0, tiled=True)  47.7 us
    all_gather x1, waiting for transfers between devices, shards(): picked = lax.all_gather(row_in, 'dp', axis=0, tiled=True)  45.1 us
    all_to_all x1, blocking collectives, shards(): lax.all_to_all(send_rows, 'expert', split_axis=0, concat_axis=0, tiled=True)  21.6 us
    all_to_all x1, waiting for transfers between devices, shards(): lax.all_to_all(summed, 'expert', split_axis=0, concat_axis=0, tiled=True)  12.8 us
    all_to_all x1, starting transfers between devices, shards(): lax.all_to_all(summed, 'expert', split_axis=0, concat_axis=0, tiled=True)  7.4 us
    dot_general x1, matrix products, shards(): gate_act = jnp.dot(picked, w_gate[0], preferred_element_type=jnp.float32)  6.33 us
    dot_general x1, matrix products, shards(): jnp.dot(hidden, w_down[0], preferred_element_type=jnp.float32)  5.04 us
    all_to_all x2, local copies, waits for them, and re-layouts, shards(): lax.all_to_all(summed, 'expert', split_axis=0, concat_axis=0, tiled=True)  4.17 us
  transfers between devices with their start and end apart: 3, of which 3 were waited for; matrix products, arithmetic and copies ran while one was open for 0% of the time, Pallas kernels for 0%

profile of v3, /device:TPU:6, one launch (start us, length us, event | category | flops | bytes accessed | tf_op | source)
XLA Modules:
  0.0 179.6 jit_solution(6259342618798534106)
XLA Ops:
  6.6 0.9 multiply_subtract_fusion
  7.5 0.8 broadcast_compare_fusion
  8.2 2.3 %convert_reduce_fusion = s32[16,288]{1,0:T(8,128)S(1)} fusion(s32[16,288]{1,0:T(8,128)S(1)} %get-tuple-element.8, pred[288,288]{1,0:T(8,128)(4,1)S(1)} %iota_compare_fusion), kind=kLoop, calls=%fused_computation.4 | loop fusion | flops 5303808 | bytes 119808 | tf_op jit(solution)/shard_map/reduce_sum | solution.py:15
  10.6 0.2 convert_reduce_fusion.1
  10.8 0.1 copy.7
  10.9 0.1 copy.11
  11.0 0.1 copy.8
  11.1 0.1 reshape.90
  11.2 1.1 gather_fusion
  12.3 1.3 gather.7
  13.6 1.7 select_select_fusion
  15.3 21.6 %all_to_all.21 = bf16[16,4,7168]{2,1,0:T(4,128)(2,1)S(1)} all-to-all(bf16[16,4,7168]{2,1,0:T(4,128)(2,1)S(1)} %select_select_fusion), channel_id=1, replica_groups=mesh['dp'=8,'expert'=16] {'expert'}, dimensions={0} | all-to-all | bytes 1835008 | tf_op jit(solution)/shard_map/all_to_all | solution.py:40
  36.9 1.1 all_to_all.15
  38.1 0.0 all-gather.2.cloned.1.call-update
  38.1 0.0 reduce-scatter.2.cloned.1.call-start
  38.1 45.1 %all-gather.2.cloned.1.call-done = bf16[512,7168]{1,0:T(8,128)(2,1)} async-done(((bf16[64,7168]{1,0:T(8,128)(2,1)}), bf16[512,7168]{1,0:T(8,128)(2,1)}) %all-gather.2.cloned.1.call-update) | async-done | bytes 7340048 | tf_op jit(solution)/shard_map/all_gather | solution.py:41
  83.2 6.3 %fusion.4 = f32[512,256]{1,0:T(8,128)S(1)} fusion(bf16[512,7168]{1,0:T(8,128)(2,1)} %all-gather.2.cloned.1.call-done, bf16[1,7168,256]{2,1,0:T(8,128)(2,1)} %param.9), kind=kOutput, calls=%fused_computation.8 | convolution fusion | flops 1879048192 | bytes 11534336 | tf_op jit(solution)/shard_map/dot_general | solution.py:42
  89.6 0.9 copy-done.4
  90.5 2.1 %fusion.9 = bf16[512,256]{1,0:T(8,128)(2,1)S(1)} fusion(bf16[512,7168]{1,0:T(8,128)(2,1)S(1)} %copy-done.3, bf16[1,7168,256]{2,1,0:T(8,128)(2,1)S(1)} %copy-done.4, f32[512,256]{1,0:T(8,128)S(1)} %fusion.4), kind=kOutput, calls=%fused_computation.11 | convolution fusion | flops 1879834624 | bytes 11796480 | tf_op jit(solution)/shard_map/dot_general | solution.py:43
  92.6 5.0 %convolution_convert_fusion = bf16[512,7168]{1,0:T(8,128)(2,1)} fusion(bf16[512,256]{1,0:T(8,128)(2,1)S(1)} %fusion.9, bf16[1,256,7168]{2,1,0:T(8,128)(2,1)S(1)} %copy-done.1), kind=kOutput, calls=%fused_computation.1 | convolution fusion | flops 1882718208 | bytes 11272192 | tf_op jit(solution)/shard_map/dot_general | solution.py:46
  97.6 47.7 %reduce-scatter.2.cloned.1.call-done = bf16[64,7168]{1,0:T(8,128)(2,1)} async-done(((bf16[512,7168]{1,0:T(8,128)(2,1)}), bf16[64,7168]{1,0:T(8,128)(2,1)}) %reduce-scatter.2.cloned.1.call-update) | async-done | bytes 917520 | tf_op jit(solution)/shard_map/reduce_scatter | solution.py:47
  145.4 2.5 %all_to_all.16 = bf16[16,4,7168]{2,1,0:T(4,128)(2,1)} reshape(bf16[64,7168]{1,0:T(8,128)(2,1)} %reduce-scatter.2.cloned.1.call-done) | data formatting | bytes 1835008 | tf_op jit(solution)/shard_map/all_to_all | solution.py:48
  147.9 7.4 %all-to-all-start.1 = ((bf16[16,4,7168]{2,1,0:T(4,128)(2,1)}), bf16[16,4,7168]{2,1,0:T(4,128)(2,1)}, u32[]{:S(2)}, u32[]{:S(2)}) async-start(bf16[16,4,7168]{2,1,0:T(4,128)(2,1)} %all_to_all.16), calls=%async_computation.2 | async-start | bytes 1835008 | tf_op jit(solution)/shard_map/all_to_all | solution.py:48
  155.3 0.1 gt.25
  155.4 0.1 eq.56
  155.5 0.1 select_reduce_fusion
  155.6 0.1 copy.9
  155.7 0.1 broadcast_in_dim.46
  155.8 12.8 %all-to-all-done.1 = bf16[16,4,7168]{2,1,0:T(4,128)(2,1)} async-done(((bf16[16,4,7168]{2,1,0:T(4,128)(2,1)}), bf16[16,4,7168]{2,1,0:T(4,128)(2,1)}, u32[]{:S(2)}, u32[]{:S(2)}) %all-to-all-start.1) | async-done | bytes 917536 | tf_op jit(solution)/shard_map/all_to_all | solution.py:48
  168.6 1.7 all_to_all.18
  170.2 0.6 fusion.15
  170.9 1.9 %fusion = bf16[128,7168]{1,0:T(8,128)(2,1)} fusion(f32[128,7168]{1,0:T(8,128)S(1)} %fusion.15, bf16[64,7168]{1,0:T(8,128)(2,1)S(1)} %all_to_all.18, f32[64]{0:T(128)S(1)} %broadcast_in_dim.46, s32[64]{0:T(128)S(1)} %eq.56, pred[64]{0:T(512)(128)(4,1)S(1)} %gt.25), kind=kOutput, calls=%fused_computation.3 | convolution fusion | flops 119332864 | bytes 6423104 | tf_op jit(solution)/shard_map/dot_general | solution.py:55
  (16 shorter events, 0.1 us)
Async XLA Ops:
  6.5 4.7 %copy-start = (bf16[128,7168]{1,0:T(8,128)(2,1)S(1)}, bf16[128,7168]{1,0:T(8,128)(2,1)}, u32[]{:S(2)}) copy-start(bf16[128,7168]{1,0:T(8,128)(2,1)} %param.6) | copy-start | bytes 5505028
  6.5 76.7 %all-gather.2.cloned.1.call-start = ((), (), s32[]{:S(2)}) async-start(), calls=%async_computation.3 | async-start | bytes 8257536 | tf_op jit(solution)/shard_map/all_gather | solution.py:41
  38.1 107.3 %reduce-scatter.2.cloned.1.call-start = ((), (), s32[]{:S(2)}) async-start(), calls=%async_computation.4 | async-start | bytes 8257536 | tf_op jit(solution)/shard_map/reduce_scatter | solution.py:47
  83.2 6.3 %copy-start.3 = (bf16[512,7168]{1,0:T(8,128)(2,1)S(1)}, bf16[512,7168]{1,0:T(8,128)(2,1)}, u32[]{:S(2)}) copy-start(bf16[512,7168]{1,0:T(8,128)(2,1)} %all-gather.2.cloned.1.call-done) | copy-start | bytes 22020100
  83.2 7.3 %copy-start.4 = (bf16[1,7168,256]{2,1,0:T(8,128)(2,1)S(1)}, bf16[1,7168,256]{2,1,0:T(8,128)(2,1)}, u32[]{:S(2)}) copy-start(bf16[1,7168,256]{2,1,0:T(8,128)(2,1)} %param.10) | copy-start | bytes 11010052
  90.5 2.1 %copy-start.1 = (bf16[1,256,7168]{2,1,0:T(8,128)(2,1)S(1)}, bf16[1,256,7168]{2,1,0:T(8,128)(2,1)}, u32[]{:S(2)}) copy-start(bf16[1,256,7168]{2,1,0:T(8,128)(2,1)} %param.11) | copy-start | bytes 11010052
  97.6 57.9 %copy-start.2 = (s32[16,288]{1,0:T(8,128)S(1)}, s32[16,288]{1,0:T(8,128)}, u32[]{:S(2)}) copy-start(s32[16,288]{1,0:T(8,128)} %param.8) | copy-start | bytes 55300
  147.9 20.7 %all-to-all-start.1 = ((bf16[16,4,7168]{2,1,0:T(4,128)(2,1)}), bf16[16,4,7168]{2,1,0:T(4,128)(2,1)}, u32[]{:S(2)}, u32[]{:S(2)}) async-start(bf16[16,4,7168]{2,1,0:T(4,128)(2,1)} %all_to_all.16), calls=%async_computation.2 | async-start | bytes 1835008 | tf_op jit(solution)/shard_map/all_to_all | solution.py:48
Sparse Core Ops, SparseCore 0:
  38.2 44.9 all-gather.1
  97.7 47.5 reduce-scatter.1

commit v4 on v3

--- a/solution.py
+++ b/solution.py
@@ -14,6 +14,49 @@
     )
     ranks = jnp.sum((same & earlier[None]).astype(jnp.int32), axis=2)
     return (owners, ranks)
+
+
+def dp_pairs(dp_count, shift):
+    ny = dp_count // 2
+    return [(y * 2 + c, ((y + shift) % ny) * 2 + c) for y in range(ny) for c in range(2)]
+
+
+def sib_pairs(dp_count):
+    return [(y * 2 + c, y * 2 + 1 - c) for y in range(dp_count // 2) for c in range(2)]
+
+
+def gather_dp(x, dp_count):
+    half = x.shape[1] // 2
+    up = lax.ppermute(x, "dp", dp_pairs(dp_count, 1))
+    dn = lax.ppermute(x, "dp", dp_pairs(dp_count, -1))
+    sib = lax.ppermute(x, "dp", sib_pairs(dp_count))
+    far_a = lax.ppermute(up[:, :half], "dp", dp_pairs(dp_count, 1))
+    far_b = lax.ppermute(dn[:, half:], "dp", dp_pairs(dp_count, -1))
+    far = jnp.concatenate([far_a, far_b], axis=1)
+    s_up = lax.ppermute(up, "dp", sib_pairs(dp_count))
+    s_dn = lax.ppermute(dn, "dp", sib_pairs(dp_count))
+    s_far = lax.ppermute(far, "dp", sib_pairs(dp_count))
+    return jnp.concatenate([x, sib, up, s_up, dn, s_dn, far, s_far], axis=0)
+
+
+def scatter_dp(p, dp_count):
+    rows = p.shape[0] // 8
+    half = p.shape[1] // 2
+    f32 = jnp.float32
+    b = [p[i * rows:(i + 1) * rows] for i in range(8)]
+    got = lax.ppermute(jnp.concatenate([b[1], b[3], b[5], b[7]], axis=0), "dp", sib_pairs(dp_count))
+    g = [got[i * rows:(i + 1) * rows].astype(f32) for i in range(4)]
+    q_self = b[0].astype(f32) + g[0]
+    q_up = b[2].astype(f32) + g[1]
+    q_dn = b[4].astype(f32) + g[2]
+    q_far = (b[6].astype(f32) + g[3]).astype(jnp.bfloat16)
+    r_a = lax.ppermute(q_far[:, :half], "dp", dp_pairs(dp_count, 1)).astype(f32)
+    r_b = lax.ppermute(q_far[:, half:], "dp", dp_pairs(dp_count, -1)).astype(f32)
+    s_a = jnp.concatenate([q_dn[:, :half] + r_a, q_dn[:, half:]], axis=1).astype(jnp.bfloat16)
+    s_b = jnp.concatenate([q_up[:, :half], q_up[:, half:] + r_b], axis=1).astype(jnp.bfloat16)
+    a_a = lax.ppermute(s_a, "dp", dp_pairs(dp_count, 1)).astype(f32)
+    a_b = lax.ppermute(s_b, "dp", dp_pairs(dp_count, -1)).astype(f32)
+    return (q_self + a_a + a_b).astype(jnp.bfloat16)
 
 
 def shards(tokens, chosen, combine_fixed, w_gate, w_up, w_down):
@@ -38,13 +81,13 @@
     send_rows = jnp.take(tokens, source_idx.reshape(-1), axis=0)
     send_rows = jnp.where(present.reshape(-1, 1) > 0, send_rows, jnp.zeros_like(send_rows))
     row_in = lax.all_to_all(send_rows, "expert", split_axis=0, concat_axis=0, tiled=True)
-    picked = lax.all_gather(row_in, "dp", axis=0, tiled=True)
+    picked = gather_dp(row_in, dp_count)
     gate_act = jnp.dot(picked, w_gate[0], preferred_element_type=jnp.float32)
     up_act = jnp.dot(picked, w_up[0], preferred_element_type=jnp.float32)
     hidden = (jax.nn.silu(gate_act) * up_act).astype(jnp.bfloat16)
     hidden = lax.optimization_barrier(hidden)
     result = jnp.dot(hidden, w_down[0], preferred_element_type=jnp.float32).astype(jnp.bfloat16)
-    summed = lax.psum_scatter(result, "dp", scatter_dimension=0, tiled=True)
+    summed = scatter_dp(result, dp_count)
     returned = lax.all_to_all(summed, "expert", split_axis=0, concat_axis=0, tiled=True)
     placed = (jnp.arange(tok_count, dtype=jnp.int32)[:, None] == source_idx.reshape(1, -1)) & (
         present.reshape(1, -1) > 0

time: 182 us -> 141 us (0.77)
  waiting for transfers between devices: 106 us -> 76.9 us
  between operations: 13.5 us -> 0.39 us
  starting transfers between devices: 7.45 us -> 20 us
  matrix products: 15.9 us -> 8.7 us
  local copies, waits for them, and re-layouts: 9.33 us -> 4.83 us
    ppermute x0 -> x13, waiting for transfers between devices: none -> 64.9 us  [the longest x1 19.4 us: scatter_dp(): a_a = lax.ppermute(s_a, 'dp', dp_pairs(dp_count, 1)).astype(f32)]
    reduce_scatter x1 -> x0, waiting for transfers between devices: 47.7 us -> none  [shards(): summed = lax.psum_scatter(result, 'dp', scatter_dimension=0, tiled=True)]
    all_gather x1 -> x0, waiting for transfers between devices: 45.1 us -> none  [shards(): picked = lax.all_gather(row_in, 'dp', axis=0, tiled=True)]
    ppermute x0 -> x13, starting transfers between devices: none -> 14.4 us  [the longest x1 3.28 us: scatter_dp(): a_b = lax.ppermute(s_b, 'dp', dp_pairs(dp_count, -1)).astype(f32)]
    dot_general x1, matrix products: 6.33 us -> 2.06 us  [shards(): gate_act = jnp.dot(picked, w_gate[0], preferred_element_type=jnp.float32)]
    dot_general x1, matrix products: 5.04 us -> 2.08 us  [shards(): jnp.dot(hidden, w_down[0], preferred_element_type=jnp.float32)]
    all_to_all x2, local copies, waits for them, and re-layouts: 4.17 us -> 1.46 us  [shards(): lax.all_to_all(summed, 'expert', split_axis=0, concat_axis=0, tiled=True)]
  transfers between devices with their start and end apart: 3 -> 14, of which waited for: 3 -> 7; matrix products, arithmetic and copies ran while one was open for 0% -> 1% of each run, Pallas kernels for 0% -> 0%
where the time goes in v4:
time: 141 us; the launch traced here: 139 us
  waiting for transfers between devices  76.9 us (55%)
  blocking collectives  21.6 us (15%)
  starting transfers between devices  20 us (14%)
  matrix products  8.7 us (6%)
  other arithmetic  6.69 us (5%)
  local copies, waits for them, and re-layouts  4.83 us (3%)
    all_to_all x1, blocking collectives, shards(): lax.all_to_all(send_rows, 'expert', split_axis=0, concat_axis=0, tiled=True)  21.6 us
    ppermute x1, waiting for transfers between devices, scatter_dp(): a_a = lax.ppermute(s_a, 'dp', dp_pairs(dp_count, 1)).astype(f32)  19.4 us
    ppermute x1, waiting for transfers between devices, gather_dp(): up = lax.ppermute(x, 'dp', dp_pairs(dp_count, 1))  19 us
    all_to_all x1, waiting for transfers between devices, shards(): lax.all_to_all(summed, 'expert', split_axis=0, concat_axis=0, tiled=True)  12 us
    ppermute x1, waiting for transfers between devices, scatter_dp(): r_a = lax.ppermute(q_far[:, :half], 'dp', dp_pairs(dp_count, 1)).astype(f32)  10.5 us
    ppermute x1, waiting for transfers between devices, gather_dp(): far_a = lax.ppermute(up[:, :half], 'dp', dp_pairs(dp_count, 1))  7.61 us
    ppermute x1, waiting for transfers between devices, scatter_dp(): lax.ppermute(jnp.concatenate([b[1], b[3], b[5], b[7]], axis=0), 'dp', sib...  6.27 us
    all_to_all x1, starting transfers between devices, shards(): lax.all_to_all(summed, 'expert', split_axis=0, concat_axis=0, tiled=True)  5.62 us
  transfers between devices with their start and end apart: 14, of which 7 were waited for; matrix products, arithmetic and copies ran while one was open for 1% of the time, Pallas kernels for 0%

profile of v4, /device:TPU:6, one launch (start us, length us, event | category | flops | bytes accessed | tf_op | source)
XLA Modules:
  0.0 139.1 jit_solution(17841620044248673155)
XLA Ops:
  0.0 0.9 multiply_subtract_fusion
  0.9 0.8 broadcast_compare_fusion
  1.7 2.3 %convert_reduce_fusion = s32[16,288]{1,0:T(8,128)S(1)} fusion(s32[16,288]{1,0:T(8,128)S(1)} %get-tuple-element.17, pred[288,288]{1,0:T(8,128)(4,1)S(1)} %iota_compare_fusion), kind=kLoop, calls=%fused_computation.4 | loop fusion | flops 5303808 | bytes 119808 | tf_op jit(solution)/shard_map/reduce_sum | solution.py:15
  4.7 1.1 gather_fusion
  5.8 0.3 gather.7
  6.1 0.5 select_select_fusion
  6.7 21.6 %all_to_all.21 = bf16[16,4,7168]{2,1,0:T(4,128)(2,1)S(1)} all-to-all(bf16[16,4,7168]{2,1,0:T(4,128)(2,1)S(1)} %select_select_fusion), channel_id=1, replica_groups=mesh['dp'=8,'expert'=16] {'expert'}, dimensions={0} | all-to-all | bytes 1835008 | tf_op jit(solution)/shard_map/all_to_all | solution.py:83
  28.5 1.6 %collective-permute-start.1 = (bf16[64,7168]{1,0:T(8,128)(2,1)S(1)}, bf16[64,7168]{1,0:T(8,128)(2,1)S(1)}, u32[]{:S(2)}, u32[]{:S(2)}) collective-permute-start(bf16[64,7168]{1,0:T(8,128)(2,1)S(1)} %all_to_all.15), channel_id=1, source_target_pairs={{0,32},{16,48},{32,64},{48,80},{64,96},{80,112},{96,0},{112,16},{1... | collective-permute-start | bytes 2752520 | tf_op jit(solution)/shard_map/ppermute | solution.py:30
  30.1 1.7 %collective-permute-start.3 = (bf16[64,7168]{1,0:T(8,128)(2,1)S(1)}, bf16[64,7168]{1,0:T(8,128)(2,1)S(1)}, u32[]{:S(2)}, u32[]{:S(2)}) collective-permute-start(bf16[64,7168]{1,0:T(8,128)(2,1)S(1)} %all_to_all.15), channel_id=1, source_target_pairs={{0,96},{16,112},{32,0},{48,16},{64,32},{80,48},{96,64},{112,80},{1... | collective-permute-start | bytes 2752520 | tf_op jit(solution)/shard_map/ppermute | solution.py:31
  31.9 19.0 %collective-permute-done.1 = bf16[64,7168]{1,0:T(8,128)(2,1)S(1)} collective-permute-done((bf16[64,7168]{1,0:T(8,128)(2,1)S(1)}, bf16[64,7168]{1,0:T(8,128)(2,1)S(1)}, u32[]{:S(2)}, u32[]{:S(2)}) %collective-permute-start.1) | collective-permute-done | bytes 917536 | tf_op jit(solution)/shard_map/ppermute | solution.py:30
  50.9 0.4 collective-permute-start.5
  51.3 3.0 %collective-permute-start.6 = (bf16[64,3584]{1,0:T(8,128)(2,1)S(1)}, bf16[64,3584]{1,0:T(8,128)(2,1)S(1)}, u32[]{:S(2)}, u32[]{:S(2)}) collective-permute-start(bf16[64,3584]{1,0:T(8,128)(2,1)S(1)} %slice.85), channel_id=1, source_target_pairs={{0,96},{16,112},{32,0},{48,16},{64,32},{80,48},{96,64},{112,80},{1... | collective-permute-start | bytes 1376264 | tf_op jit(solution)/shard_map/ppermute | solution.py:34
  54.3 0.5 collective-permute-start.4
  55.0 7.6 %collective-permute-done.5 = bf16[64,3584]{1,0:T(8,128)(2,1)S(1)} collective-permute-done((bf16[64,3584]{1,0:T(8,128)(2,1)S(1)}, bf16[64,3584]{1,0:T(8,128)(2,1)S(1)}, u32[]{:S(2)}, u32[]{:S(2)}) %collective-permute-start.5) | collective-permute-done | bytes 458784 | tf_op jit(solution)/shard_map/ppermute | solution.py:33
  63.2 2.1 %collective-permute-done.7 = bf16[64,7168]{1,0:T(8,128)(2,1)S(1)} collective-permute-done((bf16[64,7168]{1,0:T(8,128)(2,1)S(1)}, bf16[64,7168]{1,0:T(8,128)(2,1)S(1)}, u32[]{:S(2)}, u32[]{:S(2)}) %collective-permute-start.7) | collective-permute-done | bytes 917536 | tf_op jit(solution)/shard_map/ppermute | solution.py:38
  65.5 2.1 %fusion.4 = f32[512,256]{1,0:T(8,128)S(1)} fusion(bf16[512,7168]{1,0:T(8,128)(2,1)S(1)} %constant_dynamic-update-slice_fusion, bf16[1,7168,256]{2,1,0:T(8,128)(2,1)S(1)} %copy-done.4), kind=kOutput, calls=%fused_computation.9 | convolution fusion | flops 1879048192 | bytes 11534336 | tf_op jit(solution)/shard_map/dot_general | solution.py:85
  67.5 2.1 %multiply_convert_fusion = bf16[512,256]{1,0:T(8,128)(2,1)S(1)} fusion(f32[512,256]{1,0:T(8,128)S(1)} %fusion.4, bf16[512,7168]{1,0:T(8,128)(2,1)S(1)} %constant_dynamic-update-slice_fusion, bf16[1,7168,256]{2,1,0:T(8,128)(2,1)S(1)} %copy-done.5), kind=kOutput, calls=%fused_computation.25 | convolution fusion | flops 1879834624 | bytes 11796480 | tf_op jit(solution)/shard_map/dot_general | solution.py:86
  69.6 2.1 %convolution_convert_fusion = bf16[512,7168]{1,0:T(8,128)(2,1)S(1)} fusion(bf16[512,256]{1,0:T(8,128)(2,1)S(1)} %multiply_convert_fusion, bf16[1,256,7168]{2,1,0:T(8,128)(2,1)S(1)} %copy-done.2), kind=kOutput, calls=%fused_computation.1 | convolution fusion | flops 1882718208 | bytes 11272192 | tf_op jit(solution)/shard_map/dot_general | solution.py:89
  71.9 0.3 pad_maximum_fusion
  72.5 6.3 %collective-permute-done.8 = bf16[256,7168]{1,0:T(8,128)(2,1)S(1)} collective-permute-done((bf16[256,7168]{1,0:T(8,128)(2,1)S(1)}, bf16[256,7168]{1,0:T(8,128)(2,1)S(1)}, u32[]{:S(2)}, u32[]{:S(2)}) %collective-permute-start.8) | collective-permute-done | bytes 3670048 | tf_op jit(solution)/shard_map/ppermute | solution.py:47
  78.7 0.7 convert_add_fusion.1
  79.5 0.5 collective-permute-start.9
  80.1 2.9 %collective-permute-start.11 = (bf16[64,3584]{1,0:T(8,128)(2,1)S(1)}, bf16[64,3584]{1,0:T(8,128)(2,1)S(1)}, u32[]{:S(2)}, u32[]{:S(2)}) collective-permute-start(bf16[64,3584]{1,0:T(8,128)(2,1)S(1)} %get-tuple-element.15), channel_id=1, source_target_pairs={{0,96},{16,112},{32,0},{48,16},{64,32},{80,48},{96,64},{112,80},{1... | collective-permute-start | bytes 1376264 | tf_op jit(solution)/shard_map/ppermute | solution.py:54
  83.0 10.5 %collective-permute-done.9 = bf16[64,3584]{1,0:T(8,128)(2,1)S(1)} collective-permute-done((bf16[64,3584]{1,0:T(8,128)(2,1)S(1)}, bf16[64,3584]{1,0:T(8,128)(2,1)S(1)}, u32[]{:S(2)}, u32[]{:S(2)}) %collective-permute-start.9) | collective-permute-done | bytes 458784 | tf_op jit(solution)/shard_map/ppermute | solution.py:53
  93.9 3.3 %collective-permute-start.12 = (bf16[64,7168]{1,0:T(8,128)(2,1)S(1)}, bf16[64,7168]{1,0:T(8,128)(2,1)S(1)}, u32[]{:S(2)}, u32[]{:S(2)}) collective-permute-start(bf16[64,7168]{1,0:T(8,128)(2,1)S(1)} %pad_maximum_fusion.3), channel_id=1, source_target_pairs={{0,96},{16,112},{32,0},{48,16},{64,32},{80,48},{96,64},{112,80},{1... | collective-permute-start | bytes 2752520 | tf_op jit(solution)/shard_map/ppermute | solution.py:58
  97.2 19.4 %collective-permute-done.10 = bf16[64,7168]{1,0:T(8,128)(2,1)S(1)} collective-permute-done((bf16[64,7168]{1,0:T(8,128)(2,1)S(1)}, bf16[64,7168]{1,0:T(8,128)(2,1)S(1)}, u32[]{:S(2)}, u32[]{:S(2)}) %collective-permute-start.10) | collective-permute-done | bytes 917536 | tf_op jit(solution)/shard_map/ppermute | solution.py:57
  116.6 0.5 add_convert_fusion
  117.0 1.3 all_to_all.16
  118.3 5.6 %all-to-all-start.1 = ((bf16[16,4,7168]{2,1,0:T(4,128)(2,1)}), bf16[16,4,7168]{2,1,0:T(4,128)(2,1)S(1)}, u32[]{:S(2)}, u32[]{:S(2)}) async-start(bf16[16,4,7168]{2,1,0:T(4,128)(2,1)} %all_to_all.16), calls=%async_computation.1 | async-start | bytes 1835008 | tf_op jit(solution)/shard_map/all_to_all | solution.py:91
  124.4 12.0 %all-to-all-done.1 = bf16[16,4,7168]{2,1,0:T(4,128)(2,1)S(1)} async-done(((bf16[16,4,7168]{2,1,0:T(4,128)(2,1)}), bf16[16,4,7168]{2,1,0:T(4,128)(2,1)S(1)}, u32[]{:S(2)}, u32[]{:S(2)}) %all-to-all-start.1) | async-done | bytes 917536 | tf_op jit(solution)/shard_map/all_to_all | solution.py:91
  136.6 0.6 fusion.11
  137.2 1.9 %fusion = bf16[128,7168]{1,0:T(8,128)(2,1)} fusion(f32[128,7168]{1,0:T(8,128)S(1)} %fusion.11, bf16[64,7168]{1,0:T(8,128)(2,1)S(1)} %all_to_all.18, f32[64]{0:T(128)S(1)} %broadcast_in_dim.46, s32[64]{0:T(128)S(1)} %eq.56, pred[64]{0:T(512)(128)(4,1)S(1)} %gt.25), kind=kOutput, calls=%fused_computation.3 | convolution fusion | flops 119332864 | bytes 6423104 | tf_op jit(solution)/shard_map/dot_general | solution.py:98
  (61 shorter events, 3.4 us)
Async XLA Ops:
  0.0 4.6 %copy-start = (bf16[128,7168]{1,0:T(8,128)(2,1)S(1)}, bf16[128,7168]{1,0:T(8,128)(2,1)}, u32[]{:S(2)}) copy-start(bf16[128,7168]{1,0:T(8,128)(2,1)} %param.6) | copy-start | bytes 5505028
  28.5 22.4 %collective-permute-start.1 = (bf16[64,7168]{1,0:T(8,128)(2,1)S(1)}, bf16[64,7168]{1,0:T(8,128)(2,1)S(1)}, u32[]{:S(2)}, u32[]{:S(2)}) collective-permute-start(bf16[64,7168]{1,0:T(8,128)(2,1)S(1)} %all_to_all.15), channel_id=1, source_target_pairs={{0,32},{16,48},{32,64},{48,80},{64,96},{80,112},{96,0},{112,16},{1... | collective-permute-start | bytes 2752520 | tf_op jit(solution)/shard_map/ppermute | solution.py:30
  30.1 21.1 %collective-permute-start.3 = (bf16[64,7168]{1,0:T(8,128)(2,1)S(1)}, bf16[64,7168]{1,0:T(8,128)(2,1)S(1)}, u32[]{:S(2)}, u32[]{:S(2)}) collective-permute-start(bf16[64,7168]{1,0:T(8,128)(2,1)S(1)} %all_to_all.15), channel_id=1, source_target_pairs={{0,96},{16,112},{32,0},{48,16},{64,32},{80,48},{96,64},{112,80},{1... | collective-permute-start | bytes 2752520 | tf_op jit(solution)/shard_map/ppermute | solution.py:31
  31.8 23.0 %collective-permute-start = (bf16[64,7168]{1,0:T(8,128)(2,1)S(1)}, bf16[64,7168]{1,0:T(8,128)(2,1)S(1)}, u32[]{:S(2)}, u32[]{:S(2)}) collective-permute-start(bf16[64,7168]{1,0:T(8,128)(2,1)S(1)} %all_to_all.15), channel_id=1, source_target_pairs={{0,16},{16,0},{32,48},{48,32},{64,80},{80,64},{96,112},{112,96},{1... | collective-permute-start | bytes 2752520 | tf_op jit(solution)/shard_map/ppermute | solution.py:32
  50.9 11.7 %collective-permute-start.5 = (bf16[64,3584]{1,0:T(8,128)(2,1)S(1)}, bf16[64,3584]{1,0:T(8,128)(2,1)S(1)}, u32[]{:S(2)}, u32[]{:S(2)}) collective-permute-start(bf16[64,3584]{1,0:T(8,128)(2,1)S(1)} %slice.84), channel_id=1, source_target_pairs={{0,32},{16,48},{32,64},{48,80},{64,96},{80,112},{96,0},{112,16},{1... | collective-permute-start | bytes 1376264 | tf_op jit(solution)/shard_map/ppermute | solution.py:33
  51.3 11.3 %collective-permute-start.6 = (bf16[64,3584]{1,0:T(8,128)(2,1)S(1)}, bf16[64,3584]{1,0:T(8,128)(2,1)S(1)}, u32[]{:S(2)}, u32[]{:S(2)}) collective-permute-start(bf16[64,3584]{1,0:T(8,128)(2,1)S(1)} %slice.85), channel_id=1, source_target_pairs={{0,96},{16,112},{32,0},{48,16},{64,32},{80,48},{96,64},{112,80},{1... | collective-permute-start | bytes 1376264 | tf_op jit(solution)/shard_map/ppermute | solution.py:34
  54.3 8.6 %collective-permute-start.2 = (bf16[64,7168]{1,0:T(8,128)(2,1)S(1)}, bf16[64,7168]{1,0:T(8,128)(2,1)S(1)}, u32[]{:S(2)}, u32[]{:S(2)}) collective-permute-start(bf16[64,7168]{1,0:T(8,128)(2,1)S(1)} %collective-permute-done.1), channel_id=1, source_target_pairs={{0,16},{16,0},{32,48},{48,32},{64,80},{80,64},{96,112},{112,96},{1... | collective-permute-start | bytes 2752520 | tf_op jit(solution)/shard_map/ppermute | solution.py:36
  54.3 8.8 %collective-permute-start.4 = (bf16[64,7168]{1,0:T(8,128)(2,1)S(1)}, bf16[64,7168]{1,0:T(8,128)(2,1)S(1)}, u32[]{:S(2)}, u32[]{:S(2)}) collective-permute-start(bf16[64,7168]{1,0:T(8,128)(2,1)S(1)} %collective-permute-done.3), channel_id=1, source_target_pairs={{0,16},{16,0},{32,48},{48,32},{64,80},{80,64},{96,112},{112,96},{1... | collective-permute-start | bytes 2752520 | tf_op jit(solution)/shard_map/ppermute | solution.py:37
  62.6 2.7 %collective-permute-start.7 = (bf16[64,7168]{1,0:T(8,128)(2,1)S(1)}, bf16[64,7168]{1,0:T(8,128)(2,1)S(1)}, u32[]{:S(2)}, u32[]{:S(2)}) collective-permute-start(bf16[64,7168]{1,0:T(8,128)(2,1)S(1)} %pad_maximum_fusion.1), channel_id=1, source_target_pairs={{0,16},{16,0},{32,48},{48,32},{64,80},{80,64},{96,112},{112,96},{1... | collective-permute-start | bytes 2752520 | tf_op jit(solution)/shard_map/ppermute | solution.py:38
  63.0 2.4 %copy-start.4 = (bf16[1,7168,256]{2,1,0:T(8,128)(2,1)S(1)}, bf16[1,7168,256]{2,1,0:T(8,128)(2,1)}, u32[]{:S(2)}) copy-start(bf16[1,7168,256]{2,1,0:T(8,128)(2,1)} %param.9) | copy-start | bytes 11010052
  65.4 2.1 %copy-start.5 = (bf16[1,7168,256]{2,1,0:T(8,128)(2,1)S(1)}, bf16[1,7168,256]{2,1,0:T(8,128)(2,1)}, u32[]{:S(2)}) copy-start(bf16[1,7168,256]{2,1,0:T(8,128)(2,1)} %param.10) | copy-start | bytes 11010052
  67.5 2.1 %copy-start.2 = (bf16[1,256,7168]{2,1,0:T(8,128)(2,1)S(1)}, bf16[1,256,7168]{2,1,0:T(8,128)(2,1)}, u32[]{:S(2)}) copy-start(bf16[1,256,7168]{2,1,0:T(8,128)(2,1)} %param.11) | copy-start | bytes 11010052
  72.3 6.5 %collective-permute-start.8 = (bf16[256,7168]{1,0:T(8,128)(2,1)S(1)}, bf16[256,7168]{1,0:T(8,128)(2,1)S(1)}, u32[]{:S(2)}, u32[]{:S(2)}) collective-permute-start(bf16[256,7168]{1,0:T(8,128)(2,1)S(1)} %pad_maximum_fusion), channel_id=1, source_target_pairs={{0,16},{16,0},{32,48},{48,32},{64,80},{80,64},{96,112},{112,96},{1... | collective-permute-start | bytes 11010056 | tf_op jit(solution)/shard_map/ppermute | solution.py:47
  79.5 13.9 %collective-permute-start.9 = (bf16[64,3584]{1,0:T(8,128)(2,1)S(1)}, bf16[64,3584]{1,0:T(8,128)(2,1)S(1)}, u32[]{:S(2)}, u32[]{:S(2)}) collective-permute-start(bf16[64,3584]{1,0:T(8,128)(2,1)S(1)} %get-tuple-element.14), channel_id=1, source_target_pairs={{0,32},{16,48},{32,64},{48,80},{64,96},{80,112},{96,0},{112,16},{1... | collective-permute-start | bytes 1376264 | tf_op jit(solution)/shard_map/ppermute | solution.py:53
  80.1 13.7 %collective-permute-start.11 = (bf16[64,3584]{1,0:T(8,128)(2,1)S(1)}, bf16[64,3584]{1,0:T(8,128)(2,1)S(1)}, u32[]{:S(2)}, u32[]{:S(2)}) collective-permute-start(bf16[64,3584]{1,0:T(8,128)(2,1)S(1)} %get-tuple-element.15), channel_id=1, source_target_pairs={{0,96},{16,112},{32,0},{48,16},{64,32},{80,48},{96,64},{112,80},{1... | collective-permute-start | bytes 1376264 | tf_op jit(solution)/shard_map/ppermute | solution.py:54
  93.6 22.9 %collective-permute-start.10 = (bf16[64,7168]{1,0:T(8,128)(2,1)S(1)}, bf16[64,7168]{1,0:T(8,128)(2,1)S(1)}, u32[]{:S(2)}, u32[]{:S(2)}) collective-permute-start(bf16[64,7168]{1,0:T(8,128)(2,1)S(1)} %pad_maximum_fusion.2), channel_id=1, source_target_pairs={{0,32},{16,48},{32,64},{48,80},{64,96},{80,112},{96,0},{112,16},{1... | collective-permute-start | bytes 2752520 | tf_op jit(solution)/shard_map/ppermute | solution.py:57
  93.9 30.2 %copy-start.3 = (s32[16,288]{1,0:T(8,128)S(1)}, s32[16,288]{1,0:T(8,128)}, u32[]{:S(2)}) copy-start(s32[16,288]{1,0:T(8,128)} %param.8) | copy-start | bytes 55300
  93.9 22.7 %collective-permute-start.12 = (bf16[64,7168]{1,0:T(8,128)(2,1)S(1)}, bf16[64,7168]{1,0:T(8,128)(2,1)S(1)}, u32[]{:S(2)}, u32[]{:S(2)}) collective-permute-start(bf16[64,7168]{1,0:T(8,128)(2,1)S(1)} %pad_maximum_fusion.3), channel_id=1, source_target_pairs={{0,96},{16,112},{32,0},{48,16},{64,32},{80,48},{96,64},{112,80},{1... | collective-permute-start | bytes 2752520 | tf_op jit(solution)/shard_map/ppermute | solution.py:58
  118.3 18.1 %all-to-all-start.1 = ((bf16[16,4,7168]{2,1,0:T(4,128)(2,1)}), bf16[16,4,7168]{2,1,0:T(4,128)(2,1)S(1)}, u32[]{:S(2)}, u32[]{:S(2)}) async-start(bf16[16,4,7168]{2,1,0:T(4,128)(2,1)} %all_to_all.16), calls=%async_computation.1 | async-start | bytes 1835008 | tf_op jit(solution)/shard_map/all_to_all | solution.py:91
  136.6 2.5 %copy-start.1 = (bf16[128,7168]{1,0:T(8,128)(2,1)S(1)}, bf16[128,7168]{1,0:T(8,128)(2,1)}, u32[]{:S(2)}) copy-start(bf16[128,7168]{1,0:T(8,128)(2,1)} %param.6) | copy-start | bytes 5505028

commit v5 on v4

--- a/solution.py
+++ b/solution.py
@@ -4,17 +4,16 @@
 from jax.sharding import PartitionSpec as P
 
 
-def slot_tables(chosen, tok_count):
+def slot_tables(chosen, tok_count, my_index):
     owners = chosen // tok_count
     capacity = chosen.shape[1]
-    same = owners[:, :, None] == owners[:, None, :]
+    is_mine = owners == my_index
     earlier = (
-        jnp.arange(capacity, dtype=jnp.int32)[None, :]
-        < jnp.arange(capacity, dtype=jnp.int32)[:, None]
-    )
-    ranks = jnp.sum((same & earlier[None]).astype(jnp.int32), axis=2)
-    return (owners, ranks)
-
+        jnp.arange(capacity, dtype=jnp.int32)[:, None]
+        < jnp.arange(capacity, dtype=jnp.int32)[None, :]
+    ).astype(jnp.bfloat16)
+    ranks = jnp.dot(is_mine.astype(jnp.bfloat16), earlier, preferred_element_type=jnp.float32)
+    return (owners, is_mine, ranks.astype(jnp.int32))
 
 def dp_pairs(dp_count, shift):
     ny = dp_count // 2
@@ -44,8 +43,9 @@
     half = p.shape[1] // 2
     f32 = jnp.float32
     b = [p[i * rows:(i + 1) * rows] for i in range(8)]
-    got = lax.ppermute(jnp.concatenate([b[1], b[3], b[5], b[7]], axis=0), "dp", sib_pairs(dp_count))
-    g = [got[i * rows:(i + 1) * rows].astype(f32) for i in range(4)]
+    got_far = lax.ppermute(b[7], "dp", sib_pairs(dp_count))
+    got = lax.ppermute(jnp.concatenate([b[1], b[3], b[5]], axis=0), "dp", sib_pairs(dp_count))
+    g = [got[i * rows:(i + 1) * rows].astype(f32) for i in range(3)] + [got_far.astype(f32)]
     q_self = b[0].astype(f32) + g[0]
     q_up = b[2].astype(f32) + g[1]
     q_dn = b[4].astype(f32) + g[2]
@@ -67,9 +67,8 @@
     expert_total, capacity = chosen.shape
     slot_count = min(tok_count, max(4, 2 * capacity // worker_ordinal))
     my_index = lax.axis_index("dp") * ex_count + lax.axis_index("expert")
-    owners, ranks = slot_tables(chosen, tok_count)
+    owners, is_mine, ranks = slot_tables(chosen, tok_count, my_index)
     local_idx = chosen - owners * tok_count
-    is_mine = owners == my_index
     matches = is_mine[:, :, None] & (
         ranks[:, :, None] == jnp.arange(slot_count, dtype=jnp.int32)[None, None, :]
     )

time: 141 us -> 139 us (0.986)
  other arithmetic: 6.69 us -> 4.25 us
    reduce_sum x1 -> x0, other arithmetic: 2.3 us -> none  [slot_tables(): ranks = jnp.sum((same & earlier[None]).astype(jnp.int32), axis=2)]
    ppermute x1 -> x2, waiting for transfers between devices: 6.27 us -> 5.9 us  [the longest x1 5.9 us: scatter_dp(): got_far = lax.ppermute(b[7], 'dp', sib_pairs(dp_count))]
  transfers between devices with their start and end apart: 14 -> 15, of which waited for: 7 -> 7; matrix products, arithmetic and copies ran while one was open for 1% -> 1% of each run, Pallas kernels for 0% -> 0%
where the time goes in v5:
time: 139 us; the launch traced here: 137 us
  waiting for transfers between devices  76.5 us (55%)
  blocking collectives  21.6 us (16%)
  starting transfers between devices  20.2 us (15%)
  matrix products  8.86 us (6%)
  local copies, waits for them, and re-layouts  4.83 us (3%)
  other arithmetic  4.25 us (3%)
    all_to_all x1, blocking collectives, shards(): lax.all_to_all(send_rows, 'expert', split_axis=0, concat_axis=0, tiled=True)  21.6 us
    ppermute x1, waiting for transfers between devices, scatter_dp(): a_a = lax.ppermute(s_a, 'dp', dp_pairs(dp_count, 1)).astype(f32)  19.4 us
    ppermute x1, waiting for transfers between devices, gather_dp(): up = lax.ppermute(x, 'dp', dp_pairs(dp_count, 1))  19 us
    all_to_all x1, waiting for transfers between devices, shards(): lax.all_to_all(summed, 'expert', split_axis=0, concat_axis=0, tiled=True)  12 us
    ppermute x1, waiting for transfers between devices, scatter_dp(): r_a = lax.ppermute(q_far[:, :half], 'dp', dp_pairs(dp_count, 1)).astype(f32)  10.5 us
    ppermute x1, waiting for transfers between devices, gather_dp(): far_a = lax.ppermute(up[:, :half], 'dp', dp_pairs(dp_count, 1))  7.61 us
    ppermute x1, waiting for transfers between devices, scatter_dp(): got_far = lax.ppermute(b[7], 'dp', sib_pairs(dp_count))  5.9 us
    all_to_all x1, starting transfers between devices, shards(): lax.all_to_all(summed, 'expert', split_axis=0, concat_axis=0, tiled=True)  5.63 us
  transfers between devices with their start and end apart: 15, of which 7 were waited for; matrix products, arithmetic and copies ran while one was open for 1% of the time, Pallas kernels for 0%

profile of v5, /device:TPU:6, one launch (start us, length us, event | category | flops | bytes accessed | tf_op | source)
XLA Modules:
  0.0 136.7 jit_solution(1182494222958422296)
XLA Ops:
  0.0 0.9 multiply_subtract_fusion
  0.9 0.8 fusion.23
  2.5 1.1 gather_fusion
  3.6 0.3 gather.7
  3.9 0.5 select_select_fusion
  4.5 21.6 %all_to_all.21 = bf16[16,4,7168]{2,1,0:T(4,128)(2,1)S(1)} all-to-all(bf16[16,4,7168]{2,1,0:T(4,128)(2,1)S(1)} %select_select_fusion), channel_id=1, replica_groups=mesh['dp'=8,'expert'=16] {'expert'}, dimensions={0} | all-to-all | bytes 1835008 | tf_op jit(solution)/shard_map/all_to_all | solution.py:82
  26.3 1.6 %collective-permute-start.1 = (bf16[64,7168]{1,0:T(8,128)(2,1)S(1)}, bf16[64,7168]{1,0:T(8,128)(2,1)S(1)}, u32[]{:S(2)}, u32[]{:S(2)}) collective-permute-start(bf16[64,7168]{1,0:T(8,128)(2,1)S(1)} %all_to_all.15), channel_id=1, source_target_pairs={{0,32},{16,48},{32,64},{48,80},{64,96},{80,112},{96,0},{112,16},{1... | collective-permute-start | bytes 2752520 | tf_op jit(solution)/shard_map/ppermute | solution.py:29
  28.0 1.7 %collective-permute-start.3 = (bf16[64,7168]{1,0:T(8,128)(2,1)S(1)}, bf16[64,7168]{1,0:T(8,128)(2,1)S(1)}, u32[]{:S(2)}, u32[]{:S(2)}) collective-permute-start(bf16[64,7168]{1,0:T(8,128)(2,1)S(1)} %all_to_all.15), channel_id=1, source_target_pairs={{0,96},{16,112},{32,0},{48,16},{64,32},{80,48},{96,64},{112,80},{1... | collective-permute-start | bytes 2752520 | tf_op jit(solution)/shard_map/ppermute | solution.py:30
  29.7 19.0 %collective-permute-done.1 = bf16[64,7168]{1,0:T(8,128)(2,1)S(1)} collective-permute-done((bf16[64,7168]{1,0:T(8,128)(2,1)S(1)}, bf16[64,7168]{1,0:T(8,128)(2,1)S(1)}, u32[]{:S(2)}, u32[]{:S(2)}) %collective-permute-start.1) | collective-permute-done | bytes 917536 | tf_op jit(solution)/shard_map/ppermute | solution.py:29
  48.7 0.4 collective-permute-start.5
  49.1 3.0 %collective-permute-start.6 = (bf16[64,3584]{1,0:T(8,128)(2,1)S(1)}, bf16[64,3584]{1,0:T(8,128)(2,1)S(1)}, u32[]{:S(2)}, u32[]{:S(2)}) collective-permute-start(bf16[64,3584]{1,0:T(8,128)(2,1)S(1)} %slice.81), channel_id=1, source_target_pairs={{0,96},{16,112},{32,0},{48,16},{64,32},{80,48},{96,64},{112,80},{1... | collective-permute-start | bytes 1376264 | tf_op jit(solution)/shard_map/ppermute | solution.py:33
  52.1 0.5 collective-permute-start.4
  52.8 7.6 %collective-permute-done.5 = bf16[64,3584]{1,0:T(8,128)(2,1)S(1)} collective-permute-done((bf16[64,3584]{1,0:T(8,128)(2,1)S(1)}, bf16[64,3584]{1,0:T(8,128)(2,1)S(1)}, u32[]{:S(2)}, u32[]{:S(2)}) %collective-permute-start.5) | collective-permute-done | bytes 458784 | tf_op jit(solution)/shard_map/ppermute | solution.py:32
  60.9 2.1 %collective-permute-done.7 = bf16[64,7168]{1,0:T(8,128)(2,1)S(1)} collective-permute-done((bf16[64,7168]{1,0:T(8,128)(2,1)S(1)}, bf16[64,7168]{1,0:T(8,128)(2,1)S(1)}, u32[]{:S(2)}, u32[]{:S(2)}) %collective-permute-start.7) | collective-permute-done | bytes 917536 | tf_op jit(solution)/shard_map/ppermute | solution.py:37
  63.1 2.1 %fusion.4 = f32[512,256]{1,0:T(8,128)S(1)} fusion(bf16[512,7168]{1,0:T(8,128)(2,1)S(1)} %constant_dynamic-update-slice_fusion, bf16[1,7168,256]{2,1,0:T(8,128)(2,1)S(1)} %copy-done.4), kind=kOutput, calls=%fused_computation.7 | convolution fusion | flops 1879048192 | bytes 11534336 | tf_op jit(solution)/shard_map/dot_general | solution.py:84
  65.2 2.1 %multiply_convert_fusion = bf16[512,256]{1,0:T(8,128)(2,1)S(1)} fusion(f32[512,256]{1,0:T(8,128)S(1)} %fusion.4, bf16[512,7168]{1,0:T(8,128)(2,1)S(1)} %constant_dynamic-update-slice_fusion, bf16[1,7168,256]{2,1,0:T(8,128)(2,1)S(1)} %copy-done.5), kind=kOutput, calls=%fused_computation.25 | convolution fusion | flops 1879834624 | bytes 11796480 | tf_op jit(solution)/shard_map/dot_general | solution.py:85
  67.2 2.1 %convolution_convert_fusion = bf16[512,7168]{1,0:T(8,128)(2,1)S(1)} fusion(bf16[512,256]{1,0:T(8,128)(2,1)S(1)} %multiply_convert_fusion, bf16[1,256,7168]{2,1,0:T(8,128)(2,1)S(1)} %copy-done.2), kind=kOutput, calls=%fused_computation.1 | convolution fusion | flops 1882718208 | bytes 11272192 | tf_op jit(solution)/shard_map/dot_general | solution.py:88
  69.3 0.2 fusion.27
  70.0 0.4 collective-permute-start.9
  70.4 5.9 %collective-permute-done.9 = bf16[64,7168]{1,0:T(8,128)(2,1)S(1)} collective-permute-done((bf16[64,7168]{1,0:T(8,128)(2,1)S(1)}, bf16[64,7168]{1,0:T(8,128)(2,1)S(1)}, u32[]{:S(2)}, u32[]{:S(2)}) %collective-permute-start.9) | collective-permute-done | bytes 917536 | tf_op jit(solution)/shard_map/ppermute | solution.py:46
  76.3 0.7 convert_add_fusion.1
  77.1 0.5 collective-permute-start.10
  77.6 2.9 %collective-permute-start.12 = (bf16[64,3584]{1,0:T(8,128)(2,1)S(1)}, bf16[64,3584]{1,0:T(8,128)(2,1)S(1)}, u32[]{:S(2)}, u32[]{:S(2)}) collective-permute-start(bf16[64,3584]{1,0:T(8,128)(2,1)S(1)} %get-tuple-element.15), channel_id=1, source_target_pairs={{0,96},{16,112},{32,0},{48,16},{64,32},{80,48},{96,64},{112,80},{1... | collective-permute-start | bytes 1376264 | tf_op jit(solution)/shard_map/ppermute | solution.py:54
  80.5 10.5 %collective-permute-done.10 = bf16[64,3584]{1,0:T(8,128)(2,1)S(1)} collective-permute-done((bf16[64,3584]{1,0:T(8,128)(2,1)S(1)}, bf16[64,3584]{1,0:T(8,128)(2,1)S(1)}, u32[]{:S(2)}, u32[]{:S(2)}) %collective-permute-start.10) | collective-permute-done | bytes 458784 | tf_op jit(solution)/shard_map/ppermute | solution.py:53
  91.4 3.3 %collective-permute-start.13 = (bf16[64,7168]{1,0:T(8,128)(2,1)S(1)}, bf16[64,7168]{1,0:T(8,128)(2,1)S(1)}, u32[]{:S(2)}, u32[]{:S(2)}) collective-permute-start(bf16[64,7168]{1,0:T(8,128)(2,1)S(1)} %pad_maximum_fusion.3), channel_id=1, source_target_pairs={{0,96},{16,112},{32,0},{48,16},{64,32},{80,48},{96,64},{112,80},{1... | collective-permute-start | bytes 2752520 | tf_op jit(solution)/shard_map/ppermute | solution.py:58
  94.7 19.4 %collective-permute-done.11 = bf16[64,7168]{1,0:T(8,128)(2,1)S(1)} collective-permute-done((bf16[64,7168]{1,0:T(8,128)(2,1)S(1)}, bf16[64,7168]{1,0:T(8,128)(2,1)S(1)}, u32[]{:S(2)}, u32[]{:S(2)}) %collective-permute-start.11) | collective-permute-done | bytes 917536 | tf_op jit(solution)/shard_map/ppermute | solution.py:57
  114.1 0.5 add_convert_fusion
  114.5 1.3 all_to_all.16
  115.8 5.6 %all-to-all-start.1 = ((bf16[16,4,7168]{2,1,0:T(4,128)(2,1)}), bf16[16,4,7168]{2,1,0:T(4,128)(2,1)S(1)}, u32[]{:S(2)}, u32[]{:S(2)}) async-start(bf16[16,4,7168]{2,1,0:T(4,128)(2,1)} %all_to_all.16), calls=%async_computation.1 | async-start | bytes 1835008 | tf_op jit(solution)/shard_map/all_to_all | solution.py:90
  121.9 12.0 %all-to-all-done.1 = bf16[16,4,7168]{2,1,0:T(4,128)(2,1)S(1)} async-done(((bf16[16,4,7168]{2,1,0:T(4,128)(2,1)}), bf16[16,4,7168]{2,1,0:T(4,128)(2,1)S(1)}, u32[]{:S(2)}, u32[]{:S(2)}) %all-to-all-start.1) | async-done | bytes 917536 | tf_op jit(solution)/shard_map/all_to_all | solution.py:90
  134.1 0.6 fusion.11
  134.8 1.9 %fusion = bf16[128,7168]{1,0:T(8,128)(2,1)} fusion(f32[128,7168]{1,0:T(8,128)S(1)} %fusion.11, bf16[64,7168]{1,0:T(8,128)(2,1)S(1)} %all_to_all.18, f32[64]{0:T(128)S(1)} %broadcast_in_dim.43, s32[64]{0:T(128)S(1)} %eq.40, pred[64]{0:T(512)(128)(4,1)S(1)} %gt.25), kind=kOutput, calls=%fused_computation.3 | convolution fusion | flops 119332864 | bytes 6423104 | tf_op jit(solution)/shard_map/dot_general | solution.py:97
  (62 shorter events, 3.3 us)
Async XLA Ops:
  0.0 2.5 %copy-start = (bf16[128,7168]{1,0:T(8,128)(2,1)S(1)}, bf16[128,7168]{1,0:T(8,128)(2,1)}, u32[]{:S(2)}) copy-start(bf16[128,7168]{1,0:T(8,128)(2,1)} %param.6) | copy-start | bytes 5505028
  26.3 22.4 %collective-permute-start.1 = (bf16[64,7168]{1,0:T(8,128)(2,1)S(1)}, bf16[64,7168]{1,0:T(8,128)(2,1)S(1)}, u32[]{:S(2)}, u32[]{:S(2)}) collective-permute-start(bf16[64,7168]{1,0:T(8,128)(2,1)S(1)} %all_to_all.15), channel_id=1, source_target_pairs={{0,32},{16,48},{32,64},{48,80},{64,96},{80,112},{96,0},{112,16},{1... | collective-permute-start | bytes 2752520 | tf_op jit(solution)/shard_map/ppermute | solution.py:29
  28.0 21.1 %collective-permute-start.3 = (bf16[64,7168]{1,0:T(8,128)(2,1)S(1)}, bf16[64,7168]{1,0:T(8,128)(2,1)S(1)}, u32[]{:S(2)}, u32[]{:S(2)}) collective-permute-start(bf16[64,7168]{1,0:T(8,128)(2,1)S(1)} %all_to_all.15), channel_id=1, source_target_pairs={{0,96},{16,112},{32,0},{48,16},{64,32},{80,48},{96,64},{112,80},{1... | collective-permute-start | bytes 2752520 | tf_op jit(solution)/shard_map/ppermute | solution.py:30
  29.6 23.0 %collective-permute-start = (bf16[64,7168]{1,0:T(8,128)(2,1)S(1)}, bf16[64,7168]{1,0:T(8,128)(2,1)S(1)}, u32[]{:S(2)}, u32[]{:S(2)}) collective-permute-start(bf16[64,7168]{1,0:T(8,128)(2,1)S(1)} %all_to_all.15), channel_id=1, source_target_pairs={{0,16},{16,0},{32,48},{48,32},{64,80},{80,64},{96,112},{112,96},{1... | collective-permute-start | bytes 2752520 | tf_op jit(solution)/shard_map/ppermute | solution.py:31
  48.7 11.7 %collective-permute-start.5 = (bf16[64,3584]{1,0:T(8,128)(2,1)S(1)}, bf16[64,3584]{1,0:T(8,128)(2,1)S(1)}, u32[]{:S(2)}, u32[]{:S(2)}) collective-permute-start(bf16[64,3584]{1,0:T(8,128)(2,1)S(1)} %slice.80), channel_id=1, source_target_pairs={{0,32},{16,48},{32,64},{48,80},{64,96},{80,112},{96,0},{112,16},{1... | collective-permute-start | bytes 1376264 | tf_op jit(solution)/shard_map/ppermute | solution.py:32
  49.1 11.3 %collective-permute-start.6 = (bf16[64,3584]{1,0:T(8,128)(2,1)S(1)}, bf16[64,3584]{1,0:T(8,128)(2,1)S(1)}, u32[]{:S(2)}, u32[]{:S(2)}) collective-permute-start(bf16[64,3584]{1,0:T(8,128)(2,1)S(1)} %slice.81), channel_id=1, source_target_pairs={{0,96},{16,112},{32,0},{48,16},{64,32},{80,48},{96,64},{112,80},{1... | collective-permute-start | bytes 1376264 | tf_op jit(solution)/shard_map/ppermute | solution.py:33
  52.1 8.4 %collective-permute-start.2 = (bf16[64,7168]{1,0:T(8,128)(2,1)S(1)}, bf16[64,7168]{1,0:T(8,128)(2,1)S(1)}, u32[]{:S(2)}, u32[]{:S(2)}) collective-permute-start(bf16[64,7168]{1,0:T(8,128)(2,1)S(1)} %collective-permute-done.1), channel_id=1, source_target_pairs={{0,16},{16,0},{32,48},{48,32},{64,80},{80,64},{96,112},{112,96},{1... | collective-permute-start | bytes 2752520 | tf_op jit(solution)/shard_map/ppermute | solution.py:35
  52.1 8.6 %collective-permute-start.4 = (bf16[64,7168]{1,0:T(8,128)(2,1)S(1)}, bf16[64,7168]{1,0:T(8,128)(2,1)S(1)}, u32[]{:S(2)}, u32[]{:S(2)}) collective-permute-start(bf16[64,7168]{1,0:T(8,128)(2,1)S(1)} %collective-permute-done.3), channel_id=1, source_target_pairs={{0,16},{16,0},{32,48},{48,32},{64,80},{80,64},{96,112},{112,96},{1... | collective-permute-start | bytes 2752520 | tf_op jit(solution)/shard_map/ppermute | solution.py:36
  60.4 2.6 %collective-permute-start.7 = (bf16[64,7168]{1,0:T(8,128)(2,1)S(1)}, bf16[64,7168]{1,0:T(8,128)(2,1)S(1)}, u32[]{:S(2)}, u32[]{:S(2)}) collective-permute-start(bf16[64,7168]{1,0:T(8,128)(2,1)S(1)} %pad_maximum_fusion.1), channel_id=1, source_target_pairs={{0,16},{16,0},{32,48},{48,32},{64,80},{80,64},{96,112},{112,96},{1... | collective-permute-start | bytes 2752520 | tf_op jit(solution)/shard_map/ppermute | solution.py:37
  60.6 2.4 %copy-start.4 = (bf16[1,7168,256]{2,1,0:T(8,128)(2,1)S(1)}, bf16[1,7168,256]{2,1,0:T(8,128)(2,1)}, u32[]{:S(2)}) copy-start(bf16[1,7168,256]{2,1,0:T(8,128)(2,1)} %param.9) | copy-start | bytes 11010052
  63.1 2.1 %copy-start.5 = (bf16[1,7168,256]{2,1,0:T(8,128)(2,1)S(1)}, bf16[1,7168,256]{2,1,0:T(8,128)(2,1)}, u32[]{:S(2)}) copy-start(bf16[1,7168,256]{2,1,0:T(8,128)(2,1)} %param.10) | copy-start | bytes 11010052
  65.2 2.1 %copy-start.2 = (bf16[1,256,7168]{2,1,0:T(8,128)(2,1)S(1)}, bf16[1,256,7168]{2,1,0:T(8,128)(2,1)}, u32[]{:S(2)}) copy-start(bf16[1,256,7168]{2,1,0:T(8,128)(2,1)} %param.11) | copy-start | bytes 11010052
  69.8 6.5 %collective-permute-start.8 = (bf16[192,7168]{1,0:T(8,128)(2,1)S(1)}, bf16[192,7168]{1,0:T(8,128)(2,1)S(1)}, u32[]{:S(2)}, u32[]{:S(2)}) collective-permute-start(bf16[192,7168]{1,0:T(8,128)(2,1)S(1)} %pad_maximum_fusion), channel_id=1, source_target_pairs={{0,16},{16,0},{32,48},{48,32},{64,80},{80,64},{96,112},{112,96},{1... | collective-permute-start | bytes 8257544 | tf_op jit(solution)/shard_map/ppermute | solution.py:47
  70.0 6.3 %collective-permute-start.9 = (bf16[64,7168]{1,0:T(8,128)(2,1)S(1)}, bf16[64,7168]{1,0:T(8,128)(2,1)S(1)}, u32[]{:S(2)}, u32[]{:S(2)}) collective-permute-start(bf16[64,7168]{1,0:T(8,128)(2,1)S(1)} %get-tuple-element.10), channel_id=1, source_target_pairs={{0,16},{16,0},{32,48},{48,32},{64,80},{80,64},{96,112},{112,96},{1... | collective-permute-start | bytes 2752520 | tf_op jit(solution)/shard_map/ppermute | solution.py:46
  77.1 13.9 %collective-permute-start.10 = (bf16[64,3584]{1,0:T(8,128)(2,1)S(1)}, bf16[64,3584]{1,0:T(8,128)(2,1)S(1)}, u32[]{:S(2)}, u32[]{:S(2)}) collective-permute-start(bf16[64,3584]{1,0:T(8,128)(2,1)S(1)} %get-tuple-element.14), channel_id=1, source_target_pairs={{0,32},{16,48},{32,64},{48,80},{64,96},{80,112},{96,0},{112,16},{1... | collective-permute-start | bytes 1376264 | tf_op jit(solution)/shard_map/ppermute | solution.py:53
  77.6 13.6 %collective-permute-start.12 = (bf16[64,3584]{1,0:T(8,128)(2,1)S(1)}, bf16[64,3584]{1,0:T(8,128)(2,1)S(1)}, u32[]{:S(2)}, u32[]{:S(2)}) collective-permute-start(bf16[64,3584]{1,0:T(8,128)(2,1)S(1)} %get-tuple-element.15), channel_id=1, source_target_pairs={{0,96},{16,112},{32,0},{48,16},{64,32},{80,48},{96,64},{112,80},{1... | collective-permute-start | bytes 1376264 | tf_op jit(solution)/shard_map/ppermute | solution.py:54
  91.2 22.9 %collective-permute-start.11 = (bf16[64,7168]{1,0:T(8,128)(2,1)S(1)}, bf16[64,7168]{1,0:T(8,128)(2,1)S(1)}, u32[]{:S(2)}, u32[]{:S(2)}) collective-permute-start(bf16[64,7168]{1,0:T(8,128)(2,1)S(1)} %pad_maximum_fusion.2), channel_id=1, source_target_pairs={{0,32},{16,48},{32,64},{48,80},{64,96},{80,112},{96,0},{112,16},{1... | collective-permute-start | bytes 2752520 | tf_op jit(solution)/shard_map/ppermute | solution.py:57
  91.4 30.2 %copy-start.3 = (s32[16,288]{1,0:T(8,128)S(1)}, s32[16,288]{1,0:T(8,128)}, u32[]{:S(2)}) copy-start(s32[16,288]{1,0:T(8,128)} %param.8) | copy-start | bytes 55300
  91.4 22.7 %collective-permute-start.13 = (bf16[64,7168]{1,0:T(8,128)(2,1)S(1)}, bf16[64,7168]{1,0:T(8,128)(2,1)S(1)}, u32[]{:S(2)}, u32[]{:S(2)}) collective-permute-start(bf16[64,7168]{1,0:T(8,128)(2,1)S(1)} %pad_maximum_fusion.3), channel_id=1, source_target_pairs={{0,96},{16,112},{32,0},{48,16},{64,32},{80,48},{96,64},{112,80},{1... | collective-permute-start | bytes 2752520 | tf_op jit(solution)/shard_map/ppermute | solution.py:58
  115.8 18.1 %all-to-all-start.1 = ((bf16[16,4,7168]{2,1,0:T(4,128)(2,1)}), bf16[16,4,7168]{2,1,0:T(4,128)(2,1)S(1)}, u32[]{:S(2)}, u32[]{:S(2)}) async-start(bf16[16,4,7168]{2,1,0:T(4,128)(2,1)} %all_to_all.16), calls=%async_computation.1 | async-start | bytes 1835008 | tf_op jit(solution)/shard_map/all_to_all | solution.py:90
  134.1 2.5 %copy-start.1 = (bf16[128,7168]{1,0:T(8,128)(2,1)S(1)}, bf16[128,7168]{1,0:T(8,128)(2,1)}, u32[]{:S(2)}) copy-start(bf16[128,7168]{1,0:T(8,128)(2,1)} %param.6) | copy-start | bytes 5505028

commit v6 on v5

--- a/solution.py
+++ b/solution.py
@@ -79,15 +79,27 @@
     weights = jnp.sum(matches.astype(jnp.float32) * scaled[:, :, None], axis=1)
     send_rows = jnp.take(tokens, source_idx.reshape(-1), axis=0)
     send_rows = jnp.where(present.reshape(-1, 1) > 0, send_rows, jnp.zeros_like(send_rows))
-    row_in = lax.all_to_all(send_rows, "expert", split_axis=0, concat_axis=0, tiled=True)
-    picked = gather_dp(row_in, dp_count)
-    gate_act = jnp.dot(picked, w_gate[0], preferred_element_type=jnp.float32)
-    up_act = jnp.dot(picked, w_up[0], preferred_element_type=jnp.float32)
+    halves = 2
+    width = model_width // halves
+    gate_act = None
+    up_act = None
+    for c in range(halves):
+        cols = slice(c * width, (c + 1) * width)
+        row_in = lax.all_to_all(send_rows[:, cols], "expert", split_axis=0, concat_axis=0, tiled=True)
+        picked = gather_dp(row_in, dp_count)
+        g = jnp.dot(picked, w_gate[0, cols], preferred_element_type=jnp.float32)
+        u = jnp.dot(picked, w_up[0, cols], preferred_element_type=jnp.float32)
+        gate_act = g if gate_act is None else gate_act + g
+        up_act = u if up_act is None else up_act + u
     hidden = (jax.nn.silu(gate_act) * up_act).astype(jnp.bfloat16)
     hidden = lax.optimization_barrier(hidden)
-    result = jnp.dot(hidden, w_down[0], preferred_element_type=jnp.float32).astype(jnp.bfloat16)
-    summed = scatter_dp(result, dp_count)
-    returned = lax.all_to_all(summed, "expert", split_axis=0, concat_axis=0, tiled=True)
+    back = []
+    for c in range(halves):
+        cols = slice(c * width, (c + 1) * width)
+        result = jnp.dot(hidden, w_down[0, :, cols], preferred_element_type=jnp.float32).astype(jnp.bfloat16)
+        summed = scatter_dp(result, dp_count)
+        back.append(lax.all_to_all(summed, "expert", split_axis=0, concat_axis=0, tiled=True))
+    returned = jnp.concatenate(back, axis=1)
     placed = (jnp.arange(tok_count, dtype=jnp.int32)[:, None] == source_idx.reshape(1, -1)) & (
         present.reshape(1, -1) > 0
     )

time: 139 us -> 151 us (1.086)
  starting transfers between devices: 20.2 us -> 53.2 us
  blocking collectives: 21.6 us -> 0 us
  waiting for transfers between devices: 76.5 us -> 64.7 us
  local copies, waits for them, and re-layouts: 4.83 us -> 15.6 us
    all_to_all x1 -> x0, blocking collectives: 21.6 us -> none  [shards(): lax.all_to_all(send_rows, 'expert', split_axis=0, concat_axis=0, tiled=True)]
    all_to_all x0 -> x2, starting transfers between devices: none -> 13.8 us  [shards(): lax.all_to_all(send_rows[:, cols], 'expert', split_axis=0, concat_axis=0,...]
    all_to_all x0 -> x2, waiting for transfers between devices: none -> 11.1 us  [shards(): lax.all_to_all(send_rows[:, cols], 'expert', split_axis=0, concat_axis=0,...]
    unnamed x20 -> x33, local copies, waits for them, and re-layouts: 0.47 us -> 9.31 us
    ppermute x1 -> x2, waiting for transfers between devices: 19 us -> 11.6 us  [gather_dp(): up = lax.ppermute(x, 'dp', dp_pairs(dp_count, 1))]
    all_to_all x1 -> x2, starting transfers between devices: 5.63 us -> 12.7 us  [shards(): lax.all_to_all(summed, 'expert', split_axis=0, concat_axis=0, tiled=True)]
    ppermute x1 -> x2, waiting for transfers between devices: 7.61 us -> 0.87 us  [gather_dp(): far_a = lax.ppermute(up[:, :half], 'dp', dp_pairs(dp_count, 1))]
    ppermute x1 -> x2, waiting for transfers between devices: 19.4 us -> 14.6 us  [scatter_dp(): a_a = lax.ppermute(s_a, 'dp', dp_pairs(dp_count, 1)).astype(f32)]
  transfers between devices with their start and end apart: 15 -> 32, of which waited for: 7 -> 14; matrix products, arithmetic and copies ran while one was open for 1% -> 8% of each run, Pallas kernels for 0% -> 0%
where the time goes in v6:
time: 151 us; the launch traced here: 149 us
  waiting for transfers between devices  64.7 us (43%)
  starting transfers between devices  53.2 us (35%)
  local copies, waits for them, and re-layouts  15.6 us (10%)
  matrix products  9.35 us (6%)
  other arithmetic  5.1 us (3%)
    ppermute x2, waiting for transfers between devices, scatter_dp(): a_a = lax.ppermute(s_a, 'dp', dp_pairs(dp_count, 1)).astype(f32)  14.6 us
    all_to_all x2, starting transfers between devices, shards(): lax.all_to_all(send_rows[:, cols], 'expert', split_axis=0, concat_axis=0,...  13.8 us
    all_to_all x2, waiting for transfers between devices, shards(): lax.all_to_all(summed, 'expert', split_axis=0, concat_axis=0, tiled=True)  13.4 us
    all_to_all x2, starting transfers between devices, shards(): lax.all_to_all(summed, 'expert', split_axis=0, concat_axis=0, tiled=True)  12.7 us
    ppermute x2, waiting for transfers between devices, gather_dp(): up = lax.ppermute(x, 'dp', dp_pairs(dp_count, 1))  11.6 us
    all_to_all x2, waiting for transfers between devices, shards(): lax.all_to_all(send_rows[:, cols], 'expert', split_axis=0, concat_axis=0,...  11.1 us
    unnamed x33, local copies, waits for them, and re-layouts  9.31 us
    ppermute x2, waiting for transfers between devices, scatter_dp(): r_a = lax.ppermute(q_far[:, :half], 'dp', dp_pairs(dp_count, 1)).astype(f32)  7.29 us
  transfers between devices with their start and end apart: 32, of which 14 were waited for; matrix products, arithmetic and copies ran while one was open for 8% of the time, Pallas kernels for 0%

profile of v6, /device:TPU:6, one launch (start us, length us, event | category | flops | bytes accessed | tf_op | source)
XLA Modules:
  0.0 148.6 jit_solution(2812786776836899832)
XLA Ops:
  2.6 1.1 gather_fusion
  4.9 8.3 %all-to-all-start = ((bf16[16,4,3584]{2,1,0:T(4,128)(2,1)}), bf16[16,4,3584]{2,1,0:T(4,128)(2,1)S(1)}, u32[]{:S(2)}, u32[]{:S(2)}) async-start(bf16[16,4,3584]{2,1,0:T(4,128)(2,1)} %all_to_all.32), calls=%async_computation | async-start | bytes 917504 | tf_op jit(solution)/shard_map/all_to_all | solution.py:88
  14.3 7.6 %all-to-all-done = bf16[16,4,3584]{2,1,0:T(4,128)(2,1)S(1)} async-done(((bf16[16,4,3584]{2,1,0:T(4,128)(2,1)}), bf16[16,4,3584]{2,1,0:T(4,128)(2,1)S(1)}, u32[]{:S(2)}, u32[]{:S(2)}) %all-to-all-start) | async-done | bytes 458784 | tf_op jit(solution)/shard_map/all_to_all | solution.py:88
  21.9 5.5 %all-to-all-start.1 = ((bf16[16,4,3584]{2,1,0:T(4,128)(2,1)}), bf16[16,4,3584]{2,1,0:T(4,128)(2,1)S(1)}, u32[]{:S(2)}, u32[]{:S(2)}) async-start(bf16[16,4,3584]{2,1,0:T(4,128)(2,1)} %all_to_all.35), calls=%async_computation.1 | async-start | bytes 917504 | tf_op jit(solution)/shard_map/all_to_all | solution.py:88
  27.6 1.6 %collective-permute-start.1 = (bf16[64,3584]{1,0:T(8,128)(2,1)S(1)}, bf16[64,3584]{1,0:T(8,128)(2,1)S(1)}, u32[]{:S(2)}, u32[]{:S(2)}) collective-permute-start(bf16[64,3584]{1,0:T(8,128)(2,1)S(1)} %all_to_all.34), channel_id=1, source_target_pairs={{0,32},{16,48},{32,64},{48,80},{64,96},{80,112},{96,0},{112,16},{1... | collective-permute-start | bytes 1376264 | tf_op jit(solution)/shard_map/ppermute | solution.py:29
  29.3 1.7 %collective-permute-start.3 = (bf16[64,3584]{1,0:T(8,128)(2,1)S(1)}, bf16[64,3584]{1,0:T(8,128)(2,1)S(1)}, u32[]{:S(2)}, u32[]{:S(2)}) collective-permute-start(bf16[64,3584]{1,0:T(8,128)(2,1)S(1)} %all_to_all.34), channel_id=1, source_target_pairs={{0,96},{16,112},{32,0},{48,16},{64,32},{80,48},{96,64},{112,80},{1... | collective-permute-start | bytes 1376264 | tf_op jit(solution)/shard_map/ppermute | solution.py:30
  31.7 3.4 %all-to-all-done.1 = bf16[16,4,3584]{2,1,0:T(4,128)(2,1)S(1)} async-done(((bf16[16,4,3584]{2,1,0:T(4,128)(2,1)}), bf16[16,4,3584]{2,1,0:T(4,128)(2,1)S(1)}, u32[]{:S(2)}, u32[]{:S(2)}) %all-to-all-start.1) | async-done | bytes 458784 | tf_op jit(solution)/shard_map/all_to_all | solution.py:88
  35.3 1.6 %collective-permute-start.9 = (bf16[64,3584]{1,0:T(8,128)(2,1)S(1)}, bf16[64,3584]{1,0:T(8,128)(2,1)S(1)}, u32[]{:S(2)}, u32[]{:S(2)}) collective-permute-start(bf16[64,3584]{1,0:T(8,128)(2,1)S(1)} %all_to_all.37), channel_id=1, source_target_pairs={{0,32},{16,48},{32,64},{48,80},{64,96},{80,112},{96,0},{112,16},{1... | collective-permute-start | bytes 1376264 | tf_op jit(solution)/shard_map/ppermute | solution.py:29
  36.9 1.7 %collective-permute-start.11 = (bf16[64,3584]{1,0:T(8,128)(2,1)S(1)}, bf16[64,3584]{1,0:T(8,128)(2,1)S(1)}, u32[]{:S(2)}, u32[]{:S(2)}) collective-permute-start(bf16[64,3584]{1,0:T(8,128)(2,1)S(1)} %all_to_all.37), channel_id=1, source_target_pairs={{0,96},{16,112},{32,0},{48,16},{64,32},{80,48},{96,64},{112,80},{1... | collective-permute-start | bytes 1376264 | tf_op jit(solution)/shard_map/ppermute | solution.py:30
  38.6 3.7 %collective-permute-done.1 = bf16[64,3584]{1,0:T(8,128)(2,1)S(1)} collective-permute-done((bf16[64,3584]{1,0:T(8,128)(2,1)S(1)}, bf16[64,3584]{1,0:T(8,128)(2,1)S(1)}, u32[]{:S(2)}, u32[]{:S(2)}) %collective-permute-start.1) | collective-permute-done | bytes 458784 | tf_op jit(solution)/shard_map/ppermute | solution.py:29
  42.7 1.6 %collective-permute-start.5 = (bf16[64,1792]{1,0:T(8,128)(2,1)S(1)}, bf16[64,1792]{1,0:T(8,128)(2,1)S(1)}, u32[]{:S(2)}, u32[]{:S(2)}) collective-permute-start(bf16[64,1792]{1,0:T(8,128)(2,1)S(1)} %slice.191), channel_id=1, source_target_pairs={{0,32},{16,48},{32,64},{48,80},{64,96},{80,112},{96,0},{112,16},{1... | collective-permute-start | bytes 688136 | tf_op jit(solution)/shard_map/ppermute | solution.py:32
  44.3 7.9 %collective-permute-done.9 = bf16[64,3584]{1,0:T(8,128)(2,1)S(1)} collective-permute-done((bf16[64,3584]{1,0:T(8,128)(2,1)S(1)}, bf16[64,3584]{1,0:T(8,128)(2,1)S(1)}, u32[]{:S(2)}, u32[]{:S(2)}) %collective-permute-start.9) | collective-permute-done | bytes 458784 | tf_op jit(solution)/shard_map/ppermute | solution.py:29
  52.1 1.8 %collective-permute-start.6 = (bf16[64,1792]{1,0:T(8,128)(2,1)S(1)}, bf16[64,1792]{1,0:T(8,128)(2,1)S(1)}, u32[]{:S(2)}, u32[]{:S(2)}) collective-permute-start(bf16[64,1792]{1,0:T(8,128)(2,1)S(1)} %slice.192), channel_id=1, source_target_pairs={{0,96},{16,112},{32,0},{48,16},{64,32},{80,48},{96,64},{112,80},{1... | collective-permute-start | bytes 688136 | tf_op jit(solution)/shard_map/ppermute | solution.py:33
  54.3 3.1 %collective-permute-start.14 = (bf16[64,1792]{1,0:T(8,128)(2,1)S(1)}, bf16[64,1792]{1,0:T(8,128)(2,1)S(1)}, u32[]{:S(2)}, u32[]{:S(2)}) collective-permute-start(bf16[64,1792]{1,0:T(8,128)(2,1)S(1)} %slice.195), channel_id=1, source_target_pairs={{0,96},{16,112},{32,0},{48,16},{64,32},{80,48},{96,64},{112,80},{1... | collective-permute-start | bytes 688136 | tf_op jit(solution)/shard_map/ppermute | solution.py:33
  61.5 2.2 %collective-permute-done.14 = bf16[64,1792]{1,0:T(8,128)(2,1)S(1)} collective-permute-done((bf16[64,1792]{1,0:T(8,128)(2,1)S(1)}, bf16[64,1792]{1,0:T(8,128)(2,1)S(1)}, u32[]{:S(2)}, u32[]{:S(2)}) %collective-permute-start.14) | collective-permute-done | bytes 229408 | tf_op jit(solution)/shard_map/ppermute | solution.py:33
  72.8 1.1 fusion.17
  73.9 1.1 multiply_convert_fusion
  75.9 1.1 convolution_convert_fusion
  77.1 1.1 convolution_convert_fusion.1
  79.8 2.5 %collective-permute-done.23 = bf16[64,3584]{1,0:T(8,128)(2,1)S(1)} collective-permute-done((bf16[64,3584]{1,0:T(8,128)(2,1)S(1)}, bf16[64,3584]{1,0:T(8,128)(2,1)S(1)}, u32[]{:S(2)}, u32[]{:S(2)}) %collective-permute-start.23) | collective-permute-done | bytes 458784 | tf_op jit(solution)/shard_map/ppermute | solution.py:46
  83.0 3.1 %collective-permute-start.26 = (bf16[64,1792]{1,0:T(8,128)(2,1)S(1)}, bf16[64,1792]{1,0:T(8,128)(2,1)S(1)}, u32[]{:S(2)}, u32[]{:S(2)}) collective-permute-start(bf16[64,1792]{1,0:T(8,128)(2,1)S(1)} %get-tuple-element.24), channel_id=1, source_target_pairs={{0,96},{16,112},{32,0},{48,16},{64,32},{80,48},{96,64},{112,80},{1... | collective-permute-start | bytes 688136 | tf_op jit(solution)/shard_map/ppermute | solution.py:54
  86.6 3.3 %collective-permute-start.20 = (bf16[64,1792]{1,0:T(8,128)(2,1)S(1)}, bf16[64,1792]{1,0:T(8,128)(2,1)S(1)}, u32[]{:S(2)}, u32[]{:S(2)}) collective-permute-start(bf16[64,1792]{1,0:T(8,128)(2,1)S(1)} %get-tuple-element.26), channel_id=1, source_target_pairs={{0,96},{16,112},{32,0},{48,16},{64,32},{80,48},{96,64},{112,80},{1... | collective-permute-start | bytes 688136 | tf_op jit(solution)/shard_map/ppermute | solution.py:54
  89.9 2.5 %collective-permute-done.24 = bf16[64,1792]{1,0:T(8,128)(2,1)S(1)} collective-permute-done((bf16[64,1792]{1,0:T(8,128)(2,1)S(1)}, bf16[64,1792]{1,0:T(8,128)(2,1)S(1)}, u32[]{:S(2)}, u32[]{:S(2)}) %collective-permute-start.24) | collective-permute-done | bytes 229408 | tf_op jit(solution)/shard_map/ppermute | solution.py:53
  92.6 4.7 %collective-permute-done.18 = bf16[64,1792]{1,0:T(8,128)(2,1)S(1)} collective-permute-done((bf16[64,1792]{1,0:T(8,128)(2,1)S(1)}, bf16[64,1792]{1,0:T(8,128)(2,1)S(1)}, u32[]{:S(2)}, u32[]{:S(2)}) %collective-permute-start.18) | collective-permute-done | bytes 229408 | tf_op jit(solution)/shard_map/ppermute | solution.py:53
  97.6 3.3 %collective-permute-start.21 = (bf16[64,3584]{1,0:T(8,128)(2,1)S(1)}, bf16[64,3584]{1,0:T(8,128)(2,1)S(1)}, u32[]{:S(2)}, u32[]{:S(2)}) collective-permute-start(bf16[64,3584]{1,0:T(8,128)(2,1)S(1)} %pad_maximum_fusion.5), channel_id=1, source_target_pairs={{0,96},{16,112},{32,0},{48,16},{64,32},{80,48},{96,64},{112,80},{1... | collective-permute-start | bytes 1376264 | tf_op jit(solution)/shard_map/ppermute | solution.py:58
  101.5 14.6 %collective-permute-done.19 = bf16[64,3584]{1,0:T(8,128)(2,1)S(1)} collective-permute-done((bf16[64,3584]{1,0:T(8,128)(2,1)S(1)}, bf16[64,3584]{1,0:T(8,128)(2,1)S(1)}, u32[]{:S(2)}, u32[]{:S(2)}) %collective-permute-start.19) | collective-permute-done | bytes 458784 | tf_op jit(solution)/shard_map/ppermute | solution.py:57
  117.3 7.2 %all-to-all-start.2 = ((bf16[16,4,3584]{2,1,0:T(4,128)(2,1)}), bf16[16,4,3584]{2,1,0:T(4,128)(2,1)S(1)}, u32[]{:S(2)}, u32[]{:S(2)}) async-start(bf16[16,4,3584]{2,1,0:T(4,128)(2,1)} %all_to_all.38), calls=%async_computation.2 | async-start | bytes 917504 | tf_op jit(solution)/shard_map/all_to_all | solution.py:101
  124.5 1.5 %add_convert_fusion = bf16[64,3584]{1,0:T(8,128)(2,1)S(1)} fusion(bf16[64,3584]{1,0:T(8,128)(2,1)} %collective-permute-done.27, bf16[64,3584]{1,0:T(8,128)(2,1)} %collective-permute-done.25, bf16[192,3584]{1,0:T(8,128)(2,1)S(1)} %collective-permute-done.22, bf16[512,3584]{1,0:T(8,128)(2,1)} %copy-done.2), kind=kLoop, calls=%fused_computation.26 | loop fusion | flops 1835008 | bytes 2293760 | tf_op jit(solution)/shard_map/convert_element_type | solution.py:59
  126.9 5.8 %all-to-all-done.2 = bf16[16,4,3584]{2,1,0:T(4,128)(2,1)S(1)} async-done(((bf16[16,4,3584]{2,1,0:T(4,128)(2,1)}), bf16[16,4,3584]{2,1,0:T(4,128)(2,1)S(1)}, u32[]{:S(2)}, u32[]{:S(2)}) %all-to-all-start.2) | async-done | bytes 458784 | tf_op jit(solution)/shard_map/all_to_all | solution.py:101
  132.7 5.5 %all-to-all-start.3 = ((bf16[16,4,3584]{2,1,0:T(4,128)(2,1)}), bf16[16,4,3584]{2,1,0:T(4,128)(2,1)S(1)}, u32[]{:S(2)}, u32[]{:S(2)}) async-start(bf16[16,4,3584]{2,1,0:T(4,128)(2,1)} %all_to_all.41), calls=%async_computation.3 | async-start | bytes 917504 | tf_op jit(solution)/shard_map/all_to_all | solution.py:101
  138.4 7.6 %all-to-all-done.3 = bf16[16,4,3584]{2,1,0:T(4,128)(2,1)S(1)} async-done(((bf16[16,4,3584]{2,1,0:T(4,128)(2,1)}), bf16[16,4,3584]{2,1,0:T(4,128)(2,1)S(1)}, u32[]{:S(2)}, u32[]{:S(2)}) %all-to-all-start.3) | async-done | bytes 458784 | tf_op jit(solution)/shard_map/all_to_all | solution.py:101
  146.7 1.9 %fusion = bf16[128,7168]{1,0:T(8,128)(2,1)} fusion(f32[128,7168]{1,0:T(8,128)S(1)} %fusion.30, bf16[64,7168]{1,0:T(8,128)(2,1)S(1)} %constant_dynamic-update-slice_fusion.16, f32[64]{0:T(128)S(1)} %broadcast_in_dim.43, s32[64]{0:T(128)S(1)} %eq.40, pred[64]{0:T(512)(128)(4,1)S(1)} %gt.27), kind=kOutput, calls=%fused_computation.2 | convolution fusion | flops 119332864 | bytes 6423104 | tf_op jit(solution)/shard_map/dot_general | solution.py:109
  (132 shorter events, 27.3 us)
Async XLA Ops:
  4.9 17.1 %all-to-all-start = ((bf16[16,4,3584]{2,1,0:T(4,128)(2,1)}), bf16[16,4,3584]{2,1,0:T(4,128)(2,1)S(1)}, u32[]{:S(2)}, u32[]{:S(2)}) async-start(bf16[16,4,3584]{2,1,0:T(4,128)(2,1)} %all_to_all.32), calls=%async_computation | async-start | bytes 917504 | tf_op jit(solution)/shard_map/all_to_all | solution.py:88
  21.9 13.2 %all-to-all-start.1 = ((bf16[16,4,3584]{2,1,0:T(4,128)(2,1)}), bf16[16,4,3584]{2,1,0:T(4,128)(2,1)S(1)}, u32[]{:S(2)}, u32[]{:S(2)}) async-start(bf16[16,4,3584]{2,1,0:T(4,128)(2,1)} %all_to_all.35), calls=%async_computation.1 | async-start | bytes 917504 | tf_op jit(solution)/shard_map/all_to_all | solution.py:88
  27.5 26.7 %collective-permute-start = (bf16[64,3584]{1,0:T(8,128)(2,1)S(1)}, bf16[64,3584]{1,0:T(8,128)(2,1)S(1)}, u32[]{:S(2)}, u32[]{:S(2)}) collective-permute-start(bf16[64,3584]{1,0:T(8,128)(2,1)S(1)} %all_to_all.34), channel_id=1, source_target_pairs={{0,16},{16,0},{32,48},{48,32},{64,80},{80,64},{96,112},{112,96},{1... | collective-permute-start | bytes 1376264 | tf_op jit(solution)/shard_map/ppermute | solution.py:31
  27.6 14.7 %collective-permute-start.1 = (bf16[64,3584]{1,0:T(8,128)(2,1)S(1)}, bf16[64,3584]{1,0:T(8,128)(2,1)S(1)}, u32[]{:S(2)}, u32[]{:S(2)}) collective-permute-start(bf16[64,3584]{1,0:T(8,128)(2,1)S(1)} %all_to_all.34), channel_id=1, source_target_pairs={{0,32},{16,48},{32,64},{48,80},{64,96},{80,112},{96,0},{112,16},{1... | collective-permute-start | bytes 1376264 | tf_op jit(solution)/shard_map/ppermute | solution.py:29
  29.3 13.4 %collective-permute-start.3 = (bf16[64,3584]{1,0:T(8,128)(2,1)S(1)}, bf16[64,3584]{1,0:T(8,128)(2,1)S(1)}, u32[]{:S(2)}, u32[]{:S(2)}) collective-permute-start(bf16[64,3584]{1,0:T(8,128)(2,1)S(1)} %all_to_all.34), channel_id=1, source_target_pairs={{0,96},{16,112},{32,0},{48,16},{64,32},{80,48},{96,64},{112,80},{1... | collective-permute-start | bytes 1376264 | tf_op jit(solution)/shard_map/ppermute | solution.py:30
  35.3 16.9 %collective-permute-start.9 = (bf16[64,3584]{1,0:T(8,128)(2,1)S(1)}, bf16[64,3584]{1,0:T(8,128)(2,1)S(1)}, u32[]{:S(2)}, u32[]{:S(2)}) collective-permute-start(bf16[64,3584]{1,0:T(8,128)(2,1)S(1)} %all_to_all.37), channel_id=1, source_target_pairs={{0,32},{16,48},{32,64},{48,80},{64,96},{80,112},{96,0},{112,16},{1... | collective-permute-start | bytes 1376264 | tf_op jit(solution)/shard_map/ppermute | solution.py:29
  36.9 17.0 %collective-permute-start.11 = (bf16[64,3584]{1,0:T(8,128)(2,1)S(1)}, bf16[64,3584]{1,0:T(8,128)(2,1)S(1)}, u32[]{:S(2)}, u32[]{:S(2)}) collective-permute-start(bf16[64,3584]{1,0:T(8,128)(2,1)S(1)} %all_to_all.37), channel_id=1, source_target_pairs={{0,96},{16,112},{32,0},{48,16},{64,32},{80,48},{96,64},{112,80},{1... | collective-permute-start | bytes 1376264 | tf_op jit(solution)/shard_map/ppermute | solution.py:30
  42.3 16.7 %collective-permute-start.8 = (bf16[64,3584]{1,0:T(8,128)(2,1)S(1)}, bf16[64,3584]{1,0:T(8,128)(2,1)S(1)}, u32[]{:S(2)}, u32[]{:S(2)}) collective-permute-start(bf16[64,3584]{1,0:T(8,128)(2,1)S(1)} %all_to_all.37), channel_id=1, source_target_pairs={{0,16},{16,0},{32,48},{48,32},{64,80},{80,64},{96,112},{112,96},{1... | collective-permute-start | bytes 1376264 | tf_op jit(solution)/shard_map/ppermute | solution.py:31
  42.7 16.4 %collective-permute-start.5 = (bf16[64,1792]{1,0:T(8,128)(2,1)S(1)}, bf16[64,1792]{1,0:T(8,128)(2,1)S(1)}, u32[]{:S(2)}, u32[]{:S(2)}) collective-permute-start(bf16[64,1792]{1,0:T(8,128)(2,1)S(1)} %slice.191), channel_id=1, source_target_pairs={{0,32},{16,48},{32,64},{48,80},{64,96},{80,112},{96,0},{112,16},{1... | collective-permute-start | bytes 688136 | tf_op jit(solution)/shard_map/ppermute | solution.py:32
  52.1 8.5 %collective-permute-start.6 = (bf16[64,1792]{1,0:T(8,128)(2,1)S(1)}, bf16[64,1792]{1,0:T(8,128)(2,1)S(1)}, u32[]{:S(2)}, u32[]{:S(2)}) collective-permute-start(bf16[64,1792]{1,0:T(8,128)(2,1)S(1)} %slice.192), channel_id=1, source_target_pairs={{0,96},{16,112},{32,0},{48,16},{64,32},{80,48},{96,64},{112,80},{1... | collective-permute-start | bytes 688136 | tf_op jit(solution)/shard_map/ppermute | solution.py:33
  54.0 7.5 %collective-permute-start.13 = (bf16[64,1792]{1,0:T(8,128)(2,1)S(1)}, bf16[64,1792]{1,0:T(8,128)(2,1)S(1)}, u32[]{:S(2)}, u32[]{:S(2)}) collective-permute-start(bf16[64,1792]{1,0:T(8,128)(2,1)S(1)} %slice.194), channel_id=1, source_target_pairs={{0,32},{16,48},{32,64},{48,80},{64,96},{80,112},{96,0},{112,16},{1... | collective-permute-start | bytes 688136 | tf_op jit(solution)/shard_map/ppermute | solution.py:32
  54.3 9.4 %collective-permute-start.14 = (bf16[64,1792]{1,0:T(8,128)(2,1)S(1)}, bf16[64,1792]{1,0:T(8,128)(2,1)S(1)}, u32[]{:S(2)}, u32[]{:S(2)}) collective-permute-start(bf16[64,1792]{1,0:T(8,128)(2,1)S(1)} %slice.195), channel_id=1, source_target_pairs={{0,96},{16,112},{32,0},{48,16},{64,32},{80,48},{96,64},{112,80},{1... | collective-permute-start | bytes 688136 | tf_op jit(solution)/shard_map/ppermute | solution.py:33
  59.0 4.7 %collective-permute-start.2 = (bf16[64,3584]{1,0:T(8,128)(2,1)S(1)}, bf16[64,3584]{1,0:T(8,128)(2,1)S(1)}, u32[]{:S(2)}, u32[]{:S(2)}) collective-permute-start(bf16[64,3584]{1,0:T(8,128)(2,1)S(1)} %collective-permute-done.1), channel_id=1, source_target_pairs={{0,16},{16,0},{32,48},{48,32},{64,80},{80,64},{96,112},{112,96},{1... | collective-permute-start | bytes 1376264 | tf_op jit(solution)/shard_map/ppermute | solution.py:35
  59.1 7.0 %collective-permute-start.4 = (bf16[64,3584]{1,0:T(8,128)(2,1)S(1)}, bf16[64,3584]{1,0:T(8,128)(2,1)S(1)}, u32[]{:S(2)}, u32[]{:S(2)}) collective-permute-start(bf16[64,3584]{1,0:T(8,128)(2,1)S(1)} %collective-permute-done.3), channel_id=1, source_target_pairs={{0,16},{16,0},{32,48},{48,32},{64,80},{80,64},{96,112},{112,96},{1... | collective-permute-start | bytes 1376264 | tf_op jit(solution)/shard_map/ppermute | solution.py:36
  60.6 7.8 %collective-permute-start.10 = (bf16[64,3584]{1,0:T(8,128)(2,1)S(1)}, bf16[64,3584]{1,0:T(8,128)(2,1)S(1)}, u32[]{:S(2)}, u32[]{:S(2)}) collective-permute-start(bf16[64,3584]{1,0:T(8,128)(2,1)S(1)} %collective-permute-done.9), channel_id=1, source_target_pairs={{0,16},{16,0},{32,48},{48,32},{64,80},{80,64},{96,112},{112,96},{1... | collective-permute-start | bytes 1376264 | tf_op jit(solution)/shard_map/ppermute | solution.py:35
  61.5 7.0 %collective-permute-start.12 = (bf16[64,3584]{1,0:T(8,128)(2,1)S(1)}, bf16[64,3584]{1,0:T(8,128)(2,1)S(1)}, u32[]{:S(2)}, u32[]{:S(2)}) collective-permute-start(bf16[64,3584]{1,0:T(8,128)(2,1)S(1)} %collective-permute-done.11), channel_id=1, source_target_pairs={{0,16},{16,0},{32,48},{48,32},{64,80},{80,64},{96,112},{112,96},{1... | collective-permute-start | bytes 1376264 | tf_op jit(solution)/shard_map/ppermute | solution.py:36
  63.7 8.1 %collective-permute-start.7 = (bf16[64,3584]{1,0:T(8,128)(2,1)S(1)}, bf16[64,3584]{1,0:T(8,128)(2,1)S(1)}, u32[]{:S(2)}, u32[]{:S(2)}) collective-permute-start(bf16[64,3584]{1,0:T(8,128)(2,1)S(1)} %pad_maximum_fusion.2), channel_id=1, source_target_pairs={{0,16},{16,0},{32,48},{48,32},{64,80},{80,64},{96,112},{112,96},{1... | collective-permute-start | bytes 1376264 | tf_op jit(solution)/shard_map/ppermute | solution.py:37
  63.8 4.8 %collective-permute-start.15 = (bf16[64,3584]{1,0:T(8,128)(2,1)S(1)}, bf16[64,3584]{1,0:T(8,128)(2,1)S(1)}, u32[]{:S(2)}, u32[]{:S(2)}) collective-permute-start(bf16[64,3584]{1,0:T(8,128)(2,1)S(1)} %pad_maximum_fusion.3), channel_id=1, source_target_pairs={{0,16},{16,0},{32,48},{48,32},{64,80},{80,64},{96,112},{112,96},{1... | collective-permute-start | bytes 1376264 | tf_op jit(solution)/shard_map/ppermute | solution.py:37
  78.4 3.9 %collective-permute-start.22 = (bf16[192,3584]{1,0:T(8,128)(2,1)S(1)}, bf16[192,3584]{1,0:T(8,128)(2,1)S(1)}, u32[]{:S(2)}, u32[]{:S(2)}) collective-permute-start(bf16[192,3584]{1,0:T(8,128)(2,1)S(1)} %pad_maximum_fusion.1), channel_id=1, source_target_pairs={{0,16},{16,0},{32,48},{48,32},{64,80},{80,64},{96,112},{112,96},{1... | collective-permute-start | bytes 4128776 | tf_op jit(solution)/shard_map/ppermute | solution.py:47
  78.5 3.8 %collective-permute-start.23 = (bf16[64,3584]{1,0:T(8,128)(2,1)S(1)}, bf16[64,3584]{1,0:T(8,128)(2,1)S(1)}, u32[]{:S(2)}, u32[]{:S(2)}) collective-permute-start(bf16[64,3584]{1,0:T(8,128)(2,1)S(1)} %get-tuple-element.12), channel_id=1, source_target_pairs={{0,16},{16,0},{32,48},{48,32},{64,80},{80,64},{96,112},{112,96},{1... | collective-permute-start | bytes 1376264 | tf_op jit(solution)/shard_map/ppermute | solution.py:46
  79.3 6.8 %collective-permute-start.16 = (bf16[192,3584]{1,0:T(8,128)(2,1)S(1)}, bf16[192,3584]{1,0:T(8,128)(2,1)S(1)}, u32[]{:S(2)}, u32[]{:S(2)}) collective-permute-start(bf16[192,3584]{1,0:T(8,128)(2,1)S(1)} %pad_maximum_fusion), channel_id=1, source_target_pairs={{0,16},{16,0},{32,48},{48,32},{64,80},{80,64},{96,112},{112,96},{1... | collective-permute-start | bytes 4128776 | tf_op jit(solution)/shard_map/ppermute | solution.py:47
  79.4 6.6 %collective-permute-start.17 = (bf16[64,3584]{1,0:T(8,128)(2,1)S(1)}, bf16[64,3584]{1,0:T(8,128)(2,1)S(1)}, u32[]{:S(2)}, u32[]{:S(2)}) collective-permute-start(bf16[64,3584]{1,0:T(8,128)(2,1)S(1)} %get-tuple-element.17), channel_id=1, source_target_pairs={{0,16},{16,0},{32,48},{48,32},{64,80},{80,64},{96,112},{112,96},{1... | collective-permute-start | bytes 1376264 | tf_op jit(solution)/shard_map/ppermute | solution.py:46
  82.7 9.8 %collective-permute-start.24 = (bf16[64,1792]{1,0:T(8,128)(2,1)S(1)}, bf16[64,1792]{1,0:T(8,128)(2,1)S(1)}, u32[]{:S(2)}, u32[]{:S(2)}) collective-permute-start(bf16[64,1792]{1,0:T(8,128)(2,1)S(1)} %get-tuple-element.23), channel_id=1, source_target_pairs={{0,32},{16,48},{32,64},{48,80},{64,96},{80,112},{96,0},{112,16},{1... | collective-permute-start | bytes 688136 | tf_op jit(solution)/shard_map/ppermute | solution.py:53
  83.0 17.9 %collective-permute-start.26 = (bf16[64,1792]{1,0:T(8,128)(2,1)S(1)}, bf16[64,1792]{1,0:T(8,128)(2,1)S(1)}, u32[]{:S(2)}, u32[]{:S(2)}) collective-permute-start(bf16[64,1792]{1,0:T(8,128)(2,1)S(1)} %get-tuple-element.24), channel_id=1, source_target_pairs={{0,96},{16,112},{32,0},{48,16},{64,32},{80,48},{96,64},{112,80},{1... | collective-permute-start | bytes 688136 | tf_op jit(solution)/shard_map/ppermute | solution.py:54
  86.4 10.9 %collective-permute-start.18 = (bf16[64,1792]{1,0:T(8,128)(2,1)S(1)}, bf16[64,1792]{1,0:T(8,128)(2,1)S(1)}, u32[]{:S(2)}, u32[]{:S(2)}) collective-permute-start(bf16[64,1792]{1,0:T(8,128)(2,1)S(1)} %get-tuple-element.25), channel_id=1, source_target_pairs={{0,32},{16,48},{32,64},{48,80},{64,96},{80,112},{96,0},{112,16},{1... | collective-permute-start | bytes 688136 | tf_op jit(solution)/shard_map/ppermute | solution.py:53
  86.6 11.0 %collective-permute-start.20 = (bf16[64,1792]{1,0:T(8,128)(2,1)S(1)}, bf16[64,1792]{1,0:T(8,128)(2,1)S(1)}, u32[]{:S(2)}, u32[]{:S(2)}) collective-permute-start(bf16[64,1792]{1,0:T(8,128)(2,1)S(1)} %get-tuple-element.26), channel_id=1, source_target_pairs={{0,96},{16,112},{32,0},{48,16},{64,32},{80,48},{96,64},{112,80},{1... | collective-permute-start | bytes 688136 | tf_op jit(solution)/shard_map/ppermute | solution.py:54
  92.5 32.0 %collective-permute-start.25 = (bf16[64,3584]{1,0:T(8,128)(2,1)S(1)}, bf16[64,3584]{1,0:T(8,128)(2,1)}, u32[]{:S(2)}, u32[]{:S(2)}) collective-permute-start(bf16[64,3584]{1,0:T(8,128)(2,1)S(1)} %pad_maximum_fusion.6), channel_id=1, source_target_pairs={{0,32},{16,48},{32,64},{48,80},{64,96},{80,112},{96,0},{112,16},{1... | collective-permute-start | bytes 1376264 | tf_op jit(solution)/shard_map/ppermute | solution.py:57
  97.4 18.7 %collective-permute-start.19 = (bf16[64,3584]{1,0:T(8,128)(2,1)S(1)}, bf16[64,3584]{1,0:T(8,128)(2,1)S(1)}, u32[]{:S(2)}, u32[]{:S(2)}) collective-permute-start(bf16[64,3584]{1,0:T(8,128)(2,1)S(1)} %pad_maximum_fusion.4), channel_id=1, source_target_pairs={{0,32},{16,48},{32,64},{48,80},{64,96},{80,112},{96,0},{112,16},{1... | collective-permute-start | bytes 1376264 | tf_op jit(solution)/shard_map/ppermute | solution.py:57
  97.6 18.6 %collective-permute-start.21 = (bf16[64,3584]{1,0:T(8,128)(2,1)S(1)}, bf16[64,3584]{1,0:T(8,128)(2,1)S(1)}, u32[]{:S(2)}, u32[]{:S(2)}) collective-permute-start(bf16[64,3584]{1,0:T(8,128)(2,1)S(1)} %pad_maximum_fusion.5), channel_id=1, source_target_pairs={{0,96},{16,112},{32,0},{48,16},{64,32},{80,48},{96,64},{112,80},{1... | collective-permute-start | bytes 1376264 | tf_op jit(solution)/shard_map/ppermute | solution.py:58
  101.0 23.5 %collective-permute-start.27 = (bf16[64,3584]{1,0:T(8,128)(2,1)S(1)}, bf16[64,3584]{1,0:T(8,128)(2,1)}, u32[]{:S(2)}, u32[]{:S(2)}) collective-permute-start(bf16[64,3584]{1,0:T(8,128)(2,1)S(1)} %pad_maximum_fusion.7), channel_id=1, source_target_pairs={{0,96},{16,112},{32,0},{48,16},{64,32},{80,48},{96,64},{112,80},{1... | collective-permute-start | bytes 1376264 | tf_op jit(solution)/shard_map/ppermute | solution.py:58
  117.3 15.4 %all-to-all-start.2 = ((bf16[16,4,3584]{2,1,0:T(4,128)(2,1)}), bf16[16,4,3584]{2,1,0:T(4,128)(2,1)S(1)}, u32[]{:S(2)}, u32[]{:S(2)}) async-start(bf16[16,4,3584]{2,1,0:T(4,128)(2,1)} %all_to_all.38), calls=%async_computation.2 | async-start | bytes 917504 | tf_op jit(solution)/shard_map/all_to_all | solution.py:101
  132.7 13.2 %all-to-all-start.3 = ((bf16[16,4,3584]{2,1,0:T(4,128)(2,1)}), bf16[16,4,3584]{2,1,0:T(4,128)(2,1)S(1)}, u32[]{:S(2)}, u32[]{:S(2)}) async-start(bf16[16,4,3584]{2,1,0:T(4,128)(2,1)} %all_to_all.41), calls=%async_computation.3 | async-start | bytes 917504 | tf_op jit(solution)/shard_map/all_to_all | solution.py:101
  (8 other events, 30.1 us)

commit v7 on v5

--- a/solution.py
+++ b/solution.py
@@ -2,6 +2,8 @@
 import jax.numpy as jnp
 from jax import lax
 from jax.sharding import PartitionSpec as P
+
+COMPACT_ROWS = 56
 
 
 def slot_tables(chosen, tok_count, my_index):
@@ -67,6 +69,7 @@
     expert_total, capacity = chosen.shape
     slot_count = min(tok_count, max(4, 2 * capacity // worker_ordinal))
     my_index = lax.axis_index("dp") * ex_count + lax.axis_index("expert")
+    my_expert_idx = lax.axis_index("expert")
     owners, is_mine, ranks = slot_tables(chosen, tok_count, my_index)
     local_idx = chosen - owners * tok_count
     matches = is_mine[:, :, None] & (
@@ -80,13 +83,51 @@
     send_rows = jnp.take(tokens, source_idx.reshape(-1), axis=0)
     send_rows = jnp.where(present.reshape(-1, 1) > 0, send_rows, jnp.zeros_like(send_rows))
     row_in = lax.all_to_all(send_rows, "expert", split_axis=0, concat_axis=0, tiled=True)
-    picked = gather_dp(row_in, dp_count)
-    gate_act = jnp.dot(picked, w_gate[0], preferred_element_type=jnp.float32)
-    up_act = jnp.dot(picked, w_up[0], preferred_element_type=jnp.float32)
-    hidden = (jax.nn.silu(gate_act) * up_act).astype(jnp.bfloat16)
-    hidden = lax.optimization_barrier(hidden)
-    result = jnp.dot(hidden, w_down[0], preferred_element_type=jnp.float32).astype(jnp.bfloat16)
-    summed = scatter_dp(result, dp_count)
+    def expert_rows(rows, w_g, w_u, w_d):
+        picked = gather_dp(rows, dp_count)
+        gate_act = jnp.dot(picked, w_g, preferred_element_type=jnp.float32)
+        up_act = jnp.dot(picked, w_u, preferred_element_type=jnp.float32)
+        hidden = (jax.nn.silu(gate_act) * up_act).astype(jnp.bfloat16)
+        hidden = lax.optimization_barrier(hidden)
+        result = jnp.dot(hidden, w_d, preferred_element_type=jnp.float32).astype(jnp.bfloat16)
+        return scatter_dp(result, dp_count)
+
+    dp_rows = owners // ex_count
+    my_dp = lax.axis_index("dp")
+    counts = jnp.sum(
+        (dp_rows[:, :, None] == jnp.arange(dp_count, dtype=jnp.int32)[None, None, :]).astype(jnp.int32),
+        axis=1,
+    )
+    compact = min(ex_count * slot_count, COMPACT_ROWS)
+    row_owners = lax.dynamic_index_in_dim(owners, my_expert_idx, 0, keepdims=False)
+    same_owner = row_owners[:, None] == row_owners[None, :]
+    tri = (
+        jnp.arange(capacity, dtype=jnp.int32)[:, None]
+        < jnp.arange(capacity, dtype=jnp.int32)[None, :]
+    )
+    row_ranks = jnp.sum((same_owner & tri).astype(jnp.int32), axis=0)
+    in_group = (row_owners // ex_count) == my_dp
+    group_pos = jnp.sum((in_group[:, None] & tri).astype(jnp.int32), axis=0)
+    slot_of = (row_owners % ex_count) * slot_count + row_ranks
+    pick_q = in_group[None, :] & (group_pos[None, :] == jnp.arange(compact, dtype=jnp.int32)[:, None])
+    comp_src = jnp.sum(pick_q.astype(jnp.int32) * slot_of[None, :], axis=1)
+    comp_ok = jnp.sum(pick_q.astype(jnp.int32), axis=1) > 0
+    pick_s = in_group[None, :] & (
+        slot_of[None, :] == jnp.arange(ex_count * slot_count, dtype=jnp.int32)[:, None]
+    )
+    back_src = jnp.sum(pick_s.astype(jnp.int32) * group_pos[None, :], axis=1)
+    back_ok = jnp.sum(pick_s.astype(jnp.int32), axis=1) > 0
+
+    def short_path(rows, w_g, w_u, w_d):
+        packed = jnp.take(rows, comp_src, axis=0)
+        packed = jnp.where(comp_ok[:, None], packed, jnp.zeros_like(packed))
+        out = expert_rows(packed, w_g, w_u, w_d)
+        spread = jnp.take(out, back_src, axis=0)
+        return jnp.where(back_ok[:, None], spread, jnp.zeros_like(spread))
+
+    summed = lax.cond(
+        jnp.max(counts) <= compact, short_path, expert_rows, row_in, w_gate[0], w_up[0], w_down[0]
+    )
     returned = lax.all_to_all(summed, "expert", split_axis=0, concat_axis=0, tiled=True)
     placed = (jnp.arange(tok_count, dtype=jnp.int32)[:, None] == source_idx.reshape(1, -1)) & (
         present.reshape(1, -1) > 0

time: 139 us -> 138 us (level)
  blocking collectives: 21.6 us -> 0 us
  starting transfers between devices: 20.2 us -> 29.7 us
  other arithmetic: 4.25 us -> 8.61 us
  local copies, waits for them, and re-layouts: 4.83 us -> 8.82 us
  waiting for transfers between devices: 76.5 us -> 78.8 us
    all_to_all x1 -> x0, blocking collectives: 21.6 us -> none  [shards(): lax.all_to_all(send_rows, 'expert', split_axis=0, concat_axis=0, tiled=True)]
    all_to_all x0 -> x1, waiting for transfers between devices: none -> 11.7 us  [shards(): lax.all_to_all(send_rows, 'expert', split_axis=0, concat_axis=0, tiled=True)]
    all_to_all x0 -> x1, starting transfers between devices: none -> 8.27 us  [shards(): lax.all_to_all(send_rows, 'expert', split_axis=0, concat_axis=0, tiled=True)]
    ppermute x1, waiting for transfers between devices: 19 us -> 16.1 us  [gather_dp(): up = lax.ppermute(x, 'dp', dp_pairs(dp_count, 1))]
    ppermute x1, waiting for transfers between devices: 19.4 us -> 16.7 us  [scatter_dp(): a_a = lax.ppermute(s_a, 'dp', dp_pairs(dp_count, 1)).astype(f32)]
    gather x0 -> x2, local copies, waits for them, and re-layouts: none -> 2.17 us  [the longest x1 1.12 us: short_path(): spread = jnp.take(out, back_src, axis=0)]
    ppermute x1, waiting for transfers between devices: 7.61 us -> 5.89 us  [gather_dp(): far_a = lax.ppermute(up[:, :half], 'dp', dp_pairs(dp_count, 1))]
    cond x0 -> x17, local copies, waits for them, and re-layouts: none -> 1.69 us
  transfers between devices with their start and end apart: 15 -> 16, of which waited for: 7 -> 8; matrix products, arithmetic and copies ran while one was open for 1% -> 2% of each run, Pallas kernels for 0% -> 0%
where the time goes in v7:
time: 138 us; the launch traced here: 135 us
  waiting for transfers between devices  78.8 us (57%)
  starting transfers between devices  29.7 us (22%)
  local copies, waits for them, and re-layouts  8.82 us (6%)
  other arithmetic  8.61 us (6%)
  matrix products  8.16 us (6%)
    ppermute x1, waiting for transfers between devices, scatter_dp(): a_a = lax.ppermute(s_a, 'dp', dp_pairs(dp_count, 1)).astype(f32)  16.7 us
    ppermute x1, waiting for transfers between devices, gather_dp(): up = lax.ppermute(x, 'dp', dp_pairs(dp_count, 1))  16.1 us
    all_to_all x1, waiting for transfers between devices, shards(): lax.all_to_all(summed, 'expert', split_axis=0, concat_axis=0, tiled=True)  11.9 us
    all_to_all x1, waiting for transfers between devices, shards(): lax.all_to_all(send_rows, 'expert', split_axis=0, concat_axis=0, tiled=True)  11.7 us
    ppermute x1, waiting for transfers between devices, scatter_dp(): r_a = lax.ppermute(q_far[:, :half], 'dp', dp_pairs(dp_count, 1)).astype(f32)  9.26 us
    all_to_all x1, starting transfers between devices, shards(): lax.all_to_all(send_rows, 'expert', split_axis=0, concat_axis=0, tiled=True)  8.27 us
    all_to_all x1, starting transfers between devices, shards(): lax.all_to_all(summed, 'expert', split_axis=0, concat_axis=0, tiled=True)  6.87 us
    ppermute x1, waiting for transfers between devices, gather_dp(): far_a = lax.ppermute(up[:, :half], 'dp', dp_pairs(dp_count, 1))  5.89 us
  transfers between devices with their start and end apart: 16, of which 8 were waited for; matrix products, arithmetic and copies ran while one was open for 2% of the time, Pallas kernels for 0%

profile of v7, /device:TPU:6, one launch (start us, length us, event | category | flops | bytes accessed | tf_op | source)
XLA Modules:
  0.0 135.5 jit_solution(1915429479809395591)
XLA Ops:
  0.0 0.9 add_select_fusion.1
  0.9 0.8 broadcast_compare_fusion.2
  1.9 0.6 copy-done.6
  3.1 1.1 gather_fusion.2
  4.6 1.5 %select_select_fusion.2 = bf16[16,4,7168]{2,1,0:T(4,128)(2,1)} fusion(bf16[16,4,7168]{2,1,0:T(4,128)(2,1)S(1)} %gather.15, pred[16,4]{1,0:T(8,128)(4,1)S(1)} %copy.12, pred[16,4]{1,0:T(8,128)(4,1)S(1)} %copy.8), kind=kLoop, calls=%fused_computation.72 | loop fusion | flops 917504 | bytes 1835136 | tf_op jit(solution)/shard_map/jit(_where)/select_n | solution.py:84
  6.0 8.3 %all-to-all-start = ((bf16[16,4,7168]{2,1,0:T(4,128)(2,1)}), bf16[16,4,7168]{2,1,0:T(4,128)(2,1)S(1)}, u32[]{:S(2)}, u32[]{:S(2)}) async-start(bf16[16,4,7168]{2,1,0:T(4,128)(2,1)} %select_select_fusion.2), calls=%async_computation | async-start | bytes 1835008 | tf_op jit(solution)/shard_map/all_to_all | solution.py:85
  14.8 0.7 reduce_max.9
  16.4 11.7 %all-to-all-done = bf16[16,4,7168]{2,1,0:T(4,128)(2,1)S(1)} async-done(((bf16[16,4,7168]{2,1,0:T(4,128)(2,1)}), bf16[16,4,7168]{2,1,0:T(4,128)(2,1)S(1)}, u32[]{:S(2)}, u32[]{:S(2)}) %all-to-all-start) | async-done | bytes 917536 | tf_op jit(solution)/shard_map/all_to_all | solution.py:85
  28.2 83.9 %conditional.1 = (bf16[64,7168]{1,0:T(8,128)(2,1)S(1)}) conditional(s32[]{:T(128)} %convert_element_type.149, (bf16[64,7168]{1,0:T(8,128)(2,1)S(1)}, bf16[7168,256]{1,0:T(8,128)(2,1)}, bf16[7168,256]{1,0:T(8,128)(2,1)}, bf16[256,7168]{1,0:T(8,128)(2,1)}) %tuple.41, (s32[64,288]{1,0:T(8,128)S(1)}, s32[]{:T(128)}, s32[288]{0:T(512)S(1)}, ...), branch_computations={%region_7.8_spmd, %region_8.13_spmd} | conditional | flops 5664997376 | bytes 212017024 | solution.py:128
  28.7 1.1 gather_fusion
  30.1 1.6 %collective-permute-start.15 = (bf16[56,7168]{1,0:T(8,128)(2,1)S(1)}, bf16[56,7168]{1,0:T(8,128)(2,1)S(1)}, u32[]{:S(2)}, u32[]{:S(2)}) collective-permute-start(bf16[56,7168]{1,0:T(8,128)(2,1)S(1)} %get-tuple-element.77), channel_id=1, source_target_pairs={{0,32},{16,48},{32,64},{48,80},{64,96},{80,112},{96,0},{112,16},{1... | collective-permute-start | bytes 2408456 | tf_op jit(solution)/shard_map/cond/branch_1_fun/ppermute | solution.py:31
  31.7 1.7 %collective-permute-start.17 = (bf16[56,7168]{1,0:T(8,128)(2,1)S(1)}, bf16[56,7168]{1,0:T(8,128)(2,1)S(1)}, u32[]{:S(2)}, u32[]{:S(2)}) collective-permute-start(bf16[56,7168]{1,0:T(8,128)(2,1)S(1)} %get-tuple-element.77), channel_id=1, source_target_pairs={{0,96},{16,112},{32,0},{48,16},{64,32},{80,48},{96,64},{112,80},{1... | collective-permute-start | bytes 2408456 | tf_op jit(solution)/shard_map/cond/branch_1_fun/ppermute | solution.py:32
  33.4 16.1 %collective-permute-done.15 = bf16[56,7168]{1,0:T(8,128)(2,1)S(1)} collective-permute-done((bf16[56,7168]{1,0:T(8,128)(2,1)S(1)}, bf16[56,7168]{1,0:T(8,128)(2,1)S(1)}, u32[]{:S(2)}, u32[]{:S(2)}) %collective-permute-start.15) | collective-permute-done | bytes 802848 | tf_op jit(solution)/shard_map/cond/branch_1_fun/ppermute | solution.py:31
  49.9 3.0 %collective-permute-start.20 = (bf16[56,3584]{1,0:T(8,128)(2,1)S(1)}, bf16[56,3584]{1,0:T(8,128)(2,1)S(1)}, u32[]{:S(2)}, u32[]{:S(2)}) collective-permute-start(bf16[56,3584]{1,0:T(8,128)(2,1)S(1)} %slice.144), channel_id=1, source_target_pairs={{0,96},{16,112},{32,0},{48,16},{64,32},{80,48},{96,64},{112,80},{1... | collective-permute-start | bytes 1204232 | tf_op jit(solution)/shard_map/cond/branch_1_fun/ppermute | solution.py:35
  53.5 5.9 %collective-permute-done.19 = bf16[56,3584]{1,0:T(8,128)(2,1)S(1)} collective-permute-done((bf16[56,3584]{1,0:T(8,128)(2,1)S(1)}, bf16[56,3584]{1,0:T(8,128)(2,1)S(1)}, u32[]{:S(2)}, u32[]{:S(2)}) %collective-permute-start.19) | collective-permute-done | bytes 401440 | tf_op jit(solution)/shard_map/cond/branch_1_fun/ppermute | solution.py:34
  59.9 2.0 %collective-permute-done.21 = bf16[56,7168]{1,0:T(8,128)(2,1)S(1)} collective-permute-done((bf16[56,7168]{1,0:T(8,128)(2,1)S(1)}, bf16[56,7168]{1,0:T(8,128)(2,1)S(1)}, u32[]{:S(2)}, u32[]{:S(2)}) %collective-permute-start.21) | collective-permute-done | bytes 802848 | tf_op jit(solution)/shard_map/cond/branch_1_fun/ppermute | solution.py:39
  62.0 1.8 %fusion.45 = f32[448,256]{1,0:T(8,128)S(1)} fusion(bf16[448,7168]{1,0:T(8,128)(2,1)S(1)} %constant_dynamic-update-slice_fusion.9, bf16[7168,256]{1,0:T(8,128)(2,1)S(1)} %copy-done.10), kind=kOutput, calls=%fused_computation.154 | convolution fusion | flops 1644167168 | bytes 10551296 | tf_op jit(solution)/shard_map/cond/branch_1_fun/dot_general | solution.py:88
  64.0 1.8 %multiply_convert_fusion.1 = bf16[448,256]{1,0:T(8,128)(2,1)S(1)} fusion(f32[448,256]{1,0:T(8,128)S(1)} %fusion.45, bf16[448,7168]{1,0:T(8,128)(2,1)S(1)} %constant_dynamic-update-slice_fusion.9, bf16[7168,256]{1,0:T(8,128)(2,1)S(1)} %copy-done.12), kind=kOutput, calls=%fused_computation.45 | convolution fusion | flops 1644855296 | bytes 10780672 | tf_op jit(solution)/shard_map/cond/branch_1_fun/dot_general | solution.py:89
  66.0 1.9 %convolution_convert_fusion.1 = bf16[448,7168]{1,0:T(8,128)(2,1)S(1)} fusion(bf16[448,256]{1,0:T(8,128)(2,1)S(1)} %multiply_convert_fusion.1, bf16[256,7168]{1,0:T(8,128)(2,1)S(1)} %copy-done.4), kind=kOutput, calls=%fused_computation.28 | convolution fusion | flops 1647378432 | bytes 10321920 | tf_op jit(solution)/shard_map/cond/branch_1_fun/dot_general | solution.py:92
  68.9 5.2 %collective-permute-done.23 = bf16[56,7168]{1,0:T(8,128)(2,1)S(1)} collective-permute-done((bf16[56,7168]{1,0:T(8,128)(2,1)S(1)}, bf16[56,7168]{1,0:T(8,128)(2,1)S(1)}, u32[]{:S(2)}, u32[]{:S(2)}) %collective-permute-start.23) | collective-permute-done | bytes 802848 | tf_op jit(solution)/shard_map/cond/branch_1_fun/ppermute | solution.py:48
  74.7 0.9 copy-done.5
  76.3 2.9 %collective-permute-start.26 = (bf16[56,3584]{1,0:T(8,128)(2,1)S(1)}, bf16[56,3584]{1,0:T(8,128)(2,1)S(1)}, u32[]{:S(2)}, u32[]{:S(2)}) collective-permute-start(bf16[56,3584]{1,0:T(8,128)(2,1)S(1)} %get-tuple-element.97), channel_id=1, source_target_pairs={{0,96},{16,112},{32,0},{48,16},{64,32},{80,48},{96,64},{112,80},{1... | collective-permute-start | bytes 1204232 | tf_op jit(solution)/shard_map/cond/branch_1_fun/ppermute | solution.py:56
  79.2 9.3 %collective-permute-done.24 = bf16[56,3584]{1,0:T(8,128)(2,1)S(1)} collective-permute-done((bf16[56,3584]{1,0:T(8,128)(2,1)S(1)}, bf16[56,3584]{1,0:T(8,128)(2,1)S(1)}, u32[]{:S(2)}, u32[]{:S(2)}) %collective-permute-start.24) | collective-permute-done | bytes 401440 | tf_op jit(solution)/shard_map/cond/branch_1_fun/ppermute | solution.py:55
  88.8 3.3 %collective-permute-start.27 = (bf16[56,7168]{1,0:T(8,128)(2,1)S(1)}, bf16[56,7168]{1,0:T(8,128)(2,1)S(1)}, u32[]{:S(2)}, u32[]{:S(2)}) collective-permute-start(bf16[56,7168]{1,0:T(8,128)(2,1)S(1)} %pad_maximum_fusion.7), channel_id=1, source_target_pairs={{0,96},{16,112},{32,0},{48,16},{64,32},{80,48},{96,64},{112,80},{1... | collective-permute-start | bytes 2408456 | tf_op jit(solution)/shard_map/cond/branch_1_fun/ppermute | solution.py:60
  92.4 16.7 %collective-permute-done.25 = bf16[56,7168]{1,0:T(8,128)(2,1)S(1)} collective-permute-done((bf16[56,7168]{1,0:T(8,128)(2,1)S(1)}, bf16[56,7168]{1,0:T(8,128)(2,1)S(1)}, u32[]{:S(2)}, u32[]{:S(2)}) %collective-permute-start.25) | collective-permute-done | bytes 802848 | tf_op jit(solution)/shard_map/cond/branch_1_fun/ppermute | solution.py:59
  109.1 1.8 %add_convert_fusion.2 = bf16[56,7168]{1,0:T(8,128)(2,1)S(1)} fusion(bf16[56,7168]{1,0:T(8,128)(2,1)S(1)} %collective-permute-done.27, bf16[56,7168]{1,0:T(8,128)(2,1)S(1)} %collective-permute-done.25, bf16[168,7168]{1,0:T(8,128)(2,1)} %copy-done.5, bf16[448,7168]{1,0:T(8,128)(2,1)} %copy-done.2), kind=kLoop, calls=%fused_computation.30 | loop fusion | flops 3211264 | bytes 4014080 | tf_op jit(solution)/shard_map/cond/branch_1_fun/convert_element_type | solution.py:61
  110.8 1.1 gather_fusion.1
  112.2 1.3 all_to_all.16
  113.4 6.9 %all-to-all-start.1 = ((bf16[16,4,7168]{2,1,0:T(4,128)(2,1)}), bf16[16,4,7168]{2,1,0:T(4,128)(2,1)S(1)}, u32[]{:S(2)}, u32[]{:S(2)}) async-start(bf16[16,4,7168]{2,1,0:T(4,128)(2,1)} %all_to_all.16), calls=%async_computation.1 | async-start | bytes 1835008 | tf_op jit(solution)/shard_map/all_to_all | solution.py:131
  120.8 11.9 %all-to-all-done.1 = bf16[16,4,7168]{2,1,0:T(4,128)(2,1)S(1)} async-done(((bf16[16,4,7168]{2,1,0:T(4,128)(2,1)}), bf16[16,4,7168]{2,1,0:T(4,128)(2,1)S(1)}, u32[]{:S(2)}, u32[]{:S(2)}) %all-to-all-start.1) | async-done | bytes 917536 | tf_op jit(solution)/shard_map/all_to_all | solution.py:131
  132.9 0.6 fusion.14
  133.6 1.9 %fusion.6 = bf16[128,7168]{1,0:T(8,128)(2,1)} fusion(f32[128,7168]{1,0:T(8,128)S(1)} %fusion.14, bf16[64,7168]{1,0:T(8,128)(2,1)S(1)} %all_to_all.18, f32[64]{0:T(128)S(1)} %broadcast_in_dim.90, s32[64]{0:T(128)S(1)} %eq.109, pred[64]{0:T(512)(128)(4,1)S(1)} %gt.40), kind=kOutput, calls=%fused_computation.70 | convolution fusion | flops 119332864 | bytes 6423104 | tf_op jit(solution)/shard_map/dot_general | solution.py:138
  (95 shorter events, 8.1 us)
Async XLA Ops:
  0.0 3.1 %copy-start = (bf16[128,7168]{1,0:T(8,128)(2,1)S(1)}, bf16[128,7168]{1,0:T(8,128)(2,1)}, u32[]{:S(2)}) copy-start(bf16[128,7168]{1,0:T(8,128)(2,1)} %param.8) | copy-start | bytes 5505028
  1.8 0.6 copy-start.6
  6.0 22.0 %all-to-all-start = ((bf16[16,4,7168]{2,1,0:T(4,128)(2,1)}), bf16[16,4,7168]{2,1,0:T(4,128)(2,1)S(1)}, u32[]{:S(2)}, u32[]{:S(2)}) async-start(bf16[16,4,7168]{2,1,0:T(4,128)(2,1)} %select_select_fusion.2), calls=%async_computation | async-start | bytes 1835008 | tf_op jit(solution)/shard_map/all_to_all | solution.py:85
  30.1 19.4 %collective-permute-start.15 = (bf16[56,7168]{1,0:T(8,128)(2,1)S(1)}, bf16[56,7168]{1,0:T(8,128)(2,1)S(1)}, u32[]{:S(2)}, u32[]{:S(2)}) collective-permute-start(bf16[56,7168]{1,0:T(8,128)(2,1)S(1)} %get-tuple-element.77), channel_id=1, source_target_pairs={{0,32},{16,48},{32,64},{48,80},{64,96},{80,112},{96,0},{112,16},{1... | collective-permute-start | bytes 2408456 | tf_op jit(solution)/shard_map/cond/branch_1_fun/ppermute | solution.py:31
  31.7 18.2 %collective-permute-start.17 = (bf16[56,7168]{1,0:T(8,128)(2,1)S(1)}, bf16[56,7168]{1,0:T(8,128)(2,1)S(1)}, u32[]{:S(2)}, u32[]{:S(2)}) collective-permute-start(bf16[56,7168]{1,0:T(8,128)(2,1)S(1)} %get-tuple-element.77), channel_id=1, source_target_pairs={{0,96},{16,112},{32,0},{48,16},{64,32},{80,48},{96,64},{112,80},{1... | collective-permute-start | bytes 2408456 | tf_op jit(solution)/shard_map/cond/branch_1_fun/ppermute | solution.py:32
  33.4 20.0 %collective-permute-start.14 = (bf16[56,7168]{1,0:T(8,128)(2,1)S(1)}, bf16[56,7168]{1,0:T(8,128)(2,1)S(1)}, u32[]{:S(2)}, u32[]{:S(2)}) collective-permute-start(bf16[56,7168]{1,0:T(8,128)(2,1)S(1)} %get-tuple-element.77), channel_id=1, source_target_pairs={{0,16},{16,0},{32,48},{48,32},{64,80},{80,64},{96,112},{112,96},{1... | collective-permute-start | bytes 2408456 | tf_op jit(solution)/shard_map/cond/branch_1_fun/ppermute | solution.py:33
  49.5 9.9 %collective-permute-start.19 = (bf16[56,3584]{1,0:T(8,128)(2,1)S(1)}, bf16[56,3584]{1,0:T(8,128)(2,1)S(1)}, u32[]{:S(2)}, u32[]{:S(2)}) collective-permute-start(bf16[56,3584]{1,0:T(8,128)(2,1)S(1)} %slice.143), channel_id=1, source_target_pairs={{0,32},{16,48},{32,64},{48,80},{64,96},{80,112},{96,0},{112,16},{1... | collective-permute-start | bytes 1204232 | tf_op jit(solution)/shard_map/cond/branch_1_fun/ppermute | solution.py:34
  49.9 9.5 %collective-permute-start.20 = (bf16[56,3584]{1,0:T(8,128)(2,1)S(1)}, bf16[56,3584]{1,0:T(8,128)(2,1)S(1)}, u32[]{:S(2)}, u32[]{:S(2)}) collective-permute-start(bf16[56,3584]{1,0:T(8,128)(2,1)S(1)} %slice.144), channel_id=1, source_target_pairs={{0,96},{16,112},{32,0},{48,16},{64,32},{80,48},{96,64},{112,80},{1... | collective-permute-start | bytes 1204232 | tf_op jit(solution)/shard_map/cond/branch_1_fun/ppermute | solution.py:35
  52.9 6.7 %collective-permute-start.16 = (bf16[56,7168]{1,0:T(8,128)(2,1)S(1)}, bf16[56,7168]{1,0:T(8,128)(2,1)S(1)}, u32[]{:S(2)}, u32[]{:S(2)}) collective-permute-start(bf16[56,7168]{1,0:T(8,128)(2,1)S(1)} %collective-permute-done.15), channel_id=1, source_target_pairs={{0,16},{16,0},{32,48},{48,32},{64,80},{80,64},{96,112},{112,96},{1... | collective-permute-start | bytes 2408456 | tf_op jit(solution)/shard_map/cond/branch_1_fun/ppermute | solution.py:37
  52.9 6.8 %collective-permute-start.18 = (bf16[56,7168]{1,0:T(8,128)(2,1)S(1)}, bf16[56,7168]{1,0:T(8,128)(2,1)S(1)}, u32[]{:S(2)}, u32[]{:S(2)}) collective-permute-start(bf16[56,7168]{1,0:T(8,128)(2,1)S(1)} %collective-permute-done.17), channel_id=1, source_target_pairs={{0,16},{16,0},{32,48},{48,32},{64,80},{80,64},{96,112},{112,96},{1... | collective-permute-start | bytes 2408456 | tf_op jit(solution)/shard_map/cond/branch_1_fun/ppermute | solution.py:38
  59.5 2.5 %copy-start.10 = (bf16[7168,256]{1,0:T(8,128)(2,1)S(1)}, bf16[7168,256]{1,0:T(8,128)(2,1)}, u32[]{:S(2)}) copy-start(bf16[7168,256]{1,0:T(8,128)(2,1)} %get-tuple-element.70) | copy-start | bytes 11010052 | tf_op jit(solution)/shard_map/cond
  59.5 2.4 %collective-permute-start.21 = (bf16[56,7168]{1,0:T(8,128)(2,1)S(1)}, bf16[56,7168]{1,0:T(8,128)(2,1)S(1)}, u32[]{:S(2)}, u32[]{:S(2)}) collective-permute-start(bf16[56,7168]{1,0:T(8,128)(2,1)S(1)} %pad_maximum_fusion.5), channel_id=1, source_target_pairs={{0,16},{16,0},{32,48},{48,32},{64,80},{80,64},{96,112},{112,96},{1... | collective-permute-start | bytes 2408456 | tf_op jit(solution)/shard_map/cond/branch_1_fun/ppermute | solution.py:39
  62.0 2.0 %copy-start.12 = (bf16[7168,256]{1,0:T(8,128)(2,1)S(1)}, bf16[7168,256]{1,0:T(8,128)(2,1)}, u32[]{:S(2)}) copy-start(bf16[7168,256]{1,0:T(8,128)(2,1)} %get-tuple-element.71) | copy-start | bytes 11010052 | tf_op jit(solution)/shard_map/cond
  64.0 2.0 %copy-start.4 = (bf16[256,7168]{1,0:T(8,128)(2,1)S(1)}, bf16[256,7168]{1,0:T(8,128)(2,1)}, u32[]{:S(2)}) copy-start(bf16[256,7168]{1,0:T(8,128)(2,1)} %get-tuple-element.72) | copy-start | bytes 11010052 | tf_op jit(solution)/shard_map/cond
  67.9 6.3 %copy-start.2 = (bf16[448,7168]{1,0:T(8,128)(2,1)}, bf16[448,7168]{1,0:T(8,128)(2,1)S(1)}, u32[]{:S(2)}) copy-start(bf16[448,7168]{1,0:T(8,128)(2,1)S(1)} %convolution_convert_fusion.1) | copy-start | bytes 19267588 | tf_op jit(solution)/shard_map/cond
  68.3 5.8 %collective-permute-start.22 = (bf16[168,7168]{1,0:T(8,128)(2,1)S(1)}, bf16[168,7168]{1,0:T(8,128)(2,1)S(1)}, u32[]{:S(2)}, u32[]{:S(2)}) collective-permute-start(bf16[168,7168]{1,0:T(8,128)(2,1)S(1)} %pad_maximum_fusion.4), channel_id=1, source_target_pairs={{0,16},{16,0},{32,48},{48,32},{64,80},{80,64},{96,112},{112,96},{1... | collective-permute-start | bytes 7225352 | tf_op jit(solution)/shard_map/cond/branch_1_fun/ppermute | solution.py:49
  68.5 5.6 %collective-permute-start.23 = (bf16[56,7168]{1,0:T(8,128)(2,1)S(1)}, bf16[56,7168]{1,0:T(8,128)(2,1)S(1)}, u32[]{:S(2)}, u32[]{:S(2)}) collective-permute-start(bf16[56,7168]{1,0:T(8,128)(2,1)S(1)} %get-tuple-element.92), channel_id=1, source_target_pairs={{0,16},{16,0},{32,48},{48,32},{64,80},{80,64},{96,112},{112,96},{1... | collective-permute-start | bytes 2408456 | tf_op jit(solution)/shard_map/cond/branch_1_fun/ppermute | solution.py:48
  74.2 1.5 %copy-start.5 = (bf16[168,7168]{1,0:T(8,128)(2,1)}, bf16[168,7168]{1,0:T(8,128)(2,1)S(1)}, u32[]{:S(2)}) copy-start(bf16[168,7168]{1,0:T(8,128)(2,1)S(1)} %collective-permute-done.22) | copy-start | bytes 7225348 | tf_op jit(solution)/shard_map/cond
  75.7 12.7 %collective-permute-start.24 = (bf16[56,3584]{1,0:T(8,128)(2,1)S(1)}, bf16[56,3584]{1,0:T(8,128)(2,1)S(1)}, u32[]{:S(2)}, u32[]{:S(2)}) collective-permute-start(bf16[56,3584]{1,0:T(8,128)(2,1)S(1)} %get-tuple-element.96), channel_id=1, source_target_pairs={{0,32},{16,48},{32,64},{48,80},{64,96},{80,112},{96,0},{112,16},{1... | collective-permute-start | bytes 1204232 | tf_op jit(solution)/shard_map/cond/branch_1_fun/ppermute | solution.py:55
  76.3 12.4 %collective-permute-start.26 = (bf16[56,3584]{1,0:T(8,128)(2,1)S(1)}, bf16[56,3584]{1,0:T(8,128)(2,1)S(1)}, u32[]{:S(2)}, u32[]{:S(2)}) collective-permute-start(bf16[56,3584]{1,0:T(8,128)(2,1)S(1)} %get-tuple-element.97), channel_id=1, source_target_pairs={{0,96},{16,112},{32,0},{48,16},{64,32},{80,48},{96,64},{112,80},{1... | collective-permute-start | bytes 1204232 | tf_op jit(solution)/shard_map/cond/branch_1_fun/ppermute | solution.py:56
  88.6 20.5 %collective-permute-start.25 = (bf16[56,7168]{1,0:T(8,128)(2,1)S(1)}, bf16[56,7168]{1,0:T(8,128)(2,1)S(1)}, u32[]{:S(2)}, u32[]{:S(2)}) collective-permute-start(bf16[56,7168]{1,0:T(8,128)(2,1)S(1)} %pad_maximum_fusion.6), channel_id=1, source_target_pairs={{0,32},{16,48},{32,64},{48,80},{64,96},{80,112},{96,0},{112,16},{1... | collective-permute-start | bytes 2408456 | tf_op jit(solution)/shard_map/cond/branch_1_fun/ppermute | solution.py:59
  88.8 20.2 %collective-permute-start.27 = (bf16[56,7168]{1,0:T(8,128)(2,1)S(1)}, bf16[56,7168]{1,0:T(8,128)(2,1)S(1)}, u32[]{:S(2)}, u32[]{:S(2)}) collective-permute-start(bf16[56,7168]{1,0:T(8,128)(2,1)S(1)} %pad_maximum_fusion.7), channel_id=1, source_target_pairs={{0,96},{16,112},{32,0},{48,16},{64,32},{80,48},{96,64},{112,80},{1... | collective-permute-start | bytes 2408456 | tf_op jit(solution)/shard_map/cond/branch_1_fun/ppermute | solution.py:60
  112.1 8.3 %copy-start.8 = (s32[16,288]{1,0:T(8,128)S(1)}, s32[16,288]{1,0:T(8,128)}, u32[]{:S(2)}) copy-start(s32[16,288]{1,0:T(8,128)} %param.10) | copy-start | bytes 55300
  112.2 8.3 %copy-start.7 = (s32[16,288]{1,0:T(8,128)S(1)}, s32[16,288]{1,0:T(8,128)}, u32[]{:S(2)}) copy-start(s32[16,288]{1,0:T(8,128)} %copy-done.6) | copy-start | bytes 55300
  113.4 19.3 %all-to-all-start.1 = ((bf16[16,4,7168]{2,1,0:T(4,128)(2,1)}), bf16[16,4,7168]{2,1,0:T(4,128)(2,1)S(1)}, u32[]{:S(2)}, u32[]{:S(2)}) async-start(bf16[16,4,7168]{2,1,0:T(4,128)(2,1)} %all_to_all.16), calls=%async_computation.1 | async-start | bytes 1835008 | tf_op jit(solution)/shard_map/all_to_all | solution.py:131
  132.9 2.5 %copy-start.1 = (bf16[128,7168]{1,0:T(8,128)(2,1)S(1)}, bf16[128,7168]{1,0:T(8,128)(2,1)}, u32[]{:S(2)}) copy-start(bf16[128,7168]{1,0:T(8,128)(2,1)} %param.8) | copy-start | bytes 5505028

commit v8 on v7

--- a/solution.py
+++ b/solution.py
@@ -3,7 +3,7 @@
 from jax import lax
 from jax.sharding import PartitionSpec as P
 
-COMPACT_ROWS = 56
+CHIP_ROWS = 96
 
 
 def slot_tables(chosen, tok_count, my_index):
@@ -94,39 +94,47 @@
 
     dp_rows = owners // ex_count
     my_dp = lax.axis_index("dp")
+    my_core = my_dp % 2
     counts = jnp.sum(
-        (dp_rows[:, :, None] == jnp.arange(dp_count, dtype=jnp.int32)[None, None, :]).astype(jnp.int32),
+        (dp_rows[:, :, None] // 2 == jnp.arange(dp_count // 2, dtype=jnp.int32)[None, None, :]).astype(jnp.int32),
         axis=1,
     )
-    compact = min(ex_count * slot_count, COMPACT_ROWS)
+    chip_rows = min(2 * ex_count * slot_count, CHIP_ROWS)
+    half_rows = chip_rows // 2
+    slots = ex_count * slot_count
     row_owners = lax.dynamic_index_in_dim(owners, my_expert_idx, 0, keepdims=False)
+    row_dp = row_owners // ex_count
     same_owner = row_owners[:, None] == row_owners[None, :]
     tri = (
         jnp.arange(capacity, dtype=jnp.int32)[:, None]
         < jnp.arange(capacity, dtype=jnp.int32)[None, :]
     )
     row_ranks = jnp.sum((same_owner & tri).astype(jnp.int32), axis=0)
-    in_group = (row_owners // ex_count) == my_dp
-    group_pos = jnp.sum((in_group[:, None] & tri).astype(jnp.int32), axis=0)
+    in_chip = (row_dp // 2) == (my_dp // 2)
+    chip_pos = jnp.sum((in_chip[:, None] & tri).astype(jnp.int32), axis=0)
     slot_of = (row_owners % ex_count) * slot_count + row_ranks
-    pick_q = in_group[None, :] & (group_pos[None, :] == jnp.arange(compact, dtype=jnp.int32)[:, None])
-    comp_src = jnp.sum(pick_q.astype(jnp.int32) * slot_of[None, :], axis=1)
+    local_slot = ((row_dp % 2) * slots + slot_of + my_core * slots) % (2 * slots)
+    wanted = my_core * half_rows + jnp.arange(half_rows, dtype=jnp.int32)
+    pick_q = in_chip[None, :] & (chip_pos[None, :] == wanted[:, None])
+    comp_src = jnp.sum(pick_q.astype(jnp.int32) * local_slot[None, :], axis=1)
     comp_ok = jnp.sum(pick_q.astype(jnp.int32), axis=1) > 0
-    pick_s = in_group[None, :] & (
-        slot_of[None, :] == jnp.arange(ex_count * slot_count, dtype=jnp.int32)[:, None]
-    )
-    back_src = jnp.sum(pick_s.astype(jnp.int32) * group_pos[None, :], axis=1)
+    in_group = row_dp == my_dp
+    pick_s = in_group[None, :] & (slot_of[None, :] == jnp.arange(slots, dtype=jnp.int32)[:, None])
+    local_pos = (chip_pos + my_core * half_rows) % chip_rows
+    back_src = jnp.sum(pick_s.astype(jnp.int32) * local_pos[None, :], axis=1)
     back_ok = jnp.sum(pick_s.astype(jnp.int32), axis=1) > 0
 
     def short_path(rows, w_g, w_u, w_d):
-        packed = jnp.take(rows, comp_src, axis=0)
+        both = jnp.concatenate([rows, lax.ppermute(rows, "dp", sib_pairs(dp_count))], axis=0)
+        packed = jnp.take(both, comp_src, axis=0)
         packed = jnp.where(comp_ok[:, None], packed, jnp.zeros_like(packed))
         out = expert_rows(packed, w_g, w_u, w_d)
-        spread = jnp.take(out, back_src, axis=0)
+        full = jnp.concatenate([out, lax.ppermute(out, "dp", sib_pairs(dp_count))], axis=0)
+        spread = jnp.take(full, back_src, axis=0)
         return jnp.where(back_ok[:, None], spread, jnp.zeros_like(spread))
 
     summed = lax.cond(
-        jnp.max(counts) <= compact, short_path, expert_rows, row_in, w_gate[0], w_up[0], w_down[0]
+        jnp.max(counts) <= chip_rows, short_path, expert_rows, row_in, w_gate[0], w_up[0], w_down[0]
     )
     returned = lax.all_to_all(summed, "expert", split_axis=0, concat_axis=0, tiled=True)
     placed = (jnp.arange(tok_count, dtype=jnp.int32)[:, None] == source_idx.reshape(1, -1)) & (

time: 138 us -> 139 us (level)
  waiting for transfers between devices: 78.8 us -> 81 us
    ppermute x0 -> x2, waiting for transfers between devices: none -> 4.36 us  [the longest x1 2.28 us: short_path(): lax.ppermute(rows, 'dp', sib_pairs(dp_count))]
    ppermute x1, waiting for transfers between devices: 16.7 us -> 14.2 us  [scatter_dp(): a_a = lax.ppermute(s_a, 'dp', dp_pairs(dp_count, 1)).astype(f32)]
    all_to_all x1, waiting for transfers between devices: 11.9 us -> 14 us  [shards(): lax.all_to_all(summed, 'expert', split_axis=0, concat_axis=0, tiled=True)]
  transfers between devices with their start and end apart: 16 -> 18, of which waited for: 8 -> 10; matrix products, arithmetic and copies ran while one was open for 2% -> 2% of each run, Pallas kernels for 0% -> 0%
where the time goes in v8:
time: 139 us; the launch traced here: 136 us
  waiting for transfers between devices  81 us (58%)
  starting transfers between devices  29 us (21%)
  other arithmetic  9.58 us (7%)
  local copies, waits for them, and re-layouts  7.59 us (5%)
  matrix products  7.44 us (5%)
    ppermute x1, waiting for transfers between devices, gather_dp(): up = lax.ppermute(x, 'dp', dp_pairs(dp_count, 1))  15.5 us
    ppermute x1, waiting for transfers between devices, scatter_dp(): a_a = lax.ppermute(s_a, 'dp', dp_pairs(dp_count, 1)).astype(f32)  14.2 us
    all_to_all x1, waiting for transfers between devices, shards(): lax.all_to_all(summed, 'expert', split_axis=0, concat_axis=0, tiled=True)  14 us
    all_to_all x1, waiting for transfers between devices, shards(): lax.all_to_all(send_rows, 'expert', split_axis=0, concat_axis=0, tiled=True)  11.9 us
    all_to_all x1, starting transfers between devices, shards(): lax.all_to_all(send_rows, 'expert', split_axis=0, concat_axis=0, tiled=True)  8.27 us
    ppermute x1, waiting for transfers between devices, scatter_dp(): r_a = lax.ppermute(q_far[:, :half], 'dp', dp_pairs(dp_count, 1)).astype(f32)  8.03 us
    ppermute x1, waiting for transfers between devices, gather_dp(): far_a = lax.ppermute(up[:, :half], 'dp', dp_pairs(dp_count, 1))  6.56 us
    all_to_all x1, starting transfers between devices, shards(): lax.all_to_all(summed, 'expert', split_axis=0, concat_axis=0, tiled=True)  5.96 us
  transfers between devices with their start and end apart: 18, of which 10 were waited for; matrix products, arithmetic and copies ran while one was open for 2% of the time, Pallas kernels for 0%

profile of v8, /device:TPU:6, one launch (start us, length us, event | category | flops | bytes accessed | tf_op | source)
XLA Modules:
  0.0 136.1 jit_solution(14566164075472571089)
XLA Ops:
  0.0 0.9 add_select_fusion.3
  0.9 0.8 broadcast_compare_fusion.2
  2.4 1.1 gather_fusion.2
  4.0 1.5 %select_select_fusion.2 = bf16[16,4,7168]{2,1,0:T(4,128)(2,1)} fusion(bf16[16,4,7168]{2,1,0:T(4,128)(2,1)S(1)} %gather.15, pred[16,4]{1,0:T(8,128)(4,1)S(1)} %copy.11, pred[16,4]{1,0:T(8,128)(4,1)S(1)} %copy.8), kind=kLoop, calls=%fused_computation.84 | loop fusion | flops 917504 | bytes 1835136 | tf_op jit(solution)/shard_map/jit(_where)/select_n | solution.py:84
  5.5 8.3 %all-to-all-start = ((bf16[16,4,7168]{2,1,0:T(4,128)(2,1)}), bf16[16,4,7168]{2,1,0:T(4,128)(2,1)S(1)}, u32[]{:S(2)}, u32[]{:S(2)}) async-start(bf16[16,4,7168]{2,1,0:T(4,128)(2,1)} %select_select_fusion.2), calls=%async_computation | async-start | bytes 1835008 | tf_op jit(solution)/shard_map/all_to_all | solution.py:85
  14.0 0.7 reduce_max.9
  15.7 11.9 %all-to-all-done = bf16[16,4,7168]{2,1,0:T(4,128)(2,1)S(1)} async-done(((bf16[16,4,7168]{2,1,0:T(4,128)(2,1)}), bf16[16,4,7168]{2,1,0:T(4,128)(2,1)S(1)}, u32[]{:S(2)}, u32[]{:S(2)}) %all-to-all-start) | async-done | bytes 917536 | tf_op jit(solution)/shard_map/all_to_all | solution.py:85
  27.7 83.9 %conditional.1 = (bf16[64,7168]{1,0:T(8,128)(2,1)S(1)}) conditional(s32[]{:T(128)} %convert_element_type.149, (bf16[64,7168]{1,0:T(8,128)(2,1)S(1)}, bf16[7168,256]{1,0:T(8,128)(2,1)}, bf16[7168,256]{1,0:T(8,128)(2,1)}, bf16[256,7168]{1,0:T(8,128)(2,1)}) %tuple.53, (s32[64,288]{1,0:T(8,128)S(1)}, s32[]{:T(128)}, s32[]{:T(128)}, s32[288]{0:T(512)S(1)}, ...), branch_computations={%region_7.8_spmd, %region_8.13_spmd} | conditional | flops 5664997376 | bytes 202987232 | solution.py:136
  28.4 2.3 %collective-permute-done.14 = bf16[64,7168]{1,0:T(8,128)(2,1)} collective-permute-done((bf16[64,7168]{1,0:T(8,128)(2,1)S(1)}, bf16[64,7168]{1,0:T(8,128)(2,1)}, u32[]{:S(2)}, u32[]{:S(2)}) %collective-permute-start.14) | collective-permute-done | bytes 917536 | tf_op jit(solution)/shard_map/cond/branch_1_fun/ppermute | solution.py:128
  30.7 1.3 pad_maximum_fusion.5
  32.0 1.0 gather_fusion
  33.2 1.6 %collective-permute-start.16 = (bf16[48,7168]{1,0:T(8,128)(2,1)S(1)}, bf16[48,7168]{1,0:T(8,128)(2,1)S(1)}, u32[]{:S(2)}, u32[]{:S(2)}) collective-permute-start(bf16[48,7168]{1,0:T(8,128)(2,1)S(1)} %get-tuple-element.149), channel_id=1, source_target_pairs={{0,32},{16,48},{32,64},{48,80},{64,96},{80,112},{96,0},{112,16},{1... | collective-permute-start | bytes 2064392 | tf_op jit(solution)/shard_map/cond/branch_1_fun/ppermute | solution.py:31
  34.8 1.7 %collective-permute-start.18 = (bf16[48,7168]{1,0:T(8,128)(2,1)S(1)}, bf16[48,7168]{1,0:T(8,128)(2,1)S(1)}, u32[]{:S(2)}, u32[]{:S(2)}) collective-permute-start(bf16[48,7168]{1,0:T(8,128)(2,1)S(1)} %get-tuple-element.149), channel_id=1, source_target_pairs={{0,96},{16,112},{32,0},{48,16},{64,32},{80,48},{96,64},{112,80},{1... | collective-permute-start | bytes 2064392 | tf_op jit(solution)/shard_map/cond/branch_1_fun/ppermute | solution.py:32
  36.5 15.5 %collective-permute-done.16 = bf16[48,7168]{1,0:T(8,128)(2,1)S(1)} collective-permute-done((bf16[48,7168]{1,0:T(8,128)(2,1)S(1)}, bf16[48,7168]{1,0:T(8,128)(2,1)S(1)}, u32[]{:S(2)}, u32[]{:S(2)}) %collective-permute-start.16) | collective-permute-done | bytes 688160 | tf_op jit(solution)/shard_map/cond/branch_1_fun/ppermute | solution.py:31
  52.4 3.0 %collective-permute-start.21 = (bf16[48,3584]{1,0:T(8,128)(2,1)S(1)}, bf16[48,3584]{1,0:T(8,128)(2,1)S(1)}, u32[]{:S(2)}, u32[]{:S(2)}) collective-permute-start(bf16[48,3584]{1,0:T(8,128)(2,1)S(1)} %slice.144), channel_id=1, source_target_pairs={{0,96},{16,112},{32,0},{48,16},{64,32},{80,48},{96,64},{112,80},{1... | collective-permute-start | bytes 1032200 | tf_op jit(solution)/shard_map/cond/branch_1_fun/ppermute | solution.py:35
  56.1 6.6 %collective-permute-done.20 = bf16[48,3584]{1,0:T(8,128)(2,1)S(1)} collective-permute-done((bf16[48,3584]{1,0:T(8,128)(2,1)S(1)}, bf16[48,3584]{1,0:T(8,128)(2,1)S(1)}, u32[]{:S(2)}, u32[]{:S(2)}) %collective-permute-start.20) | collective-permute-done | bytes 344096 | tf_op jit(solution)/shard_map/cond/branch_1_fun/ppermute | solution.py:34
  63.0 1.9 %collective-permute-done.22 = bf16[48,7168]{1,0:T(8,128)(2,1)S(1)} collective-permute-done((bf16[48,7168]{1,0:T(8,128)(2,1)S(1)}, bf16[48,7168]{1,0:T(8,128)(2,1)S(1)}, u32[]{:S(2)}, u32[]{:S(2)}) %collective-permute-start.22) | collective-permute-done | bytes 688160 | tf_op jit(solution)/shard_map/cond/branch_1_fun/ppermute | solution.py:39
  65.0 1.6 %fusion.52 = f32[384,256]{1,0:T(8,128)S(1)} fusion(bf16[384,7168]{1,0:T(8,128)(2,1)S(1)} %constant_dynamic-update-slice_fusion.9, bf16[7168,256]{1,0:T(8,128)(2,1)S(1)} %copy-done.8), kind=kOutput, calls=%fused_computation.186 | convolution fusion | flops 1409286144 | bytes 9568256 | tf_op jit(solution)/shard_map/cond/branch_1_fun/dot_general | solution.py:88
  67.0 1.6 %multiply_convert_fusion.1 = bf16[384,256]{1,0:T(8,128)(2,1)S(1)} fusion(f32[384,256]{1,0:T(8,128)S(1)} %fusion.52, bf16[384,7168]{1,0:T(8,128)(2,1)S(1)} %constant_dynamic-update-slice_fusion.9, bf16[7168,256]{1,0:T(8,128)(2,1)S(1)} %copy-done.10), kind=kOutput, calls=%fused_computation.47 | convolution fusion | flops 1409875968 | bytes 9764864 | tf_op jit(solution)/shard_map/cond/branch_1_fun/dot_general | solution.py:89
  69.1 1.6 %convolution_convert_fusion.1 = bf16[384,7168]{1,0:T(8,128)(2,1)S(1)} fusion(bf16[384,256]{1,0:T(8,128)(2,1)S(1)} %multiply_convert_fusion.1, bf16[256,7168]{1,0:T(8,128)(2,1)S(1)} %copy-done.4), kind=kOutput, calls=%fused_computation.28 | convolution fusion | flops 1412038656 | bytes 9371648 | tf_op jit(solution)/shard_map/cond/branch_1_fun/dot_general | solution.py:92
  71.6 4.6 %collective-permute-done.24 = bf16[48,7168]{1,0:T(8,128)(2,1)S(1)} collective-permute-done((bf16[48,7168]{1,0:T(8,128)(2,1)S(1)}, bf16[48,7168]{1,0:T(8,128)(2,1)S(1)}, u32[]{:S(2)}, u32[]{:S(2)}) %collective-permute-start.24) | collective-permute-done | bytes 688160 | tf_op jit(solution)/shard_map/cond/branch_1_fun/ppermute | solution.py:48
  77.3 2.9 %collective-permute-start.27 = (bf16[48,3584]{1,0:T(8,128)(2,1)S(1)}, bf16[48,3584]{1,0:T(8,128)(2,1)S(1)}, u32[]{:S(2)}, u32[]{:S(2)}) collective-permute-start(bf16[48,3584]{1,0:T(8,128)(2,1)S(1)} %get-tuple-element.173), channel_id=1, source_target_pairs={{0,96},{16,112},{32,0},{48,16},{64,32},{80,48},{96,64},{112,80},{1... | collective-permute-start | bytes 1032200 | tf_op jit(solution)/shard_map/cond/branch_1_fun/ppermute | solution.py:56
  80.2 8.0 %collective-permute-done.25 = bf16[48,3584]{1,0:T(8,128)(2,1)S(1)} collective-permute-done((bf16[48,3584]{1,0:T(8,128)(2,1)S(1)}, bf16[48,3584]{1,0:T(8,128)(2,1)S(1)}, u32[]{:S(2)}, u32[]{:S(2)}) %collective-permute-start.25) | collective-permute-done | bytes 344096 | tf_op jit(solution)/shard_map/cond/branch_1_fun/ppermute | solution.py:55
  88.6 3.3 %collective-permute-start.28 = (bf16[48,7168]{1,0:T(8,128)(2,1)S(1)}, bf16[48,7168]{1,0:T(8,128)(2,1)S(1)}, u32[]{:S(2)}, u32[]{:S(2)}) collective-permute-start(bf16[48,7168]{1,0:T(8,128)(2,1)S(1)} %pad_maximum_fusion.9), channel_id=1, source_target_pairs={{0,96},{16,112},{32,0},{48,16},{64,32},{80,48},{96,64},{112,80},{1... | collective-permute-start | bytes 2064392 | tf_op jit(solution)/shard_map/cond/branch_1_fun/ppermute | solution.py:60
  92.1 14.2 %collective-permute-done.26 = bf16[48,7168]{1,0:T(8,128)(2,1)S(1)} collective-permute-done((bf16[48,7168]{1,0:T(8,128)(2,1)S(1)}, bf16[48,7168]{1,0:T(8,128)(2,1)S(1)}, u32[]{:S(2)}, u32[]{:S(2)}) %collective-permute-start.26) | collective-permute-done | bytes 688160 | tf_op jit(solution)/shard_map/cond/branch_1_fun/ppermute | solution.py:59
  106.3 1.6 %add_convert_fusion.2 = bf16[48,7168]{1,0:T(8,128)(2,1)S(1)} fusion(bf16[48,7168]{1,0:T(8,128)(2,1)S(1)} %collective-permute-done.28, bf16[48,7168]{1,0:T(8,128)(2,1)S(1)} %collective-permute-done.26, bf16[144,7168]{1,0:T(8,128)(2,1)} %copy-done.5, bf16[384,7168]{1,0:T(8,128)(2,1)} %copy-done.2), kind=kLoop, calls=%fused_computation.32 | loop fusion | flops 2752512 | bytes 3440640 | tf_op jit(solution)/shard_map/cond/branch_1_fun/convert_element_type | solution.py:61
  108.1 2.1 %collective-permute-done.29 = bf16[48,7168]{1,0:T(8,128)(2,1)S(1)} collective-permute-done((bf16[48,7168]{1,0:T(8,128)(2,1)S(1)}, bf16[48,7168]{1,0:T(8,128)(2,1)S(1)}, u32[]{:S(2)}, u32[]{:S(2)}) %collective-permute-start.29) | collective-permute-done | bytes 688160 | tf_op jit(solution)/shard_map/cond/branch_1_fun/ppermute | solution.py:132
  110.3 1.1 gather_fusion.1
  111.6 1.3 all_to_all.16
  112.9 6.0 %all-to-all-start.1 = ((bf16[16,4,7168]{2,1,0:T(4,128)(2,1)}), bf16[16,4,7168]{2,1,0:T(4,128)(2,1)S(1)}, u32[]{:S(2)}, u32[]{:S(2)}) async-start(bf16[16,4,7168]{2,1,0:T(4,128)(2,1)} %all_to_all.16), calls=%async_computation.1 | async-start | bytes 1835008 | tf_op jit(solution)/shard_map/all_to_all | solution.py:139
  119.3 14.0 %all-to-all-done.1 = bf16[16,4,7168]{2,1,0:T(4,128)(2,1)S(1)} async-done(((bf16[16,4,7168]{2,1,0:T(4,128)(2,1)}), bf16[16,4,7168]{2,1,0:T(4,128)(2,1)S(1)}, u32[]{:S(2)}, u32[]{:S(2)}) %all-to-all-start.1) | async-done | bytes 917536 | tf_op jit(solution)/shard_map/all_to_all | solution.py:139
  134.2 1.9 %fusion.9 = bf16[128,7168]{1,0:T(8,128)(2,1)} fusion(f32[128,7168]{1,0:T(8,128)S(1)} %fusion.16, bf16[64,7168]{1,0:T(8,128)(2,1)S(1)} %all_to_all.18, f32[64]{0:T(128)S(1)} %broadcast_in_dim.90, s32[64]{0:T(128)S(1)} %eq.123, pred[64]{0:T(512)(128)(4,1)S(1)} %gt.40), kind=kOutput, calls=%fused_computation.82 | convolution fusion | flops 119332864 | bytes 6423104 | tf_op jit(solution)/shard_map/dot_general | solution.py:146
  (103 shorter events, 9.0 us)
Async XLA Ops:
  0.0 2.4 %copy-start = (bf16[128,7168]{1,0:T(8,128)(2,1)S(1)}, bf16[128,7168]{1,0:T(8,128)(2,1)}, u32[]{:S(2)}) copy-start(bf16[128,7168]{1,0:T(8,128)(2,1)} %param.8) | copy-start | bytes 5505028
  5.5 22.0 %all-to-all-start = ((bf16[16,4,7168]{2,1,0:T(4,128)(2,1)}), bf16[16,4,7168]{2,1,0:T(4,128)(2,1)S(1)}, u32[]{:S(2)}, u32[]{:S(2)}) async-start(bf16[16,4,7168]{2,1,0:T(4,128)(2,1)} %select_select_fusion.2), calls=%async_computation | async-start | bytes 1835008 | tf_op jit(solution)/shard_map/all_to_all | solution.py:85
  28.0 2.7 %collective-permute-start.14 = (bf16[64,7168]{1,0:T(8,128)(2,1)S(1)}, bf16[64,7168]{1,0:T(8,128)(2,1)}, u32[]{:S(2)}, u32[]{:S(2)}) collective-permute-start(bf16[64,7168]{1,0:T(8,128)(2,1)S(1)} %get-tuple-element.119), channel_id=1, source_target_pairs={{0,16},{16,0},{32,48},{48,32},{64,80},{80,64},{96,112},{112,96},{1... | collective-permute-start | bytes 2752520 | tf_op jit(solution)/shard_map/cond/branch_1_fun/ppermute | solution.py:128
  33.2 18.8 %collective-permute-start.16 = (bf16[48,7168]{1,0:T(8,128)(2,1)S(1)}, bf16[48,7168]{1,0:T(8,128)(2,1)S(1)}, u32[]{:S(2)}, u32[]{:S(2)}) collective-permute-start(bf16[48,7168]{1,0:T(8,128)(2,1)S(1)} %get-tuple-element.149), channel_id=1, source_target_pairs={{0,32},{16,48},{32,64},{48,80},{64,96},{80,112},{96,0},{112,16},{1... | collective-permute-start | bytes 2064392 | tf_op jit(solution)/shard_map/cond/branch_1_fun/ppermute | solution.py:31
  34.8 17.6 %collective-permute-start.18 = (bf16[48,7168]{1,0:T(8,128)(2,1)S(1)}, bf16[48,7168]{1,0:T(8,128)(2,1)S(1)}, u32[]{:S(2)}, u32[]{:S(2)}) collective-permute-start(bf16[48,7168]{1,0:T(8,128)(2,1)S(1)} %get-tuple-element.149), channel_id=1, source_target_pairs={{0,96},{16,112},{32,0},{48,16},{64,32},{80,48},{96,64},{112,80},{1... | collective-permute-start | bytes 2064392 | tf_op jit(solution)/shard_map/cond/branch_1_fun/ppermute | solution.py:32
  36.5 19.5 %collective-permute-start.15 = (bf16[48,7168]{1,0:T(8,128)(2,1)S(1)}, bf16[48,7168]{1,0:T(8,128)(2,1)S(1)}, u32[]{:S(2)}, u32[]{:S(2)}) collective-permute-start(bf16[48,7168]{1,0:T(8,128)(2,1)S(1)} %get-tuple-element.149), channel_id=1, source_target_pairs={{0,16},{16,0},{32,48},{48,32},{64,80},{80,64},{96,112},{112,96},{1... | collective-permute-start | bytes 2064392 | tf_op jit(solution)/shard_map/cond/branch_1_fun/ppermute | solution.py:33
  52.0 10.6 %collective-permute-start.20 = (bf16[48,3584]{1,0:T(8,128)(2,1)S(1)}, bf16[48,3584]{1,0:T(8,128)(2,1)S(1)}, u32[]{:S(2)}, u32[]{:S(2)}) collective-permute-start(bf16[48,3584]{1,0:T(8,128)(2,1)S(1)} %slice.143), channel_id=1, source_target_pairs={{0,32},{16,48},{32,64},{48,80},{64,96},{80,112},{96,0},{112,16},{1... | collective-permute-start | bytes 1032200 | tf_op jit(solution)/shard_map/cond/branch_1_fun/ppermute | solution.py:34
  52.4 10.2 %collective-permute-start.21 = (bf16[48,3584]{1,0:T(8,128)(2,1)S(1)}, bf16[48,3584]{1,0:T(8,128)(2,1)S(1)}, u32[]{:S(2)}, u32[]{:S(2)}) collective-permute-start(bf16[48,3584]{1,0:T(8,128)(2,1)S(1)} %slice.144), channel_id=1, source_target_pairs={{0,96},{16,112},{32,0},{48,16},{64,32},{80,48},{96,64},{112,80},{1... | collective-permute-start | bytes 1032200 | tf_op jit(solution)/shard_map/cond/branch_1_fun/ppermute | solution.py:35
  55.4 7.3 %collective-permute-start.17 = (bf16[48,7168]{1,0:T(8,128)(2,1)S(1)}, bf16[48,7168]{1,0:T(8,128)(2,1)S(1)}, u32[]{:S(2)}, u32[]{:S(2)}) collective-permute-start(bf16[48,7168]{1,0:T(8,128)(2,1)S(1)} %collective-permute-done.16), channel_id=1, source_target_pairs={{0,16},{16,0},{32,48},{48,32},{64,80},{80,64},{96,112},{112,96},{1... | collective-permute-start | bytes 2064392 | tf_op jit(solution)/shard_map/cond/branch_1_fun/ppermute | solution.py:37
  55.4 7.5 %collective-permute-start.19 = (bf16[48,7168]{1,0:T(8,128)(2,1)S(1)}, bf16[48,7168]{1,0:T(8,128)(2,1)S(1)}, u32[]{:S(2)}, u32[]{:S(2)}) collective-permute-start(bf16[48,7168]{1,0:T(8,128)(2,1)S(1)} %collective-permute-done.18), channel_id=1, source_target_pairs={{0,16},{16,0},{32,48},{48,32},{64,80},{80,64},{96,112},{112,96},{1... | collective-permute-start | bytes 2064392 | tf_op jit(solution)/shard_map/cond/branch_1_fun/ppermute | solution.py:38
  62.7 2.3 %copy-start.8 = (bf16[7168,256]{1,0:T(8,128)(2,1)S(1)}, bf16[7168,256]{1,0:T(8,128)(2,1)}, u32[]{:S(2)}) copy-start(bf16[7168,256]{1,0:T(8,128)(2,1)} %get-tuple-element.120) | copy-start | bytes 11010052 | tf_op jit(solution)/shard_map/cond
  62.7 2.2 %collective-permute-start.22 = (bf16[48,7168]{1,0:T(8,128)(2,1)S(1)}, bf16[48,7168]{1,0:T(8,128)(2,1)S(1)}, u32[]{:S(2)}, u32[]{:S(2)}) collective-permute-start(bf16[48,7168]{1,0:T(8,128)(2,1)S(1)} %pad_maximum_fusion.7), channel_id=1, source_target_pairs={{0,16},{16,0},{32,48},{48,32},{64,80},{80,64},{96,112},{112,96},{1... | collective-permute-start | bytes 2064392 | tf_op jit(solution)/shard_map/cond/branch_1_fun/ppermute | solution.py:39
  65.0 2.0 %copy-start.10 = (bf16[7168,256]{1,0:T(8,128)(2,1)S(1)}, bf16[7168,256]{1,0:T(8,128)(2,1)}, u32[]{:S(2)}) copy-start(bf16[7168,256]{1,0:T(8,128)(2,1)} %get-tuple-element.121) | copy-start | bytes 11010052 | tf_op jit(solution)/shard_map/cond
  67.0 2.0 %copy-start.4 = (bf16[256,7168]{1,0:T(8,128)(2,1)S(1)}, bf16[256,7168]{1,0:T(8,128)(2,1)}, u32[]{:S(2)}) copy-start(bf16[256,7168]{1,0:T(8,128)(2,1)} %get-tuple-element.122) | copy-start | bytes 11010052 | tf_op jit(solution)/shard_map/cond
  70.7 5.5 %copy-start.2 = (bf16[384,7168]{1,0:T(8,128)(2,1)}, bf16[384,7168]{1,0:T(8,128)(2,1)S(1)}, u32[]{:S(2)}) copy-start(bf16[384,7168]{1,0:T(8,128)(2,1)S(1)} %convolution_convert_fusion.1) | copy-start | bytes 16515076 | tf_op jit(solution)/shard_map/cond
  71.0 5.2 %collective-permute-start.23 = (bf16[144,7168]{1,0:T(8,128)(2,1)S(1)}, bf16[144,7168]{1,0:T(8,128)(2,1)S(1)}, u32[]{:S(2)}, u32[]{:S(2)}) collective-permute-start(bf16[144,7168]{1,0:T(8,128)(2,1)S(1)} %pad_maximum_fusion.4), channel_id=1, source_target_pairs={{0,16},{16,0},{32,48},{48,32},{64,80},{80,64},{96,112},{112,96},{1... | collective-permute-start | bytes 6193160 | tf_op jit(solution)/shard_map/cond/branch_1_fun/ppermute | solution.py:49
  71.2 5.0 %collective-permute-start.24 = (bf16[48,7168]{1,0:T(8,128)(2,1)S(1)}, bf16[48,7168]{1,0:T(8,128)(2,1)S(1)}, u32[]{:S(2)}, u32[]{:S(2)}) collective-permute-start(bf16[48,7168]{1,0:T(8,128)(2,1)S(1)} %get-tuple-element.168), channel_id=1, source_target_pairs={{0,16},{16,0},{32,48},{48,32},{64,80},{80,64},{96,112},{112,96},{1... | collective-permute-start | bytes 2064392 | tf_op jit(solution)/shard_map/cond/branch_1_fun/ppermute | solution.py:48
  76.2 12.3 %copy-start.5 = (bf16[144,7168]{1,0:T(8,128)(2,1)}, bf16[144,7168]{1,0:T(8,128)(2,1)S(1)}, u32[]{:S(2)}) copy-start(bf16[144,7168]{1,0:T(8,128)(2,1)S(1)} %collective-permute-done.23) | copy-start | bytes 6193156 | tf_op jit(solution)/shard_map/cond
  76.7 11.5 %collective-permute-start.25 = (bf16[48,3584]{1,0:T(8,128)(2,1)S(1)}, bf16[48,3584]{1,0:T(8,128)(2,1)S(1)}, u32[]{:S(2)}, u32[]{:S(2)}) collective-permute-start(bf16[48,3584]{1,0:T(8,128)(2,1)S(1)} %get-tuple-element.172), channel_id=1, source_target_pairs={{0,32},{16,48},{32,64},{48,80},{64,96},{80,112},{96,0},{112,16},{1... | collective-permute-start | bytes 1032200 | tf_op jit(solution)/shard_map/cond/branch_1_fun/ppermute | solution.py:55
  77.3 11.2 %collective-permute-start.27 = (bf16[48,3584]{1,0:T(8,128)(2,1)S(1)}, bf16[48,3584]{1,0:T(8,128)(2,1)S(1)}, u32[]{:S(2)}, u32[]{:S(2)}) collective-permute-start(bf16[48,3584]{1,0:T(8,128)(2,1)S(1)} %get-tuple-element.173), channel_id=1, source_target_pairs={{0,96},{16,112},{32,0},{48,16},{64,32},{80,48},{96,64},{112,80},{1... | collective-permute-start | bytes 1032200 | tf_op jit(solution)/shard_map/cond/branch_1_fun/ppermute | solution.py:56
  88.3 18.0 %collective-permute-start.26 = (bf16[48,7168]{1,0:T(8,128)(2,1)S(1)}, bf16[48,7168]{1,0:T(8,128)(2,1)S(1)}, u32[]{:S(2)}, u32[]{:S(2)}) collective-permute-start(bf16[48,7168]{1,0:T(8,128)(2,1)S(1)} %pad_maximum_fusion.8), channel_id=1, source_target_pairs={{0,32},{16,48},{32,64},{48,80},{64,96},{80,112},{96,0},{112,16},{1... | collective-permute-start | bytes 2064392 | tf_op jit(solution)/shard_map/cond/branch_1_fun/ppermute | solution.py:59
  88.6 17.8 %collective-permute-start.28 = (bf16[48,7168]{1,0:T(8,128)(2,1)S(1)}, bf16[48,7168]{1,0:T(8,128)(2,1)S(1)}, u32[]{:S(2)}, u32[]{:S(2)}) collective-permute-start(bf16[48,7168]{1,0:T(8,128)(2,1)S(1)} %pad_maximum_fusion.9), channel_id=1, source_target_pairs={{0,96},{16,112},{32,0},{48,16},{64,32},{80,48},{96,64},{112,80},{1... | collective-permute-start | bytes 2064392 | tf_op jit(solution)/shard_map/cond/branch_1_fun/ppermute | solution.py:60
  108.0 2.2 %collective-permute-start.29 = (bf16[48,7168]{1,0:T(8,128)(2,1)S(1)}, bf16[48,7168]{1,0:T(8,128)(2,1)S(1)}, u32[]{:S(2)}, u32[]{:S(2)}) collective-permute-start(bf16[48,7168]{1,0:T(8,128)(2,1)S(1)} %add_convert_fusion.2), channel_id=1, source_target_pairs={{0,16},{16,0},{32,48},{48,32},{64,80},{80,64},{96,112},{112,96},{1... | collective-permute-start | bytes 2064392 | tf_op jit(solution)/shard_map/cond/branch_1_fun/ppermute | solution.py:132
  111.6 7.4 %copy-start.6 = (s32[16,288]{1,0:T(8,128)S(1)}, s32[16,288]{1,0:T(8,128)}, u32[]{:S(2)}) copy-start(s32[16,288]{1,0:T(8,128)} %param.10) | copy-start | bytes 55300
  112.9 20.4 %all-to-all-start.1 = ((bf16[16,4,7168]{2,1,0:T(4,128)(2,1)}), bf16[16,4,7168]{2,1,0:T(4,128)(2,1)S(1)}, u32[]{:S(2)}, u32[]{:S(2)}) async-start(bf16[16,4,7168]{2,1,0:T(4,128)(2,1)} %all_to_all.16), calls=%async_computation.1 | async-start | bytes 1835008 | tf_op jit(solution)/shard_map/all_to_all | solution.py:139
  133.5 2.5 %copy-start.1 = (bf16[128,7168]{1,0:T(8,128)(2,1)S(1)}, bf16[128,7168]{1,0:T(8,128)(2,1)}, u32[]{:S(2)}) copy-start(bf16[128,7168]{1,0:T(8,128)(2,1)} %param.8) | copy-start | bytes 5505028

commit v9 on v8

--- a/solution.py
+++ b/solution.py
@@ -26,11 +26,12 @@
     return [(y * 2 + c, y * 2 + 1 - c) for y in range(dp_count // 2) for c in range(2)]
 
 
-def gather_dp(x, dp_count):
+def gather_dp(x, dp_count, sib=None):
     half = x.shape[1] // 2
     up = lax.ppermute(x, "dp", dp_pairs(dp_count, 1))
     dn = lax.ppermute(x, "dp", dp_pairs(dp_count, -1))
-    sib = lax.ppermute(x, "dp", sib_pairs(dp_count))
+    if sib is None:
+        sib = lax.ppermute(x, "dp", sib_pairs(dp_count))
     far_a = lax.ppermute(up[:, :half], "dp", dp_pairs(dp_count, 1))
     far_b = lax.ppermute(dn[:, half:], "dp", dp_pairs(dp_count, -1))
     far = jnp.concatenate([far_a, far_b], axis=1)
@@ -83,8 +84,8 @@
     send_rows = jnp.take(tokens, source_idx.reshape(-1), axis=0)
     send_rows = jnp.where(present.reshape(-1, 1) > 0, send_rows, jnp.zeros_like(send_rows))
     row_in = lax.all_to_all(send_rows, "expert", split_axis=0, concat_axis=0, tiled=True)
-    def expert_rows(rows, w_g, w_u, w_d):
-        picked = gather_dp(rows, dp_count)
+    def expert_rows(rows, w_g, w_u, w_d, sib_rows=None):
+        picked = gather_dp(rows, dp_count, sib_rows)
         gate_act = jnp.dot(picked, w_g, preferred_element_type=jnp.float32)
         up_act = jnp.dot(picked, w_u, preferred_element_type=jnp.float32)
         hidden = (jax.nn.silu(gate_act) * up_act).astype(jnp.bfloat16)
@@ -114,24 +115,21 @@
     chip_pos = jnp.sum((in_chip[:, None] & tri).astype(jnp.int32), axis=0)
     slot_of = (row_owners % ex_count) * slot_count + row_ranks
     local_slot = ((row_dp % 2) * slots + slot_of + my_core * slots) % (2 * slots)
-    wanted = my_core * half_rows + jnp.arange(half_rows, dtype=jnp.int32)
+    wanted = jnp.arange(chip_rows, dtype=jnp.int32)
     pick_q = in_chip[None, :] & (chip_pos[None, :] == wanted[:, None])
     comp_src = jnp.sum(pick_q.astype(jnp.int32) * local_slot[None, :], axis=1)
-    comp_ok = jnp.sum(pick_q.astype(jnp.int32), axis=1) > 0
+    comp_src = jnp.roll(comp_src.reshape(2, half_rows), -my_core, axis=0).reshape(-1)
     in_group = row_dp == my_dp
     pick_s = in_group[None, :] & (slot_of[None, :] == jnp.arange(slots, dtype=jnp.int32)[:, None])
     local_pos = (chip_pos + my_core * half_rows) % chip_rows
     back_src = jnp.sum(pick_s.astype(jnp.int32) * local_pos[None, :], axis=1)
-    back_ok = jnp.sum(pick_s.astype(jnp.int32), axis=1) > 0
 
     def short_path(rows, w_g, w_u, w_d):
         both = jnp.concatenate([rows, lax.ppermute(rows, "dp", sib_pairs(dp_count))], axis=0)
         packed = jnp.take(both, comp_src, axis=0)
-        packed = jnp.where(comp_ok[:, None], packed, jnp.zeros_like(packed))
-        out = expert_rows(packed, w_g, w_u, w_d)
+        out = expert_rows(packed[:half_rows], w_g, w_u, w_d, packed[half_rows:])
         full = jnp.concatenate([out, lax.ppermute(out, "dp", sib_pairs(dp_count))], axis=0)
-        spread = jnp.take(full, back_src, axis=0)
-        return jnp.where(back_ok[:, None], spread, jnp.zeros_like(spread))
+        return jnp.take(full, back_src, axis=0)
 
     summed = lax.cond(
         jnp.max(counts) <= chip_rows, short_path, expert_rows, row_in, w_gate[0], w_up[0], w_down[0]

time: 139 us -> 139 us (level)
  transfers between devices with their start and end apart: 18 -> 17, of which waited for: 10 -> 10; matrix products, arithmetic and copies ran while one was open for 2% -> 2% of each run, Pallas kernels for 0% -> 0%
where the time goes in v9:
time: 139 us; the launch traced here: 137 us
  waiting for transfers between devices  81.2 us (58%)
  starting transfers between devices  29 us (21%)
  other arithmetic  9.3 us (7%)
  local copies, waits for them, and re-layouts  8.28 us (6%)
  matrix products  7.44 us (5%)
    ppermute x1, waiting for transfers between devices, gather_dp(): up = lax.ppermute(x, 'dp', dp_pairs(dp_count, 1))  15.5 us
    ppermute x1, waiting for transfers between devices, scatter_dp(): a_a = lax.ppermute(s_a, 'dp', dp_pairs(dp_count, 1)).astype(f32)  14.5 us
    all_to_all x1, waiting for transfers between devices, shards(): lax.all_to_all(summed, 'expert', split_axis=0, concat_axis=0, tiled=True)  14 us
    all_to_all x1, waiting for transfers between devices, shards(): lax.all_to_all(send_rows, 'expert', split_axis=0, concat_axis=0, tiled=True)  11.8 us
    all_to_all x1, starting transfers between devices, shards(): lax.all_to_all(send_rows, 'expert', split_axis=0, concat_axis=0, tiled=True)  8.27 us
    ppermute x1, waiting for transfers between devices, scatter_dp(): r_a = lax.ppermute(q_far[:, :half], 'dp', dp_pairs(dp_count, 1)).astype(f32)  8.03 us
    ppermute x1, waiting for transfers between devices, gather_dp(): far_a = lax.ppermute(up[:, :half], 'dp', dp_pairs(dp_count, 1))  6.62 us
    all_to_all x1, starting transfers between devices, shards(): lax.all_to_all(summed, 'expert', split_axis=0, concat_axis=0, tiled=True)  5.95 us
  transfers between devices with their start and end apart: 17, of which 10 were waited for; matrix products, arithmetic and copies ran while one was open for 2% of the time, Pallas kernels for 0%

profile of v9, /device:TPU:6, one launch (start us, length us, event | category | flops | bytes accessed | tf_op | source)
XLA Modules:
  0.0 136.6 jit_solution(2352164095150881486)
XLA Ops:
  0.0 0.9 add_select_fusion.3
  0.9 0.8 broadcast_compare_fusion
  2.4 1.1 gather_fusion.2
  4.0 1.5 %select_select_fusion = bf16[16,4,7168]{2,1,0:T(4,128)(2,1)} fusion(bf16[16,4,7168]{2,1,0:T(4,128)(2,1)S(1)} %gather.15, pred[16,4]{1,0:T(8,128)(4,1)S(1)} %copy.11, pred[16,4]{1,0:T(8,128)(4,1)S(1)} %copy.8), kind=kLoop, calls=%fused_computation.74 | loop fusion | flops 917504 | bytes 1835136 | tf_op jit(solution)/shard_map/jit(_where)/select_n | solution.py:85
  5.5 8.3 %all-to-all-start = ((bf16[16,4,7168]{2,1,0:T(4,128)(2,1)}), bf16[16,4,7168]{2,1,0:T(4,128)(2,1)S(1)}, u32[]{:S(2)}, u32[]{:S(2)}) async-start(bf16[16,4,7168]{2,1,0:T(4,128)(2,1)} %select_select_fusion), calls=%async_computation | async-start | bytes 1835008 | tf_op jit(solution)/shard_map/all_to_all | solution.py:86
  14.4 0.7 reduce_max.9
  15.7 11.8 %all-to-all-done = bf16[16,4,7168]{2,1,0:T(4,128)(2,1)S(1)} async-done(((bf16[16,4,7168]{2,1,0:T(4,128)(2,1)}), bf16[16,4,7168]{2,1,0:T(4,128)(2,1)S(1)}, u32[]{:S(2)}, u32[]{:S(2)}) %all-to-all-start) | async-done | bytes 917536 | tf_op jit(solution)/shard_map/all_to_all | solution.py:86
  27.7 84.4 %conditional.1 = (bf16[64,7168]{1,0:T(8,128)(2,1)S(1)}) conditional(s32[]{:T(128)} %convert_element_type.143, (bf16[64,7168]{1,0:T(8,128)(2,1)S(1)}, bf16[7168,256]{1,0:T(8,128)(2,1)}, bf16[7168,256]{1,0:T(8,128)(2,1)}, bf16[256,7168]{1,0:T(8,128)(2,1)}) %tuple.57, (s32[]{:T(128)}, s32[1,288]{1,0:T(1,128)S(1)}, s32[1,288]{1,0:T(1,128)S(1)}, ...), branch_computations={%region_8.9_spmd, %region_9.11_spmd} | conditional | flops 5664997376 | bytes 203586816 | solution.py:134
  28.3 2.4 %collective-permute-done.14 = bf16[64,7168]{1,0:T(8,128)(2,1)} collective-permute-done((bf16[64,7168]{1,0:T(8,128)(2,1)S(1)}, bf16[64,7168]{1,0:T(8,128)(2,1)}, u32[]{:S(2)}, u32[]{:S(2)}) %collective-permute-start.14) | collective-permute-done | bytes 917536 | tf_op jit(solution)/shard_map/cond/branch_1_fun/ppermute | solution.py:128
  30.7 1.3 pad_maximum_fusion.5
  32.0 1.4 %gather_fusion = bf16[96,7168]{1,0:T(8,128)(2,1)S(1)} fusion(bf16[128,7168]{1,0:T(8,128)(2,1)S(1)} %pad_maximum_fusion.5, s32[1024]{0:T(1024)S(1)} %pad_clamp_fusion.1), kind=kCustom, calls=%fused_computation | custom fusion | bytes 2752896 | tf_op jit(solution)/shard_map/cond/branch_1_fun/jit(_take)/gather | solution.py:129
  33.7 1.6 %collective-permute-start.15 = (bf16[48,7168]{1,0:T(8,128)(2,1)S(1)}, bf16[48,7168]{1,0:T(8,128)(2,1)S(1)}, u32[]{:S(2)}, u32[]{:S(2)}) collective-permute-start(bf16[48,7168]{1,0:T(8,128)(2,1)S(1)} %slice.148), channel_id=1, source_target_pairs={{0,32},{16,48},{32,64},{48,80},{64,96},{80,112},{96,0},{112,16},{1... | collective-permute-start | bytes 2064392 | tf_op jit(solution)/shard_map/cond/branch_1_fun/ppermute | solution.py:31
  35.4 1.7 %collective-permute-start.17 = (bf16[48,7168]{1,0:T(8,128)(2,1)S(1)}, bf16[48,7168]{1,0:T(8,128)(2,1)S(1)}, u32[]{:S(2)}, u32[]{:S(2)}) collective-permute-start(bf16[48,7168]{1,0:T(8,128)(2,1)S(1)} %slice.148), channel_id=1, source_target_pairs={{0,96},{16,112},{32,0},{48,16},{64,32},{80,48},{96,64},{112,80},{1... | collective-permute-start | bytes 2064392 | tf_op jit(solution)/shard_map/cond/branch_1_fun/ppermute | solution.py:32
  37.1 15.5 %collective-permute-done.15 = bf16[48,7168]{1,0:T(8,128)(2,1)S(1)} collective-permute-done((bf16[48,7168]{1,0:T(8,128)(2,1)S(1)}, bf16[48,7168]{1,0:T(8,128)(2,1)S(1)}, u32[]{:S(2)}, u32[]{:S(2)}) %collective-permute-start.15) | collective-permute-done | bytes 688160 | tf_op jit(solution)/shard_map/cond/branch_1_fun/ppermute | solution.py:31
  53.0 3.0 %collective-permute-start.20 = (bf16[48,3584]{1,0:T(8,128)(2,1)S(1)}, bf16[48,3584]{1,0:T(8,128)(2,1)S(1)}, u32[]{:S(2)}, u32[]{:S(2)}) collective-permute-start(bf16[48,3584]{1,0:T(8,128)(2,1)S(1)} %slice.150), channel_id=1, source_target_pairs={{0,96},{16,112},{32,0},{48,16},{64,32},{80,48},{96,64},{112,80},{1... | collective-permute-start | bytes 1032200 | tf_op jit(solution)/shard_map/cond/branch_1_fun/ppermute | solution.py:36
  56.6 6.6 %collective-permute-done.19 = bf16[48,3584]{1,0:T(8,128)(2,1)S(1)} collective-permute-done((bf16[48,3584]{1,0:T(8,128)(2,1)S(1)}, bf16[48,3584]{1,0:T(8,128)(2,1)S(1)}, u32[]{:S(2)}, u32[]{:S(2)}) %collective-permute-start.19) | collective-permute-done | bytes 344096 | tf_op jit(solution)/shard_map/cond/branch_1_fun/ppermute | solution.py:35
  63.6 1.9 %collective-permute-done.21 = bf16[48,7168]{1,0:T(8,128)(2,1)S(1)} collective-permute-done((bf16[48,7168]{1,0:T(8,128)(2,1)S(1)}, bf16[48,7168]{1,0:T(8,128)(2,1)S(1)}, u32[]{:S(2)}, u32[]{:S(2)}) %collective-permute-start.21) | collective-permute-done | bytes 688160 | tf_op jit(solution)/shard_map/cond/branch_1_fun/ppermute | solution.py:40
  65.5 1.6 %fusion.50 = f32[384,256]{1,0:T(8,128)S(1)} fusion(bf16[384,7168]{1,0:T(8,128)(2,1)S(1)} %constant_dynamic-update-slice_fusion.9, bf16[7168,256]{1,0:T(8,128)(2,1)S(1)} %copy-done.8), kind=kOutput, calls=%fused_computation.179 | convolution fusion | flops 1409286144 | bytes 9568256 | tf_op jit(solution)/shard_map/cond/branch_1_fun/dot_general | solution.py:89
  67.6 1.6 %multiply_convert_fusion.1 = bf16[384,256]{1,0:T(8,128)(2,1)S(1)} fusion(f32[384,256]{1,0:T(8,128)S(1)} %fusion.50, bf16[384,7168]{1,0:T(8,128)(2,1)S(1)} %constant_dynamic-update-slice_fusion.9, bf16[7168,256]{1,0:T(8,128)(2,1)S(1)} %copy-done.10), kind=kOutput, calls=%fused_computation.47 | convolution fusion | flops 1409875968 | bytes 9764864 | tf_op jit(solution)/shard_map/cond/branch_1_fun/dot_general | solution.py:90
  69.6 1.6 %convolution_convert_fusion.1 = bf16[384,7168]{1,0:T(8,128)(2,1)S(1)} fusion(bf16[384,256]{1,0:T(8,128)(2,1)S(1)} %multiply_convert_fusion.1, bf16[256,7168]{1,0:T(8,128)(2,1)S(1)} %copy-done.4), kind=kOutput, calls=%fused_computation.28 | convolution fusion | flops 1412038656 | bytes 9371648 | tf_op jit(solution)/shard_map/cond/branch_1_fun/dot_general | solution.py:93
  72.2 4.6 %collective-permute-done.23 = bf16[48,7168]{1,0:T(8,128)(2,1)S(1)} collective-permute-done((bf16[48,7168]{1,0:T(8,128)(2,1)S(1)}, bf16[48,7168]{1,0:T(8,128)(2,1)S(1)}, u32[]{:S(2)}, u32[]{:S(2)}) %collective-permute-start.23) | collective-permute-done | bytes 688160 | tf_op jit(solution)/shard_map/cond/branch_1_fun/ppermute | solution.py:49
  77.8 2.9 %collective-permute-start.26 = (bf16[48,3584]{1,0:T(8,128)(2,1)S(1)}, bf16[48,3584]{1,0:T(8,128)(2,1)S(1)}, u32[]{:S(2)}, u32[]{:S(2)}) collective-permute-start(bf16[48,3584]{1,0:T(8,128)(2,1)S(1)} %get-tuple-element.153), channel_id=1, source_target_pairs={{0,96},{16,112},{32,0},{48,16},{64,32},{80,48},{96,64},{112,80},{1... | collective-permute-start | bytes 1032200 | tf_op jit(solution)/shard_map/cond/branch_1_fun/ppermute | solution.py:57
  80.7 8.0 %collective-permute-done.24 = bf16[48,3584]{1,0:T(8,128)(2,1)S(1)} collective-permute-done((bf16[48,3584]{1,0:T(8,128)(2,1)S(1)}, bf16[48,3584]{1,0:T(8,128)(2,1)S(1)}, u32[]{:S(2)}, u32[]{:S(2)}) %collective-permute-start.24) | collective-permute-done | bytes 344096 | tf_op jit(solution)/shard_map/cond/branch_1_fun/ppermute | solution.py:56
  89.1 3.3 %collective-permute-start.27 = (bf16[48,7168]{1,0:T(8,128)(2,1)S(1)}, bf16[48,7168]{1,0:T(8,128)(2,1)S(1)}, u32[]{:S(2)}, u32[]{:S(2)}) collective-permute-start(bf16[48,7168]{1,0:T(8,128)(2,1)S(1)} %pad_maximum_fusion.9), channel_id=1, source_target_pairs={{0,96},{16,112},{32,0},{48,16},{64,32},{80,48},{96,64},{112,80},{1... | collective-permute-start | bytes 2064392 | tf_op jit(solution)/shard_map/cond/branch_1_fun/ppermute | solution.py:61
  92.4 14.5 %collective-permute-done.25 = bf16[48,7168]{1,0:T(8,128)(2,1)S(1)} collective-permute-done((bf16[48,7168]{1,0:T(8,128)(2,1)S(1)}, bf16[48,7168]{1,0:T(8,128)(2,1)S(1)}, u32[]{:S(2)}, u32[]{:S(2)}) %collective-permute-start.25) | collective-permute-done | bytes 688160 | tf_op jit(solution)/shard_map/cond/branch_1_fun/ppermute | solution.py:60
  106.9 1.6 %add_convert_fusion.2 = bf16[48,7168]{1,0:T(8,128)(2,1)S(1)} fusion(bf16[48,7168]{1,0:T(8,128)(2,1)S(1)} %collective-permute-done.27, bf16[48,7168]{1,0:T(8,128)(2,1)S(1)} %collective-permute-done.25, bf16[144,7168]{1,0:T(8,128)(2,1)} %copy-done.5, bf16[384,7168]{1,0:T(8,128)(2,1)} %copy-done.2), kind=kLoop, calls=%fused_computation.32 | loop fusion | flops 2752512 | bytes 3440640 | tf_op jit(solution)/shard_map/cond/branch_1_fun/convert_element_type | solution.py:62
  108.9 1.9 %collective-permute-done.28 = bf16[48,7168]{1,0:T(8,128)(2,1)S(1)} collective-permute-done((bf16[48,7168]{1,0:T(8,128)(2,1)S(1)}, bf16[48,7168]{1,0:T(8,128)(2,1)S(1)}, u32[]{:S(2)}, u32[]{:S(2)}) %collective-permute-start.28) | collective-permute-done | bytes 688160 | tf_op jit(solution)/shard_map/cond/branch_1_fun/ppermute | solution.py:131
  110.9 1.1 gather_fusion.1
  112.2 1.3 all_to_all.16
  113.4 6.0 %all-to-all-start.1 = ((bf16[16,4,7168]{2,1,0:T(4,128)(2,1)}), bf16[16,4,7168]{2,1,0:T(4,128)(2,1)S(1)}, u32[]{:S(2)}, u32[]{:S(2)}) async-start(bf16[16,4,7168]{2,1,0:T(4,128)(2,1)} %all_to_all.16), calls=%async_computation.1 | async-start | bytes 1835008 | tf_op jit(solution)/shard_map/all_to_all | solution.py:137
  119.9 14.0 %all-to-all-done.1 = bf16[16,4,7168]{2,1,0:T(4,128)(2,1)S(1)} async-done(((bf16[16,4,7168]{2,1,0:T(4,128)(2,1)}), bf16[16,4,7168]{2,1,0:T(4,128)(2,1)S(1)}, u32[]{:S(2)}, u32[]{:S(2)}) %all-to-all-start.1) | async-done | bytes 917536 | tf_op jit(solution)/shard_map/all_to_all | solution.py:137
  134.7 1.9 %fusion.6 = bf16[128,7168]{1,0:T(8,128)(2,1)} fusion(f32[128,7168]{1,0:T(8,128)S(1)} %fusion.13, bf16[64,7168]{1,0:T(8,128)(2,1)S(1)} %all_to_all.18, f32[64]{0:T(128)S(1)} %broadcast_in_dim.50, s32[64]{0:T(128)S(1)} %eq.130, pred[64]{0:T(512)(128)(4,1)S(1)} %gt.25), kind=kOutput, calls=%fused_computation.72 | convolution fusion | flops 119332864 | bytes 6423104 | tf_op jit(solution)/shard_map/dot_general | solution.py:144
  (100 shorter events, 9.0 us)
Async XLA Ops:
  0.0 2.4 %copy-start = (bf16[128,7168]{1,0:T(8,128)(2,1)S(1)}, bf16[128,7168]{1,0:T(8,128)(2,1)}, u32[]{:S(2)}) copy-start(bf16[128,7168]{1,0:T(8,128)(2,1)} %param.8) | copy-start | bytes 5505028
  5.5 22.0 %all-to-all-start = ((bf16[16,4,7168]{2,1,0:T(4,128)(2,1)}), bf16[16,4,7168]{2,1,0:T(4,128)(2,1)S(1)}, u32[]{:S(2)}, u32[]{:S(2)}) async-start(bf16[16,4,7168]{2,1,0:T(4,128)(2,1)} %select_select_fusion), calls=%async_computation | async-start | bytes 1835008 | tf_op jit(solution)/shard_map/all_to_all | solution.py:86
  28.0 2.7 %collective-permute-start.14 = (bf16[64,7168]{1,0:T(8,128)(2,1)S(1)}, bf16[64,7168]{1,0:T(8,128)(2,1)}, u32[]{:S(2)}, u32[]{:S(2)}) collective-permute-start(bf16[64,7168]{1,0:T(8,128)(2,1)S(1)} %get-tuple-element.116), channel_id=1, source_target_pairs={{0,16},{16,0},{32,48},{48,32},{64,80},{80,64},{96,112},{112,96},{1... | collective-permute-start | bytes 2752520 | tf_op jit(solution)/shard_map/cond/branch_1_fun/ppermute | solution.py:128
  33.7 18.8 %collective-permute-start.15 = (bf16[48,7168]{1,0:T(8,128)(2,1)S(1)}, bf16[48,7168]{1,0:T(8,128)(2,1)S(1)}, u32[]{:S(2)}, u32[]{:S(2)}) collective-permute-start(bf16[48,7168]{1,0:T(8,128)(2,1)S(1)} %slice.148), channel_id=1, source_target_pairs={{0,32},{16,48},{32,64},{48,80},{64,96},{80,112},{96,0},{112,16},{1... | collective-permute-start | bytes 2064392 | tf_op jit(solution)/shard_map/cond/branch_1_fun/ppermute | solution.py:31
  35.4 17.6 %collective-permute-start.17 = (bf16[48,7168]{1,0:T(8,128)(2,1)S(1)}, bf16[48,7168]{1,0:T(8,128)(2,1)S(1)}, u32[]{:S(2)}, u32[]{:S(2)}) collective-permute-start(bf16[48,7168]{1,0:T(8,128)(2,1)S(1)} %slice.148), channel_id=1, source_target_pairs={{0,96},{16,112},{32,0},{48,16},{64,32},{80,48},{96,64},{112,80},{1... | collective-permute-start | bytes 2064392 | tf_op jit(solution)/shard_map/cond/branch_1_fun/ppermute | solution.py:32
  52.6 10.6 %collective-permute-start.19 = (bf16[48,3584]{1,0:T(8,128)(2,1)S(1)}, bf16[48,3584]{1,0:T(8,128)(2,1)S(1)}, u32[]{:S(2)}, u32[]{:S(2)}) collective-permute-start(bf16[48,3584]{1,0:T(8,128)(2,1)S(1)} %slice.149), channel_id=1, source_target_pairs={{0,32},{16,48},{32,64},{48,80},{64,96},{80,112},{96,0},{112,16},{1... | collective-permute-start | bytes 1032200 | tf_op jit(solution)/shard_map/cond/branch_1_fun/ppermute | solution.py:35
  53.0 10.2 %collective-permute-start.20 = (bf16[48,3584]{1,0:T(8,128)(2,1)S(1)}, bf16[48,3584]{1,0:T(8,128)(2,1)S(1)}, u32[]{:S(2)}, u32[]{:S(2)}) collective-permute-start(bf16[48,3584]{1,0:T(8,128)(2,1)S(1)} %slice.150), channel_id=1, source_target_pairs={{0,96},{16,112},{32,0},{48,16},{64,32},{80,48},{96,64},{112,80},{1... | collective-permute-start | bytes 1032200 | tf_op jit(solution)/shard_map/cond/branch_1_fun/ppermute | solution.py:36
  56.0 7.3 %collective-permute-start.16 = (bf16[48,7168]{1,0:T(8,128)(2,1)S(1)}, bf16[48,7168]{1,0:T(8,128)(2,1)S(1)}, u32[]{:S(2)}, u32[]{:S(2)}) collective-permute-start(bf16[48,7168]{1,0:T(8,128)(2,1)S(1)} %collective-permute-done.15), channel_id=1, source_target_pairs={{0,16},{16,0},{32,48},{48,32},{64,80},{80,64},{96,112},{112,96},{1... | collective-permute-start | bytes 2064392 | tf_op jit(solution)/shard_map/cond/branch_1_fun/ppermute | solution.py:38
  56.0 7.5 %collective-permute-start.18 = (bf16[48,7168]{1,0:T(8,128)(2,1)S(1)}, bf16[48,7168]{1,0:T(8,128)(2,1)S(1)}, u32[]{:S(2)}, u32[]{:S(2)}) collective-permute-start(bf16[48,7168]{1,0:T(8,128)(2,1)S(1)} %collective-permute-done.17), channel_id=1, source_target_pairs={{0,16},{16,0},{32,48},{48,32},{64,80},{80,64},{96,112},{112,96},{1... | collective-permute-start | bytes 2064392 | tf_op jit(solution)/shard_map/cond/branch_1_fun/ppermute | solution.py:39
  63.2 2.3 %copy-start.8 = (bf16[7168,256]{1,0:T(8,128)(2,1)S(1)}, bf16[7168,256]{1,0:T(8,128)(2,1)}, u32[]{:S(2)}) copy-start(bf16[7168,256]{1,0:T(8,128)(2,1)} %get-tuple-element.117) | copy-start | bytes 11010052 | tf_op jit(solution)/shard_map/cond
  63.2 2.2 %collective-permute-start.21 = (bf16[48,7168]{1,0:T(8,128)(2,1)S(1)}, bf16[48,7168]{1,0:T(8,128)(2,1)S(1)}, u32[]{:S(2)}, u32[]{:S(2)}) collective-permute-start(bf16[48,7168]{1,0:T(8,128)(2,1)S(1)} %pad_maximum_fusion.7), channel_id=1, source_target_pairs={{0,16},{16,0},{32,48},{48,32},{64,80},{80,64},{96,112},{112,96},{1... | collective-permute-start | bytes 2064392 | tf_op jit(solution)/shard_map/cond/branch_1_fun/ppermute | solution.py:40
  65.5 2.0 %copy-start.10 = (bf16[7168,256]{1,0:T(8,128)(2,1)S(1)}, bf16[7168,256]{1,0:T(8,128)(2,1)}, u32[]{:S(2)}) copy-start(bf16[7168,256]{1,0:T(8,128)(2,1)} %get-tuple-element.118) | copy-start | bytes 11010052 | tf_op jit(solution)/shard_map/cond
  67.6 2.0 %copy-start.4 = (bf16[256,7168]{1,0:T(8,128)(2,1)S(1)}, bf16[256,7168]{1,0:T(8,128)(2,1)}, u32[]{:S(2)}) copy-start(bf16[256,7168]{1,0:T(8,128)(2,1)} %get-tuple-element.119) | copy-start | bytes 11010052 | tf_op jit(solution)/shard_map/cond
  71.2 5.5 %copy-start.2 = (bf16[384,7168]{1,0:T(8,128)(2,1)}, bf16[384,7168]{1,0:T(8,128)(2,1)S(1)}, u32[]{:S(2)}) copy-start(bf16[384,7168]{1,0:T(8,128)(2,1)S(1)} %convolution_convert_fusion.1) | copy-start | bytes 16515076 | tf_op jit(solution)/shard_map/cond
  71.6 5.2 %collective-permute-start.22 = (bf16[144,7168]{1,0:T(8,128)(2,1)S(1)}, bf16[144,7168]{1,0:T(8,128)(2,1)S(1)}, u32[]{:S(2)}, u32[]{:S(2)}) collective-permute-start(bf16[144,7168]{1,0:T(8,128)(2,1)S(1)} %pad_maximum_fusion.4), channel_id=1, source_target_pairs={{0,16},{16,0},{32,48},{48,32},{64,80},{80,64},{96,112},{112,96},{1... | collective-permute-start | bytes 6193160 | tf_op jit(solution)/shard_map/cond/branch_1_fun/ppermute | solution.py:50
  71.8 5.0 %collective-permute-start.23 = (bf16[48,7168]{1,0:T(8,128)(2,1)S(1)}, bf16[48,7168]{1,0:T(8,128)(2,1)S(1)}, u32[]{:S(2)}, u32[]{:S(2)}) collective-permute-start(bf16[48,7168]{1,0:T(8,128)(2,1)S(1)} %get-tuple-element.148), channel_id=1, source_target_pairs={{0,16},{16,0},{32,48},{48,32},{64,80},{80,64},{96,112},{112,96},{1... | collective-permute-start | bytes 2064392 | tf_op jit(solution)/shard_map/cond/branch_1_fun/ppermute | solution.py:49
  76.8 12.3 %copy-start.5 = (bf16[144,7168]{1,0:T(8,128)(2,1)}, bf16[144,7168]{1,0:T(8,128)(2,1)S(1)}, u32[]{:S(2)}) copy-start(bf16[144,7168]{1,0:T(8,128)(2,1)S(1)} %collective-permute-done.22) | copy-start | bytes 6193156 | tf_op jit(solution)/shard_map/cond
  77.3 11.5 %collective-permute-start.24 = (bf16[48,3584]{1,0:T(8,128)(2,1)S(1)}, bf16[48,3584]{1,0:T(8,128)(2,1)S(1)}, u32[]{:S(2)}, u32[]{:S(2)}) collective-permute-start(bf16[48,3584]{1,0:T(8,128)(2,1)S(1)} %get-tuple-element.152), channel_id=1, source_target_pairs={{0,32},{16,48},{32,64},{48,80},{64,96},{80,112},{96,0},{112,16},{1... | collective-permute-start | bytes 1032200 | tf_op jit(solution)/shard_map/cond/branch_1_fun/ppermute | solution.py:56
  77.8 11.2 %collective-permute-start.26 = (bf16[48,3584]{1,0:T(8,128)(2,1)S(1)}, bf16[48,3584]{1,0:T(8,128)(2,1)S(1)}, u32[]{:S(2)}, u32[]{:S(2)}) collective-permute-start(bf16[48,3584]{1,0:T(8,128)(2,1)S(1)} %get-tuple-element.153), channel_id=1, source_target_pairs={{0,96},{16,112},{32,0},{48,16},{64,32},{80,48},{96,64},{112,80},{1... | collective-permute-start | bytes 1032200 | tf_op jit(solution)/shard_map/cond/branch_1_fun/ppermute | solution.py:57
  88.9 18.0 %collective-permute-start.25 = (bf16[48,7168]{1,0:T(8,128)(2,1)S(1)}, bf16[48,7168]{1,0:T(8,128)(2,1)S(1)}, u32[]{:S(2)}, u32[]{:S(2)}) collective-permute-start(bf16[48,7168]{1,0:T(8,128)(2,1)S(1)} %pad_maximum_fusion.8), channel_id=1, source_target_pairs={{0,32},{16,48},{32,64},{48,80},{64,96},{80,112},{96,0},{112,16},{1... | collective-permute-start | bytes 2064392 | tf_op jit(solution)/shard_map/cond/branch_1_fun/ppermute | solution.py:60
  89.1 17.8 %collective-permute-start.27 = (bf16[48,7168]{1,0:T(8,128)(2,1)S(1)}, bf16[48,7168]{1,0:T(8,128)(2,1)S(1)}, u32[]{:S(2)}, u32[]{:S(2)}) collective-permute-start(bf16[48,7168]{1,0:T(8,128)(2,1)S(1)} %pad_maximum_fusion.9), channel_id=1, source_target_pairs={{0,96},{16,112},{32,0},{48,16},{64,32},{80,48},{96,64},{112,80},{1... | collective-permute-start | bytes 2064392 | tf_op jit(solution)/shard_map/cond/branch_1_fun/ppermute | solution.py:61
  108.6 2.2 %collective-permute-start.28 = (bf16[48,7168]{1,0:T(8,128)(2,1)S(1)}, bf16[48,7168]{1,0:T(8,128)(2,1)S(1)}, u32[]{:S(2)}, u32[]{:S(2)}) collective-permute-start(bf16[48,7168]{1,0:T(8,128)(2,1)S(1)} %add_convert_fusion.2), channel_id=1, source_target_pairs={{0,16},{16,0},{32,48},{48,32},{64,80},{80,64},{96,112},{112,96},{1... | collective-permute-start | bytes 2064392 | tf_op jit(solution)/shard_map/cond/branch_1_fun/ppermute | solution.py:131
  112.2 7.4 %copy-start.6 = (s32[16,288]{1,0:T(8,128)S(1)}, s32[16,288]{1,0:T(8,128)}, u32[]{:S(2)}) copy-start(s32[16,288]{1,0:T(8,128)} %param.10) | copy-start | bytes 55300
  113.4 20.4 %all-to-all-start.1 = ((bf16[16,4,7168]{2,1,0:T(4,128)(2,1)}), bf16[16,4,7168]{2,1,0:T(4,128)(2,1)S(1)}, u32[]{:S(2)}, u32[]{:S(2)}) async-start(bf16[16,4,7168]{2,1,0:T(4,128)(2,1)} %all_to_all.16), calls=%async_computation.1 | async-start | bytes 1835008 | tf_op jit(solution)/shard_map/all_to_all | solution.py:137
  134.1 2.5 %copy-start.1 = (bf16[128,7168]{1,0:T(8,128)(2,1)S(1)}, bf16[128,7168]{1,0:T(8,128)(2,1)}, u32[]{:S(2)}) copy-start(bf16[128,7168]{1,0:T(8,128)(2,1)} %param.8) | copy-start | bytes 5505028

commit v10 on v5

--- a/solution.py
+++ b/solution.py
@@ -35,14 +35,14 @@
     s_up = lax.ppermute(up, "dp", sib_pairs(dp_count))
     s_dn = lax.ppermute(dn, "dp", sib_pairs(dp_count))
     s_far = lax.ppermute(far, "dp", sib_pairs(dp_count))
-    return jnp.concatenate([x, sib, up, s_up, dn, s_dn, far, s_far], axis=0)
+    return [x, sib, up, s_up, dn, s_dn, far, s_far]
 
 
 def scatter_dp(p, dp_count):
-    rows = p.shape[0] // 8
-    half = p.shape[1] // 2
+    rows = p[0].shape[0]
+    half = p[0].shape[1] // 2
     f32 = jnp.float32
-    b = [p[i * rows:(i + 1) * rows] for i in range(8)]
+    b = p
     got_far = lax.ppermute(b[7], "dp", sib_pairs(dp_count))
     got = lax.ppermute(jnp.concatenate([b[1], b[3], b[5]], axis=0), "dp", sib_pairs(dp_count))
     g = [got[i * rows:(i + 1) * rows].astype(f32) for i in range(3)] + [got_far.astype(f32)]
@@ -80,12 +80,23 @@
     send_rows = jnp.take(tokens, source_idx.reshape(-1), axis=0)
     send_rows = jnp.where(present.reshape(-1, 1) > 0, send_rows, jnp.zeros_like(send_rows))
     row_in = lax.all_to_all(send_rows, "expert", split_axis=0, concat_axis=0, tiled=True)
-    picked = gather_dp(row_in, dp_count)
-    gate_act = jnp.dot(picked, w_gate[0], preferred_element_type=jnp.float32)
-    up_act = jnp.dot(picked, w_up[0], preferred_element_type=jnp.float32)
-    hidden = (jax.nn.silu(gate_act) * up_act).astype(jnp.bfloat16)
-    hidden = lax.optimization_barrier(hidden)
-    result = jnp.dot(hidden, w_down[0], preferred_element_type=jnp.float32).astype(jnp.bfloat16)
+    blocks = gather_dp(row_in, dp_count)
+    rows = row_in.shape[0]
+    hidden = []
+    for part in (blocks[:6], blocks[6:]):
+        picked = jnp.concatenate(part, axis=0)
+        gate_act = jnp.dot(picked, w_gate[0], preferred_element_type=jnp.float32)
+        up_act = jnp.dot(picked, w_up[0], preferred_element_type=jnp.float32)
+        hidden.append((jax.nn.silu(gate_act) * up_act).astype(jnp.bfloat16))
+    hidden = lax.optimization_barrier(jnp.concatenate(hidden, axis=0))
+    hb = [hidden[i * rows:(i + 1) * rows] for i in range(8)]
+    result = [None] * 8
+    for group in ((1, 3, 5, 7), (0, 2, 4, 6)):
+        out = jnp.dot(
+            jnp.concatenate([hb[i] for i in group], axis=0), w_down[0], preferred_element_type=jnp.float32
+        ).astype(jnp.bfloat16)
+        for n, i in enumerate(group):
+            result[i] = out[n * rows:(n + 1) * rows]
     summed = scatter_dp(result, dp_count)
     returned = lax.all_to_all(summed, "expert", split_axis=0, concat_axis=0, tiled=True)
     placed = (jnp.arange(tok_count, dtype=jnp.int32)[:, None] == source_idx.reshape(1, -1)) & (

time: 139 us -> 138 us (level)
  waiting for transfers between devices: 76.5 us -> 73.6 us
  local copies, waits for them, and re-layouts: 4.83 us -> 6.54 us
    ppermute x1, waiting for transfers between devices: 2.14 us -> 0.01 us  [gather_dp(): s_far = lax.ppermute(far, 'dp', sib_pairs(dp_count))]
    unnamed x20 -> x18, local copies, waits for them, and re-layouts: 0.47 us -> 2.12 us
  transfers between devices with their start and end apart: 15 -> 15, of which waited for: 7 -> 6; matrix products, arithmetic and copies ran while one was open for 1% -> 4% of each run, Pallas kernels for 0% -> 0%
where the time goes in v10:
time: 138 us; the launch traced here: 136 us
  waiting for transfers between devices  73.6 us (53%)
  blocking collectives  21.6 us (16%)
  starting transfers between devices  20.5 us (15%)
  matrix products  9.36 us (7%)
  local copies, waits for them, and re-layouts  6.54 us (5%)
  other arithmetic  4.04 us (3%)
    all_to_all x1, blocking collectives, shards(): lax.all_to_all(send_rows, 'expert', split_axis=0, concat_axis=0, tiled=True)  21.6 us
    ppermute x1, waiting for transfers between devices, scatter_dp(): a_a = lax.ppermute(s_a, 'dp', dp_pairs(dp_count, 1)).astype(f32)  19.5 us
    ppermute x1, waiting for transfers between devices, gather_dp(): up = lax.ppermute(x, 'dp', dp_pairs(dp_count, 1))  19 us
    all_to_all x1, waiting for transfers between devices, shards(): lax.all_to_all(summed, 'expert', split_axis=0, concat_axis=0, tiled=True)  12.2 us
    ppermute x1, waiting for transfers between devices, scatter_dp(): r_a = lax.ppermute(q_far[:, :half], 'dp', dp_pairs(dp_count, 1)).astype(f32)  10.7 us
    ppermute x1, waiting for transfers between devices, gather_dp(): far_a = lax.ppermute(up[:, :half], 'dp', dp_pairs(dp_count, 1))  7.6 us
    all_to_all x1, starting transfers between devices, shards(): lax.all_to_all(summed, 'expert', split_axis=0, concat_axis=0, tiled=True)  5.62 us
    ppermute x1, waiting for transfers between devices, scatter_dp(): got_far = lax.ppermute(b[7], 'dp', sib_pairs(dp_count))  4.56 us
  transfers between devices with their start and end apart: 15, of which 6 were waited for; matrix products, arithmetic and copies ran while one was open for 4% of the time, Pallas kernels for 0%

profile of v10, /device:TPU:6, one launch (start us, length us, event | category | flops | bytes accessed | tf_op | source)
XLA Modules:
  0.0 136.0 jit_solution(13551545241476696640)
XLA Ops:
  0.0 0.9 multiply_subtract_fusion
  0.9 0.8 fusion.42
  2.5 1.1 gather_fusion
  3.9 0.5 select_select_fusion
  4.5 21.6 %all_to_all.21 = bf16[16,4,7168]{2,1,0:T(4,128)(2,1)S(1)} all-to-all(bf16[16,4,7168]{2,1,0:T(4,128)(2,1)S(1)} %select_select_fusion), channel_id=1, replica_groups=mesh['dp'=8,'expert'=16] {'expert'}, dimensions={0} | all-to-all | bytes 1835008 | tf_op jit(solution)/shard_map/all_to_all | solution.py:82
  26.3 1.6 %collective-permute-start.1 = (bf16[64,7168]{1,0:T(8,128)(2,1)S(1)}, bf16[64,7168]{1,0:T(8,128)(2,1)S(1)}, u32[]{:S(2)}, u32[]{:S(2)}) collective-permute-start(bf16[64,7168]{1,0:T(8,128)(2,1)S(1)} %all_to_all.15), channel_id=1, source_target_pairs={{0,32},{16,48},{32,64},{48,80},{64,96},{80,112},{96,0},{112,16},{1... | collective-permute-start | bytes 2752520 | tf_op jit(solution)/shard_map/ppermute | solution.py:29
  28.0 1.7 %collective-permute-start.3 = (bf16[64,7168]{1,0:T(8,128)(2,1)S(1)}, bf16[64,7168]{1,0:T(8,128)(2,1)S(1)}, u32[]{:S(2)}, u32[]{:S(2)}) collective-permute-start(bf16[64,7168]{1,0:T(8,128)(2,1)S(1)} %all_to_all.15), channel_id=1, source_target_pairs={{0,96},{16,112},{32,0},{48,16},{64,32},{80,48},{96,64},{112,80},{1... | collective-permute-start | bytes 2752520 | tf_op jit(solution)/shard_map/ppermute | solution.py:30
  29.7 19.0 %collective-permute-done.1 = bf16[64,7168]{1,0:T(8,128)(2,1)S(1)} collective-permute-done((bf16[64,7168]{1,0:T(8,128)(2,1)S(1)}, bf16[64,7168]{1,0:T(8,128)(2,1)S(1)}, u32[]{:S(2)}, u32[]{:S(2)}) %collective-permute-start.1) | collective-permute-done | bytes 917536 | tf_op jit(solution)/shard_map/ppermute | solution.py:29
  49.1 3.0 %collective-permute-start.6 = (bf16[64,3584]{1,0:T(8,128)(2,1)S(1)}, bf16[64,3584]{1,0:T(8,128)(2,1)S(1)}, u32[]{:S(2)}, u32[]{:S(2)}) collective-permute-start(bf16[64,3584]{1,0:T(8,128)(2,1)S(1)} %slice.108), channel_id=1, source_target_pairs={{0,96},{16,112},{32,0},{48,16},{64,32},{80,48},{96,64},{112,80},{1... | collective-permute-start | bytes 1376264 | tf_op jit(solution)/shard_map/ppermute | solution.py:33
  52.1 0.5 collective-permute-start.4
  52.8 7.6 %collective-permute-done.5 = bf16[64,3584]{1,0:T(8,128)(2,1)S(1)} collective-permute-done((bf16[64,3584]{1,0:T(8,128)(2,1)S(1)}, bf16[64,3584]{1,0:T(8,128)(2,1)S(1)}, u32[]{:S(2)}, u32[]{:S(2)}) %collective-permute-start.5) | collective-permute-done | bytes 458784 | tf_op jit(solution)/shard_map/ppermute | solution.py:32
  60.8 1.6 %fusion.9 = f32[384,256]{1,0:T(8,128)S(1)} fusion(bf16[384,7168]{1,0:T(8,128)(2,1)S(1)} %constant_dynamic-update-slice_fusion, bf16[1,7168,256]{2,1,0:T(8,128)(2,1)S(1)} %copy-done.4), kind=kOutput, calls=%fused_computation.13 | convolution fusion | flops 1409286144 | bytes 9568256 | tf_op jit(solution)/shard_map/dot_general | solution.py:88
  62.4 0.4 copy-done.5
  62.8 1.6 %multiply_convert_fusion = bf16[384,256]{1,0:T(8,128)(2,1)S(1)} fusion(f32[384,256]{1,0:T(8,128)S(1)} %fusion.9, bf16[384,7168]{1,0:T(8,128)(2,1)S(1)} %constant_dynamic-update-slice_fusion, bf16[1,7168,256]{2,1,0:T(8,128)(2,1)S(1)} %copy-done.5), kind=kOutput, calls=%fused_computation.31 | convolution fusion | flops 1409875968 | bytes 9764864 | tf_op jit(solution)/shard_map/dot_general | solution.py:89
  64.4 0.6 fusion.7
  65.1 0.6 multiply_convert_fusion.1
  65.8 1.3 copy-done.2
  67.1 1.1 convolution_convert_fusion
  68.5 0.6 collective-permute-start.8
  69.4 1.1 convolution_convert_fusion.1
  70.5 4.6 %collective-permute-done.9 = bf16[64,7168]{1,0:T(8,128)(2,1)S(1)} collective-permute-done((bf16[64,7168]{1,0:T(8,128)(2,1)S(1)}, bf16[64,7168]{1,0:T(8,128)(2,1)S(1)}, u32[]{:S(2)}, u32[]{:S(2)}) %collective-permute-start.9) | collective-permute-done | bytes 917536 | tf_op jit(solution)/shard_map/ppermute | solution.py:46
  75.1 0.7 convert_add_fusion.1
  76.3 2.9 %collective-permute-start.12 = (bf16[64,3584]{1,0:T(8,128)(2,1)S(1)}, bf16[64,3584]{1,0:T(8,128)(2,1)S(1)}, u32[]{:S(2)}, u32[]{:S(2)}) collective-permute-start(bf16[64,3584]{1,0:T(8,128)(2,1)S(1)} %get-tuple-element.11), channel_id=1, source_target_pairs={{0,96},{16,112},{32,0},{48,16},{64,32},{80,48},{96,64},{112,80},{1... | collective-permute-start | bytes 1376264 | tf_op jit(solution)/shard_map/ppermute | solution.py:54
  79.3 10.7 %collective-permute-done.10 = bf16[64,3584]{1,0:T(8,128)(2,1)S(1)} collective-permute-done((bf16[64,3584]{1,0:T(8,128)(2,1)S(1)}, bf16[64,3584]{1,0:T(8,128)(2,1)S(1)}, u32[]{:S(2)}, u32[]{:S(2)}) %collective-permute-start.10) | collective-permute-done | bytes 458784 | tf_op jit(solution)/shard_map/ppermute | solution.py:53
  90.4 3.3 %collective-permute-start.13 = (bf16[64,7168]{1,0:T(8,128)(2,1)S(1)}, bf16[64,7168]{1,0:T(8,128)(2,1)S(1)}, u32[]{:S(2)}, u32[]{:S(2)}) collective-permute-start(bf16[64,7168]{1,0:T(8,128)(2,1)S(1)} %pad_maximum_fusion.4), channel_id=1, source_target_pairs={{0,96},{16,112},{32,0},{48,16},{64,32},{80,48},{96,64},{112,80},{1... | collective-permute-start | bytes 2752520 | tf_op jit(solution)/shard_map/ppermute | solution.py:58
  93.7 19.5 %collective-permute-done.11 = bf16[64,7168]{1,0:T(8,128)(2,1)S(1)} collective-permute-done((bf16[64,7168]{1,0:T(8,128)(2,1)S(1)}, bf16[64,7168]{1,0:T(8,128)(2,1)S(1)}, u32[]{:S(2)}, u32[]{:S(2)}) %collective-permute-start.11) | collective-permute-done | bytes 917536 | tf_op jit(solution)/shard_map/ppermute | solution.py:57
  113.3 0.5 add_convert_fusion
  113.7 1.3 all_to_all.16
  115.0 5.6 %all-to-all-start.1 = ((bf16[16,4,7168]{2,1,0:T(4,128)(2,1)}), bf16[16,4,7168]{2,1,0:T(4,128)(2,1)S(1)}, u32[]{:S(2)}, u32[]{:S(2)}) async-start(bf16[16,4,7168]{2,1,0:T(4,128)(2,1)} %all_to_all.16), calls=%async_computation.1 | async-start | bytes 1835008 | tf_op jit(solution)/shard_map/all_to_all | solution.py:101
  121.1 12.2 %all-to-all-done.1 = bf16[16,4,7168]{2,1,0:T(4,128)(2,1)S(1)} async-done(((bf16[16,4,7168]{2,1,0:T(4,128)(2,1)}), bf16[16,4,7168]{2,1,0:T(4,128)(2,1)S(1)}, u32[]{:S(2)}, u32[]{:S(2)}) %all-to-all-start.1) | async-done | bytes 917536 | tf_op jit(solution)/shard_map/all_to_all | solution.py:101
  133.5 0.6 fusion.30
  134.1 1.9 %fusion = bf16[128,7168]{1,0:T(8,128)(2,1)} fusion(f32[128,7168]{1,0:T(8,128)S(1)} %fusion.30, bf16[64,7168]{1,0:T(8,128)(2,1)S(1)} %all_to_all.18, f32[64]{0:T(128)S(1)} %broadcast_in_dim.43, s32[64]{0:T(128)S(1)} %eq.40, pred[64]{0:T(512)(128)(4,1)S(1)} %gt.25), kind=kOutput, calls=%fused_computation.4 | convolution fusion | flops 119332864 | bytes 6423104 | tf_op jit(solution)/shard_map/dot_general | solution.py:108
  (65 shorter events, 4.5 us)
Async XLA Ops:
  0.0 2.5 %copy-start = (bf16[128,7168]{1,0:T(8,128)(2,1)S(1)}, bf16[128,7168]{1,0:T(8,128)(2,1)}, u32[]{:S(2)}) copy-start(bf16[128,7168]{1,0:T(8,128)(2,1)} %param.6) | copy-start | bytes 5505028
  26.3 22.4 %collective-permute-start.1 = (bf16[64,7168]{1,0:T(8,128)(2,1)S(1)}, bf16[64,7168]{1,0:T(8,128)(2,1)S(1)}, u32[]{:S(2)}, u32[]{:S(2)}) collective-permute-start(bf16[64,7168]{1,0:T(8,128)(2,1)S(1)} %all_to_all.15), channel_id=1, source_target_pairs={{0,32},{16,48},{32,64},{48,80},{64,96},{80,112},{96,0},{112,16},{1... | collective-permute-start | bytes 2752520 | tf_op jit(solution)/shard_map/ppermute | solution.py:29
  28.0 21.1 %collective-permute-start.3 = (bf16[64,7168]{1,0:T(8,128)(2,1)S(1)}, bf16[64,7168]{1,0:T(8,128)(2,1)S(1)}, u32[]{:S(2)}, u32[]{:S(2)}) collective-permute-start(bf16[64,7168]{1,0:T(8,128)(2,1)S(1)} %all_to_all.15), channel_id=1, source_target_pairs={{0,96},{16,112},{32,0},{48,16},{64,32},{80,48},{96,64},{112,80},{1... | collective-permute-start | bytes 2752520 | tf_op jit(solution)/shard_map/ppermute | solution.py:30
  29.6 23.0 %collective-permute-start = (bf16[64,7168]{1,0:T(8,128)(2,1)S(1)}, bf16[64,7168]{1,0:T(8,128)(2,1)S(1)}, u32[]{:S(2)}, u32[]{:S(2)}) collective-permute-start(bf16[64,7168]{1,0:T(8,128)(2,1)S(1)} %all_to_all.15), channel_id=1, source_target_pairs={{0,16},{16,0},{32,48},{48,32},{64,80},{80,64},{96,112},{112,96},{1... | collective-permute-start | bytes 2752520 | tf_op jit(solution)/shard_map/ppermute | solution.py:31
  48.7 11.7 %collective-permute-start.5 = (bf16[64,3584]{1,0:T(8,128)(2,1)S(1)}, bf16[64,3584]{1,0:T(8,128)(2,1)S(1)}, u32[]{:S(2)}, u32[]{:S(2)}) collective-permute-start(bf16[64,3584]{1,0:T(8,128)(2,1)S(1)} %slice.107), channel_id=1, source_target_pairs={{0,32},{16,48},{32,64},{48,80},{64,96},{80,112},{96,0},{112,16},{1... | collective-permute-start | bytes 1376264 | tf_op jit(solution)/shard_map/ppermute | solution.py:32
  49.1 11.3 %collective-permute-start.6 = (bf16[64,3584]{1,0:T(8,128)(2,1)S(1)}, bf16[64,3584]{1,0:T(8,128)(2,1)S(1)}, u32[]{:S(2)}, u32[]{:S(2)}) collective-permute-start(bf16[64,3584]{1,0:T(8,128)(2,1)S(1)} %slice.108), channel_id=1, source_target_pairs={{0,96},{16,112},{32,0},{48,16},{64,32},{80,48},{96,64},{112,80},{1... | collective-permute-start | bytes 1376264 | tf_op jit(solution)/shard_map/ppermute | solution.py:33
  52.1 8.4 %collective-permute-start.2 = (bf16[64,7168]{1,0:T(8,128)(2,1)S(1)}, bf16[64,7168]{1,0:T(8,128)(2,1)S(1)}, u32[]{:S(2)}, u32[]{:S(2)}) collective-permute-start(bf16[64,7168]{1,0:T(8,128)(2,1)S(1)} %collective-permute-done.1), channel_id=1, source_target_pairs={{0,16},{16,0},{32,48},{48,32},{64,80},{80,64},{96,112},{112,96},{1... | collective-permute-start | bytes 2752520 | tf_op jit(solution)/shard_map/ppermute | solution.py:35
  52.1 8.6 %collective-permute-start.4 = (bf16[64,7168]{1,0:T(8,128)(2,1)S(1)}, bf16[64,7168]{1,0:T(8,128)(2,1)S(1)}, u32[]{:S(2)}, u32[]{:S(2)}) collective-permute-start(bf16[64,7168]{1,0:T(8,128)(2,1)S(1)} %collective-permute-done.3), channel_id=1, source_target_pairs={{0,16},{16,0},{32,48},{48,32},{64,80},{80,64},{96,112},{112,96},{1... | collective-permute-start | bytes 2752520 | tf_op jit(solution)/shard_map/ppermute | solution.py:36
  52.8 8.0 %copy-start.4 = (bf16[1,7168,256]{2,1,0:T(8,128)(2,1)S(1)}, bf16[1,7168,256]{2,1,0:T(8,128)(2,1)}, u32[]{:S(2)}) copy-start(bf16[1,7168,256]{2,1,0:T(8,128)(2,1)} %param.9) | copy-start | bytes 11010052
  60.5 4.0 %collective-permute-start.7 = (bf16[64,7168]{1,0:T(8,128)(2,1)S(1)}, bf16[64,7168]{1,0:T(8,128)(2,1)S(1)}, u32[]{:S(2)}, u32[]{:S(2)}) collective-permute-start(bf16[64,7168]{1,0:T(8,128)(2,1)S(1)} %constant_dynamic-update-slice_fusion.6), channel_id=1, source_target_pairs={{0,16},{16,0},{32,48},{48,32},{64,80},{80,64},{96,112},{112,96},{1... | collective-permute-start | bytes 2752520 | tf_op jit(solution)/shard_map/ppermute | solution.py:37
  60.8 2.0 %copy-start.5 = (bf16[1,7168,256]{2,1,0:T(8,128)(2,1)S(1)}, bf16[1,7168,256]{2,1,0:T(8,128)(2,1)}, u32[]{:S(2)}) copy-start(bf16[1,7168,256]{2,1,0:T(8,128)(2,1)} %param.10) | copy-start | bytes 11010052
  65.1 2.0 %copy-start.2 = (bf16[1,256,7168]{2,1,0:T(8,128)(2,1)S(1)}, bf16[1,256,7168]{2,1,0:T(8,128)(2,1)}, u32[]{:S(2)}) copy-start(bf16[1,256,7168]{2,1,0:T(8,128)(2,1)} %param.11) | copy-start | bytes 11010052
  68.5 6.6 %collective-permute-start.8 = (bf16[192,7168]{1,0:T(8,128)(2,1)S(1)}, bf16[192,7168]{1,0:T(8,128)(2,1)S(1)}, u32[]{:S(2)}, u32[]{:S(2)}) collective-permute-start(bf16[192,7168]{1,0:T(8,128)(2,1)S(1)} %slice.118), channel_id=1, source_target_pairs={{0,16},{16,0},{32,48},{48,32},{64,80},{80,64},{96,112},{112,96},{1... | collective-permute-start | bytes 8257544 | tf_op jit(solution)/shard_map/ppermute | solution.py:47
  69.1 6.0 %collective-permute-start.9 = (bf16[64,7168]{1,0:T(8,128)(2,1)S(1)}, bf16[64,7168]{1,0:T(8,128)(2,1)S(1)}, u32[]{:S(2)}, u32[]{:S(2)}) collective-permute-start(bf16[64,7168]{1,0:T(8,128)(2,1)S(1)} %slice.124), channel_id=1, source_target_pairs={{0,16},{16,0},{32,48},{48,32},{64,80},{80,64},{96,112},{112,96},{1... | collective-permute-start | bytes 2752520 | tf_op jit(solution)/shard_map/ppermute | solution.py:46
  75.9 14.1 %collective-permute-start.10 = (bf16[64,3584]{1,0:T(8,128)(2,1)S(1)}, bf16[64,3584]{1,0:T(8,128)(2,1)S(1)}, u32[]{:S(2)}, u32[]{:S(2)}) collective-permute-start(bf16[64,3584]{1,0:T(8,128)(2,1)S(1)} %get-tuple-element.10), channel_id=1, source_target_pairs={{0,32},{16,48},{32,64},{48,80},{64,96},{80,112},{96,0},{112,16},{1... | collective-permute-start | bytes 1376264 | tf_op jit(solution)/shard_map/ppermute | solution.py:53
  76.3 13.9 %collective-permute-start.12 = (bf16[64,3584]{1,0:T(8,128)(2,1)S(1)}, bf16[64,3584]{1,0:T(8,128)(2,1)S(1)}, u32[]{:S(2)}, u32[]{:S(2)}) collective-permute-start(bf16[64,3584]{1,0:T(8,128)(2,1)S(1)} %get-tuple-element.11), channel_id=1, source_target_pairs={{0,96},{16,112},{32,0},{48,16},{64,32},{80,48},{96,64},{112,80},{1... | collective-permute-start | bytes 1376264 | tf_op jit(solution)/shard_map/ppermute | solution.py:54
  90.1 23.1 %collective-permute-start.11 = (bf16[64,7168]{1,0:T(8,128)(2,1)S(1)}, bf16[64,7168]{1,0:T(8,128)(2,1)S(1)}, u32[]{:S(2)}, u32[]{:S(2)}) collective-permute-start(bf16[64,7168]{1,0:T(8,128)(2,1)S(1)} %pad_maximum_fusion.3), channel_id=1, source_target_pairs={{0,32},{16,48},{32,64},{48,80},{64,96},{80,112},{96,0},{112,16},{1... | collective-permute-start | bytes 2752520 | tf_op jit(solution)/shard_map/ppermute | solution.py:57
  90.4 30.4 %copy-start.3 = (s32[16,288]{1,0:T(8,128)S(1)}, s32[16,288]{1,0:T(8,128)}, u32[]{:S(2)}) copy-start(s32[16,288]{1,0:T(8,128)} %param.8) | copy-start | bytes 55300
  90.4 22.8 %collective-permute-start.13 = (bf16[64,7168]{1,0:T(8,128)(2,1)S(1)}, bf16[64,7168]{1,0:T(8,128)(2,1)S(1)}, u32[]{:S(2)}, u32[]{:S(2)}) collective-permute-start(bf16[64,7168]{1,0:T(8,128)(2,1)S(1)} %pad_maximum_fusion.4), channel_id=1, source_target_pairs={{0,96},{16,112},{32,0},{48,16},{64,32},{80,48},{96,64},{112,80},{1... | collective-permute-start | bytes 2752520 | tf_op jit(solution)/shard_map/ppermute | solution.py:58
  115.0 18.3 %all-to-all-start.1 = ((bf16[16,4,7168]{2,1,0:T(4,128)(2,1)}), bf16[16,4,7168]{2,1,0:T(4,128)(2,1)S(1)}, u32[]{:S(2)}, u32[]{:S(2)}) async-start(bf16[16,4,7168]{2,1,0:T(4,128)(2,1)} %all_to_all.16), calls=%async_computation.1 | async-start | bytes 1835008 | tf_op jit(solution)/shard_map/all_to_all | solution.py:101
  133.5 2.5 %copy-start.1 = (bf16[128,7168]{1,0:T(8,128)(2,1)S(1)}, bf16[128,7168]{1,0:T(8,128)(2,1)}, u32[]{:S(2)}) copy-start(bf16[128,7168]{1,0:T(8,128)(2,1)} %param.6) | copy-start | bytes 5505028

commit v11 on v10

--- a/solution.py
+++ b/solution.py
@@ -91,7 +91,7 @@
     hidden = lax.optimization_barrier(jnp.concatenate(hidden, axis=0))
     hb = [hidden[i * rows:(i + 1) * rows] for i in range(8)]
     result = [None] * 8
-    for group in ((1, 3, 5, 7), (0, 2, 4, 6)):
+    for group in ((7,), (6,), (1, 3, 5), (0, 2, 4)):
         out = jnp.dot(
             jnp.concatenate([hb[i] for i in group], axis=0), w_down[0], preferred_element_type=jnp.float32
         ).astype(jnp.bfloat16)

time: 138 us -> 144 us (1.043)
  local copies, waits for them, and re-layouts: 6.54 us -> 10.1 us
    all_to_all x2, local copies, waits for them, and re-layouts: 1.46 us -> 2.91 us  [shards(): lax.all_to_all(summed, 'expert', split_axis=0, concat_axis=0, tiled=True)]
    all_to_all x1, local copies, waits for them, and re-layouts: 0.21 us -> 1.66 us  [shards(): lax.all_to_all(send_rows, 'expert', split_axis=0, concat_axis=0, tiled=True)]
    dot_general x2 -> x4, matrix products: 2.24 us -> 3.28 us  [shards(): jnp.dot(jnp.concatenate([hb[i] for i in group], axis=0), w_down[0], prefe...]
  transfers between devices with their start and end apart: 15 -> 15, of which waited for: 6 -> 6; matrix products, arithmetic and copies ran while one was open for 4% -> 5% of each run, Pallas kernels for 0% -> 0%
where the time goes in v11:
time: 144 us; the launch traced here: 141 us
  waiting for transfers between devices  73 us (51%)
  blocking collectives  21.7 us (15%)
  starting transfers between devices  20.9 us (15%)
  matrix products  10.4 us (7%)
  local copies, waits for them, and re-layouts  10.1 us (7%)
  other arithmetic  4.91 us (3%)
    all_to_all x1, blocking collectives, shards(): lax.all_to_all(send_rows, 'expert', split_axis=0, concat_axis=0, tiled=True)  21.7 us
    ppermute x1, waiting for transfers between devices, scatter_dp(): a_a = lax.ppermute(s_a, 'dp', dp_pairs(dp_count, 1)).astype(f32)  19.5 us
    ppermute x1, waiting for transfers between devices, gather_dp(): up = lax.ppermute(x, 'dp', dp_pairs(dp_count, 1))  19 us
    all_to_all x1, waiting for transfers between devices, shards(): lax.all_to_all(summed, 'expert', split_axis=0, concat_axis=0, tiled=True)  12.4 us
    ppermute x1, waiting for transfers between devices, scatter_dp(): r_a = lax.ppermute(q_far[:, :half], 'dp', dp_pairs(dp_count, 1)).astype(f32)  10.3 us
    ppermute x1, waiting for transfers between devices, gather_dp(): far_a = lax.ppermute(up[:, :half], 'dp', dp_pairs(dp_count, 1))  7.59 us
    all_to_all x1, starting transfers between devices, shards(): lax.all_to_all(summed, 'expert', split_axis=0, concat_axis=0, tiled=True)  6.11 us
    ppermute x1, waiting for transfers between devices, scatter_dp(): got_far = lax.ppermute(b[7], 'dp', sib_pairs(dp_count))  4.09 us
  transfers between devices with their start and end apart: 15, of which 6 were waited for; matrix products, arithmetic and copies ran while one was open for 5% of the time, Pallas kernels for 0%

profile of v11, /device:TPU:6, one launch (start us, length us, event | category | flops | bytes accessed | tf_op | source)
XLA Modules:
  0.0 141.5 jit_solution(7525752558763656620)
XLA Ops:
  0.0 0.9 multiply_subtract_fusion
  0.9 0.8 fusion.47
  2.5 1.1 gather_fusion
  3.6 1.3 gather.7
  4.9 1.7 %select_select_fusion = bf16[16,4,7168]{2,1,0:T(4,128)(2,1)S(1)} fusion(bf16[16,4,7168]{2,1,0:T(4,128)(2,1)} %gather.7, pred[16,4]{1,0:T(8,128)(4,1)S(1)} %copy.11, pred[16,4]{1,0:T(8,128)(4,1)S(1)} %copy.8), kind=kLoop, calls=%fused_computation.34 | loop fusion | flops 917504 | bytes 1835136 | tf_op jit(solution)/shard_map/jit(_where)/select_n | solution.py:81
  6.6 21.7 %all_to_all.21 = bf16[16,4,7168]{2,1,0:T(4,128)(2,1)} all-to-all(bf16[16,4,7168]{2,1,0:T(4,128)(2,1)S(1)} %select_select_fusion), channel_id=1, replica_groups=mesh['dp'=8,'expert'=16] {'expert'}, dimensions={0} | all-to-all | bytes 1835008 | tf_op jit(solution)/shard_map/all_to_all | solution.py:82
  28.3 1.7 %all_to_all.15 = bf16[64,7168]{1,0:T(8,128)(2,1)S(1)} reshape(bf16[16,4,7168]{2,1,0:T(4,128)(2,1)} %all_to_all.21) | data formatting | bytes 1835008 | tf_op jit(solution)/shard_map/all_to_all | solution.py:82
  30.0 1.6 %collective-permute-start.1 = (bf16[64,7168]{1,0:T(8,128)(2,1)S(1)}, bf16[64,7168]{1,0:T(8,128)(2,1)S(1)}, u32[]{:S(2)}, u32[]{:S(2)}) collective-permute-start(bf16[64,7168]{1,0:T(8,128)(2,1)S(1)} %all_to_all.15), channel_id=1, source_target_pairs={{0,32},{16,48},{32,64},{48,80},{64,96},{80,112},{96,0},{112,16},{1... | collective-permute-start | bytes 2752520 | tf_op jit(solution)/shard_map/ppermute | solution.py:29
  31.6 1.7 %collective-permute-start.3 = (bf16[64,7168]{1,0:T(8,128)(2,1)S(1)}, bf16[64,7168]{1,0:T(8,128)(2,1)S(1)}, u32[]{:S(2)}, u32[]{:S(2)}) collective-permute-start(bf16[64,7168]{1,0:T(8,128)(2,1)S(1)} %all_to_all.15), channel_id=1, source_target_pairs={{0,96},{16,112},{32,0},{48,16},{64,32},{80,48},{96,64},{112,80},{1... | collective-permute-start | bytes 2752520 | tf_op jit(solution)/shard_map/ppermute | solution.py:30
  33.3 19.0 %collective-permute-done.1 = bf16[64,7168]{1,0:T(8,128)(2,1)S(1)} collective-permute-done((bf16[64,7168]{1,0:T(8,128)(2,1)S(1)}, bf16[64,7168]{1,0:T(8,128)(2,1)S(1)}, u32[]{:S(2)}, u32[]{:S(2)}) %collective-permute-start.1) | collective-permute-done | bytes 917536 | tf_op jit(solution)/shard_map/ppermute | solution.py:29
  52.8 3.0 %collective-permute-start.6 = (bf16[64,3584]{1,0:T(8,128)(2,1)S(1)}, bf16[64,3584]{1,0:T(8,128)(2,1)S(1)}, u32[]{:S(2)}, u32[]{:S(2)}) collective-permute-start(bf16[64,3584]{1,0:T(8,128)(2,1)S(1)} %slice.97), channel_id=1, source_target_pairs={{0,96},{16,112},{32,0},{48,16},{64,32},{80,48},{96,64},{112,80},{1... | collective-permute-start | bytes 1376264 | tf_op jit(solution)/shard_map/ppermute | solution.py:33
  56.4 7.6 %collective-permute-done.5 = bf16[64,3584]{1,0:T(8,128)(2,1)S(1)} collective-permute-done((bf16[64,3584]{1,0:T(8,128)(2,1)S(1)}, bf16[64,3584]{1,0:T(8,128)(2,1)S(1)}, u32[]{:S(2)}, u32[]{:S(2)}) %collective-permute-start.5) | collective-permute-done | bytes 458784 | tf_op jit(solution)/shard_map/ppermute | solution.py:32
  64.5 1.6 %fusion.12 = f32[384,256]{1,0:T(8,128)S(1)} fusion(bf16[384,7168]{1,0:T(8,128)(2,1)S(1)} %constant_dynamic-update-slice_fusion, bf16[1,7168,256]{2,1,0:T(8,128)(2,1)S(1)} %copy-done.3), kind=kOutput, calls=%fused_computation.18 | convolution fusion | flops 1409286144 | bytes 9568256 | tf_op jit(solution)/shard_map/dot_general | solution.py:88
  66.5 1.6 %multiply_convert_fusion = bf16[384,256]{1,0:T(8,128)(2,1)S(1)} fusion(f32[384,256]{1,0:T(8,128)S(1)} %fusion.12, bf16[384,7168]{1,0:T(8,128)(2,1)S(1)} %constant_dynamic-update-slice_fusion, bf16[1,7168,256]{2,1,0:T(8,128)(2,1)S(1)} %copy-done.4), kind=kOutput, calls=%fused_computation.36 | convolution fusion | flops 1409875968 | bytes 9764864 | tf_op jit(solution)/shard_map/dot_general | solution.py:89
  68.1 0.6 fusion.10
  68.7 0.6 multiply_convert_fusion.1
  69.5 1.3 copy-done.1
  70.8 0.9 convolution_convert_fusion
  72.2 0.8 convolution_convert_fusion.2
  73.3 0.9 convolution_convert_fusion.1
  74.2 4.1 %collective-permute-done.9 = bf16[64,7168]{1,0:T(8,128)(2,1)S(1)} collective-permute-done((bf16[64,7168]{1,0:T(8,128)(2,1)S(1)}, bf16[64,7168]{1,0:T(8,128)(2,1)S(1)}, u32[]{:S(2)}, u32[]{:S(2)}) %collective-permute-start.9) | collective-permute-done | bytes 917536 | tf_op jit(solution)/shard_map/ppermute | solution.py:46
  78.3 0.8 add_convert_fusion.1
  79.6 2.9 %collective-permute-start.12 = (bf16[64,3584]{1,0:T(8,128)(2,1)S(1)}, bf16[64,3584]{1,0:T(8,128)(2,1)S(1)}, u32[]{:S(2)}, u32[]{:S(2)}) collective-permute-start(bf16[64,3584]{1,0:T(8,128)(2,1)S(1)} %get-tuple-element.10), channel_id=1, source_target_pairs={{0,96},{16,112},{32,0},{48,16},{64,32},{80,48},{96,64},{112,80},{1... | collective-permute-start | bytes 1376264 | tf_op jit(solution)/shard_map/ppermute | solution.py:54
  82.9 10.3 %collective-permute-done.10 = bf16[64,3584]{1,0:T(8,128)(2,1)S(1)} collective-permute-done((bf16[64,3584]{1,0:T(8,128)(2,1)S(1)}, bf16[64,3584]{1,0:T(8,128)(2,1)S(1)}, u32[]{:S(2)}, u32[]{:S(2)}) %collective-permute-start.10) | collective-permute-done | bytes 458784 | tf_op jit(solution)/shard_map/ppermute | solution.py:53
  93.7 3.3 %collective-permute-start.13 = (bf16[64,7168]{1,0:T(8,128)(2,1)S(1)}, bf16[64,7168]{1,0:T(8,128)(2,1)S(1)}, u32[]{:S(2)}, u32[]{:S(2)}) collective-permute-start(bf16[64,7168]{1,0:T(8,128)(2,1)S(1)} %pad_maximum_fusion.4), channel_id=1, source_target_pairs={{0,96},{16,112},{32,0},{48,16},{64,32},{80,48},{96,64},{112,80},{1... | collective-permute-start | bytes 2752520 | tf_op jit(solution)/shard_map/ppermute | solution.py:58
  97.0 19.5 %collective-permute-done.11 = bf16[64,7168]{1,0:T(8,128)(2,1)S(1)} collective-permute-done((bf16[64,7168]{1,0:T(8,128)(2,1)S(1)}, bf16[64,7168]{1,0:T(8,128)(2,1)S(1)}, u32[]{:S(2)}, u32[]{:S(2)}) %collective-permute-start.11) | collective-permute-done | bytes 917536 | tf_op jit(solution)/shard_map/ppermute | solution.py:57
  117.0 1.3 all_to_all.16
  118.2 6.1 %all-to-all-start.1 = ((bf16[16,4,7168]{2,1,0:T(4,128)(2,1)}), bf16[16,4,7168]{2,1,0:T(4,128)(2,1)}, u32[]{:S(2)}, u32[]{:S(2)}) async-start(bf16[16,4,7168]{2,1,0:T(4,128)(2,1)} %all_to_all.16), calls=%async_computation.1 | async-start | bytes 1835008 | tf_op jit(solution)/shard_map/all_to_all | solution.py:101
  124.8 12.4 %all-to-all-done.1 = bf16[16,4,7168]{2,1,0:T(4,128)(2,1)} async-done(((bf16[16,4,7168]{2,1,0:T(4,128)(2,1)}), bf16[16,4,7168]{2,1,0:T(4,128)(2,1)}, u32[]{:S(2)}, u32[]{:S(2)}) %all-to-all-start.1) | async-done | bytes 917536 | tf_op jit(solution)/shard_map/all_to_all | solution.py:101
  137.3 1.7 %all_to_all.18 = bf16[64,7168]{1,0:T(8,128)(2,1)S(1)} reshape(bf16[16,4,7168]{2,1,0:T(4,128)(2,1)} %all-to-all-done.1) | data formatting | bytes 1835008 | tf_op jit(solution)/shard_map/all_to_all | solution.py:101
  138.9 0.6 fusion.29
  139.6 1.9 %fusion = bf16[128,7168]{1,0:T(8,128)(2,1)} fusion(f32[128,7168]{1,0:T(8,128)S(1)} %fusion.29, bf16[64,7168]{1,0:T(8,128)(2,1)S(1)} %all_to_all.18, f32[64]{0:T(128)S(1)} %broadcast_in_dim.43, s32[64]{0:T(128)S(1)} %eq.40, pred[64]{0:T(512)(128)(4,1)S(1)} %gt.25), kind=kOutput, calls=%fused_computation.4 | convolution fusion | flops 119332864 | bytes 6423104 | tf_op jit(solution)/shard_map/dot_general | solution.py:108
  (63 shorter events, 5.9 us)
Async XLA Ops:
  0.0 2.5 %copy-start = (bf16[128,7168]{1,0:T(8,128)(2,1)S(1)}, bf16[128,7168]{1,0:T(8,128)(2,1)}, u32[]{:S(2)}) copy-start(bf16[128,7168]{1,0:T(8,128)(2,1)} %param.6) | copy-start | bytes 5505028
  30.0 22.4 %collective-permute-start.1 = (bf16[64,7168]{1,0:T(8,128)(2,1)S(1)}, bf16[64,7168]{1,0:T(8,128)(2,1)S(1)}, u32[]{:S(2)}, u32[]{:S(2)}) collective-permute-start(bf16[64,7168]{1,0:T(8,128)(2,1)S(1)} %all_to_all.15), channel_id=1, source_target_pairs={{0,32},{16,48},{32,64},{48,80},{64,96},{80,112},{96,0},{112,16},{1... | collective-permute-start | bytes 2752520 | tf_op jit(solution)/shard_map/ppermute | solution.py:29
  31.6 21.1 %collective-permute-start.3 = (bf16[64,7168]{1,0:T(8,128)(2,1)S(1)}, bf16[64,7168]{1,0:T(8,128)(2,1)S(1)}, u32[]{:S(2)}, u32[]{:S(2)}) collective-permute-start(bf16[64,7168]{1,0:T(8,128)(2,1)S(1)} %all_to_all.15), channel_id=1, source_target_pairs={{0,96},{16,112},{32,0},{48,16},{64,32},{80,48},{96,64},{112,80},{1... | collective-permute-start | bytes 2752520 | tf_op jit(solution)/shard_map/ppermute | solution.py:30
  33.3 23.0 %collective-permute-start = (bf16[64,7168]{1,0:T(8,128)(2,1)S(1)}, bf16[64,7168]{1,0:T(8,128)(2,1)S(1)}, u32[]{:S(2)}, u32[]{:S(2)}) collective-permute-start(bf16[64,7168]{1,0:T(8,128)(2,1)S(1)} %all_to_all.15), channel_id=1, source_target_pairs={{0,16},{16,0},{32,48},{48,32},{64,80},{80,64},{96,112},{112,96},{1... | collective-permute-start | bytes 2752520 | tf_op jit(solution)/shard_map/ppermute | solution.py:31
  52.4 11.7 %collective-permute-start.5 = (bf16[64,3584]{1,0:T(8,128)(2,1)S(1)}, bf16[64,3584]{1,0:T(8,128)(2,1)S(1)}, u32[]{:S(2)}, u32[]{:S(2)}) collective-permute-start(bf16[64,3584]{1,0:T(8,128)(2,1)S(1)} %slice.96), channel_id=1, source_target_pairs={{0,32},{16,48},{32,64},{48,80},{64,96},{80,112},{96,0},{112,16},{1... | collective-permute-start | bytes 1376264 | tf_op jit(solution)/shard_map/ppermute | solution.py:32
  52.8 11.3 %collective-permute-start.6 = (bf16[64,3584]{1,0:T(8,128)(2,1)S(1)}, bf16[64,3584]{1,0:T(8,128)(2,1)S(1)}, u32[]{:S(2)}, u32[]{:S(2)}) collective-permute-start(bf16[64,3584]{1,0:T(8,128)(2,1)S(1)} %slice.97), channel_id=1, source_target_pairs={{0,96},{16,112},{32,0},{48,16},{64,32},{80,48},{96,64},{112,80},{1... | collective-permute-start | bytes 1376264 | tf_op jit(solution)/shard_map/ppermute | solution.py:33
  55.8 8.4 %collective-permute-start.2 = (bf16[64,7168]{1,0:T(8,128)(2,1)S(1)}, bf16[64,7168]{1,0:T(8,128)(2,1)S(1)}, u32[]{:S(2)}, u32[]{:S(2)}) collective-permute-start(bf16[64,7168]{1,0:T(8,128)(2,1)S(1)} %collective-permute-done.1), channel_id=1, source_target_pairs={{0,16},{16,0},{32,48},{48,32},{64,80},{80,64},{96,112},{112,96},{1... | collective-permute-start | bytes 2752520 | tf_op jit(solution)/shard_map/ppermute | solution.py:35
  55.8 8.6 %collective-permute-start.4 = (bf16[64,7168]{1,0:T(8,128)(2,1)S(1)}, bf16[64,7168]{1,0:T(8,128)(2,1)S(1)}, u32[]{:S(2)}, u32[]{:S(2)}) collective-permute-start(bf16[64,7168]{1,0:T(8,128)(2,1)S(1)} %collective-permute-done.3), channel_id=1, source_target_pairs={{0,16},{16,0},{32,48},{48,32},{64,80},{80,64},{96,112},{112,96},{1... | collective-permute-start | bytes 2752520 | tf_op jit(solution)/shard_map/ppermute | solution.py:36
  56.4 8.0 %copy-start.3 = (bf16[1,7168,256]{2,1,0:T(8,128)(2,1)S(1)}, bf16[1,7168,256]{2,1,0:T(8,128)(2,1)}, u32[]{:S(2)}) copy-start(bf16[1,7168,256]{2,1,0:T(8,128)(2,1)} %param.9) | copy-start | bytes 11010052
  64.1 4.0 %collective-permute-start.7 = (bf16[64,7168]{1,0:T(8,128)(2,1)S(1)}, bf16[64,7168]{1,0:T(8,128)(2,1)S(1)}, u32[]{:S(2)}, u32[]{:S(2)}) collective-permute-start(bf16[64,7168]{1,0:T(8,128)(2,1)S(1)} %constant_dynamic-update-slice_fusion.6), channel_id=1, source_target_pairs={{0,16},{16,0},{32,48},{48,32},{64,80},{80,64},{96,112},{112,96},{1... | collective-permute-start | bytes 2752520 | tf_op jit(solution)/shard_map/ppermute | solution.py:37
  64.4 2.0 %copy-start.4 = (bf16[1,7168,256]{2,1,0:T(8,128)(2,1)S(1)}, bf16[1,7168,256]{2,1,0:T(8,128)(2,1)}, u32[]{:S(2)}) copy-start(bf16[1,7168,256]{2,1,0:T(8,128)(2,1)} %param.10) | copy-start | bytes 11010052
  68.7 2.0 %copy-start.1 = (bf16[1,256,7168]{2,1,0:T(8,128)(2,1)S(1)}, bf16[1,256,7168]{2,1,0:T(8,128)(2,1)}, u32[]{:S(2)}) copy-start(bf16[1,256,7168]{2,1,0:T(8,128)(2,1)} %param.11) | copy-start | bytes 11010052
  71.7 10.7 %collective-permute-start.8 = (bf16[192,7168]{1,0:T(8,128)(2,1)S(1)}, bf16[192,7168]{1,0:T(8,128)(2,1)S(1)}, u32[]{:S(2)}, u32[]{:S(2)}) collective-permute-start(bf16[192,7168]{1,0:T(8,128)(2,1)S(1)} %convolution_convert_fusion), channel_id=1, source_target_pairs={{0,16},{16,0},{32,48},{48,32},{64,80},{80,64},{96,112},{112,96},{1... | collective-permute-start | bytes 8257544 | tf_op jit(solution)/shard_map/ppermute | solution.py:47
  73.0 5.3 %collective-permute-start.9 = (bf16[64,7168]{1,0:T(8,128)(2,1)S(1)}, bf16[64,7168]{1,0:T(8,128)(2,1)S(1)}, u32[]{:S(2)}, u32[]{:S(2)}) collective-permute-start(bf16[64,7168]{1,0:T(8,128)(2,1)S(1)} %convolution_convert_fusion.2), channel_id=1, source_target_pairs={{0,16},{16,0},{32,48},{48,32},{64,80},{80,64},{96,112},{112,96},{1... | collective-permute-start | bytes 2752520 | tf_op jit(solution)/shard_map/ppermute | solution.py:46
  79.1 14.1 %collective-permute-start.10 = (bf16[64,3584]{1,0:T(8,128)(2,1)S(1)}, bf16[64,3584]{1,0:T(8,128)(2,1)S(1)}, u32[]{:S(2)}, u32[]{:S(2)}) collective-permute-start(bf16[64,3584]{1,0:T(8,128)(2,1)S(1)} %get-tuple-element.9), channel_id=1, source_target_pairs={{0,32},{16,48},{32,64},{48,80},{64,96},{80,112},{96,0},{112,16},{1... | collective-permute-start | bytes 1376264 | tf_op jit(solution)/shard_map/ppermute | solution.py:53
  79.6 14.0 %collective-permute-start.12 = (bf16[64,3584]{1,0:T(8,128)(2,1)S(1)}, bf16[64,3584]{1,0:T(8,128)(2,1)S(1)}, u32[]{:S(2)}, u32[]{:S(2)}) collective-permute-start(bf16[64,3584]{1,0:T(8,128)(2,1)S(1)} %get-tuple-element.10), channel_id=1, source_target_pairs={{0,96},{16,112},{32,0},{48,16},{64,32},{80,48},{96,64},{112,80},{1... | collective-permute-start | bytes 1376264 | tf_op jit(solution)/shard_map/ppermute | solution.py:54
  93.4 23.1 %collective-permute-start.11 = (bf16[64,7168]{1,0:T(8,128)(2,1)S(1)}, bf16[64,7168]{1,0:T(8,128)(2,1)S(1)}, u32[]{:S(2)}, u32[]{:S(2)}) collective-permute-start(bf16[64,7168]{1,0:T(8,128)(2,1)S(1)} %pad_maximum_fusion.3), channel_id=1, source_target_pairs={{0,32},{16,48},{32,64},{48,80},{64,96},{80,112},{96,0},{112,16},{1... | collective-permute-start | bytes 2752520 | tf_op jit(solution)/shard_map/ppermute | solution.py:57
  93.7 30.8 %copy-start.2 = (s32[16,288]{1,0:T(8,128)S(1)}, s32[16,288]{1,0:T(8,128)}, u32[]{:S(2)}) copy-start(s32[16,288]{1,0:T(8,128)} %param.8) | copy-start | bytes 55300
  93.7 22.8 %collective-permute-start.13 = (bf16[64,7168]{1,0:T(8,128)(2,1)S(1)}, bf16[64,7168]{1,0:T(8,128)(2,1)S(1)}, u32[]{:S(2)}, u32[]{:S(2)}) collective-permute-start(bf16[64,7168]{1,0:T(8,128)(2,1)S(1)} %pad_maximum_fusion.4), channel_id=1, source_target_pairs={{0,96},{16,112},{32,0},{48,16},{64,32},{80,48},{96,64},{112,80},{1... | collective-permute-start | bytes 2752520 | tf_op jit(solution)/shard_map/ppermute | solution.py:58
  118.2 19.1 %all-to-all-start.1 = ((bf16[16,4,7168]{2,1,0:T(4,128)(2,1)}), bf16[16,4,7168]{2,1,0:T(4,128)(2,1)}, u32[]{:S(2)}, u32[]{:S(2)}) async-start(bf16[16,4,7168]{2,1,0:T(4,128)(2,1)} %all_to_all.16), calls=%async_computation.1 | async-start | bytes 1835008 | tf_op jit(solution)/shard_map/all_to_all | solution.py:101

commit v12 on v10

--- a/solution.py
+++ b/solution.py
@@ -98,6 +98,7 @@
         for n, i in enumerate(group):
             result[i] = out[n * rows:(n + 1) * rows]
     summed = scatter_dp(result, dp_count)
+    summed = summed.reshape(ex_count, slot_count, model_width)
     returned = lax.all_to_all(summed, "expert", split_axis=0, concat_axis=0, tiled=True)
     placed = (jnp.arange(tok_count, dtype=jnp.int32)[:, None] == source_idx.reshape(1, -1)) & (
         present.reshape(1, -1) > 0
@@ -105,8 +106,11 @@
     mixing = jnp.where(placed, weights.reshape(1, -1), 0.0)
     mix_hi = mixing.astype(jnp.bfloat16)
     mix_lo = (mixing - mix_hi.astype(jnp.float32)).astype(jnp.bfloat16)
-    mixed = jnp.dot(mix_hi, returned, preferred_element_type=jnp.float32) + jnp.dot(
-        mix_lo, returned, preferred_element_type=jnp.float32
+    dims = (((1, 2), (0, 1)), ((), ()))
+    mix_hi = mix_hi.reshape(tok_count, ex_count, slot_count)
+    mix_lo = mix_lo.reshape(tok_count, ex_count, slot_count)
+    mixed = lax.dot_general(mix_hi, returned, dims, preferred_element_type=jnp.float32) + lax.dot_general(
+        mix_lo, returned, dims, preferred_element_type=jnp.float32
     )
     return mixed.astype(jnp.bfloat16)
 

time: 138 us -> 138 us (level)
    all_to_all x2 -> x0, local copies, waits for them, and re-layouts: 1.46 us -> none  [shards(): lax.all_to_all(summed, 'expert', split_axis=0, concat_axis=0, tiled=True)]
where the time goes in v12:
time: 138 us; the launch traced here: 136 us
  waiting for transfers between devices  73.9 us (54%)
  blocking collectives  21.6 us (16%)
  starting transfers between devices  20.5 us (15%)
  matrix products  9.6 us (7%)
  local copies, waits for them, and re-layouts  5.98 us (4%)
  other arithmetic  4.04 us (3%)
    all_to_all x1, blocking collectives, shards(): lax.all_to_all(send_rows, 'expert', split_axis=0, concat_axis=0, tiled=True)  21.6 us
    ppermute x1, waiting for transfers between devices, scatter_dp(): a_a = lax.ppermute(s_a, 'dp', dp_pairs(dp_count, 1)).astype(f32)  19.5 us
    ppermute x1, waiting for transfers between devices, gather_dp(): up = lax.ppermute(x, 'dp', dp_pairs(dp_count, 1))  19 us
    all_to_all x1, waiting for transfers between devices, shards(): lax.all_to_all(summed, 'expert', split_axis=0, concat_axis=0, tiled=True)  12.6 us
    ppermute x1, waiting for transfers between devices, scatter_dp(): r_a = lax.ppermute(q_far[:, :half], 'dp', dp_pairs(dp_count, 1)).astype(f32)  10.7 us
    ppermute x1, waiting for transfers between devices, gather_dp(): far_a = lax.ppermute(up[:, :half], 'dp', dp_pairs(dp_count, 1))  7.59 us
    all_to_all x1, starting transfers between devices, shards(): lax.all_to_all(summed, 'expert', split_axis=0, concat_axis=0, tiled=True)  5.61 us
    ppermute x1, waiting for transfers between devices, scatter_dp(): got_far = lax.ppermute(b[7], 'dp', sib_pairs(dp_count))  4.56 us
  transfers between devices with their start and end apart: 15, of which 6 were waited for; matrix products, arithmetic and copies ran while one was open for 4% of the time, Pallas kernels for 0%

profile of v12, /device:TPU:6, one launch (start us, length us, event | category | flops | bytes accessed | tf_op | source)
XLA Modules:
  0.0 136.0 jit_solution(4424601999857856154)
XLA Ops:
  0.0 0.9 multiply_subtract_fusion
  0.9 0.8 fusion.44
  2.5 1.1 gather_fusion
  3.9 0.5 select_select_fusion
  4.5 21.6 %all_to_all.14 = bf16[16,4,7168]{2,1,0:T(4,128)(2,1)S(1)} all-to-all(bf16[16,4,7168]{2,1,0:T(4,128)(2,1)S(1)} %select_select_fusion), channel_id=1, replica_groups=mesh['dp'=8,'expert'=16] {'expert'}, dimensions={0} | all-to-all | bytes 1835008 | tf_op jit(solution)/shard_map/all_to_all | solution.py:82
  26.3 1.6 %collective-permute-start.1 = (bf16[64,7168]{1,0:T(8,128)(2,1)S(1)}, bf16[64,7168]{1,0:T(8,128)(2,1)S(1)}, u32[]{:S(2)}, u32[]{:S(2)}) collective-permute-start(bf16[64,7168]{1,0:T(8,128)(2,1)S(1)} %all_to_all.10), channel_id=1, source_target_pairs={{0,32},{16,48},{32,64},{48,80},{64,96},{80,112},{96,0},{112,16},{1... | collective-permute-start | bytes 2752520 | tf_op jit(solution)/shard_map/ppermute | solution.py:29
  28.0 1.7 %collective-permute-start.3 = (bf16[64,7168]{1,0:T(8,128)(2,1)S(1)}, bf16[64,7168]{1,0:T(8,128)(2,1)S(1)}, u32[]{:S(2)}, u32[]{:S(2)}) collective-permute-start(bf16[64,7168]{1,0:T(8,128)(2,1)S(1)} %all_to_all.10), channel_id=1, source_target_pairs={{0,96},{16,112},{32,0},{48,16},{64,32},{80,48},{96,64},{112,80},{1... | collective-permute-start | bytes 2752520 | tf_op jit(solution)/shard_map/ppermute | solution.py:30
  29.7 19.0 %collective-permute-done.1 = bf16[64,7168]{1,0:T(8,128)(2,1)S(1)} collective-permute-done((bf16[64,7168]{1,0:T(8,128)(2,1)S(1)}, bf16[64,7168]{1,0:T(8,128)(2,1)S(1)}, u32[]{:S(2)}, u32[]{:S(2)}) %collective-permute-start.1) | collective-permute-done | bytes 917536 | tf_op jit(solution)/shard_map/ppermute | solution.py:29
  49.1 3.0 %collective-permute-start.6 = (bf16[64,3584]{1,0:T(8,128)(2,1)S(1)}, bf16[64,3584]{1,0:T(8,128)(2,1)S(1)}, u32[]{:S(2)}, u32[]{:S(2)}) collective-permute-start(bf16[64,3584]{1,0:T(8,128)(2,1)S(1)} %slice.108), channel_id=1, source_target_pairs={{0,96},{16,112},{32,0},{48,16},{64,32},{80,48},{96,64},{112,80},{1... | collective-permute-start | bytes 1376264 | tf_op jit(solution)/shard_map/ppermute | solution.py:33
  52.1 0.5 collective-permute-start.4
  52.8 7.6 %collective-permute-done.5 = bf16[64,3584]{1,0:T(8,128)(2,1)S(1)} collective-permute-done((bf16[64,3584]{1,0:T(8,128)(2,1)S(1)}, bf16[64,3584]{1,0:T(8,128)(2,1)S(1)}, u32[]{:S(2)}, u32[]{:S(2)}) %collective-permute-start.5) | collective-permute-done | bytes 458784 | tf_op jit(solution)/shard_map/ppermute | solution.py:32
  60.8 1.6 %fusion.10 = f32[384,256]{1,0:T(8,128)S(1)} fusion(bf16[384,7168]{1,0:T(8,128)(2,1)S(1)} %constant_dynamic-update-slice_fusion, bf16[1,7168,256]{2,1,0:T(8,128)(2,1)S(1)} %copy-done.4), kind=kOutput, calls=%fused_computation.15 | convolution fusion | flops 1409286144 | bytes 9568256 | tf_op jit(solution)/shard_map/dot_general | solution.py:88
  62.8 1.6 %multiply_convert_fusion = bf16[384,256]{1,0:T(8,128)(2,1)S(1)} fusion(f32[384,256]{1,0:T(8,128)S(1)} %fusion.10, bf16[384,7168]{1,0:T(8,128)(2,1)S(1)} %constant_dynamic-update-slice_fusion, bf16[1,7168,256]{2,1,0:T(8,128)(2,1)S(1)} %copy-done.5), kind=kOutput, calls=%fused_computation.35 | convolution fusion | flops 1409875968 | bytes 9764864 | tf_op jit(solution)/shard_map/dot_general | solution.py:89
  64.4 0.6 fusion.8
  65.1 0.6 multiply_convert_fusion.1
  65.8 1.3 copy-done.2
  67.1 1.1 convolution_convert_fusion
  68.4 0.6 collective-permute-start.8
  69.4 1.1 convolution_convert_fusion.1
  70.5 4.6 %collective-permute-done.9 = bf16[64,7168]{1,0:T(8,128)(2,1)S(1)} collective-permute-done((bf16[64,7168]{1,0:T(8,128)(2,1)S(1)}, bf16[64,7168]{1,0:T(8,128)(2,1)S(1)}, u32[]{:S(2)}, u32[]{:S(2)}) %collective-permute-start.9) | collective-permute-done | bytes 917536 | tf_op jit(solution)/shard_map/ppermute | solution.py:46
  75.0 0.7 convert_add_fusion.1
  75.8 0.5 collective-permute-start.10
  76.3 2.9 %collective-permute-start.12 = (bf16[64,3584]{1,0:T(8,128)(2,1)S(1)}, bf16[64,3584]{1,0:T(8,128)(2,1)S(1)}, u32[]{:S(2)}, u32[]{:S(2)}) collective-permute-start(bf16[64,3584]{1,0:T(8,128)(2,1)S(1)} %get-tuple-element.11), channel_id=1, source_target_pairs={{0,96},{16,112},{32,0},{48,16},{64,32},{80,48},{96,64},{112,80},{1... | collective-permute-start | bytes 1376264 | tf_op jit(solution)/shard_map/ppermute | solution.py:54
  79.3 10.7 %collective-permute-done.10 = bf16[64,3584]{1,0:T(8,128)(2,1)S(1)} collective-permute-done((bf16[64,3584]{1,0:T(8,128)(2,1)S(1)}, bf16[64,3584]{1,0:T(8,128)(2,1)S(1)}, u32[]{:S(2)}, u32[]{:S(2)}) %collective-permute-start.10) | collective-permute-done | bytes 458784 | tf_op jit(solution)/shard_map/ppermute | solution.py:53
  90.4 3.3 %collective-permute-start.13 = (bf16[64,7168]{1,0:T(8,128)(2,1)S(1)}, bf16[64,7168]{1,0:T(8,128)(2,1)S(1)}, u32[]{:S(2)}, u32[]{:S(2)}) collective-permute-start(bf16[64,7168]{1,0:T(8,128)(2,1)S(1)} %pad_maximum_fusion.4), channel_id=1, source_target_pairs={{0,96},{16,112},{32,0},{48,16},{64,32},{80,48},{96,64},{112,80},{1... | collective-permute-start | bytes 2752520 | tf_op jit(solution)/shard_map/ppermute | solution.py:58
  93.7 19.5 %collective-permute-done.11 = bf16[64,7168]{1,0:T(8,128)(2,1)S(1)} collective-permute-done((bf16[64,7168]{1,0:T(8,128)(2,1)S(1)}, bf16[64,7168]{1,0:T(8,128)(2,1)S(1)}, u32[]{:S(2)}, u32[]{:S(2)}) %collective-permute-start.11) | collective-permute-done | bytes 917536 | tf_op jit(solution)/shard_map/ppermute | solution.py:57
  113.2 0.5 add_convert_fusion
  113.7 1.3 reshape.113
  115.0 5.6 %all-to-all-start.1 = ((bf16[16,4,7168]{2,1,0:T(4,128)(2,1)}), bf16[16,4,7168]{2,1,0:T(4,128)(2,1)S(1)}, u32[]{:S(2)}, u32[]{:S(2)}) async-start(bf16[16,4,7168]{2,1,0:T(4,128)(2,1)} %reshape.113), calls=%async_computation.1 | async-start | bytes 1835008 | tf_op jit(solution)/shard_map/all_to_all | solution.py:102
  120.7 12.6 %all-to-all-done.1 = bf16[16,4,7168]{2,1,0:T(4,128)(2,1)S(1)} async-done(((bf16[16,4,7168]{2,1,0:T(4,128)(2,1)}), bf16[16,4,7168]{2,1,0:T(4,128)(2,1)S(1)}, u32[]{:S(2)}, u32[]{:S(2)}) %all-to-all-start.1) | async-done | bytes 917536 | tf_op jit(solution)/shard_map/all_to_all | solution.py:102
  133.3 0.8 convolution_bitcast_fusion
  134.0 2.0 %fusion.1 = bf16[128,7168]{1,0:T(8,128)(2,1)} fusion(f32[128,7168]{1,0:T(8,128)S(1)} %convolution_bitcast_fusion, bf16[16,4,7168]{2,1,0:T(4,128)(2,1)S(1)} %all-to-all-done.1, f32[16,4]{0,1:T(4,128)S(1)} %select_reduce_fusion, s32[16,4]{0,1:T(4,128)S(1)} %get-tuple-element.6, pred[16,4]{0,1:T(4,128)(4,1)S(1)} %get-tuple-element.21), kind=kOutput, calls=%fused_computation.6 | convolution fusion | flops 119300096 | bytes 6423104 | tf_op jit(solution)/shard_map/dot_general | solution.py:112
  (60 shorter events, 4.0 us)
Async XLA Ops:
  0.0 2.5 %copy-start = (bf16[128,7168]{1,0:T(8,128)(2,1)S(1)}, bf16[128,7168]{1,0:T(8,128)(2,1)}, u32[]{:S(2)}) copy-start(bf16[128,7168]{1,0:T(8,128)(2,1)} %param.6) | copy-start | bytes 5505028
  26.3 22.4 %collective-permute-start.1 = (bf16[64,7168]{1,0:T(8,128)(2,1)S(1)}, bf16[64,7168]{1,0:T(8,128)(2,1)S(1)}, u32[]{:S(2)}, u32[]{:S(2)}) collective-permute-start(bf16[64,7168]{1,0:T(8,128)(2,1)S(1)} %all_to_all.10), channel_id=1, source_target_pairs={{0,32},{16,48},{32,64},{48,80},{64,96},{80,112},{96,0},{112,16},{1... | collective-permute-start | bytes 2752520 | tf_op jit(solution)/shard_map/ppermute | solution.py:29
  28.0 21.1 %collective-permute-start.3 = (bf16[64,7168]{1,0:T(8,128)(2,1)S(1)}, bf16[64,7168]{1,0:T(8,128)(2,1)S(1)}, u32[]{:S(2)}, u32[]{:S(2)}) collective-permute-start(bf16[64,7168]{1,0:T(8,128)(2,1)S(1)} %all_to_all.10), channel_id=1, source_target_pairs={{0,96},{16,112},{32,0},{48,16},{64,32},{80,48},{96,64},{112,80},{1... | collective-permute-start | bytes 2752520 | tf_op jit(solution)/shard_map/ppermute | solution.py:30
  29.6 23.0 %collective-permute-start = (bf16[64,7168]{1,0:T(8,128)(2,1)S(1)}, bf16[64,7168]{1,0:T(8,128)(2,1)S(1)}, u32[]{:S(2)}, u32[]{:S(2)}) collective-permute-start(bf16[64,7168]{1,0:T(8,128)(2,1)S(1)} %all_to_all.10), channel_id=1, source_target_pairs={{0,16},{16,0},{32,48},{48,32},{64,80},{80,64},{96,112},{112,96},{1... | collective-permute-start | bytes 2752520 | tf_op jit(solution)/shard_map/ppermute | solution.py:31
  48.7 11.7 %collective-permute-start.5 = (bf16[64,3584]{1,0:T(8,128)(2,1)S(1)}, bf16[64,3584]{1,0:T(8,128)(2,1)S(1)}, u32[]{:S(2)}, u32[]{:S(2)}) collective-permute-start(bf16[64,3584]{1,0:T(8,128)(2,1)S(1)} %slice.107), channel_id=1, source_target_pairs={{0,32},{16,48},{32,64},{48,80},{64,96},{80,112},{96,0},{112,16},{1... | collective-permute-start | bytes 1376264 | tf_op jit(solution)/shard_map/ppermute | solution.py:32
  49.1 11.3 %collective-permute-start.6 = (bf16[64,3584]{1,0:T(8,128)(2,1)S(1)}, bf16[64,3584]{1,0:T(8,128)(2,1)S(1)}, u32[]{:S(2)}, u32[]{:S(2)}) collective-permute-start(bf16[64,3584]{1,0:T(8,128)(2,1)S(1)} %slice.108), channel_id=1, source_target_pairs={{0,96},{16,112},{32,0},{48,16},{64,32},{80,48},{96,64},{112,80},{1... | collective-permute-start | bytes 1376264 | tf_op jit(solution)/shard_map/ppermute | solution.py:33
  52.1 8.4 %collective-permute-start.2 = (bf16[64,7168]{1,0:T(8,128)(2,1)S(1)}, bf16[64,7168]{1,0:T(8,128)(2,1)S(1)}, u32[]{:S(2)}, u32[]{:S(2)}) collective-permute-start(bf16[64,7168]{1,0:T(8,128)(2,1)S(1)} %collective-permute-done.1), channel_id=1, source_target_pairs={{0,16},{16,0},{32,48},{48,32},{64,80},{80,64},{96,112},{112,96},{1... | collective-permute-start | bytes 2752520 | tf_op jit(solution)/shard_map/ppermute | solution.py:35
  52.1 8.6 %collective-permute-start.4 = (bf16[64,7168]{1,0:T(8,128)(2,1)S(1)}, bf16[64,7168]{1,0:T(8,128)(2,1)S(1)}, u32[]{:S(2)}, u32[]{:S(2)}) collective-permute-start(bf16[64,7168]{1,0:T(8,128)(2,1)S(1)} %collective-permute-done.3), channel_id=1, source_target_pairs={{0,16},{16,0},{32,48},{48,32},{64,80},{80,64},{96,112},{112,96},{1... | collective-permute-start | bytes 2752520 | tf_op jit(solution)/shard_map/ppermute | solution.py:36
  52.8 8.0 %copy-start.4 = (bf16[1,7168,256]{2,1,0:T(8,128)(2,1)S(1)}, bf16[1,7168,256]{2,1,0:T(8,128)(2,1)}, u32[]{:S(2)}) copy-start(bf16[1,7168,256]{2,1,0:T(8,128)(2,1)} %param.9) | copy-start | bytes 11010052
  60.4 4.0 %collective-permute-start.7 = (bf16[64,7168]{1,0:T(8,128)(2,1)S(1)}, bf16[64,7168]{1,0:T(8,128)(2,1)S(1)}, u32[]{:S(2)}, u32[]{:S(2)}) collective-permute-start(bf16[64,7168]{1,0:T(8,128)(2,1)S(1)} %constant_dynamic-update-slice_fusion.6), channel_id=1, source_target_pairs={{0,16},{16,0},{32,48},{48,32},{64,80},{80,64},{96,112},{112,96},{1... | collective-permute-start | bytes 2752520 | tf_op jit(solution)/shard_map/ppermute | solution.py:37
  60.8 2.0 %copy-start.5 = (bf16[1,7168,256]{2,1,0:T(8,128)(2,1)S(1)}, bf16[1,7168,256]{2,1,0:T(8,128)(2,1)}, u32[]{:S(2)}) copy-start(bf16[1,7168,256]{2,1,0:T(8,128)(2,1)} %param.10) | copy-start | bytes 11010052
  65.1 2.0 %copy-start.2 = (bf16[1,256,7168]{2,1,0:T(8,128)(2,1)S(1)}, bf16[1,256,7168]{2,1,0:T(8,128)(2,1)}, u32[]{:S(2)}) copy-start(bf16[1,256,7168]{2,1,0:T(8,128)(2,1)} %param.11) | copy-start | bytes 11010052
  68.4 6.6 %collective-permute-start.8 = (bf16[192,7168]{1,0:T(8,128)(2,1)S(1)}, bf16[192,7168]{1,0:T(8,128)(2,1)S(1)}, u32[]{:S(2)}, u32[]{:S(2)}) collective-permute-start(bf16[192,7168]{1,0:T(8,128)(2,1)S(1)} %slice.118), channel_id=1, source_target_pairs={{0,16},{16,0},{32,48},{48,32},{64,80},{80,64},{96,112},{112,96},{1... | collective-permute-start | bytes 8257544 | tf_op jit(solution)/shard_map/ppermute | solution.py:47
  69.1 6.0 %collective-permute-start.9 = (bf16[64,7168]{1,0:T(8,128)(2,1)S(1)}, bf16[64,7168]{1,0:T(8,128)(2,1)S(1)}, u32[]{:S(2)}, u32[]{:S(2)}) collective-permute-start(bf16[64,7168]{1,0:T(8,128)(2,1)S(1)} %slice.124), channel_id=1, source_target_pairs={{0,16},{16,0},{32,48},{48,32},{64,80},{80,64},{96,112},{112,96},{1... | collective-permute-start | bytes 2752520 | tf_op jit(solution)/shard_map/ppermute | solution.py:46
  75.8 14.1 %collective-permute-start.10 = (bf16[64,3584]{1,0:T(8,128)(2,1)S(1)}, bf16[64,3584]{1,0:T(8,128)(2,1)S(1)}, u32[]{:S(2)}, u32[]{:S(2)}) collective-permute-start(bf16[64,3584]{1,0:T(8,128)(2,1)S(1)} %get-tuple-element.10), channel_id=1, source_target_pairs={{0,32},{16,48},{32,64},{48,80},{64,96},{80,112},{96,0},{112,16},{1... | collective-permute-start | bytes 1376264 | tf_op jit(solution)/shard_map/ppermute | solution.py:53
  76.3 13.9 %collective-permute-start.12 = (bf16[64,3584]{1,0:T(8,128)(2,1)S(1)}, bf16[64,3584]{1,0:T(8,128)(2,1)S(1)}, u32[]{:S(2)}, u32[]{:S(2)}) collective-permute-start(bf16[64,3584]{1,0:T(8,128)(2,1)S(1)} %get-tuple-element.11), channel_id=1, source_target_pairs={{0,96},{16,112},{32,0},{48,16},{64,32},{80,48},{96,64},{112,80},{1... | collective-permute-start | bytes 1376264 | tf_op jit(solution)/shard_map/ppermute | solution.py:54
  90.1 23.1 %collective-permute-start.11 = (bf16[64,7168]{1,0:T(8,128)(2,1)S(1)}, bf16[64,7168]{1,0:T(8,128)(2,1)S(1)}, u32[]{:S(2)}, u32[]{:S(2)}) collective-permute-start(bf16[64,7168]{1,0:T(8,128)(2,1)S(1)} %pad_maximum_fusion.3), channel_id=1, source_target_pairs={{0,32},{16,48},{32,64},{48,80},{64,96},{80,112},{96,0},{112,16},{1... | collective-permute-start | bytes 2752520 | tf_op jit(solution)/shard_map/ppermute | solution.py:57
  90.4 30.2 %copy-start.3 = (s32[16,288]{1,0:T(8,128)S(1)}, s32[16,288]{1,0:T(8,128)}, u32[]{:S(2)}) copy-start(s32[16,288]{1,0:T(8,128)} %param.8) | copy-start | bytes 55300
  90.4 22.8 %collective-permute-start.13 = (bf16[64,7168]{1,0:T(8,128)(2,1)S(1)}, bf16[64,7168]{1,0:T(8,128)(2,1)S(1)}, u32[]{:S(2)}, u32[]{:S(2)}) collective-permute-start(bf16[64,7168]{1,0:T(8,128)(2,1)S(1)} %pad_maximum_fusion.4), channel_id=1, source_target_pairs={{0,96},{16,112},{32,0},{48,16},{64,32},{80,48},{96,64},{112,80},{1... | collective-permute-start | bytes 2752520 | tf_op jit(solution)/shard_map/ppermute | solution.py:58
  115.0 18.3 %all-to-all-start.1 = ((bf16[16,4,7168]{2,1,0:T(4,128)(2,1)}), bf16[16,4,7168]{2,1,0:T(4,128)(2,1)S(1)}, u32[]{:S(2)}, u32[]{:S(2)}) async-start(bf16[16,4,7168]{2,1,0:T(4,128)(2,1)} %reshape.113), calls=%async_computation.1 | async-start | bytes 1835008 | tf_op jit(solution)/shard_map/all_to_all | solution.py:102
  133.3 2.8 %copy-start.1 = (bf16[128,7168]{1,0:T(8,128)(2,1)S(1)}, bf16[128,7168]{1,0:T(8,128)(2,1)}, u32[]{:S(2)}) copy-start(bf16[128,7168]{1,0:T(8,128)(2,1)} %param.6) | copy-start | bytes 5505028

commit v13 on v12

--- a/solution.py
+++ b/solution.py
@@ -45,11 +45,12 @@
     b = p
     got_far = lax.ppermute(b[7], "dp", sib_pairs(dp_count))
     got = lax.ppermute(jnp.concatenate([b[1], b[3], b[5]], axis=0), "dp", sib_pairs(dp_count))
-    g = [got[i * rows:(i + 1) * rows].astype(f32) for i in range(3)] + [got_far.astype(f32)]
+    g = [got[i * rows:(i + 1) * rows].astype(f32) for i in range(3)]
+    own_far, sib_far = lax.optimization_barrier((b[6], got_far))
+    q_far = (own_far.astype(f32) + sib_far.astype(f32)).astype(jnp.bfloat16)
     q_self = b[0].astype(f32) + g[0]
     q_up = b[2].astype(f32) + g[1]
     q_dn = b[4].astype(f32) + g[2]
-    q_far = (b[6].astype(f32) + g[3]).astype(jnp.bfloat16)
     r_a = lax.ppermute(q_far[:, :half], "dp", dp_pairs(dp_count, 1)).astype(f32)
     r_b = lax.ppermute(q_far[:, half:], "dp", dp_pairs(dp_count, -1)).astype(f32)
     s_a = jnp.concatenate([q_dn[:, :half] + r_a, q_dn[:, half:]], axis=1).astype(jnp.bfloat16)

time: 138 us -> 134 us (0.971)
  waiting for transfers between devices: 73.9 us -> 69.4 us
    ppermute x1, waiting for transfers between devices: 4.56 us -> 0.43 us  [scatter_dp(): got_far = lax.ppermute(b[7], 'dp', sib_pairs(dp_count))]
  transfers between devices with their start and end apart: 15 -> 15, of which waited for: 6 -> 7; matrix products, arithmetic and copies ran while one was open for 4% -> 5% of each run, Pallas kernels for 0% -> 0%
where the time goes in v13:
time: 134 us; the launch traced here: 132 us
  waiting for transfers between devices  69.4 us (52%)
  blocking collectives  21.6 us (16%)
  starting transfers between devices  20.4 us (15%)
  matrix products  9.59 us (7%)
  local copies, waits for them, and re-layouts  6.04 us (5%)
  other arithmetic  4.01 us (3%)
    all_to_all x1, blocking collectives, shards(): lax.all_to_all(send_rows, 'expert', split_axis=0, concat_axis=0, tiled=True)  21.6 us
    ppermute x1, waiting for transfers between devices, scatter_dp(): a_a = lax.ppermute(s_a, 'dp', dp_pairs(dp_count, 1)).astype(f32)  19.5 us
    ppermute x1, waiting for transfers between devices, gather_dp(): up = lax.ppermute(x, 'dp', dp_pairs(dp_count, 1))  19 us
    all_to_all x1, waiting for transfers between devices, shards(): lax.all_to_all(summed, 'expert', split_axis=0, concat_axis=0, tiled=True)  12.6 us
    ppermute x1, waiting for transfers between devices, scatter_dp(): r_a = lax.ppermute(q_far[:, :half], 'dp', dp_pairs(dp_count, 1)).astype(f32)  10 us
    ppermute x1, waiting for transfers between devices, gather_dp(): far_a = lax.ppermute(up[:, :half], 'dp', dp_pairs(dp_count, 1))  7.6 us
    all_to_all x1, starting transfers between devices, shards(): lax.all_to_all(summed, 'expert', split_axis=0, concat_axis=0, tiled=True)  5.62 us
    ppermute x1, starting transfers between devices, scatter_dp(): a_b = lax.ppermute(s_b, 'dp', dp_pairs(dp_count, -1)).astype(f32)  3.29 us
  transfers between devices with their start and end apart: 15, of which 7 were waited for; matrix products, arithmetic and copies ran while one was open for 5% of the time, Pallas kernels for 0%

profile of v13, /device:TPU:6, one launch (start us, length us, event | category | flops | bytes accessed | tf_op | source)
XLA Modules:
  0.0 131.5 jit_solution(4315116361664057002)
XLA Ops:
  0.0 0.9 multiply_subtract_fusion
  0.9 0.8 fusion.44
  2.5 1.1 gather_fusion
  3.9 0.5 select_select_fusion
  4.5 21.6 %all_to_all.14 = bf16[16,4,7168]{2,1,0:T(4,128)(2,1)S(1)} all-to-all(bf16[16,4,7168]{2,1,0:T(4,128)(2,1)S(1)} %select_select_fusion), channel_id=1, replica_groups=mesh['dp'=8,'expert'=16] {'expert'}, dimensions={0} | all-to-all | bytes 1835008 | tf_op jit(solution)/shard_map/all_to_all | solution.py:83
  26.3 1.6 %collective-permute-start.1 = (bf16[64,7168]{1,0:T(8,128)(2,1)S(1)}, bf16[64,7168]{1,0:T(8,128)(2,1)S(1)}, u32[]{:S(2)}, u32[]{:S(2)}) collective-permute-start(bf16[64,7168]{1,0:T(8,128)(2,1)S(1)} %all_to_all.10), channel_id=1, source_target_pairs={{0,32},{16,48},{32,64},{48,80},{64,96},{80,112},{96,0},{112,16},{1... | collective-permute-start | bytes 2752520 | tf_op jit(solution)/shard_map/ppermute | solution.py:29
  28.0 1.7 %collective-permute-start.3 = (bf16[64,7168]{1,0:T(8,128)(2,1)S(1)}, bf16[64,7168]{1,0:T(8,128)(2,1)S(1)}, u32[]{:S(2)}, u32[]{:S(2)}) collective-permute-start(bf16[64,7168]{1,0:T(8,128)(2,1)S(1)} %all_to_all.10), channel_id=1, source_target_pairs={{0,96},{16,112},{32,0},{48,16},{64,32},{80,48},{96,64},{112,80},{1... | collective-permute-start | bytes 2752520 | tf_op jit(solution)/shard_map/ppermute | solution.py:30
  29.7 19.0 %collective-permute-done.1 = bf16[64,7168]{1,0:T(8,128)(2,1)S(1)} collective-permute-done((bf16[64,7168]{1,0:T(8,128)(2,1)S(1)}, bf16[64,7168]{1,0:T(8,128)(2,1)S(1)}, u32[]{:S(2)}, u32[]{:S(2)}) %collective-permute-start.1) | collective-permute-done | bytes 917536 | tf_op jit(solution)/shard_map/ppermute | solution.py:29
  49.1 3.0 %collective-permute-start.6 = (bf16[64,3584]{1,0:T(8,128)(2,1)S(1)}, bf16[64,3584]{1,0:T(8,128)(2,1)S(1)}, u32[]{:S(2)}, u32[]{:S(2)}) collective-permute-start(bf16[64,3584]{1,0:T(8,128)(2,1)S(1)} %slice.108), channel_id=1, source_target_pairs={{0,96},{16,112},{32,0},{48,16},{64,32},{80,48},{96,64},{112,80},{1... | collective-permute-start | bytes 1376264 | tf_op jit(solution)/shard_map/ppermute | solution.py:33
  52.1 0.5 collective-permute-start.4
  52.8 7.6 %collective-permute-done.5 = bf16[64,3584]{1,0:T(8,128)(2,1)S(1)} collective-permute-done((bf16[64,3584]{1,0:T(8,128)(2,1)S(1)}, bf16[64,3584]{1,0:T(8,128)(2,1)S(1)}, u32[]{:S(2)}, u32[]{:S(2)}) %collective-permute-start.5) | collective-permute-done | bytes 458784 | tf_op jit(solution)/shard_map/ppermute | solution.py:32
  60.8 1.6 %fusion.10 = f32[384,256]{1,0:T(8,128)S(1)} fusion(bf16[384,7168]{1,0:T(8,128)(2,1)S(1)} %constant_dynamic-update-slice_fusion, bf16[1,7168,256]{2,1,0:T(8,128)(2,1)S(1)} %copy-done.4), kind=kOutput, calls=%fused_computation.15 | convolution fusion | flops 1409286144 | bytes 9568256 | tf_op jit(solution)/shard_map/dot_general | solution.py:89
  62.4 0.4 copy-done.5
  62.8 1.6 %multiply_convert_fusion = bf16[384,256]{1,0:T(8,128)(2,1)S(1)} fusion(f32[384,256]{1,0:T(8,128)S(1)} %fusion.10, bf16[384,7168]{1,0:T(8,128)(2,1)S(1)} %constant_dynamic-update-slice_fusion, bf16[1,7168,256]{2,1,0:T(8,128)(2,1)S(1)} %copy-done.5), kind=kOutput, calls=%fused_computation.35 | convolution fusion | flops 1409875968 | bytes 9764864 | tf_op jit(solution)/shard_map/dot_general | solution.py:90
  64.4 0.6 fusion.8
  65.1 0.6 multiply_convert_fusion.1
  65.8 1.3 %copy-done.2 = bf16[1,256,7168]{2,1,0:T(8,128)(2,1)S(1)} copy-done((bf16[1,256,7168]{2,1,0:T(8,128)(2,1)S(1)}, bf16[1,256,7168]{2,1,0:T(8,128)(2,1)}, u32[]{:S(2)}) %copy-start.2) | copy-done | bytes 3670040
  67.1 1.1 convolution_convert_fusion
  68.3 0.6 collective-permute-start.9
  69.4 1.1 convolution_convert_fusion.1
  70.6 0.4 collective-permute-done.9
  71.3 0.5 collective-permute-start.10
  71.8 2.9 %collective-permute-start.12 = (bf16[64,3584]{1,0:T(8,128)(2,1)S(1)}, bf16[64,3584]{1,0:T(8,128)(2,1)S(1)}, u32[]{:S(2)}, u32[]{:S(2)}) collective-permute-start(bf16[64,3584]{1,0:T(8,128)(2,1)S(1)} %get-tuple-element.14), channel_id=1, source_target_pairs={{0,96},{16,112},{32,0},{48,16},{64,32},{80,48},{96,64},{112,80},{1... | collective-permute-start | bytes 1376264 | tf_op jit(solution)/shard_map/ppermute | solution.py:55
  75.4 10.0 %collective-permute-done.10 = bf16[64,3584]{1,0:T(8,128)(2,1)S(1)} collective-permute-done((bf16[64,3584]{1,0:T(8,128)(2,1)S(1)}, bf16[64,3584]{1,0:T(8,128)(2,1)S(1)}, u32[]{:S(2)}, u32[]{:S(2)}) %collective-permute-start.10) | collective-permute-done | bytes 458784 | tf_op jit(solution)/shard_map/ppermute | solution.py:54
  86.0 3.3 %collective-permute-start.13 = (bf16[64,7168]{1,0:T(8,128)(2,1)S(1)}, bf16[64,7168]{1,0:T(8,128)(2,1)S(1)}, u32[]{:S(2)}, u32[]{:S(2)}) collective-permute-start(bf16[64,7168]{1,0:T(8,128)(2,1)S(1)} %pad_maximum_fusion.4), channel_id=1, source_target_pairs={{0,96},{16,112},{32,0},{48,16},{64,32},{80,48},{96,64},{112,80},{1... | collective-permute-start | bytes 2752520 | tf_op jit(solution)/shard_map/ppermute | solution.py:59
  89.3 19.5 %collective-permute-done.11 = bf16[64,7168]{1,0:T(8,128)(2,1)S(1)} collective-permute-done((bf16[64,7168]{1,0:T(8,128)(2,1)S(1)}, bf16[64,7168]{1,0:T(8,128)(2,1)S(1)}, u32[]{:S(2)}, u32[]{:S(2)}) %collective-permute-start.11) | collective-permute-done | bytes 917536 | tf_op jit(solution)/shard_map/ppermute | solution.py:58
  108.7 0.5 add_convert_fusion
  109.2 1.3 reshape.113
  110.5 5.6 %all-to-all-start.1 = ((bf16[16,4,7168]{2,1,0:T(4,128)(2,1)}), bf16[16,4,7168]{2,1,0:T(4,128)(2,1)S(1)}, u32[]{:S(2)}, u32[]{:S(2)}) async-start(bf16[16,4,7168]{2,1,0:T(4,128)(2,1)} %reshape.113), calls=%async_computation.1 | async-start | bytes 1835008 | tf_op jit(solution)/shard_map/all_to_all | solution.py:103
  116.2 12.6 %all-to-all-done.1 = bf16[16,4,7168]{2,1,0:T(4,128)(2,1)S(1)} async-done(((bf16[16,4,7168]{2,1,0:T(4,128)(2,1)}), bf16[16,4,7168]{2,1,0:T(4,128)(2,1)S(1)}, u32[]{:S(2)}, u32[]{:S(2)}) %all-to-all-start.1) | async-done | bytes 917536 | tf_op jit(solution)/shard_map/all_to_all | solution.py:103
  128.8 0.8 convolution_bitcast_fusion
  129.5 2.0 %fusion.1 = bf16[128,7168]{1,0:T(8,128)(2,1)} fusion(f32[128,7168]{1,0:T(8,128)S(1)} %convolution_bitcast_fusion, bf16[16,4,7168]{2,1,0:T(4,128)(2,1)S(1)} %all-to-all-done.1, f32[16,4]{0,1:T(4,128)S(1)} %select_reduce_fusion, s32[16,4]{0,1:T(4,128)S(1)} %get-tuple-element.10, pred[16,4]{0,1:T(4,128)(4,1)S(1)} %get-tuple-element.24), kind=kOutput, calls=%fused_computation.6 | convolution fusion | flops 119300096 | bytes 6423104 | tf_op jit(solution)/shard_map/dot_general | solution.py:113
  (62 shorter events, 4.6 us)
Async XLA Ops:
  0.0 2.5 %copy-start = (bf16[128,7168]{1,0:T(8,128)(2,1)S(1)}, bf16[128,7168]{1,0:T(8,128)(2,1)}, u32[]{:S(2)}) copy-start(bf16[128,7168]{1,0:T(8,128)(2,1)} %param.6) | copy-start | bytes 5505028
  26.3 22.4 %collective-permute-start.1 = (bf16[64,7168]{1,0:T(8,128)(2,1)S(1)}, bf16[64,7168]{1,0:T(8,128)(2,1)S(1)}, u32[]{:S(2)}, u32[]{:S(2)}) collective-permute-start(bf16[64,7168]{1,0:T(8,128)(2,1)S(1)} %all_to_all.10), channel_id=1, source_target_pairs={{0,32},{16,48},{32,64},{48,80},{64,96},{80,112},{96,0},{112,16},{1... | collective-permute-start | bytes 2752520 | tf_op jit(solution)/shard_map/ppermute | solution.py:29
  28.0 21.1 %collective-permute-start.3 = (bf16[64,7168]{1,0:T(8,128)(2,1)S(1)}, bf16[64,7168]{1,0:T(8,128)(2,1)S(1)}, u32[]{:S(2)}, u32[]{:S(2)}) collective-permute-start(bf16[64,7168]{1,0:T(8,128)(2,1)S(1)} %all_to_all.10), channel_id=1, source_target_pairs={{0,96},{16,112},{32,0},{48,16},{64,32},{80,48},{96,64},{112,80},{1... | collective-permute-start | bytes 2752520 | tf_op jit(solution)/shard_map/ppermute | solution.py:30
  29.6 23.0 %collective-permute-start = (bf16[64,7168]{1,0:T(8,128)(2,1)S(1)}, bf16[64,7168]{1,0:T(8,128)(2,1)S(1)}, u32[]{:S(2)}, u32[]{:S(2)}) collective-permute-start(bf16[64,7168]{1,0:T(8,128)(2,1)S(1)} %all_to_all.10), channel_id=1, source_target_pairs={{0,16},{16,0},{32,48},{48,32},{64,80},{80,64},{96,112},{112,96},{1... | collective-permute-start | bytes 2752520 | tf_op jit(solution)/shard_map/ppermute | solution.py:31
  48.7 11.7 %collective-permute-start.5 = (bf16[64,3584]{1,0:T(8,128)(2,1)S(1)}, bf16[64,3584]{1,0:T(8,128)(2,1)S(1)}, u32[]{:S(2)}, u32[]{:S(2)}) collective-permute-start(bf16[64,3584]{1,0:T(8,128)(2,1)S(1)} %slice.107), channel_id=1, source_target_pairs={{0,32},{16,48},{32,64},{48,80},{64,96},{80,112},{96,0},{112,16},{1... | collective-permute-start | bytes 1376264 | tf_op jit(solution)/shard_map/ppermute | solution.py:32
  49.1 11.3 %collective-permute-start.6 = (bf16[64,3584]{1,0:T(8,128)(2,1)S(1)}, bf16[64,3584]{1,0:T(8,128)(2,1)S(1)}, u32[]{:S(2)}, u32[]{:S(2)}) collective-permute-start(bf16[64,3584]{1,0:T(8,128)(2,1)S(1)} %slice.108), channel_id=1, source_target_pairs={{0,96},{16,112},{32,0},{48,16},{64,32},{80,48},{96,64},{112,80},{1... | collective-permute-start | bytes 1376264 | tf_op jit(solution)/shard_map/ppermute | solution.py:33
  52.1 8.4 %collective-permute-start.2 = (bf16[64,7168]{1,0:T(8,128)(2,1)S(1)}, bf16[64,7168]{1,0:T(8,128)(2,1)S(1)}, u32[]{:S(2)}, u32[]{:S(2)}) collective-permute-start(bf16[64,7168]{1,0:T(8,128)(2,1)S(1)} %collective-permute-done.1), channel_id=1, source_target_pairs={{0,16},{16,0},{32,48},{48,32},{64,80},{80,64},{96,112},{112,96},{1... | collective-permute-start | bytes 2752520 | tf_op jit(solution)/shard_map/ppermute | solution.py:35
  52.1 8.6 %collective-permute-start.4 = (bf16[64,7168]{1,0:T(8,128)(2,1)S(1)}, bf16[64,7168]{1,0:T(8,128)(2,1)S(1)}, u32[]{:S(2)}, u32[]{:S(2)}) collective-permute-start(bf16[64,7168]{1,0:T(8,128)(2,1)S(1)} %collective-permute-done.3), channel_id=1, source_target_pairs={{0,16},{16,0},{32,48},{48,32},{64,80},{80,64},{96,112},{112,96},{1... | collective-permute-start | bytes 2752520 | tf_op jit(solution)/shard_map/ppermute | solution.py:36
  52.8 8.0 %copy-start.4 = (bf16[1,7168,256]{2,1,0:T(8,128)(2,1)S(1)}, bf16[1,7168,256]{2,1,0:T(8,128)(2,1)}, u32[]{:S(2)}) copy-start(bf16[1,7168,256]{2,1,0:T(8,128)(2,1)} %param.9) | copy-start | bytes 11010052
  60.5 4.0 %collective-permute-start.7 = (bf16[64,7168]{1,0:T(8,128)(2,1)S(1)}, bf16[64,7168]{1,0:T(8,128)(2,1)S(1)}, u32[]{:S(2)}, u32[]{:S(2)}) collective-permute-start(bf16[64,7168]{1,0:T(8,128)(2,1)S(1)} %constant_dynamic-update-slice_fusion.6), channel_id=1, source_target_pairs={{0,16},{16,0},{32,48},{48,32},{64,80},{80,64},{96,112},{112,96},{1... | collective-permute-start | bytes 2752520 | tf_op jit(solution)/shard_map/ppermute | solution.py:37
  60.8 2.0 %copy-start.5 = (bf16[1,7168,256]{2,1,0:T(8,128)(2,1)S(1)}, bf16[1,7168,256]{2,1,0:T(8,128)(2,1)}, u32[]{:S(2)}) copy-start(bf16[1,7168,256]{2,1,0:T(8,128)(2,1)} %param.10) | copy-start | bytes 11010052
  65.1 2.0 %copy-start.2 = (bf16[1,256,7168]{2,1,0:T(8,128)(2,1)S(1)}, bf16[1,256,7168]{2,1,0:T(8,128)(2,1)}, u32[]{:S(2)}) copy-start(bf16[1,256,7168]{2,1,0:T(8,128)(2,1)} %param.11) | copy-start | bytes 11010052
  68.3 2.7 %collective-permute-start.9 = (bf16[64,7168]{1,0:T(8,128)(2,1)S(1)}, bf16[64,7168]{1,0:T(8,128)(2,1)S(1)}, u32[]{:S(2)}, u32[]{:S(2)}) collective-permute-start(bf16[64,7168]{1,0:T(8,128)(2,1)S(1)} %slice.124), channel_id=1, source_target_pairs={{0,16},{16,0},{32,48},{48,32},{64,80},{80,64},{96,112},{112,96},{1... | collective-permute-start | bytes 2752520 | tf_op jit(solution)/shard_map/ppermute | solution.py:46
  69.1 5.8 %collective-permute-start.8 = (bf16[192,7168]{1,0:T(8,128)(2,1)S(1)}, bf16[192,7168]{1,0:T(8,128)(2,1)S(1)}, u32[]{:S(2)}, u32[]{:S(2)}) collective-permute-start(bf16[192,7168]{1,0:T(8,128)(2,1)S(1)} %slice.118), channel_id=1, source_target_pairs={{0,16},{16,0},{32,48},{48,32},{64,80},{80,64},{96,112},{112,96},{1... | collective-permute-start | bytes 8257544 | tf_op jit(solution)/shard_map/ppermute | solution.py:47
  71.3 14.1 %collective-permute-start.10 = (bf16[64,3584]{1,0:T(8,128)(2,1)S(1)}, bf16[64,3584]{1,0:T(8,128)(2,1)S(1)}, u32[]{:S(2)}, u32[]{:S(2)}) collective-permute-start(bf16[64,3584]{1,0:T(8,128)(2,1)S(1)} %get-tuple-element.13), channel_id=1, source_target_pairs={{0,32},{16,48},{32,64},{48,80},{64,96},{80,112},{96,0},{112,16},{1... | collective-permute-start | bytes 1376264 | tf_op jit(solution)/shard_map/ppermute | solution.py:54
  71.8 14.0 %collective-permute-start.12 = (bf16[64,3584]{1,0:T(8,128)(2,1)S(1)}, bf16[64,3584]{1,0:T(8,128)(2,1)S(1)}, u32[]{:S(2)}, u32[]{:S(2)}) collective-permute-start(bf16[64,3584]{1,0:T(8,128)(2,1)S(1)} %get-tuple-element.14), channel_id=1, source_target_pairs={{0,96},{16,112},{32,0},{48,16},{64,32},{80,48},{96,64},{112,80},{1... | collective-permute-start | bytes 1376264 | tf_op jit(solution)/shard_map/ppermute | solution.py:55
  85.6 23.1 %collective-permute-start.11 = (bf16[64,7168]{1,0:T(8,128)(2,1)S(1)}, bf16[64,7168]{1,0:T(8,128)(2,1)S(1)}, u32[]{:S(2)}, u32[]{:S(2)}) collective-permute-start(bf16[64,7168]{1,0:T(8,128)(2,1)S(1)} %pad_maximum_fusion.3), channel_id=1, source_target_pairs={{0,32},{16,48},{32,64},{48,80},{64,96},{80,112},{96,0},{112,16},{1... | collective-permute-start | bytes 2752520 | tf_op jit(solution)/shard_map/ppermute | solution.py:58
  86.0 30.1 %copy-start.3 = (s32[16,288]{1,0:T(8,128)S(1)}, s32[16,288]{1,0:T(8,128)}, u32[]{:S(2)}) copy-start(s32[16,288]{1,0:T(8,128)} %param.8) | copy-start | bytes 55300
  86.0 22.8 %collective-permute-start.13 = (bf16[64,7168]{1,0:T(8,128)(2,1)S(1)}, bf16[64,7168]{1,0:T(8,128)(2,1)S(1)}, u32[]{:S(2)}, u32[]{:S(2)}) collective-permute-start(bf16[64,7168]{1,0:T(8,128)(2,1)S(1)} %pad_maximum_fusion.4), channel_id=1, source_target_pairs={{0,96},{16,112},{32,0},{48,16},{64,32},{80,48},{96,64},{112,80},{1... | collective-permute-start | bytes 2752520 | tf_op jit(solution)/shard_map/ppermute | solution.py:59
  110.5 18.3 %all-to-all-start.1 = ((bf16[16,4,7168]{2,1,0:T(4,128)(2,1)}), bf16[16,4,7168]{2,1,0:T(4,128)(2,1)S(1)}, u32[]{:S(2)}, u32[]{:S(2)}) async-start(bf16[16,4,7168]{2,1,0:T(4,128)(2,1)} %reshape.113), calls=%async_computation.1 | async-start | bytes 1835008 | tf_op jit(solution)/shard_map/all_to_all | solution.py:103
  128.8 2.7 %copy-start.1 = (bf16[128,7168]{1,0:T(8,128)(2,1)S(1)}, bf16[128,7168]{1,0:T(8,128)(2,1)}, u32[]{:S(2)}) copy-start(bf16[128,7168]{1,0:T(8,128)(2,1)} %param.6) | copy-start | bytes 5505028

commit v14 on v13

--- a/solution.py
+++ b/solution.py
@@ -14,6 +14,7 @@
     ).astype(jnp.bfloat16)
     ranks = jnp.dot(is_mine.astype(jnp.bfloat16), earlier, preferred_element_type=jnp.float32)
     return (owners, is_mine, ranks.astype(jnp.int32))
+
 
 def dp_pairs(dp_count, shift):
     ny = dp_count // 2
@@ -60,12 +61,12 @@
     return (q_self + a_a + a_b).astype(jnp.bfloat16)
 
 
-def shards(tokens, chosen, combine_fixed, w_gate, w_up, w_down):
+def layer(tokens, chosen, combine_fixed, w_gate, w_up, w_down):
     dp_count = lax.axis_size("dp")
     ex_count = lax.axis_size("expert")
     worker_ordinal = dp_count * ex_count
     tok_count, model_width = tokens.shape
-    expert_total, capacity = chosen.shape
+    _, capacity = chosen.shape
     slot_count = min(tok_count, max(4, 2 * capacity // worker_ordinal))
     my_index = lax.axis_index("dp") * ex_count + lax.axis_index("expert")
     owners, is_mine, ranks = slot_tables(chosen, tok_count, my_index)
@@ -126,4 +127,4 @@
         P("expert", "dp", None),
     )
     out_specs = P(("dp", "expert"), None)
-    return jax.shard_map(shards, mesh=mesh, in_specs=in_specs, out_specs=out_specs, check_vma=False)
+    return jax.shard_map(layer, mesh=mesh, in_specs=in_specs, out_specs=out_specs, check_vma=False)

time: 134 us -> 134 us (level)
  no operation moved by 1% of the time
where the time goes in v14:
time: 134 us; the launch traced here: 131 us
  waiting for transfers between devices  69.4 us (52%)
  blocking collectives  21.6 us (16%)
  starting transfers between devices  20.4 us (15%)
  matrix products  9.59 us (7%)
  local copies, waits for them, and re-layouts  6.04 us (5%)
  other arithmetic  4.01 us (3%)
    all_to_all x1, blocking collectives, layer(): lax.all_to_all(send_rows, 'expert', split_axis=0, concat_axis=0, tiled=True)  21.6 us
    ppermute x1, waiting for transfers between devices, scatter_dp(): a_a = lax.ppermute(s_a, 'dp', dp_pairs(dp_count, 1)).astype(f32)  19.5 us
    ppermute x1, waiting for transfers between devices, gather_dp(): up = lax.ppermute(x, 'dp', dp_pairs(dp_count, 1))  19 us
    all_to_all x1, waiting for transfers between devices, layer(): lax.all_to_all(summed, 'expert', split_axis=0, concat_axis=0, tiled=True)  12.6 us
    ppermute x1, waiting for transfers between devices, scatter_dp(): r_a = lax.ppermute(q_far[:, :half], 'dp', dp_pairs(dp_count, 1)).astype(f32)  10 us
    ppermute x1, waiting for transfers between devices, gather_dp(): far_a = lax.ppermute(up[:, :half], 'dp', dp_pairs(dp_count, 1))  7.6 us
    all_to_all x1, starting transfers between devices, layer(): lax.all_to_all(summed, 'expert', split_axis=0, concat_axis=0, tiled=True)  5.63 us
    ppermute x1, starting transfers between devices, scatter_dp(): a_b = lax.ppermute(s_b, 'dp', dp_pairs(dp_count, -1)).astype(f32)  3.29 us
  transfers between devices with their start and end apart: 15, of which 7 were waited for; matrix products, arithmetic and copies ran while one was open for 5% of the time, Pallas kernels for 0%

profile of v14, /device:TPU:6, one launch (start us, length us, event | category | flops | bytes accessed | tf_op | source)
XLA Modules:
  0.0 131.5 jit_solution(4315116361664057002)
XLA Ops:
  0.0 0.9 multiply_subtract_fusion
  0.9 0.8 fusion.44
  2.5 1.1 gather_fusion
  3.9 0.5 select_select_fusion
  4.5 21.6 %all_to_all.14 = bf16[16,4,7168]{2,1,0:T(4,128)(2,1)S(1)} all-to-all(bf16[16,4,7168]{2,1,0:T(4,128)(2,1)S(1)} %select_select_fusion), channel_id=1, replica_groups=mesh['dp'=8,'expert'=16] {'expert'}, dimensions={0} | all-to-all | bytes 1835008 | tf_op jit(solution)/shard_map/all_to_all | solution.py:84
  26.3 1.6 %collective-permute-start.1 = (bf16[64,7168]{1,0:T(8,128)(2,1)S(1)}, bf16[64,7168]{1,0:T(8,128)(2,1)S(1)}, u32[]{:S(2)}, u32[]{:S(2)}) collective-permute-start(bf16[64,7168]{1,0:T(8,128)(2,1)S(1)} %all_to_all.10), channel_id=1, source_target_pairs={{0,32},{16,48},{32,64},{48,80},{64,96},{80,112},{96,0},{112,16},{1... | collective-permute-start | bytes 2752520 | tf_op jit(solution)/shard_map/ppermute | solution.py:30
  28.0 1.7 %collective-permute-start.3 = (bf16[64,7168]{1,0:T(8,128)(2,1)S(1)}, bf16[64,7168]{1,0:T(8,128)(2,1)S(1)}, u32[]{:S(2)}, u32[]{:S(2)}) collective-permute-start(bf16[64,7168]{1,0:T(8,128)(2,1)S(1)} %all_to_all.10), channel_id=1, source_target_pairs={{0,96},{16,112},{32,0},{48,16},{64,32},{80,48},{96,64},{112,80},{1... | collective-permute-start | bytes 2752520 | tf_op jit(solution)/shard_map/ppermute | solution.py:31
  29.7 19.0 %collective-permute-done.1 = bf16[64,7168]{1,0:T(8,128)(2,1)S(1)} collective-permute-done((bf16[64,7168]{1,0:T(8,128)(2,1)S(1)}, bf16[64,7168]{1,0:T(8,128)(2,1)S(1)}, u32[]{:S(2)}, u32[]{:S(2)}) %collective-permute-start.1) | collective-permute-done | bytes 917536 | tf_op jit(solution)/shard_map/ppermute | solution.py:30
  49.1 3.0 %collective-permute-start.6 = (bf16[64,3584]{1,0:T(8,128)(2,1)S(1)}, bf16[64,3584]{1,0:T(8,128)(2,1)S(1)}, u32[]{:S(2)}, u32[]{:S(2)}) collective-permute-start(bf16[64,3584]{1,0:T(8,128)(2,1)S(1)} %slice.108), channel_id=1, source_target_pairs={{0,96},{16,112},{32,0},{48,16},{64,32},{80,48},{96,64},{112,80},{1... | collective-permute-start | bytes 1376264 | tf_op jit(solution)/shard_map/ppermute | solution.py:34
  52.1 0.5 collective-permute-start.4
  52.8 7.6 %collective-permute-done.5 = bf16[64,3584]{1,0:T(8,128)(2,1)S(1)} collective-permute-done((bf16[64,3584]{1,0:T(8,128)(2,1)S(1)}, bf16[64,3584]{1,0:T(8,128)(2,1)S(1)}, u32[]{:S(2)}, u32[]{:S(2)}) %collective-permute-start.5) | collective-permute-done | bytes 458784 | tf_op jit(solution)/shard_map/ppermute | solution.py:33
  60.8 1.6 %fusion.10 = f32[384,256]{1,0:T(8,128)S(1)} fusion(bf16[384,7168]{1,0:T(8,128)(2,1)S(1)} %constant_dynamic-update-slice_fusion, bf16[1,7168,256]{2,1,0:T(8,128)(2,1)S(1)} %copy-done.4), kind=kOutput, calls=%fused_computation.15 | convolution fusion | flops 1409286144 | bytes 9568256 | tf_op jit(solution)/shard_map/dot_general | solution.py:90
  62.4 0.4 copy-done.5
  62.8 1.6 %multiply_convert_fusion = bf16[384,256]{1,0:T(8,128)(2,1)S(1)} fusion(f32[384,256]{1,0:T(8,128)S(1)} %fusion.10, bf16[384,7168]{1,0:T(8,128)(2,1)S(1)} %constant_dynamic-update-slice_fusion, bf16[1,7168,256]{2,1,0:T(8,128)(2,1)S(1)} %copy-done.5), kind=kOutput, calls=%fused_computation.35 | convolution fusion | flops 1409875968 | bytes 9764864 | tf_op jit(solution)/shard_map/dot_general | solution.py:91
  64.4 0.6 fusion.8
  65.1 0.6 multiply_convert_fusion.1
  65.8 1.3 %copy-done.2 = bf16[1,256,7168]{2,1,0:T(8,128)(2,1)S(1)} copy-done((bf16[1,256,7168]{2,1,0:T(8,128)(2,1)S(1)}, bf16[1,256,7168]{2,1,0:T(8,128)(2,1)}, u32[]{:S(2)}) %copy-start.2) | copy-done | bytes 3670040
  67.1 1.1 convolution_convert_fusion
  68.3 0.6 collective-permute-start.9
  69.4 1.1 convolution_convert_fusion.1
  71.3 0.5 collective-permute-start.10
  71.8 2.8 %collective-permute-start.12 = (bf16[64,3584]{1,0:T(8,128)(2,1)S(1)}, bf16[64,3584]{1,0:T(8,128)(2,1)S(1)}, u32[]{:S(2)}, u32[]{:S(2)}) collective-permute-start(bf16[64,3584]{1,0:T(8,128)(2,1)S(1)} %get-tuple-element.14), channel_id=1, source_target_pairs={{0,96},{16,112},{32,0},{48,16},{64,32},{80,48},{96,64},{112,80},{1... | collective-permute-start | bytes 1376264 | tf_op jit(solution)/shard_map/ppermute | solution.py:56
  74.9 0.4 convert_add_fusion.1
  75.4 10.0 %collective-permute-done.10 = bf16[64,3584]{1,0:T(8,128)(2,1)S(1)} collective-permute-done((bf16[64,3584]{1,0:T(8,128)(2,1)S(1)}, bf16[64,3584]{1,0:T(8,128)(2,1)S(1)}, u32[]{:S(2)}, u32[]{:S(2)}) %collective-permute-start.10) | collective-permute-done | bytes 458784 | tf_op jit(solution)/shard_map/ppermute | solution.py:55
  86.0 3.3 %collective-permute-start.13 = (bf16[64,7168]{1,0:T(8,128)(2,1)S(1)}, bf16[64,7168]{1,0:T(8,128)(2,1)S(1)}, u32[]{:S(2)}, u32[]{:S(2)}) collective-permute-start(bf16[64,7168]{1,0:T(8,128)(2,1)S(1)} %pad_maximum_fusion.4), channel_id=1, source_target_pairs={{0,96},{16,112},{32,0},{48,16},{64,32},{80,48},{96,64},{112,80},{1... | collective-permute-start | bytes 2752520 | tf_op jit(solution)/shard_map/ppermute | solution.py:60
  89.2 19.5 %collective-permute-done.11 = bf16[64,7168]{1,0:T(8,128)(2,1)S(1)} collective-permute-done((bf16[64,7168]{1,0:T(8,128)(2,1)S(1)}, bf16[64,7168]{1,0:T(8,128)(2,1)S(1)}, u32[]{:S(2)}, u32[]{:S(2)}) %collective-permute-start.11) | collective-permute-done | bytes 917536 | tf_op jit(solution)/shard_map/ppermute | solution.py:59
  108.7 0.5 add_convert_fusion
  109.2 1.3 reshape.113
  110.4 5.6 %all-to-all-start.1 = ((bf16[16,4,7168]{2,1,0:T(4,128)(2,1)}), bf16[16,4,7168]{2,1,0:T(4,128)(2,1)S(1)}, u32[]{:S(2)}, u32[]{:S(2)}) async-start(bf16[16,4,7168]{2,1,0:T(4,128)(2,1)} %reshape.113), calls=%async_computation.1 | async-start | bytes 1835008 | tf_op jit(solution)/shard_map/all_to_all | solution.py:104
  116.2 12.6 %all-to-all-done.1 = bf16[16,4,7168]{2,1,0:T(4,128)(2,1)S(1)} async-done(((bf16[16,4,7168]{2,1,0:T(4,128)(2,1)}), bf16[16,4,7168]{2,1,0:T(4,128)(2,1)S(1)}, u32[]{:S(2)}, u32[]{:S(2)}) %all-to-all-start.1) | async-done | bytes 917536 | tf_op jit(solution)/shard_map/all_to_all | solution.py:104
  128.7 0.7 convolution_bitcast_fusion
  129.5 2.0 %fusion.1 = bf16[128,7168]{1,0:T(8,128)(2,1)} fusion(f32[128,7168]{1,0:T(8,128)S(1)} %convolution_bitcast_fusion, bf16[16,4,7168]{2,1,0:T(4,128)(2,1)S(1)} %all-to-all-done.1, f32[16,4]{0,1:T(4,128)S(1)} %select_reduce_fusion, s32[16,4]{0,1:T(4,128)S(1)} %get-tuple-element.10, pred[16,4]{0,1:T(4,128)(4,1)S(1)} %get-tuple-element.24), kind=kOutput, calls=%fused_computation.6 | convolution fusion | flops 119300096 | bytes 6423104 | tf_op jit(solution)/shard_map/dot_general | solution.py:114
  (62 shorter events, 4.6 us)
Async XLA Ops:
  0.0 2.5 %copy-start = (bf16[128,7168]{1,0:T(8,128)(2,1)S(1)}, bf16[128,7168]{1,0:T(8,128)(2,1)}, u32[]{:S(2)}) copy-start(bf16[128,7168]{1,0:T(8,128)(2,1)} %param.6) | copy-start | bytes 5505028
  26.3 22.4 %collective-permute-start.1 = (bf16[64,7168]{1,0:T(8,128)(2,1)S(1)}, bf16[64,7168]{1,0:T(8,128)(2,1)S(1)}, u32[]{:S(2)}, u32[]{:S(2)}) collective-permute-start(bf16[64,7168]{1,0:T(8,128)(2,1)S(1)} %all_to_all.10), channel_id=1, source_target_pairs={{0,32},{16,48},{32,64},{48,80},{64,96},{80,112},{96,0},{112,16},{1... | collective-permute-start | bytes 2752520 | tf_op jit(solution)/shard_map/ppermute | solution.py:30
  28.0 21.1 %collective-permute-start.3 = (bf16[64,7168]{1,0:T(8,128)(2,1)S(1)}, bf16[64,7168]{1,0:T(8,128)(2,1)S(1)}, u32[]{:S(2)}, u32[]{:S(2)}) collective-permute-start(bf16[64,7168]{1,0:T(8,128)(2,1)S(1)} %all_to_all.10), channel_id=1, source_target_pairs={{0,96},{16,112},{32,0},{48,16},{64,32},{80,48},{96,64},{112,80},{1... | collective-permute-start | bytes 2752520 | tf_op jit(solution)/shard_map/ppermute | solution.py:31
  29.6 23.0 %collective-permute-start = (bf16[64,7168]{1,0:T(8,128)(2,1)S(1)}, bf16[64,7168]{1,0:T(8,128)(2,1)S(1)}, u32[]{:S(2)}, u32[]{:S(2)}) collective-permute-start(bf16[64,7168]{1,0:T(8,128)(2,1)S(1)} %all_to_all.10), channel_id=1, source_target_pairs={{0,16},{16,0},{32,48},{48,32},{64,80},{80,64},{96,112},{112,96},{1... | collective-permute-start | bytes 2752520 | tf_op jit(solution)/shard_map/ppermute | solution.py:32
  48.7 11.7 %collective-permute-start.5 = (bf16[64,3584]{1,0:T(8,128)(2,1)S(1)}, bf16[64,3584]{1,0:T(8,128)(2,1)S(1)}, u32[]{:S(2)}, u32[]{:S(2)}) collective-permute-start(bf16[64,3584]{1,0:T(8,128)(2,1)S(1)} %slice.107), channel_id=1, source_target_pairs={{0,32},{16,48},{32,64},{48,80},{64,96},{80,112},{96,0},{112,16},{1... | collective-permute-start | bytes 1376264 | tf_op jit(solution)/shard_map/ppermute | solution.py:33
  49.1 11.3 %collective-permute-start.6 = (bf16[64,3584]{1,0:T(8,128)(2,1)S(1)}, bf16[64,3584]{1,0:T(8,128)(2,1)S(1)}, u32[]{:S(2)}, u32[]{:S(2)}) collective-permute-start(bf16[64,3584]{1,0:T(8,128)(2,1)S(1)} %slice.108), channel_id=1, source_target_pairs={{0,96},{16,112},{32,0},{48,16},{64,32},{80,48},{96,64},{112,80},{1... | collective-permute-start | bytes 1376264 | tf_op jit(solution)/shard_map/ppermute | solution.py:34
  52.1 8.4 %collective-permute-start.2 = (bf16[64,7168]{1,0:T(8,128)(2,1)S(1)}, bf16[64,7168]{1,0:T(8,128)(2,1)S(1)}, u32[]{:S(2)}, u32[]{:S(2)}) collective-permute-start(bf16[64,7168]{1,0:T(8,128)(2,1)S(1)} %collective-permute-done.1), channel_id=1, source_target_pairs={{0,16},{16,0},{32,48},{48,32},{64,80},{80,64},{96,112},{112,96},{1... | collective-permute-start | bytes 2752520 | tf_op jit(solution)/shard_map/ppermute | solution.py:36
  52.1 8.6 %collective-permute-start.4 = (bf16[64,7168]{1,0:T(8,128)(2,1)S(1)}, bf16[64,7168]{1,0:T(8,128)(2,1)S(1)}, u32[]{:S(2)}, u32[]{:S(2)}) collective-permute-start(bf16[64,7168]{1,0:T(8,128)(2,1)S(1)} %collective-permute-done.3), channel_id=1, source_target_pairs={{0,16},{16,0},{32,48},{48,32},{64,80},{80,64},{96,112},{112,96},{1... | collective-permute-start | bytes 2752520 | tf_op jit(solution)/shard_map/ppermute | solution.py:37
  52.8 8.0 %copy-start.4 = (bf16[1,7168,256]{2,1,0:T(8,128)(2,1)S(1)}, bf16[1,7168,256]{2,1,0:T(8,128)(2,1)}, u32[]{:S(2)}) copy-start(bf16[1,7168,256]{2,1,0:T(8,128)(2,1)} %param.9) | copy-start | bytes 11010052
  60.5 4.0 %collective-permute-start.7 = (bf16[64,7168]{1,0:T(8,128)(2,1)S(1)}, bf16[64,7168]{1,0:T(8,128)(2,1)S(1)}, u32[]{:S(2)}, u32[]{:S(2)}) collective-permute-start(bf16[64,7168]{1,0:T(8,128)(2,1)S(1)} %constant_dynamic-update-slice_fusion.6), channel_id=1, source_target_pairs={{0,16},{16,0},{32,48},{48,32},{64,80},{80,64},{96,112},{112,96},{1... | collective-permute-start | bytes 2752520 | tf_op jit(solution)/shard_map/ppermute | solution.py:38
  60.8 2.0 %copy-start.5 = (bf16[1,7168,256]{2,1,0:T(8,128)(2,1)S(1)}, bf16[1,7168,256]{2,1,0:T(8,128)(2,1)}, u32[]{:S(2)}) copy-start(bf16[1,7168,256]{2,1,0:T(8,128)(2,1)} %param.10) | copy-start | bytes 11010052
  65.1 2.0 %copy-start.2 = (bf16[1,256,7168]{2,1,0:T(8,128)(2,1)S(1)}, bf16[1,256,7168]{2,1,0:T(8,128)(2,1)}, u32[]{:S(2)}) copy-start(bf16[1,256,7168]{2,1,0:T(8,128)(2,1)} %param.11) | copy-start | bytes 11010052
  68.3 2.7 %collective-permute-start.9 = (bf16[64,7168]{1,0:T(8,128)(2,1)S(1)}, bf16[64,7168]{1,0:T(8,128)(2,1)S(1)}, u32[]{:S(2)}, u32[]{:S(2)}) collective-permute-start(bf16[64,7168]{1,0:T(8,128)(2,1)S(1)} %slice.124), channel_id=1, source_target_pairs={{0,16},{16,0},{32,48},{48,32},{64,80},{80,64},{96,112},{112,96},{1... | collective-permute-start | bytes 2752520 | tf_op jit(solution)/shard_map/ppermute | solution.py:47
  69.1 5.8 %collective-permute-start.8 = (bf16[192,7168]{1,0:T(8,128)(2,1)S(1)}, bf16[192,7168]{1,0:T(8,128)(2,1)S(1)}, u32[]{:S(2)}, u32[]{:S(2)}) collective-permute-start(bf16[192,7168]{1,0:T(8,128)(2,1)S(1)} %slice.118), channel_id=1, source_target_pairs={{0,16},{16,0},{32,48},{48,32},{64,80},{80,64},{96,112},{112,96},{1... | collective-permute-start | bytes 8257544 | tf_op jit(solution)/shard_map/ppermute | solution.py:48
  71.3 14.1 %collective-permute-start.10 = (bf16[64,3584]{1,0:T(8,128)(2,1)S(1)}, bf16[64,3584]{1,0:T(8,128)(2,1)S(1)}, u32[]{:S(2)}, u32[]{:S(2)}) collective-permute-start(bf16[64,3584]{1,0:T(8,128)(2,1)S(1)} %get-tuple-element.13), channel_id=1, source_target_pairs={{0,32},{16,48},{32,64},{48,80},{64,96},{80,112},{96,0},{112,16},{1... | collective-permute-start | bytes 1376264 | tf_op jit(solution)/shard_map/ppermute | solution.py:55
  71.8 14.0 %collective-permute-start.12 = (bf16[64,3584]{1,0:T(8,128)(2,1)S(1)}, bf16[64,3584]{1,0:T(8,128)(2,1)S(1)}, u32[]{:S(2)}, u32[]{:S(2)}) collective-permute-start(bf16[64,3584]{1,0:T(8,128)(2,1)S(1)} %get-tuple-element.14), channel_id=1, source_target_pairs={{0,96},{16,112},{32,0},{48,16},{64,32},{80,48},{96,64},{112,80},{1... | collective-permute-start | bytes 1376264 | tf_op jit(solution)/shard_map/ppermute | solution.py:56
  85.6 23.1 %collective-permute-start.11 = (bf16[64,7168]{1,0:T(8,128)(2,1)S(1)}, bf16[64,7168]{1,0:T(8,128)(2,1)S(1)}, u32[]{:S(2)}, u32[]{:S(2)}) collective-permute-start(bf16[64,7168]{1,0:T(8,128)(2,1)S(1)} %pad_maximum_fusion.3), channel_id=1, source_target_pairs={{0,32},{16,48},{32,64},{48,80},{64,96},{80,112},{96,0},{112,16},{1... | collective-permute-start | bytes 2752520 | tf_op jit(solution)/shard_map/ppermute | solution.py:59
  85.9 30.1 %copy-start.3 = (s32[16,288]{1,0:T(8,128)S(1)}, s32[16,288]{1,0:T(8,128)}, u32[]{:S(2)}) copy-start(s32[16,288]{1,0:T(8,128)} %param.8) | copy-start | bytes 55300
  86.0 22.8 %collective-permute-start.13 = (bf16[64,7168]{1,0:T(8,128)(2,1)S(1)}, bf16[64,7168]{1,0:T(8,128)(2,1)S(1)}, u32[]{:S(2)}, u32[]{:S(2)}) collective-permute-start(bf16[64,7168]{1,0:T(8,128)(2,1)S(1)} %pad_maximum_fusion.4), channel_id=1, source_target_pairs={{0,96},{16,112},{32,0},{48,16},{64,32},{80,48},{96,64},{112,80},{1... | collective-permute-start | bytes 2752520 | tf_op jit(solution)/shard_map/ppermute | solution.py:60
  110.4 18.3 %all-to-all-start.1 = ((bf16[16,4,7168]{2,1,0:T(4,128)(2,1)}), bf16[16,4,7168]{2,1,0:T(4,128)(2,1)S(1)}, u32[]{:S(2)}, u32[]{:S(2)}) async-start(bf16[16,4,7168]{2,1,0:T(4,128)(2,1)} %reshape.113), calls=%async_computation.1 | async-start | bytes 1835008 | tf_op jit(solution)/shard_map/all_to_all | solution.py:104
  128.7 2.7 %copy-start.1 = (bf16[128,7168]{1,0:T(8,128)(2,1)S(1)}, bf16[128,7168]{1,0:T(8,128)(2,1)}, u32[]{:S(2)}) copy-start(bf16[128,7168]{1,0:T(8,128)(2,1)} %param.6) | copy-start | bytes 5505028

commit v15 on v14

--- a/solution.py
+++ b/solution.py
@@ -84,16 +84,15 @@
     row_in = lax.all_to_all(send_rows, "expert", split_axis=0, concat_axis=0, tiled=True)
     blocks = gather_dp(row_in, dp_count)
     rows = row_in.shape[0]
-    hidden = []
-    for part in (blocks[:6], blocks[6:]):
+    hb = []
+    for part in (blocks[:6], blocks[6:7], blocks[7:]):
         picked = jnp.concatenate(part, axis=0)
         gate_act = jnp.dot(picked, w_gate[0], preferred_element_type=jnp.float32)
         up_act = jnp.dot(picked, w_up[0], preferred_element_type=jnp.float32)
-        hidden.append((jax.nn.silu(gate_act) * up_act).astype(jnp.bfloat16))
-    hidden = lax.optimization_barrier(jnp.concatenate(hidden, axis=0))
-    hb = [hidden[i * rows:(i + 1) * rows] for i in range(8)]
+        hidden = lax.optimization_barrier((jax.nn.silu(gate_act) * up_act).astype(jnp.bfloat16))
+        hb += [hidden[i * rows:(i + 1) * rows] for i in range(len(part))]
     result = [None] * 8
-    for group in ((1, 3, 5, 7), (0, 2, 4, 6)):
+    for group in ((0, 2, 4, 6), (1, 3, 5, 7)):
         out = jnp.dot(
             jnp.concatenate([hb[i] for i in group], axis=0), w_down[0], preferred_element_type=jnp.float32
         ).astype(jnp.bfloat16)

time: 134 us -> 134 us (level)
  matrix products: 9.59 us -> 11.2 us
    dot_general x2 -> x3, matrix products: 2.23 us -> 3.06 us  [layer(): up_act = jnp.dot(picked, w_up[0], preferred_element_type=jnp.float32)]
    dot_general x2 -> x3, matrix products: 2.23 us -> 3.05 us  [layer(): gate_act = jnp.dot(picked, w_gate[0], preferred_element_type=jnp.float32)]
  transfers between devices with their start and end apart: 15 -> 15, of which waited for: 7 -> 6; matrix products, arithmetic and copies ran while one was open for 5% -> 6% of each run, Pallas kernels for 0% -> 0%
where the time goes in v15:
time: 134 us; the launch traced here: 132 us
  waiting for transfers between devices  69.3 us (52%)
  blocking collectives  21.6 us (16%)
  starting transfers between devices  20.4 us (15%)
  matrix products  11.2 us (8%)
  local copies, waits for them, and re-layouts  5.25 us (4%)
  other arithmetic  4 us (3%)
    all_to_all x1, blocking collectives, layer(): lax.all_to_all(send_rows, 'expert', split_axis=0, concat_axis=0, tiled=True)  21.6 us
    ppermute x1, waiting for transfers between devices, scatter_dp(): a_a = lax.ppermute(s_a, 'dp', dp_pairs(dp_count, 1)).astype(f32)  19.6 us
    ppermute x1, waiting for transfers between devices, gather_dp(): up = lax.ppermute(x, 'dp', dp_pairs(dp_count, 1))  19 us
    all_to_all x1, waiting for transfers between devices, layer(): lax.all_to_all(summed, 'expert', split_axis=0, concat_axis=0, tiled=True)  12.7 us
    ppermute x1, waiting for transfers between devices, scatter_dp(): r_a = lax.ppermute(q_far[:, :half], 'dp', dp_pairs(dp_count, 1)).astype(f32)  10.2 us
    ppermute x1, waiting for transfers between devices, gather_dp(): far_a = lax.ppermute(up[:, :half], 'dp', dp_pairs(dp_count, 1))  7.6 us
    all_to_all x1, starting transfers between devices, layer(): lax.all_to_all(summed, 'expert', split_axis=0, concat_axis=0, tiled=True)  5.62 us
    ppermute x1, starting transfers between devices, scatter_dp(): a_b = lax.ppermute(s_b, 'dp', dp_pairs(dp_count, -1)).astype(f32)  3.29 us
  transfers between devices with their start and end apart: 15, of which 6 were waited for; matrix products, arithmetic and copies ran while one was open for 6% of the time, Pallas kernels for 0%

profile of v15, /device:TPU:6, one launch (start us, length us, event | category | flops | bytes accessed | tf_op | source)
XLA Modules:
  0.0 132.2 jit_solution(11275620489539777801)
XLA Ops:
  0.0 0.9 multiply_subtract_fusion
  0.9 0.8 fusion.48
  2.5 1.1 gather_fusion
  3.9 0.5 select_select_fusion
  4.5 21.6 %all_to_all.14 = bf16[16,4,7168]{2,1,0:T(4,128)(2,1)S(1)} all-to-all(bf16[16,4,7168]{2,1,0:T(4,128)(2,1)S(1)} %select_select_fusion), channel_id=1, replica_groups=mesh['dp'=8,'expert'=16] {'expert'}, dimensions={0} | all-to-all | bytes 1835008 | tf_op jit(solution)/shard_map/all_to_all | solution.py:84
  26.3 1.6 %collective-permute-start.1 = (bf16[64,7168]{1,0:T(8,128)(2,1)S(1)}, bf16[64,7168]{1,0:T(8,128)(2,1)S(1)}, u32[]{:S(2)}, u32[]{:S(2)}) collective-permute-start(bf16[64,7168]{1,0:T(8,128)(2,1)S(1)} %all_to_all.10), channel_id=1, source_target_pairs={{0,32},{16,48},{32,64},{48,80},{64,96},{80,112},{96,0},{112,16},{1... | collective-permute-start | bytes 2752520 | tf_op jit(solution)/shard_map/ppermute | solution.py:30
  28.0 1.7 %collective-permute-start.3 = (bf16[64,7168]{1,0:T(8,128)(2,1)S(1)}, bf16[64,7168]{1,0:T(8,128)(2,1)S(1)}, u32[]{:S(2)}, u32[]{:S(2)}) collective-permute-start(bf16[64,7168]{1,0:T(8,128)(2,1)S(1)} %all_to_all.10), channel_id=1, source_target_pairs={{0,96},{16,112},{32,0},{48,16},{64,32},{80,48},{96,64},{112,80},{1... | collective-permute-start | bytes 2752520 | tf_op jit(solution)/shard_map/ppermute | solution.py:31
  29.7 19.0 %collective-permute-done.1 = bf16[64,7168]{1,0:T(8,128)(2,1)S(1)} collective-permute-done((bf16[64,7168]{1,0:T(8,128)(2,1)S(1)}, bf16[64,7168]{1,0:T(8,128)(2,1)S(1)}, u32[]{:S(2)}, u32[]{:S(2)}) %collective-permute-start.1) | collective-permute-done | bytes 917536 | tf_op jit(solution)/shard_map/ppermute | solution.py:30
  49.1 3.0 %collective-permute-start.6 = (bf16[64,3584]{1,0:T(8,128)(2,1)S(1)}, bf16[64,3584]{1,0:T(8,128)(2,1)S(1)}, u32[]{:S(2)}, u32[]{:S(2)}) collective-permute-start(bf16[64,3584]{1,0:T(8,128)(2,1)S(1)} %slice.103), channel_id=1, source_target_pairs={{0,96},{16,112},{32,0},{48,16},{64,32},{80,48},{96,64},{112,80},{1... | collective-permute-start | bytes 1376264 | tf_op jit(solution)/shard_map/ppermute | solution.py:34
  52.1 0.5 collective-permute-start.4
  52.8 7.6 %collective-permute-done.5 = bf16[64,3584]{1,0:T(8,128)(2,1)S(1)} collective-permute-done((bf16[64,3584]{1,0:T(8,128)(2,1)S(1)}, bf16[64,3584]{1,0:T(8,128)(2,1)S(1)}, u32[]{:S(2)}, u32[]{:S(2)}) %collective-permute-start.5) | collective-permute-done | bytes 458784 | tf_op jit(solution)/shard_map/ppermute | solution.py:33
  60.8 1.6 %fusion.14 = f32[384,256]{1,0:T(8,128)S(1)} fusion(bf16[384,7168]{1,0:T(8,128)(2,1)S(1)} %constant_dynamic-update-slice_fusion, bf16[1,7168,256]{2,1,0:T(8,128)(2,1)S(1)} %copy-done.3), kind=kOutput, calls=%fused_computation.19 | convolution fusion | flops 1409286144 | bytes 9568256 | tf_op jit(solution)/shard_map/dot_general | solution.py:90
  62.8 1.6 %multiply_convert_fusion = bf16[384,256]{1,0:T(8,128)(2,1)S(1)} fusion(f32[384,256]{1,0:T(8,128)S(1)} %fusion.14, bf16[384,7168]{1,0:T(8,128)(2,1)S(1)} %constant_dynamic-update-slice_fusion, bf16[1,7168,256]{2,1,0:T(8,128)(2,1)S(1)} %copy-done.4), kind=kOutput, calls=%fused_computation.38 | convolution fusion | flops 1409875968 | bytes 9764864 | tf_op jit(solution)/shard_map/dot_general | solution.py:91
  64.5 0.7 fusion.10
  65.2 0.7 multiply_convert_fusion.1
  66.0 0.6 copy-done.2
  66.5 1.1 convolution_convert_fusion
  67.7 0.6 collective-permute-start.9
  68.3 0.7 fusion.12
  69.0 0.7 multiply_convert_fusion.2
  70.2 1.1 convolution_convert_fusion.1
  71.7 0.5 collective-permute-start.10
  72.2 2.9 %collective-permute-start.12 = (bf16[64,3584]{1,0:T(8,128)(2,1)S(1)}, bf16[64,3584]{1,0:T(8,128)(2,1)S(1)}, u32[]{:S(2)}, u32[]{:S(2)}) collective-permute-start(bf16[64,3584]{1,0:T(8,128)(2,1)S(1)} %get-tuple-element.14), channel_id=1, source_target_pairs={{0,96},{16,112},{32,0},{48,16},{64,32},{80,48},{96,64},{112,80},{1... | collective-permute-start | bytes 1376264 | tf_op jit(solution)/shard_map/ppermute | solution.py:56
  75.8 10.2 %collective-permute-done.10 = bf16[64,3584]{1,0:T(8,128)(2,1)S(1)} collective-permute-done((bf16[64,3584]{1,0:T(8,128)(2,1)S(1)}, bf16[64,3584]{1,0:T(8,128)(2,1)S(1)}, u32[]{:S(2)}, u32[]{:S(2)}) %collective-permute-start.10) | collective-permute-done | bytes 458784 | tf_op jit(solution)/shard_map/ppermute | solution.py:55
  86.5 3.3 %collective-permute-start.13 = (bf16[64,7168]{1,0:T(8,128)(2,1)S(1)}, bf16[64,7168]{1,0:T(8,128)(2,1)S(1)}, u32[]{:S(2)}, u32[]{:S(2)}) collective-permute-start(bf16[64,7168]{1,0:T(8,128)(2,1)S(1)} %pad_maximum_fusion.1), channel_id=1, source_target_pairs={{0,96},{16,112},{32,0},{48,16},{64,32},{80,48},{96,64},{112,80},{1... | collective-permute-start | bytes 2752520 | tf_op jit(solution)/shard_map/ppermute | solution.py:60
  89.8 19.6 %collective-permute-done.11 = bf16[64,7168]{1,0:T(8,128)(2,1)S(1)} collective-permute-done((bf16[64,7168]{1,0:T(8,128)(2,1)S(1)}, bf16[64,7168]{1,0:T(8,128)(2,1)S(1)}, u32[]{:S(2)}, u32[]{:S(2)}) %collective-permute-start.11) | collective-permute-done | bytes 917536 | tf_op jit(solution)/shard_map/ppermute | solution.py:59
  109.4 0.5 add_convert_fusion
  109.8 1.3 reshape.113
  111.1 5.6 %all-to-all-start.1 = ((bf16[16,4,7168]{2,1,0:T(4,128)(2,1)}), bf16[16,4,7168]{2,1,0:T(4,128)(2,1)S(1)}, u32[]{:S(2)}, u32[]{:S(2)}) async-start(bf16[16,4,7168]{2,1,0:T(4,128)(2,1)} %reshape.113), calls=%async_computation.1 | async-start | bytes 1835008 | tf_op jit(solution)/shard_map/all_to_all | solution.py:103
  116.8 12.7 %all-to-all-done.1 = bf16[16,4,7168]{2,1,0:T(4,128)(2,1)S(1)} async-done(((bf16[16,4,7168]{2,1,0:T(4,128)(2,1)}), bf16[16,4,7168]{2,1,0:T(4,128)(2,1)S(1)}, u32[]{:S(2)}, u32[]{:S(2)}) %all-to-all-start.1) | async-done | bytes 917536 | tf_op jit(solution)/shard_map/all_to_all | solution.py:103
  129.5 0.7 convolution_bitcast_fusion
  130.2 2.0 %fusion.1 = bf16[128,7168]{1,0:T(8,128)(2,1)} fusion(f32[128,7168]{1,0:T(8,128)S(1)} %convolution_bitcast_fusion, bf16[16,4,7168]{2,1,0:T(4,128)(2,1)S(1)} %all-to-all-done.1, f32[16,4]{0,1:T(4,128)S(1)} %select_reduce_fusion, s32[16,4]{0,1:T(4,128)S(1)} %get-tuple-element.10, pred[16,4]{0,1:T(4,128)(4,1)S(1)} %get-tuple-element.22), kind=kOutput, calls=%fused_computation.6 | convolution fusion | flops 119300096 | bytes 6423104 | tf_op jit(solution)/shard_map/dot_general | solution.py:113
  (63 shorter events, 4.9 us)
Async XLA Ops:
  0.0 2.5 %copy-start = (bf16[128,7168]{1,0:T(8,128)(2,1)S(1)}, bf16[128,7168]{1,0:T(8,128)(2,1)}, u32[]{:S(2)}) copy-start(bf16[128,7168]{1,0:T(8,128)(2,1)} %param.6) | copy-start | bytes 5505028
  26.3 22.4 %collective-permute-start.1 = (bf16[64,7168]{1,0:T(8,128)(2,1)S(1)}, bf16[64,7168]{1,0:T(8,128)(2,1)S(1)}, u32[]{:S(2)}, u32[]{:S(2)}) collective-permute-start(bf16[64,7168]{1,0:T(8,128)(2,1)S(1)} %all_to_all.10), channel_id=1, source_target_pairs={{0,32},{16,48},{32,64},{48,80},{64,96},{80,112},{96,0},{112,16},{1... | collective-permute-start | bytes 2752520 | tf_op jit(solution)/shard_map/ppermute | solution.py:30
  28.0 21.1 %collective-permute-start.3 = (bf16[64,7168]{1,0:T(8,128)(2,1)S(1)}, bf16[64,7168]{1,0:T(8,128)(2,1)S(1)}, u32[]{:S(2)}, u32[]{:S(2)}) collective-permute-start(bf16[64,7168]{1,0:T(8,128)(2,1)S(1)} %all_to_all.10), channel_id=1, source_target_pairs={{0,96},{16,112},{32,0},{48,16},{64,32},{80,48},{96,64},{112,80},{1... | collective-permute-start | bytes 2752520 | tf_op jit(solution)/shard_map/ppermute | solution.py:31
  29.6 23.0 %collective-permute-start = (bf16[64,7168]{1,0:T(8,128)(2,1)S(1)}, bf16[64,7168]{1,0:T(8,128)(2,1)S(1)}, u32[]{:S(2)}, u32[]{:S(2)}) collective-permute-start(bf16[64,7168]{1,0:T(8,128)(2,1)S(1)} %all_to_all.10), channel_id=1, source_target_pairs={{0,16},{16,0},{32,48},{48,32},{64,80},{80,64},{96,112},{112,96},{1... | collective-permute-start | bytes 2752520 | tf_op jit(solution)/shard_map/ppermute | solution.py:32
  48.7 11.7 %collective-permute-start.5 = (bf16[64,3584]{1,0:T(8,128)(2,1)S(1)}, bf16[64,3584]{1,0:T(8,128)(2,1)S(1)}, u32[]{:S(2)}, u32[]{:S(2)}) collective-permute-start(bf16[64,3584]{1,0:T(8,128)(2,1)S(1)} %slice.102), channel_id=1, source_target_pairs={{0,32},{16,48},{32,64},{48,80},{64,96},{80,112},{96,0},{112,16},{1... | collective-permute-start | bytes 1376264 | tf_op jit(solution)/shard_map/ppermute | solution.py:33
  49.1 11.3 %collective-permute-start.6 = (bf16[64,3584]{1,0:T(8,128)(2,1)S(1)}, bf16[64,3584]{1,0:T(8,128)(2,1)S(1)}, u32[]{:S(2)}, u32[]{:S(2)}) collective-permute-start(bf16[64,3584]{1,0:T(8,128)(2,1)S(1)} %slice.103), channel_id=1, source_target_pairs={{0,96},{16,112},{32,0},{48,16},{64,32},{80,48},{96,64},{112,80},{1... | collective-permute-start | bytes 1376264 | tf_op jit(solution)/shard_map/ppermute | solution.py:34
  52.1 8.4 %collective-permute-start.2 = (bf16[64,7168]{1,0:T(8,128)(2,1)S(1)}, bf16[64,7168]{1,0:T(8,128)(2,1)S(1)}, u32[]{:S(2)}, u32[]{:S(2)}) collective-permute-start(bf16[64,7168]{1,0:T(8,128)(2,1)S(1)} %collective-permute-done.1), channel_id=1, source_target_pairs={{0,16},{16,0},{32,48},{48,32},{64,80},{80,64},{96,112},{112,96},{1... | collective-permute-start | bytes 2752520 | tf_op jit(solution)/shard_map/ppermute | solution.py:36
  52.1 8.6 %collective-permute-start.4 = (bf16[64,7168]{1,0:T(8,128)(2,1)S(1)}, bf16[64,7168]{1,0:T(8,128)(2,1)S(1)}, u32[]{:S(2)}, u32[]{:S(2)}) collective-permute-start(bf16[64,7168]{1,0:T(8,128)(2,1)S(1)} %collective-permute-done.3), channel_id=1, source_target_pairs={{0,16},{16,0},{32,48},{48,32},{64,80},{80,64},{96,112},{112,96},{1... | collective-permute-start | bytes 2752520 | tf_op jit(solution)/shard_map/ppermute | solution.py:37
  52.8 8.0 %copy-start.3 = (bf16[1,7168,256]{2,1,0:T(8,128)(2,1)S(1)}, bf16[1,7168,256]{2,1,0:T(8,128)(2,1)}, u32[]{:S(2)}) copy-start(bf16[1,7168,256]{2,1,0:T(8,128)(2,1)} %param.9) | copy-start | bytes 11010052
  60.5 4.0 %collective-permute-start.7 = (bf16[64,7168]{1,0:T(8,128)(2,1)S(1)}, bf16[64,7168]{1,0:T(8,128)(2,1)S(1)}, u32[]{:S(2)}, u32[]{:S(2)}) collective-permute-start(bf16[64,7168]{1,0:T(8,128)(2,1)S(1)} %constant_dynamic-update-slice_fusion.6), channel_id=1, source_target_pairs={{0,16},{16,0},{32,48},{48,32},{64,80},{80,64},{96,112},{112,96},{1... | collective-permute-start | bytes 2752520 | tf_op jit(solution)/shard_map/ppermute | solution.py:38
  60.8 2.0 %copy-start.4 = (bf16[1,7168,256]{2,1,0:T(8,128)(2,1)S(1)}, bf16[1,7168,256]{2,1,0:T(8,128)(2,1)}, u32[]{:S(2)}) copy-start(bf16[1,7168,256]{2,1,0:T(8,128)(2,1)} %param.10) | copy-start | bytes 11010052
  64.5 2.0 %copy-start.2 = (bf16[1,256,7168]{2,1,0:T(8,128)(2,1)S(1)}, bf16[1,256,7168]{2,1,0:T(8,128)(2,1)}, u32[]{:S(2)}) copy-start(bf16[1,256,7168]{2,1,0:T(8,128)(2,1)} %param.11) | copy-start | bytes 11010052
  67.7 3.7 %collective-permute-start.9 = (bf16[64,7168]{1,0:T(8,128)(2,1)S(1)}, bf16[64,7168]{1,0:T(8,128)(2,1)S(1)}, u32[]{:S(2)}, u32[]{:S(2)}) collective-permute-start(bf16[64,7168]{1,0:T(8,128)(2,1)S(1)} %slice.114), channel_id=1, source_target_pairs={{0,16},{16,0},{32,48},{48,32},{64,80},{80,64},{96,112},{112,96},{1... | collective-permute-start | bytes 2752520 | tf_op jit(solution)/shard_map/ppermute | solution.py:47
  69.9 5.4 %collective-permute-start.8 = (bf16[192,7168]{1,0:T(8,128)(2,1)S(1)}, bf16[192,7168]{1,0:T(8,128)(2,1)S(1)}, u32[]{:S(2)}, u32[]{:S(2)}) collective-permute-start(bf16[192,7168]{1,0:T(8,128)(2,1)S(1)} %slice.108), channel_id=1, source_target_pairs={{0,16},{16,0},{32,48},{48,32},{64,80},{80,64},{96,112},{112,96},{1... | collective-permute-start | bytes 8257544 | tf_op jit(solution)/shard_map/ppermute | solution.py:48
  71.7 14.3 %collective-permute-start.10 = (bf16[64,3584]{1,0:T(8,128)(2,1)S(1)}, bf16[64,3584]{1,0:T(8,128)(2,1)S(1)}, u32[]{:S(2)}, u32[]{:S(2)}) collective-permute-start(bf16[64,3584]{1,0:T(8,128)(2,1)S(1)} %get-tuple-element.13), channel_id=1, source_target_pairs={{0,32},{16,48},{32,64},{48,80},{64,96},{80,112},{96,0},{112,16},{1... | collective-permute-start | bytes 1376264 | tf_op jit(solution)/shard_map/ppermute | solution.py:55
  72.2 14.1 %collective-permute-start.12 = (bf16[64,3584]{1,0:T(8,128)(2,1)S(1)}, bf16[64,3584]{1,0:T(8,128)(2,1)S(1)}, u32[]{:S(2)}, u32[]{:S(2)}) collective-permute-start(bf16[64,3584]{1,0:T(8,128)(2,1)S(1)} %get-tuple-element.14), channel_id=1, source_target_pairs={{0,96},{16,112},{32,0},{48,16},{64,32},{80,48},{96,64},{112,80},{1... | collective-permute-start | bytes 1376264 | tf_op jit(solution)/shard_map/ppermute | solution.py:56
  86.2 23.2 %collective-permute-start.11 = (bf16[64,7168]{1,0:T(8,128)(2,1)S(1)}, bf16[64,7168]{1,0:T(8,128)(2,1)S(1)}, u32[]{:S(2)}, u32[]{:S(2)}) collective-permute-start(bf16[64,7168]{1,0:T(8,128)(2,1)S(1)} %pad_maximum_fusion), channel_id=1, source_target_pairs={{0,32},{16,48},{32,64},{48,80},{64,96},{80,112},{96,0},{112,16},{1... | collective-permute-start | bytes 2752520 | tf_op jit(solution)/shard_map/ppermute | solution.py:59
  86.5 30.2 %copy-start.5 = (s32[16,288]{1,0:T(8,128)S(1)}, s32[16,288]{1,0:T(8,128)}, u32[]{:S(2)}) copy-start(s32[16,288]{1,0:T(8,128)} %param.8) | copy-start | bytes 55300
  86.5 22.9 %collective-permute-start.13 = (bf16[64,7168]{1,0:T(8,128)(2,1)S(1)}, bf16[64,7168]{1,0:T(8,128)(2,1)S(1)}, u32[]{:S(2)}, u32[]{:S(2)}) collective-permute-start(bf16[64,7168]{1,0:T(8,128)(2,1)S(1)} %pad_maximum_fusion.1), channel_id=1, source_target_pairs={{0,96},{16,112},{32,0},{48,16},{64,32},{80,48},{96,64},{112,80},{1... | collective-permute-start | bytes 2752520 | tf_op jit(solution)/shard_map/ppermute | solution.py:60
  111.1 18.4 %all-to-all-start.1 = ((bf16[16,4,7168]{2,1,0:T(4,128)(2,1)}), bf16[16,4,7168]{2,1,0:T(4,128)(2,1)S(1)}, u32[]{:S(2)}, u32[]{:S(2)}) async-start(bf16[16,4,7168]{2,1,0:T(4,128)(2,1)} %reshape.113), calls=%async_computation.1 | async-start | bytes 1835008 | tf_op jit(solution)/shard_map/all_to_all | solution.py:103
  129.5 2.7 %copy-start.1 = (bf16[128,7168]{1,0:T(8,128)(2,1)S(1)}, bf16[128,7168]{1,0:T(8,128)(2,1)}, u32[]{:S(2)}) copy-start(bf16[128,7168]{1,0:T(8,128)(2,1)} %param.6) | copy-start | bytes 5505028

commit v16 on v14

--- a/solution.py
+++ b/solution.py
@@ -35,7 +35,9 @@
     far = jnp.concatenate([far_a, far_b], axis=1)
     s_up = lax.ppermute(up, "dp", sib_pairs(dp_count))
     s_dn = lax.ppermute(dn, "dp", sib_pairs(dp_count))
-    s_far = lax.ppermute(far, "dp", sib_pairs(dp_count))
+    s_far = jnp.concatenate(
+        [lax.ppermute(far_a, "dp", sib_pairs(dp_count)), lax.ppermute(far_b, "dp", sib_pairs(dp_count))], axis=1
+    )
     return [x, sib, up, s_up, dn, s_dn, far, s_far]
 
 
@@ -79,8 +81,10 @@
     present = jnp.sum(match_int, axis=1)
     scaled = combine_fixed.astype(jnp.float32) / 65536.0
     weights = jnp.sum(matches.astype(jnp.float32) * scaled[:, :, None], axis=1)
-    send_rows = jnp.take(tokens, source_idx.reshape(-1), axis=0)
-    send_rows = jnp.where(present.reshape(-1, 1) > 0, send_rows, jnp.zeros_like(send_rows))
+    pick = (source_idx.reshape(-1, 1) == jnp.arange(tok_count, dtype=jnp.int32)[None, :]) & (
+        present.reshape(-1, 1) > 0
+    )
+    send_rows = jnp.dot(pick.astype(tokens.dtype), tokens, preferred_element_type=jnp.float32).astype(tokens.dtype)
     row_in = lax.all_to_all(send_rows, "expert", split_axis=0, concat_axis=0, tiled=True)
     blocks = gather_dp(row_in, dp_count)
     rows = row_in.shape[0]

time: 134 us -> 136 us (1.015)
  local copies, waits for them, and re-layouts: 6.04 us -> 7.76 us
  matrix products: 9.59 us -> 11 us
    all_to_all x1 -> x2, local copies, waits for them, and re-layouts: 0.21 us -> 3.45 us  [layer(): lax.all_to_all(send_rows, 'expert', split_axis=0, concat_axis=0, tiled=True)]
    gather x2 -> x0, local copies, waits for them, and re-layouts: 1.45 us -> none  [layer(): send_rows = jnp.take(tokens, source_idx.reshape(-1), axis=0)]
    dot_general x0 -> x1, matrix products: none -> 1.38 us  [layer(): jnp.dot(pick.astype(tokens.dtype), tokens, preferred_element_type=jnp.flo...]
  transfers between devices with their start and end apart: 15 -> 16, of which waited for: 7 -> 7; matrix products, arithmetic and copies ran while one was open for 5% -> 5% of each run, Pallas kernels for 0% -> 0%
where the time goes in v16:
time: 136 us; the launch traced here: 134 us
  waiting for transfers between devices  68.4 us (50%)
  blocking collectives  21.7 us (16%)
  starting transfers between devices  20.8 us (15%)
  matrix products  11 us (8%)
  local copies, waits for them, and re-layouts  7.76 us (6%)
  other arithmetic  3.43 us (3%)
    all_to_all x1, blocking collectives, layer(): lax.all_to_all(send_rows, 'expert', split_axis=0, concat_axis=0, tiled=True)  21.7 us
    ppermute x1, waiting for transfers between devices, scatter_dp(): a_a = lax.ppermute(s_a, 'dp', dp_pairs(dp_count, 1)).astype(f32)  19.2 us
    ppermute x1, waiting for transfers between devices, gather_dp(): up = lax.ppermute(x, 'dp', dp_pairs(dp_count, 1))  19 us
    all_to_all x1, waiting for transfers between devices, layer(): lax.all_to_all(summed, 'expert', split_axis=0, concat_axis=0, tiled=True)  12.3 us
    ppermute x1, waiting for transfers between devices, scatter_dp(): r_a = lax.ppermute(q_far[:, :half], 'dp', dp_pairs(dp_count, 1)).astype(f32)  9.71 us
    ppermute x1, waiting for transfers between devices, gather_dp(): far_a = lax.ppermute(up[:, :half], 'dp', dp_pairs(dp_count, 1))  7.6 us
    all_to_all x1, starting transfers between devices, layer(): lax.all_to_all(summed, 'expert', split_axis=0, concat_axis=0, tiled=True)  5.63 us
    all_to_all x2, local copies, waits for them, and re-layouts, layer(): lax.all_to_all(send_rows, 'expert', split_axis=0, concat_axis=0, tiled=True)  3.45 us
  transfers between devices with their start and end apart: 16, of which 7 were waited for; matrix products, arithmetic and copies ran while one was open for 5% of the time, Pallas kernels for 0%

profile of v16, /device:TPU:6, one launch (start us, length us, event | category | flops | bytes accessed | tf_op | source)
XLA Modules:
  0.0 133.5 jit_solution(15157767141640569936)
XLA Ops:
  0.0 0.9 multiply_subtract_fusion
  0.9 0.8 fusion.48
  2.5 1.4 %convolution_convert_fusion.2 = bf16[64,7168]{1,0:T(8,128)(2,1)} fusion(bf16[128,7168]{1,0:T(8,128)(2,1)S(1)} %copy-done, s32[64]{0:T(128)S(1)} %eq.57, pred[64]{0:T(512)(128)(4,1)S(1)} %gt.23), kind=kOutput, calls=%fused_computation.6 | convolution fusion | flops 117915648 | bytes 2752832 | tf_op jit(solution)/shard_map/dot_general | solution.py:87
  3.8 1.8 %all_to_all.11 = bf16[16,4,7168]{2,1,0:T(4,128)(2,1)S(1)} reshape(bf16[64,7168]{1,0:T(8,128)(2,1)} %convolution_convert_fusion.2) | data formatting | bytes 1835008 | tf_op jit(solution)/shard_map/all_to_all | solution.py:88
  5.6 21.7 %all_to_all.17 = bf16[16,4,7168]{2,1,0:T(4,128)(2,1)} all-to-all(bf16[16,4,7168]{2,1,0:T(4,128)(2,1)S(1)} %all_to_all.11), channel_id=1, replica_groups=mesh['dp'=8,'expert'=16] {'expert'}, dimensions={0} | all-to-all | bytes 1835008 | tf_op jit(solution)/shard_map/all_to_all | solution.py:88
  27.4 1.7 %all_to_all.13 = bf16[64,7168]{1,0:T(8,128)(2,1)S(1)} reshape(bf16[16,4,7168]{2,1,0:T(4,128)(2,1)} %all_to_all.17) | data formatting | bytes 1835008 | tf_op jit(solution)/shard_map/all_to_all | solution.py:88
  29.0 1.6 %collective-permute-start.1 = (bf16[64,7168]{1,0:T(8,128)(2,1)S(1)}, bf16[64,7168]{1,0:T(8,128)(2,1)S(1)}, u32[]{:S(2)}, u32[]{:S(2)}) collective-permute-start(bf16[64,7168]{1,0:T(8,128)(2,1)S(1)} %all_to_all.13), channel_id=1, source_target_pairs={{0,32},{16,48},{32,64},{48,80},{64,96},{80,112},{96,0},{112,16},{1... | collective-permute-start | bytes 2752520 | tf_op jit(solution)/shard_map/ppermute | solution.py:30
  30.7 1.7 %collective-permute-start.3 = (bf16[64,7168]{1,0:T(8,128)(2,1)S(1)}, bf16[64,7168]{1,0:T(8,128)(2,1)S(1)}, u32[]{:S(2)}, u32[]{:S(2)}) collective-permute-start(bf16[64,7168]{1,0:T(8,128)(2,1)S(1)} %all_to_all.13), channel_id=1, source_target_pairs={{0,96},{16,112},{32,0},{48,16},{64,32},{80,48},{96,64},{112,80},{1... | collective-permute-start | bytes 2752520 | tf_op jit(solution)/shard_map/ppermute | solution.py:31
  32.4 19.0 %collective-permute-done.1 = bf16[64,7168]{1,0:T(8,128)(2,1)S(1)} collective-permute-done((bf16[64,7168]{1,0:T(8,128)(2,1)S(1)}, bf16[64,7168]{1,0:T(8,128)(2,1)S(1)}, u32[]{:S(2)}, u32[]{:S(2)}) %collective-permute-start.1) | collective-permute-done | bytes 917536 | tf_op jit(solution)/shard_map/ppermute | solution.py:30
  51.8 3.0 %collective-permute-start.6 = (bf16[64,3584]{1,0:T(8,128)(2,1)S(1)}, bf16[64,3584]{1,0:T(8,128)(2,1)S(1)}, u32[]{:S(2)}, u32[]{:S(2)}) collective-permute-start(bf16[64,3584]{1,0:T(8,128)(2,1)S(1)} %slice.106), channel_id=1, source_target_pairs={{0,96},{16,112},{32,0},{48,16},{64,32},{80,48},{96,64},{112,80},{1... | collective-permute-start | bytes 1376264 | tf_op jit(solution)/shard_map/ppermute | solution.py:34
  54.8 0.5 collective-permute-start.4
  55.5 7.6 %collective-permute-done.5 = bf16[64,3584]{1,0:T(8,128)(2,1)S(1)} collective-permute-done((bf16[64,3584]{1,0:T(8,128)(2,1)S(1)}, bf16[64,3584]{1,0:T(8,128)(2,1)S(1)}, u32[]{:S(2)}, u32[]{:S(2)}) %collective-permute-start.5) | collective-permute-done | bytes 458784 | tf_op jit(solution)/shard_map/ppermute | solution.py:33
  63.1 0.5 collective-permute-start.8
  63.8 1.6 %fusion.10 = f32[384,256]{1,0:T(8,128)S(1)} fusion(bf16[384,7168]{1,0:T(8,128)(2,1)S(1)} %constant_dynamic-update-slice_fusion, bf16[1,7168,256]{2,1,0:T(8,128)(2,1)S(1)} %copy-done.3), kind=kOutput, calls=%fused_computation.15 | convolution fusion | flops 1409286144 | bytes 9568256 | tf_op jit(solution)/shard_map/dot_general | solution.py:94
  65.4 0.4 copy-done.4
  65.9 1.6 %multiply_convert_fusion = bf16[384,256]{1,0:T(8,128)(2,1)S(1)} fusion(f32[384,256]{1,0:T(8,128)S(1)} %fusion.10, bf16[384,7168]{1,0:T(8,128)(2,1)S(1)} %constant_dynamic-update-slice_fusion, bf16[1,7168,256]{2,1,0:T(8,128)(2,1)S(1)} %copy-done.4), kind=kOutput, calls=%fused_computation.34 | convolution fusion | flops 1409875968 | bytes 9764864 | tf_op jit(solution)/shard_map/dot_general | solution.py:95
  67.5 0.6 fusion.8
  68.2 0.6 multiply_convert_fusion.1
  68.9 1.3 copy-done.1
  70.2 1.1 convolution_convert_fusion
  71.7 0.8 collective-permute-start.9
  72.5 1.1 convolution_convert_fusion.1
  74.4 3.2 %collective-permute-start.13 = (bf16[64,3584]{1,0:T(8,128)(2,1)S(1)}, bf16[64,3584]{1,0:T(8,128)(2,1)S(1)}, u32[]{:S(2)}, u32[]{:S(2)}) collective-permute-start(bf16[64,3584]{1,0:T(8,128)(2,1)S(1)} %get-tuple-element.14), channel_id=1, source_target_pairs={{0,96},{16,112},{32,0},{48,16},{64,32},{80,48},{96,64},{112,80},{1... | collective-permute-start | bytes 1376264 | tf_op jit(solution)/shard_map/ppermute | solution.py:58
  78.4 9.7 %collective-permute-done.11 = bf16[64,3584]{1,0:T(8,128)(2,1)S(1)} collective-permute-done((bf16[64,3584]{1,0:T(8,128)(2,1)S(1)}, bf16[64,3584]{1,0:T(8,128)(2,1)S(1)}, u32[]{:S(2)}, u32[]{:S(2)}) %collective-permute-start.11) | collective-permute-done | bytes 458784 | tf_op jit(solution)/shard_map/ppermute | solution.py:57
  88.6 3.3 %collective-permute-start.14 = (bf16[64,7168]{1,0:T(8,128)(2,1)S(1)}, bf16[64,7168]{1,0:T(8,128)(2,1)S(1)}, u32[]{:S(2)}, u32[]{:S(2)}) collective-permute-start(bf16[64,7168]{1,0:T(8,128)(2,1)S(1)} %pad_maximum_fusion.1), channel_id=1, source_target_pairs={{0,96},{16,112},{32,0},{48,16},{64,32},{80,48},{96,64},{112,80},{1... | collective-permute-start | bytes 2752520 | tf_op jit(solution)/shard_map/ppermute | solution.py:62
  91.9 19.2 %collective-permute-done.12 = bf16[64,7168]{1,0:T(8,128)(2,1)S(1)} collective-permute-done((bf16[64,7168]{1,0:T(8,128)(2,1)S(1)}, bf16[64,7168]{1,0:T(8,128)(2,1)S(1)}, u32[]{:S(2)}, u32[]{:S(2)}) %collective-permute-start.12) | collective-permute-done | bytes 917536 | tf_op jit(solution)/shard_map/ppermute | solution.py:61
  111.1 0.5 add_convert_fusion
  111.5 1.3 reshape.70
  112.8 5.6 %all-to-all-start.1 = ((bf16[16,4,7168]{2,1,0:T(4,128)(2,1)}), bf16[16,4,7168]{2,1,0:T(4,128)(2,1)S(1)}, u32[]{:S(2)}, u32[]{:S(2)}) async-start(bf16[16,4,7168]{2,1,0:T(4,128)(2,1)} %reshape.70), calls=%async_computation.1 | async-start | bytes 1835008 | tf_op jit(solution)/shard_map/all_to_all | solution.py:108
  118.6 12.3 %all-to-all-done.1 = bf16[16,4,7168]{2,1,0:T(4,128)(2,1)S(1)} async-done(((bf16[16,4,7168]{2,1,0:T(4,128)(2,1)}), bf16[16,4,7168]{2,1,0:T(4,128)(2,1)S(1)}, u32[]{:S(2)}, u32[]{:S(2)}) %all-to-all-start.1) | async-done | bytes 917536 | tf_op jit(solution)/shard_map/all_to_all | solution.py:108
  130.8 0.7 convolution_bitcast_fusion
  131.6 2.0 %fusion.1 = bf16[128,7168]{1,0:T(8,128)(2,1)} fusion(f32[128,7168]{1,0:T(8,128)S(1)} %convolution_bitcast_fusion, bf16[16,4,7168]{2,1,0:T(4,128)(2,1)S(1)} %all-to-all-done.1, f32[16,4]{0,1:T(4,128)S(1)} %select_reduce_fusion, s32[16,4]{0,1:T(4,128)S(1)} %get-tuple-element.10, pred[16,4]{0,1:T(4,128)(4,1)S(1)} %broadcast_compare_fusion), kind=kOutput, calls=%fused_computation.5 | convolution fusion | flops 119300096 | bytes 6423104 | tf_op jit(solution)/shard_map/dot_general | solution.py:118
  (57 shorter events, 4.1 us)
Async XLA Ops:
  0.0 2.5 %copy-start = (bf16[128,7168]{1,0:T(8,128)(2,1)S(1)}, bf16[128,7168]{1,0:T(8,128)(2,1)}, u32[]{:S(2)}) copy-start(bf16[128,7168]{1,0:T(8,128)(2,1)} %param.6) | copy-start | bytes 5505028
  29.0 22.4 %collective-permute-start.1 = (bf16[64,7168]{1,0:T(8,128)(2,1)S(1)}, bf16[64,7168]{1,0:T(8,128)(2,1)S(1)}, u32[]{:S(2)}, u32[]{:S(2)}) collective-permute-start(bf16[64,7168]{1,0:T(8,128)(2,1)S(1)} %all_to_all.13), channel_id=1, source_target_pairs={{0,32},{16,48},{32,64},{48,80},{64,96},{80,112},{96,0},{112,16},{1... | collective-permute-start | bytes 2752520 | tf_op jit(solution)/shard_map/ppermute | solution.py:30
  30.7 21.1 %collective-permute-start.3 = (bf16[64,7168]{1,0:T(8,128)(2,1)S(1)}, bf16[64,7168]{1,0:T(8,128)(2,1)S(1)}, u32[]{:S(2)}, u32[]{:S(2)}) collective-permute-start(bf16[64,7168]{1,0:T(8,128)(2,1)S(1)} %all_to_all.13), channel_id=1, source_target_pairs={{0,96},{16,112},{32,0},{48,16},{64,32},{80,48},{96,64},{112,80},{1... | collective-permute-start | bytes 2752520 | tf_op jit(solution)/shard_map/ppermute | solution.py:31
  32.3 23.0 %collective-permute-start = (bf16[64,7168]{1,0:T(8,128)(2,1)S(1)}, bf16[64,7168]{1,0:T(8,128)(2,1)S(1)}, u32[]{:S(2)}, u32[]{:S(2)}) collective-permute-start(bf16[64,7168]{1,0:T(8,128)(2,1)S(1)} %all_to_all.13), channel_id=1, source_target_pairs={{0,16},{16,0},{32,48},{48,32},{64,80},{80,64},{96,112},{112,96},{1... | collective-permute-start | bytes 2752520 | tf_op jit(solution)/shard_map/ppermute | solution.py:32
  51.4 11.7 %collective-permute-start.5 = (bf16[64,3584]{1,0:T(8,128)(2,1)S(1)}, bf16[64,3584]{1,0:T(8,128)(2,1)S(1)}, u32[]{:S(2)}, u32[]{:S(2)}) collective-permute-start(bf16[64,3584]{1,0:T(8,128)(2,1)S(1)} %slice.105), channel_id=1, source_target_pairs={{0,32},{16,48},{32,64},{48,80},{64,96},{80,112},{96,0},{112,16},{1... | collective-permute-start | bytes 1376264 | tf_op jit(solution)/shard_map/ppermute | solution.py:33
  51.8 11.3 %collective-permute-start.6 = (bf16[64,3584]{1,0:T(8,128)(2,1)S(1)}, bf16[64,3584]{1,0:T(8,128)(2,1)S(1)}, u32[]{:S(2)}, u32[]{:S(2)}) collective-permute-start(bf16[64,3584]{1,0:T(8,128)(2,1)S(1)} %slice.106), channel_id=1, source_target_pairs={{0,96},{16,112},{32,0},{48,16},{64,32},{80,48},{96,64},{112,80},{1... | collective-permute-start | bytes 1376264 | tf_op jit(solution)/shard_map/ppermute | solution.py:34
  54.8 8.8 %collective-permute-start.2 = (bf16[64,7168]{1,0:T(8,128)(2,1)S(1)}, bf16[64,7168]{1,0:T(8,128)(2,1)S(1)}, u32[]{:S(2)}, u32[]{:S(2)}) collective-permute-start(bf16[64,7168]{1,0:T(8,128)(2,1)S(1)} %collective-permute-done.1), channel_id=1, source_target_pairs={{0,16},{16,0},{32,48},{48,32},{64,80},{80,64},{96,112},{112,96},{1... | collective-permute-start | bytes 2752520 | tf_op jit(solution)/shard_map/ppermute | solution.py:36
  54.8 8.9 %collective-permute-start.4 = (bf16[64,7168]{1,0:T(8,128)(2,1)S(1)}, bf16[64,7168]{1,0:T(8,128)(2,1)S(1)}, u32[]{:S(2)}, u32[]{:S(2)}) collective-permute-start(bf16[64,7168]{1,0:T(8,128)(2,1)S(1)} %collective-permute-done.3), channel_id=1, source_target_pairs={{0,16},{16,0},{32,48},{48,32},{64,80},{80,64},{96,112},{112,96},{1... | collective-permute-start | bytes 2752520 | tf_op jit(solution)/shard_map/ppermute | solution.py:37
  55.4 8.4 %copy-start.3 = (bf16[1,7168,256]{2,1,0:T(8,128)(2,1)S(1)}, bf16[1,7168,256]{2,1,0:T(8,128)(2,1)}, u32[]{:S(2)}) copy-start(bf16[1,7168,256]{2,1,0:T(8,128)(2,1)} %param.9) | copy-start | bytes 11010052
  63.1 4.4 %collective-permute-start.7 = (bf16[64,3584]{1,0:T(8,128)(2,1)S(1)}, bf16[64,3584]{1,0:T(8,128)(2,1)S(1)}, u32[]{:S(2)}, u32[]{:S(2)}) collective-permute-start(bf16[64,3584]{1,0:T(8,128)(2,1)S(1)} %collective-permute-done.5), channel_id=1, source_target_pairs={{0,16},{16,0},{32,48},{48,32},{64,80},{80,64},{96,112},{112,96},{1... | collective-permute-start | bytes 1376264 | tf_op jit(solution)/shard_map/ppermute | solution.py:39
  63.1 4.4 %collective-permute-start.8 = (bf16[64,3584]{1,0:T(8,128)(2,1)S(1)}, bf16[64,3584]{1,0:T(8,128)(2,1)S(1)}, u32[]{:S(2)}, u32[]{:S(2)}) collective-permute-start(bf16[64,3584]{1,0:T(8,128)(2,1)S(1)} %collective-permute-done.6), channel_id=1, source_target_pairs={{0,16},{16,0},{32,48},{48,32},{64,80},{80,64},{96,112},{112,96},{1... | collective-permute-start | bytes 1376264 | tf_op jit(solution)/shard_map/ppermute | solution.py:39
  63.8 2.0 %copy-start.4 = (bf16[1,7168,256]{2,1,0:T(8,128)(2,1)S(1)}, bf16[1,7168,256]{2,1,0:T(8,128)(2,1)}, u32[]{:S(2)}) copy-start(bf16[1,7168,256]{2,1,0:T(8,128)(2,1)} %param.10) | copy-start | bytes 11010052
  68.2 2.0 %copy-start.1 = (bf16[1,256,7168]{2,1,0:T(8,128)(2,1)S(1)}, bf16[1,256,7168]{2,1,0:T(8,128)(2,1)}, u32[]{:S(2)}) copy-start(bf16[1,256,7168]{2,1,0:T(8,128)(2,1)} %param.11) | copy-start | bytes 11010052
  71.4 2.6 %collective-permute-start.10 = (bf16[64,7168]{1,0:T(8,128)(2,1)S(1)}, bf16[64,7168]{1,0:T(8,128)(2,1)S(1)}, u32[]{:S(2)}, u32[]{:S(2)}) collective-permute-start(bf16[64,7168]{1,0:T(8,128)(2,1)S(1)} %slice.122), channel_id=1, source_target_pairs={{0,16},{16,0},{32,48},{48,32},{64,80},{80,64},{96,112},{112,96},{1... | collective-permute-start | bytes 2752520 | tf_op jit(solution)/shard_map/ppermute | solution.py:49
  71.7 6.2 %collective-permute-start.9 = (bf16[192,7168]{1,0:T(8,128)(2,1)S(1)}, bf16[192,7168]{1,0:T(8,128)(2,1)S(1)}, u32[]{:S(2)}, u32[]{:S(2)}) collective-permute-start(bf16[192,7168]{1,0:T(8,128)(2,1)S(1)} %slice.116), channel_id=1, source_target_pairs={{0,16},{16,0},{32,48},{48,32},{64,80},{80,64},{96,112},{112,96},{1... | collective-permute-start | bytes 8257544 | tf_op jit(solution)/shard_map/ppermute | solution.py:50
  74.3 13.8 %collective-permute-start.11 = (bf16[64,3584]{1,0:T(8,128)(2,1)S(1)}, bf16[64,3584]{1,0:T(8,128)(2,1)S(1)}, u32[]{:S(2)}, u32[]{:S(2)}) collective-permute-start(bf16[64,3584]{1,0:T(8,128)(2,1)S(1)} %get-tuple-element.13), channel_id=1, source_target_pairs={{0,32},{16,48},{32,64},{48,80},{64,96},{80,112},{96,0},{112,16},{1... | collective-permute-start | bytes 1376264 | tf_op jit(solution)/shard_map/ppermute | solution.py:57
  74.4 14.0 %collective-permute-start.13 = (bf16[64,3584]{1,0:T(8,128)(2,1)S(1)}, bf16[64,3584]{1,0:T(8,128)(2,1)S(1)}, u32[]{:S(2)}, u32[]{:S(2)}) collective-permute-start(bf16[64,3584]{1,0:T(8,128)(2,1)S(1)} %get-tuple-element.14), channel_id=1, source_target_pairs={{0,96},{16,112},{32,0},{48,16},{64,32},{80,48},{96,64},{112,80},{1... | collective-permute-start | bytes 1376264 | tf_op jit(solution)/shard_map/ppermute | solution.py:58
  88.3 22.8 %collective-permute-start.12 = (bf16[64,7168]{1,0:T(8,128)(2,1)S(1)}, bf16[64,7168]{1,0:T(8,128)(2,1)S(1)}, u32[]{:S(2)}, u32[]{:S(2)}) collective-permute-start(bf16[64,7168]{1,0:T(8,128)(2,1)S(1)} %pad_maximum_fusion), channel_id=1, source_target_pairs={{0,32},{16,48},{32,64},{48,80},{64,96},{80,112},{96,0},{112,16},{1... | collective-permute-start | bytes 2752520 | tf_op jit(solution)/shard_map/ppermute | solution.py:61
  88.6 29.8 %copy-start.2 = (s32[16,288]{1,0:T(8,128)S(1)}, s32[16,288]{1,0:T(8,128)}, u32[]{:S(2)}) copy-start(s32[16,288]{1,0:T(8,128)} %param.8) | copy-start | bytes 55300
  88.6 22.5 %collective-permute-start.14 = (bf16[64,7168]{1,0:T(8,128)(2,1)S(1)}, bf16[64,7168]{1,0:T(8,128)(2,1)S(1)}, u32[]{:S(2)}, u32[]{:S(2)}) collective-permute-start(bf16[64,7168]{1,0:T(8,128)(2,1)S(1)} %pad_maximum_fusion.1), channel_id=1, source_target_pairs={{0,96},{16,112},{32,0},{48,16},{64,32},{80,48},{96,64},{112,80},{1... | collective-permute-start | bytes 2752520 | tf_op jit(solution)/shard_map/ppermute | solution.py:62
  112.8 18.0 %all-to-all-start.1 = ((bf16[16,4,7168]{2,1,0:T(4,128)(2,1)}), bf16[16,4,7168]{2,1,0:T(4,128)(2,1)S(1)}, u32[]{:S(2)}, u32[]{:S(2)}) async-start(bf16[16,4,7168]{2,1,0:T(4,128)(2,1)} %reshape.70), calls=%async_computation.1 | async-start | bytes 1835008 | tf_op jit(solution)/shard_map/all_to_all | solution.py:108

commit v17 on v16

--- a/solution.py
+++ b/solution.py
@@ -35,9 +35,7 @@
     far = jnp.concatenate([far_a, far_b], axis=1)
     s_up = lax.ppermute(up, "dp", sib_pairs(dp_count))
     s_dn = lax.ppermute(dn, "dp", sib_pairs(dp_count))
-    s_far = jnp.concatenate(
-        [lax.ppermute(far_a, "dp", sib_pairs(dp_count)), lax.ppermute(far_b, "dp", sib_pairs(dp_count))], axis=1
-    )
+    s_far = lax.ppermute(far, "dp", sib_pairs(dp_count))
     return [x, sib, up, s_up, dn, s_dn, far, s_far]
 
 
@@ -94,7 +92,7 @@
         gate_act = jnp.dot(picked, w_gate[0], preferred_element_type=jnp.float32)
         up_act = jnp.dot(picked, w_up[0], preferred_element_type=jnp.float32)
         hidden.append((jax.nn.silu(gate_act) * up_act).astype(jnp.bfloat16))
-    hidden = lax.optimization_barrier(jnp.concatenate(hidden, axis=0))
+    hidden = jnp.concatenate(hidden, axis=0)
     hb = [hidden[i * rows:(i + 1) * rows] for i in range(8)]
     result = [None] * 8
     for group in ((1, 3, 5, 7), (0, 2, 4, 6)):

time: 136 us -> 132 us (0.971)
  local copies, waits for them, and re-layouts: 7.76 us -> 4.96 us
    all_to_all x2, local copies, waits for them, and re-layouts: 3.45 us -> 0.54 us  [layer(): lax.all_to_all(send_rows, 'expert', split_axis=0, concat_axis=0, tiled=True)]
  transfers between devices with their start and end apart: 16 -> 15, of which waited for: 7 -> 7; matrix products, arithmetic and copies ran while one was open for 5% -> 5% of each run, Pallas kernels for 0% -> 0%
where the time goes in v17:
time: 132 us; the launch traced here: 130 us
  waiting for transfers between devices  69.4 us (53%)
  blocking collectives  21.6 us (16%)
  starting transfers between devices  20.4 us (15%)
  matrix products  10 us (8%)
  local copies, waits for them, and re-layouts  4.96 us (4%)
  other arithmetic  3.44 us (3%)
    all_to_all x1, blocking collectives, layer(): lax.all_to_all(send_rows, 'expert', split_axis=0, concat_axis=0, tiled=True)  21.6 us
    ppermute x1, waiting for transfers between devices, scatter_dp(): a_a = lax.ppermute(s_a, 'dp', dp_pairs(dp_count, 1)).astype(f32)  19.5 us
    ppermute x1, waiting for transfers between devices, gather_dp(): up = lax.ppermute(x, 'dp', dp_pairs(dp_count, 1))  19 us
    all_to_all x1, waiting for transfers between devices, layer(): lax.all_to_all(summed, 'expert', split_axis=0, concat_axis=0, tiled=True)  12.5 us
    ppermute x1, waiting for transfers between devices, scatter_dp(): r_a = lax.ppermute(q_far[:, :half], 'dp', dp_pairs(dp_count, 1)).astype(f32)  10 us
    ppermute x1, waiting for transfers between devices, gather_dp(): far_a = lax.ppermute(up[:, :half], 'dp', dp_pairs(dp_count, 1))  7.6 us
    all_to_all x1, starting transfers between devices, layer(): lax.all_to_all(summed, 'expert', split_axis=0, concat_axis=0, tiled=True)  5.63 us
    ppermute x1, starting transfers between devices, scatter_dp(): a_b = lax.ppermute(s_b, 'dp', dp_pairs(dp_count, -1)).astype(f32)  3.29 us
  transfers between devices with their start and end apart: 15, of which 7 were waited for; matrix products, arithmetic and copies ran while one was open for 5% of the time, Pallas kernels for 0%

profile of v17, /device:TPU:6, one launch (start us, length us, event | category | flops | bytes accessed | tf_op | source)
XLA Modules:
  0.0 130.3 jit_solution(10440808863808248079)
XLA Ops:
  0.0 0.9 multiply_subtract_fusion
  0.9 0.8 fusion.48
  2.5 0.5 convolution_convert_fusion.2
  3.3 21.6 %all_to_all.17 = bf16[16,4,7168]{2,1,0:T(4,128)(2,1)S(1)} all-to-all(bf16[16,4,7168]{2,1,0:T(4,128)(2,1)S(1)} %all_to_all.11), channel_id=1, replica_groups=mesh['dp'=8,'expert'=16] {'expert'}, dimensions={0} | all-to-all | bytes 1835008 | tf_op jit(solution)/shard_map/all_to_all | solution.py:86
  25.1 1.6 %collective-permute-start.1 = (bf16[64,7168]{1,0:T(8,128)(2,1)S(1)}, bf16[64,7168]{1,0:T(8,128)(2,1)S(1)}, u32[]{:S(2)}, u32[]{:S(2)}) collective-permute-start(bf16[64,7168]{1,0:T(8,128)(2,1)S(1)} %all_to_all.13), channel_id=1, source_target_pairs={{0,32},{16,48},{32,64},{48,80},{64,96},{80,112},{96,0},{112,16},{1... | collective-permute-start | bytes 2752520 | tf_op jit(solution)/shard_map/ppermute | solution.py:30
  26.7 1.7 %collective-permute-start.3 = (bf16[64,7168]{1,0:T(8,128)(2,1)S(1)}, bf16[64,7168]{1,0:T(8,128)(2,1)S(1)}, u32[]{:S(2)}, u32[]{:S(2)}) collective-permute-start(bf16[64,7168]{1,0:T(8,128)(2,1)S(1)} %all_to_all.13), channel_id=1, source_target_pairs={{0,96},{16,112},{32,0},{48,16},{64,32},{80,48},{96,64},{112,80},{1... | collective-permute-start | bytes 2752520 | tf_op jit(solution)/shard_map/ppermute | solution.py:31
  28.5 19.0 %collective-permute-done.1 = bf16[64,7168]{1,0:T(8,128)(2,1)S(1)} collective-permute-done((bf16[64,7168]{1,0:T(8,128)(2,1)S(1)}, bf16[64,7168]{1,0:T(8,128)(2,1)S(1)}, u32[]{:S(2)}, u32[]{:S(2)}) %collective-permute-start.1) | collective-permute-done | bytes 917536 | tf_op jit(solution)/shard_map/ppermute | solution.py:30
  47.9 3.0 %collective-permute-start.6 = (bf16[64,3584]{1,0:T(8,128)(2,1)S(1)}, bf16[64,3584]{1,0:T(8,128)(2,1)S(1)}, u32[]{:S(2)}, u32[]{:S(2)}) collective-permute-start(bf16[64,3584]{1,0:T(8,128)(2,1)S(1)} %slice.109), channel_id=1, source_target_pairs={{0,96},{16,112},{32,0},{48,16},{64,32},{80,48},{96,64},{112,80},{1... | collective-permute-start | bytes 1376264 | tf_op jit(solution)/shard_map/ppermute | solution.py:34
  50.9 0.5 collective-permute-start.4
  51.6 7.6 %collective-permute-done.5 = bf16[64,3584]{1,0:T(8,128)(2,1)S(1)} collective-permute-done((bf16[64,3584]{1,0:T(8,128)(2,1)S(1)}, bf16[64,3584]{1,0:T(8,128)(2,1)S(1)}, u32[]{:S(2)}, u32[]{:S(2)}) %collective-permute-start.5) | collective-permute-done | bytes 458784 | tf_op jit(solution)/shard_map/ppermute | solution.py:33
  59.6 1.6 %fusion.10 = f32[384,256]{1,0:T(8,128)S(1)} fusion(bf16[384,7168]{1,0:T(8,128)(2,1)S(1)} %constant_dynamic-update-slice_fusion, bf16[1,7168,256]{2,1,0:T(8,128)(2,1)S(1)} %copy-done.4), kind=kOutput, calls=%fused_computation.15 | convolution fusion | flops 1409286144 | bytes 9568256 | tf_op jit(solution)/shard_map/dot_general | solution.py:92
  61.2 0.4 copy-done.5
  61.6 1.6 %multiply_convert_fusion = bf16[384,256]{1,0:T(8,128)(2,1)S(1)} fusion(f32[384,256]{1,0:T(8,128)S(1)} %fusion.10, bf16[384,7168]{1,0:T(8,128)(2,1)S(1)} %constant_dynamic-update-slice_fusion, bf16[1,7168,256]{2,1,0:T(8,128)(2,1)S(1)} %copy-done.5), kind=kOutput, calls=%fused_computation.34 | convolution fusion | flops 1409875968 | bytes 9764864 | tf_op jit(solution)/shard_map/dot_general | solution.py:93
  63.2 0.6 fusion.8
  63.9 0.6 multiply_convert_fusion.1
  64.6 1.4 %copy-done.2 = bf16[1,256,7168]{2,1,0:T(8,128)(2,1)S(1)} copy-done((bf16[1,256,7168]{2,1,0:T(8,128)(2,1)S(1)}, bf16[1,256,7168]{2,1,0:T(8,128)(2,1)}, u32[]{:S(2)}) %copy-start.2) | copy-done | bytes 3670040
  65.9 1.1 convolution_convert_fusion
  67.1 0.6 collective-permute-start.9
  68.2 1.1 convolution_convert_fusion.1
  69.4 0.4 collective-permute-done.9
  70.1 0.4 collective-permute-start.10
  70.5 2.9 %collective-permute-start.12 = (bf16[64,3584]{1,0:T(8,128)(2,1)S(1)}, bf16[64,3584]{1,0:T(8,128)(2,1)S(1)}, u32[]{:S(2)}, u32[]{:S(2)}) collective-permute-start(bf16[64,3584]{1,0:T(8,128)(2,1)S(1)} %get-tuple-element.14), channel_id=1, source_target_pairs={{0,96},{16,112},{32,0},{48,16},{64,32},{80,48},{96,64},{112,80},{1... | collective-permute-start | bytes 1376264 | tf_op jit(solution)/shard_map/ppermute | solution.py:56
  73.7 0.4 convert_add_fusion.1
  74.2 10.0 %collective-permute-done.10 = bf16[64,3584]{1,0:T(8,128)(2,1)S(1)} collective-permute-done((bf16[64,3584]{1,0:T(8,128)(2,1)S(1)}, bf16[64,3584]{1,0:T(8,128)(2,1)S(1)}, u32[]{:S(2)}, u32[]{:S(2)}) %collective-permute-start.10) | collective-permute-done | bytes 458784 | tf_op jit(solution)/shard_map/ppermute | solution.py:55
  84.8 3.3 %collective-permute-start.13 = (bf16[64,7168]{1,0:T(8,128)(2,1)S(1)}, bf16[64,7168]{1,0:T(8,128)(2,1)S(1)}, u32[]{:S(2)}, u32[]{:S(2)}) collective-permute-start(bf16[64,7168]{1,0:T(8,128)(2,1)S(1)} %pad_maximum_fusion.4), channel_id=1, source_target_pairs={{0,96},{16,112},{32,0},{48,16},{64,32},{80,48},{96,64},{112,80},{1... | collective-permute-start | bytes 2752520 | tf_op jit(solution)/shard_map/ppermute | solution.py:60
  88.0 19.5 %collective-permute-done.11 = bf16[64,7168]{1,0:T(8,128)(2,1)S(1)} collective-permute-done((bf16[64,7168]{1,0:T(8,128)(2,1)S(1)}, bf16[64,7168]{1,0:T(8,128)(2,1)S(1)}, u32[]{:S(2)}, u32[]{:S(2)}) %collective-permute-start.11) | collective-permute-done | bytes 917536 | tf_op jit(solution)/shard_map/ppermute | solution.py:59
  107.5 0.5 add_convert_fusion
  108.0 1.3 reshape.70
  109.2 5.6 %all-to-all-start.1 = ((bf16[16,4,7168]{2,1,0:T(4,128)(2,1)}), bf16[16,4,7168]{2,1,0:T(4,128)(2,1)S(1)}, u32[]{:S(2)}, u32[]{:S(2)}) async-start(bf16[16,4,7168]{2,1,0:T(4,128)(2,1)} %reshape.70), calls=%async_computation.1 | async-start | bytes 1835008 | tf_op jit(solution)/shard_map/all_to_all | solution.py:106
  115.0 12.5 %all-to-all-done.1 = bf16[16,4,7168]{2,1,0:T(4,128)(2,1)S(1)} async-done(((bf16[16,4,7168]{2,1,0:T(4,128)(2,1)}), bf16[16,4,7168]{2,1,0:T(4,128)(2,1)S(1)}, u32[]{:S(2)}, u32[]{:S(2)}) %all-to-all-start.1) | async-done | bytes 917536 | tf_op jit(solution)/shard_map/all_to_all | solution.py:106
  127.5 0.7 convolution_bitcast_fusion
  128.3 2.0 %fusion.1 = bf16[128,7168]{1,0:T(8,128)(2,1)} fusion(f32[128,7168]{1,0:T(8,128)S(1)} %convolution_bitcast_fusion, bf16[16,4,7168]{2,1,0:T(4,128)(2,1)S(1)} %all-to-all-done.1, f32[16,4]{0,1:T(4,128)S(1)} %select_reduce_fusion, s32[16,4]{0,1:T(4,128)S(1)} %get-tuple-element.10, pred[16,4]{0,1:T(4,128)(4,1)S(1)} %broadcast_compare_fusion), kind=kOutput, calls=%fused_computation.5 | convolution fusion | flops 119300096 | bytes 6423104 | tf_op jit(solution)/shard_map/dot_general | solution.py:116
  (59 shorter events, 4.1 us)
Async XLA Ops:
  0.0 2.5 %copy-start = (bf16[128,7168]{1,0:T(8,128)(2,1)S(1)}, bf16[128,7168]{1,0:T(8,128)(2,1)}, u32[]{:S(2)}) copy-start(bf16[128,7168]{1,0:T(8,128)(2,1)} %param.6) | copy-start | bytes 5505028
  25.1 22.4 %collective-permute-start.1 = (bf16[64,7168]{1,0:T(8,128)(2,1)S(1)}, bf16[64,7168]{1,0:T(8,128)(2,1)S(1)}, u32[]{:S(2)}, u32[]{:S(2)}) collective-permute-start(bf16[64,7168]{1,0:T(8,128)(2,1)S(1)} %all_to_all.13), channel_id=1, source_target_pairs={{0,32},{16,48},{32,64},{48,80},{64,96},{80,112},{96,0},{112,16},{1... | collective-permute-start | bytes 2752520 | tf_op jit(solution)/shard_map/ppermute | solution.py:30
  26.7 21.1 %collective-permute-start.3 = (bf16[64,7168]{1,0:T(8,128)(2,1)S(1)}, bf16[64,7168]{1,0:T(8,128)(2,1)S(1)}, u32[]{:S(2)}, u32[]{:S(2)}) collective-permute-start(bf16[64,7168]{1,0:T(8,128)(2,1)S(1)} %all_to_all.13), channel_id=1, source_target_pairs={{0,96},{16,112},{32,0},{48,16},{64,32},{80,48},{96,64},{112,80},{1... | collective-permute-start | bytes 2752520 | tf_op jit(solution)/shard_map/ppermute | solution.py:31
  28.4 23.0 %collective-permute-start = (bf16[64,7168]{1,0:T(8,128)(2,1)S(1)}, bf16[64,7168]{1,0:T(8,128)(2,1)S(1)}, u32[]{:S(2)}, u32[]{:S(2)}) collective-permute-start(bf16[64,7168]{1,0:T(8,128)(2,1)S(1)} %all_to_all.13), channel_id=1, source_target_pairs={{0,16},{16,0},{32,48},{48,32},{64,80},{80,64},{96,112},{112,96},{1... | collective-permute-start | bytes 2752520 | tf_op jit(solution)/shard_map/ppermute | solution.py:32
  47.5 11.7 %collective-permute-start.5 = (bf16[64,3584]{1,0:T(8,128)(2,1)S(1)}, bf16[64,3584]{1,0:T(8,128)(2,1)S(1)}, u32[]{:S(2)}, u32[]{:S(2)}) collective-permute-start(bf16[64,3584]{1,0:T(8,128)(2,1)S(1)} %slice.108), channel_id=1, source_target_pairs={{0,32},{16,48},{32,64},{48,80},{64,96},{80,112},{96,0},{112,16},{1... | collective-permute-start | bytes 1376264 | tf_op jit(solution)/shard_map/ppermute | solution.py:33
  47.9 11.3 %collective-permute-start.6 = (bf16[64,3584]{1,0:T(8,128)(2,1)S(1)}, bf16[64,3584]{1,0:T(8,128)(2,1)S(1)}, u32[]{:S(2)}, u32[]{:S(2)}) collective-permute-start(bf16[64,3584]{1,0:T(8,128)(2,1)S(1)} %slice.109), channel_id=1, source_target_pairs={{0,96},{16,112},{32,0},{48,16},{64,32},{80,48},{96,64},{112,80},{1... | collective-permute-start | bytes 1376264 | tf_op jit(solution)/shard_map/ppermute | solution.py:34
  50.9 8.4 %collective-permute-start.2 = (bf16[64,7168]{1,0:T(8,128)(2,1)S(1)}, bf16[64,7168]{1,0:T(8,128)(2,1)S(1)}, u32[]{:S(2)}, u32[]{:S(2)}) collective-permute-start(bf16[64,7168]{1,0:T(8,128)(2,1)S(1)} %collective-permute-done.1), channel_id=1, source_target_pairs={{0,16},{16,0},{32,48},{48,32},{64,80},{80,64},{96,112},{112,96},{1... | collective-permute-start | bytes 2752520 | tf_op jit(solution)/shard_map/ppermute | solution.py:36
  50.9 8.6 %collective-permute-start.4 = (bf16[64,7168]{1,0:T(8,128)(2,1)S(1)}, bf16[64,7168]{1,0:T(8,128)(2,1)S(1)}, u32[]{:S(2)}, u32[]{:S(2)}) collective-permute-start(bf16[64,7168]{1,0:T(8,128)(2,1)S(1)} %collective-permute-done.3), channel_id=1, source_target_pairs={{0,16},{16,0},{32,48},{48,32},{64,80},{80,64},{96,112},{112,96},{1... | collective-permute-start | bytes 2752520 | tf_op jit(solution)/shard_map/ppermute | solution.py:37
  51.5 8.0 %copy-start.4 = (bf16[1,7168,256]{2,1,0:T(8,128)(2,1)S(1)}, bf16[1,7168,256]{2,1,0:T(8,128)(2,1)}, u32[]{:S(2)}) copy-start(bf16[1,7168,256]{2,1,0:T(8,128)(2,1)} %param.9) | copy-start | bytes 11010052
  59.2 4.0 %collective-permute-start.7 = (bf16[64,7168]{1,0:T(8,128)(2,1)S(1)}, bf16[64,7168]{1,0:T(8,128)(2,1)S(1)}, u32[]{:S(2)}, u32[]{:S(2)}) collective-permute-start(bf16[64,7168]{1,0:T(8,128)(2,1)S(1)} %constant_dynamic-update-slice_fusion.6), channel_id=1, source_target_pairs={{0,16},{16,0},{32,48},{48,32},{64,80},{80,64},{96,112},{112,96},{1... | collective-permute-start | bytes 2752520 | tf_op jit(solution)/shard_map/ppermute | solution.py:38
  59.6 2.0 %copy-start.5 = (bf16[1,7168,256]{2,1,0:T(8,128)(2,1)S(1)}, bf16[1,7168,256]{2,1,0:T(8,128)(2,1)}, u32[]{:S(2)}) copy-start(bf16[1,7168,256]{2,1,0:T(8,128)(2,1)} %param.10) | copy-start | bytes 11010052
  63.9 2.0 %copy-start.2 = (bf16[1,256,7168]{2,1,0:T(8,128)(2,1)S(1)}, bf16[1,256,7168]{2,1,0:T(8,128)(2,1)}, u32[]{:S(2)}) copy-start(bf16[1,256,7168]{2,1,0:T(8,128)(2,1)} %param.11) | copy-start | bytes 11010052
  67.1 2.7 %collective-permute-start.9 = (bf16[64,7168]{1,0:T(8,128)(2,1)S(1)}, bf16[64,7168]{1,0:T(8,128)(2,1)S(1)}, u32[]{:S(2)}, u32[]{:S(2)}) collective-permute-start(bf16[64,7168]{1,0:T(8,128)(2,1)S(1)} %slice.122), channel_id=1, source_target_pairs={{0,16},{16,0},{32,48},{48,32},{64,80},{80,64},{96,112},{112,96},{1... | collective-permute-start | bytes 2752520 | tf_op jit(solution)/shard_map/ppermute | solution.py:47
  67.9 5.8 %collective-permute-start.8 = (bf16[192,7168]{1,0:T(8,128)(2,1)S(1)}, bf16[192,7168]{1,0:T(8,128)(2,1)S(1)}, u32[]{:S(2)}, u32[]{:S(2)}) collective-permute-start(bf16[192,7168]{1,0:T(8,128)(2,1)S(1)} %slice.116), channel_id=1, source_target_pairs={{0,16},{16,0},{32,48},{48,32},{64,80},{80,64},{96,112},{112,96},{1... | collective-permute-start | bytes 8257544 | tf_op jit(solution)/shard_map/ppermute | solution.py:48
  70.1 14.1 %collective-permute-start.10 = (bf16[64,3584]{1,0:T(8,128)(2,1)S(1)}, bf16[64,3584]{1,0:T(8,128)(2,1)S(1)}, u32[]{:S(2)}, u32[]{:S(2)}) collective-permute-start(bf16[64,3584]{1,0:T(8,128)(2,1)S(1)} %get-tuple-element.13), channel_id=1, source_target_pairs={{0,32},{16,48},{32,64},{48,80},{64,96},{80,112},{96,0},{112,16},{1... | collective-permute-start | bytes 1376264 | tf_op jit(solution)/shard_map/ppermute | solution.py:55
  70.5 14.0 %collective-permute-start.12 = (bf16[64,3584]{1,0:T(8,128)(2,1)S(1)}, bf16[64,3584]{1,0:T(8,128)(2,1)S(1)}, u32[]{:S(2)}, u32[]{:S(2)}) collective-permute-start(bf16[64,3584]{1,0:T(8,128)(2,1)S(1)} %get-tuple-element.14), channel_id=1, source_target_pairs={{0,96},{16,112},{32,0},{48,16},{64,32},{80,48},{96,64},{112,80},{1... | collective-permute-start | bytes 1376264 | tf_op jit(solution)/shard_map/ppermute | solution.py:56
  84.4 23.1 %collective-permute-start.11 = (bf16[64,7168]{1,0:T(8,128)(2,1)S(1)}, bf16[64,7168]{1,0:T(8,128)(2,1)S(1)}, u32[]{:S(2)}, u32[]{:S(2)}) collective-permute-start(bf16[64,7168]{1,0:T(8,128)(2,1)S(1)} %pad_maximum_fusion.3), channel_id=1, source_target_pairs={{0,32},{16,48},{32,64},{48,80},{64,96},{80,112},{96,0},{112,16},{1... | collective-permute-start | bytes 2752520 | tf_op jit(solution)/shard_map/ppermute | solution.py:59
  84.7 30.1 %copy-start.3 = (s32[16,288]{1,0:T(8,128)S(1)}, s32[16,288]{1,0:T(8,128)}, u32[]{:S(2)}) copy-start(s32[16,288]{1,0:T(8,128)} %param.8) | copy-start | bytes 55300
  84.8 22.8 %collective-permute-start.13 = (bf16[64,7168]{1,0:T(8,128)(2,1)S(1)}, bf16[64,7168]{1,0:T(8,128)(2,1)S(1)}, u32[]{:S(2)}, u32[]{:S(2)}) collective-permute-start(bf16[64,7168]{1,0:T(8,128)(2,1)S(1)} %pad_maximum_fusion.4), channel_id=1, source_target_pairs={{0,96},{16,112},{32,0},{48,16},{64,32},{80,48},{96,64},{112,80},{1... | collective-permute-start | bytes 2752520 | tf_op jit(solution)/shard_map/ppermute | solution.py:60
  109.2 18.3 %all-to-all-start.1 = ((bf16[16,4,7168]{2,1,0:T(4,128)(2,1)}), bf16[16,4,7168]{2,1,0:T(4,128)(2,1)S(1)}, u32[]{:S(2)}, u32[]{:S(2)}) async-start(bf16[16,4,7168]{2,1,0:T(4,128)(2,1)} %reshape.70), calls=%async_computation.1 | async-start | bytes 1835008 | tf_op jit(solution)/shard_map/all_to_all | solution.py:106
  127.5 2.7 %copy-start.1 = (bf16[128,7168]{1,0:T(8,128)(2,1)S(1)}, bf16[128,7168]{1,0:T(8,128)(2,1)}, u32[]{:S(2)}) copy-start(bf16[128,7168]{1,0:T(8,128)(2,1)} %param.6) | copy-start | bytes 5505028
